TPU v7x, 32 devices: a whole 2x2x4 slice. The times are simulated.
32 devices in a mesh: zone: 2 (over core), axial: 2 (over y), azim: 8 (over z, x).
Axes of the slice: x: 2, y: 2, z: 4, core: 2. Of those that a mesh axis runs over, the one named last changes fastest.
Arguments:
- adjoint: float32 [2, 5, 4, 4, 4, 2048], P('zone', None, None, None, None, ('axial', 'azim')), may hold values from -6 to 6
- flow_prim: bfloat16 [2, 5, 4, 4, 4, 2048], P('zone', None, None, None, None, ('axial', 'azim')), may hold values from -0.75 to 1.5, as said below
- intersection_shift: int32 [4, 4096], P(None, ('axial', 'azim')), may hold values from -8 to 7
- weight_index: int32 [4, 4096], P(None, ('axial', 'azim')), may hold values from 0 to 127
- mortar_weights: float32 [128], replicated, may hold values from 0.2 to 0.6
- sector_offset: int32 [1], replicated, may hold values from 0 to 127
Outputs:
- adjoint_rate: float32 [2, 5, 4, 4, 4, 2048], P('zone', None, None, None, None, ('axial', 'azim'))
- next_adjoint: float32 [2, 5, 4, 4, 4, 2048], P('zone', None, None, None, None, ('axial', 'azim'))
Inputs may be any that keep to these rules, and one draw needn't show every extreme that they name: Entry k of stator interface row (a, t) names the rotor interface point at axial point a and azimuthal point (t + sector_offset + intersection_shift) modulo 128. `flow_prim`: channels are density, three velocity components and pressure; density lies in 0.6 to 1.4, pressure in 0.5 to 1.5, velocity components in -0.75 to 0.75.
All inputs are finite; a program needn't handle non-finite values.
Results may differ from a plain program's by a relative error of at most 0.0003.
Values sent between devices are 32-bit elements; how exact they have to be, the bound alone decides.
No kernel may reach another device: no remote copies, remote signals or barrier semaphores. Data moves between devices by JAX's collectives and lax.ppermute only.
A program may use at most 128 MiB of HBM per device.

v0:
```python
import math

import jax
import jax.numpy as jnp
from jax import lax
from jax.sharding import PartitionSpec as P

EA = 4
ET = 4
ER = 8
INTERSECTIONS = 4
NW = 128
AP = 16
TP = 16


GAMMA = 1.4
METRIC = 0.1
SECTION_STEP = 0.5


def padded(cells, sides, width, closed):
    for axis, dim in sides:
        count = lax.axis_size(axis)
        ends = count if closed else count - 1
        head = lax.slice_in_dim(cells, 0, width, axis=dim)
        tail = lax.slice_in_dim(cells, cells.shape[dim] - width, cells.shape[dim], axis=dim)
        cells = jnp.concatenate(
            [
                lax.ppermute(tail, axis, [(i, (i + 1) % count) for i in range(ends)]),
                cells,
                lax.ppermute(head, axis, [((i + 1) % count, i) for i in range(ends)]),
            ],
            axis=dim,
        )
    return cells


def from_behind(value, axis, steps):
    count = lax.axis_size(axis)
    pairs = [(source, (source + steps) % count) for source in range(count)]
    return lax.ppermute(value, axis, pairs)


def partner(value, axis, distance):
    return lax.ppermute(value, axis, [(i, i ^ 1 << distance) for i in range(lax.axis_size(axis))])


def gauss_nodes():
    root_term = math.sqrt(6.0 / 5.0)
    inner_node = math.sqrt(3.0 / 7.0 - 2.0 / 7.0 * root_term)
    outer_node = math.sqrt(3.0 / 7.0 + 2.0 / 7.0 * root_term)
    return [-outer_node, -inner_node, inner_node, outer_node]


def lagrange_value(node_list, column, position):
    result = 1.0
    for factor_index in range(4):
        if factor_index != column:
            result = (
                result
                * (position - node_list[factor_index])
                / (node_list[column] - node_list[factor_index])
            )
    return result


def lagrange_slope(node_list, column, position):
    total = 0.0
    for skipped in range(4):
        if skipped == column:
            continue
        term = 1.0 / (node_list[column] - node_list[skipped])
        for factor_index in range(4):
            if factor_index != column and factor_index != skipped:
                term = (
                    term
                    * (position - node_list[factor_index])
                    / (node_list[column] - node_list[factor_index])
                )
        total = total + term
    return total


def basis_tables():
    node_list = gauss_nodes()
    derivs = [
        [lagrange_slope(node_list, column, node_list[source]) for column in range(4)]
        for source in range(4)
    ]
    left_vals = [lagrange_value(node_list, column, -1.0) for column in range(4)]
    right_vals = [lagrange_value(node_list, column, 1.0) for column in range(4)]
    third_slope = [(15.0 * value * value - 3.0) / 2.0 for value in node_list]
    fourth_slope = [(35.0 * value**3 - 15.0 * value) / 2.0 for value in node_list]
    left_corr = [-0.5 * (third_slope[source] - fourth_slope[source]) for source in range(4)]
    right_corr = [0.5 * (third_slope[source] + fourth_slope[source]) for source in range(4)]
    return (derivs, left_vals, right_vals, left_corr, right_corr)


def apply_points(adj_field, matrix, point_dim):
    slab_list = [
        lax.index_in_dim(adj_field, source, point_dim, keepdims=False) for source in range(4)
    ]
    outputs = []
    for target in range(4):
        running = slab_list[0] * float(matrix[0][target])
        for source in range(1, 4):
            running = running + slab_list[source] * float(matrix[source][target])
        outputs.append(running)
    return jnp.stack(outputs, axis=point_dim)


def face_moment(adj_field, vector, point_dim):
    running = lax.index_in_dim(adj_field, 0, point_dim, keepdims=False) * float(vector[0])
    for source in range(1, 4):
        running = running + lax.index_in_dim(adj_field, source, point_dim, keepdims=False) * float(
            vector[source]
        )
    return running


def lift_face(face_vals, vector, point_dim):
    return jnp.stack([face_vals * float(vector[target]) for target in range(4)], axis=point_dim)


def conserved(primitive):
    density = primitive[0]
    velocity = primitive[1:4]
    pressure = primitive[4]
    energy = pressure / (GAMMA - 1.0) + 0.5 * density * jnp.sum(velocity * velocity, axis=0)
    return jnp.concatenate([density[None], density[None] * velocity, energy[None]], axis=0)


def euler_flux(cons_state, direction):
    density = cons_state[0]
    momentum = cons_state[1:4]
    energy = cons_state[4]
    velocity = momentum / density[None]
    pressure = (GAMMA - 1.0) * (energy - 0.5 * jnp.sum(momentum * velocity, axis=0))
    normal_speed = velocity[direction]
    columns = [momentum[direction]]
    for component in range(3):
        if component == direction:
            columns.append(momentum[component] * normal_speed + pressure)
        else:
            columns.append(momentum[component] * normal_speed)
    columns.append((energy + pressure) * normal_speed)
    return jnp.stack(columns, axis=0)


def transpose_flux(cons_state, cotangent, direction):
    unused, pullback = jax.vjp(lambda current: euler_flux(current, direction), cons_state)
    return pullback(cotangent)[0]


def section_rate(adj_field, cons_state, left_moments, right_moments, next_left, prev_right):
    derivs, left_vals, right_vals, left_corr, right_corr = basis_tables()
    rate_sum = jnp.zeros_like(adj_field)
    for direction in range(3):
        point_dim = 1 + direction
        bracket = apply_points(adj_field, derivs, point_dim)
        bracket = bracket + 0.5 * lift_face(
            next_left[direction] - right_moments[direction], right_vals, point_dim
        )
        bracket = bracket + 0.5 * lift_face(
            prev_right[direction] - left_moments[direction], left_vals, point_dim
        )
        rate_sum = rate_sum - METRIC * transpose_flux(cons_state, bracket, direction)
    return rate_sum


def all_moments(adj_field):
    derivs, left_vals, right_vals, left_corr, right_corr = basis_tables()
    left_moments = [face_moment(adj_field, left_corr, 1 + direction) for direction in range(3)]
    right_moments = [face_moment(adj_field, right_corr, 1 + direction) for direction in range(3)]
    return (left_moments, right_moments)


def faces_to_rows(face_vals):
    axial_elems = face_vals.shape[3]
    azim_elems = face_vals.shape[4]
    return face_vals.transpose(0, 3, 1, 4, 2).reshape(5, 4 * axial_elems, 4 * azim_elems)


def rows_to_face(rows_vals, axial_elems, azim_elems):
    return rows_vals.reshape(5, axial_elems, 4, azim_elems, 4).transpose(0, 2, 4, 1, 3)


def from_next(field, step):
    filler = jnp.zeros(field.shape[:-1] + (step,), field.dtype)
    return jnp.concatenate([field[..., step:], filler], axis=-1)


def from_prev(field, step):
    filler = jnp.zeros(field.shape[:-1] + (step,), field.dtype)
    return jnp.concatenate([filler, field[..., :-step]], axis=-1)


def local(adjoint, flow_prim, intersection_shift, weight_index, mortar_weights, sector_offset):
    elem_count = EA * ET * ER
    adj_field = adjoint[0]
    cons_state = conserved(flow_prim[0].astype(jnp.float32))
    left_moments, right_moments = all_moments(adj_field)
    is_rotor = lax.axis_index("zone") == 0
    flat_pos = jnp.arange(elem_count, dtype=jnp.int32)
    radial_pos = flat_pos % ER
    azim_pos = flat_pos // ER % ET
    axial_pos = flat_pos // (ET * ER)
    stacked_axial = jnp.stack([left_moments[0], right_moments[0]]).reshape(2, 5, 4, 4, EA, ET * ER)
    extended_axial = padded(stacked_axial, (("axial", 4),), 1, False)
    upper_axial = extended_axial[0][:, :, :, EA + 1 : EA + 2]
    lower_axial = extended_axial[1][:, :, :, 0:1]
    stacked_azim = jnp.stack([left_moments[1], right_moments[1]]).reshape(2, 5, 4, 4, EA, ET, ER)
    extended_azim = padded(stacked_azim, (("azim", 5),), 1, True)
    upper_azim = extended_azim[0][:, :, :, :, ET + 1 : ET + 2]
    lower_azim = extended_azim[1][:, :, :, :, 0:1]
    axial_shape = (5, 4, 4, EA, ET * ER)
    azim_shape = (5, 4, 4, EA, ET, ER)
    next_axial = jnp.where(
        axial_pos == EA - 1,
        jnp.broadcast_to(upper_axial, axial_shape).reshape(5, 4, 4, elem_count),
        from_next(left_moments[0], ET * ER),
    )
    prev_axial = jnp.where(
        axial_pos == 0,
        jnp.broadcast_to(lower_axial, axial_shape).reshape(5, 4, 4, elem_count),
        from_prev(right_moments[0], ET * ER),
    )
    next_azim = jnp.where(
        azim_pos == ET - 1,
        jnp.broadcast_to(upper_azim, azim_shape).reshape(5, 4, 4, elem_count),
        from_next(left_moments[1], ER),
    )
    prev_azim = jnp.where(
        azim_pos == 0,
        jnp.broadcast_to(lower_azim, azim_shape).reshape(5, 4, 4, elem_count),
        from_prev(right_moments[1], ER),
    )
    outer_radial = right_moments[2].reshape(5, 4, 4, EA, ET, ER)[..., -1]
    inner_radial = left_moments[2].reshape(5, 4, 4, EA, ET, ER)[..., 0]
    own_face = jnp.where(is_rotor, outer_radial, inner_radial)
    own_rows = faces_to_rows(own_face)
    shifts_local = intersection_shift.reshape(INTERSECTIONS, AP, TP)
    table_match = weight_index[:, :, None] == jnp.arange(NW, dtype=jnp.int32)[None, None, :]
    weights_local = jnp.sum(
        jnp.where(table_match, mortar_weights[None, None, :], 0.0), axis=2
    ).reshape(INTERSECTIONS, AP, TP)
    offset = sector_offset[0]
    t_local = jnp.arange(TP, dtype=jnp.int32)[None, :]
    axial_local = jnp.arange(AP, dtype=jnp.int32)[:, None]
    cycle_size = lax.axis_size("azim")
    device_turn = (offset + TP // 2) // TP
    residue = offset - device_turn * TP
    inner_base = t_local + residue + TP
    window_rows = padded(own_rows, (("azim", 2),), TP, True)
    contrib = jnp.zeros((5, AP * 3 * TP), jnp.float32)
    for member in range(INTERSECTIONS):
        inner = inner_base + shifts_local[member]
        flat_index = (axial_local * (3 * TP) + inner).reshape(-1)
        contrib = contrib.at[:, flat_index].add(
            (weights_local[member][None] * own_rows).reshape(5, -1)
        )
    packet = jnp.where(is_rotor, window_rows, contrib.reshape(5, AP, 3 * TP))
    amount = jnp.where(is_rotor, -device_turn, device_turn) % cycle_size
    for bit_pos in range((cycle_size - 1).bit_length()):
        turned = from_behind(packet, "azim", 2**bit_pos)
        packet = jnp.where(amount // 2**bit_pos % 2 == 1, turned, packet)
    crossed = partner(packet, "zone", 0)
    incoming = jnp.zeros((5, AP, TP), jnp.float32)
    for member in range(INTERSECTIONS):
        inner = inner_base + shifts_local[member]
        picked = jnp.take_along_axis(crossed, jnp.broadcast_to(inner[None], (5, AP, TP)), axis=2)
        incoming = incoming + weights_local[member][None] * picked
    from_lower = from_behind(crossed[:, :, 2 * TP :], "azim", 1)
    from_upper = from_behind(crossed[:, :, :TP], "azim", -1)
    returned = crossed[:, :, TP : 2 * TP] + from_lower + from_upper
    outer_face = rows_to_face(jnp.where(is_rotor, returned, 0.0), EA, ET)[..., None]
    inner_face = rows_to_face(jnp.where(is_rotor, 0.0, incoming), EA, ET)[..., None]
    outer_full = jnp.broadcast_to(outer_face, azim_shape).reshape(5, 4, 4, elem_count)
    inner_full = jnp.broadcast_to(inner_face, azim_shape).reshape(5, 4, 4, elem_count)
    next_radial = jnp.where(radial_pos == ER - 1, outer_full, from_next(left_moments[2], 1))
    prev_radial = jnp.where(radial_pos == 0, inner_full, from_prev(right_moments[2], 1))
    next_left = [next_axial, next_azim, next_radial]
    prev_right = [prev_axial, prev_azim, prev_radial]
    rate_sum = section_rate(
        adj_field, cons_state, left_moments, right_moments, next_left, prev_right
    )
    adjoint_rate = rate_sum.reshape(1, 5, 4, 4, 4, elem_count)
    next_adjoint = adjoint + SECTION_STEP * adjoint_rate
    return (adjoint_rate, next_adjoint)


def solution(mesh):
    placed = (
        P("zone", None, None, None, None, ("axial", "azim")),
        P("zone", None, None, None, None, ("axial", "azim")),
        P(None, ("axial", "azim")),
        P(None, ("axial", "azim")),
        P(),
        P(),
    )
    return jax.shard_map(
        local,
        mesh=mesh,
        in_specs=placed,
        out_specs=(
            P("zone", None, None, None, None, ("axial", "azim")),
            P("zone", None, None, None, None, ("axial", "azim")),
        ),
        check_vma=False,
    )
```

profile of v0, /device:TPU:0, one launch (start us, length us, event | category | flops | bytes accessed | tf_op | source)
XLA Modules:
  0.0 137.8 jit_solution(8875695711746563737)
XLA Ops:
  4.8 1.6 %copy.640 = f32[5,4,4,4,4,1]{0,4,5,3,2,1:T(4,128)S(1)} copy(f32[5,4,4,4,4,1]{5,4,3,0,2,1:T(4,128)S(1)} %slice.313) | data formatting | bytes 10240
  7.2 1.6 %copy.641 = f32[5,4,4,4,4,1]{0,4,5,3,2,1:T(4,128)S(1)} copy(f32[5,4,4,4,4,1]{5,4,3,0,2,1:T(4,128)S(1)} %bitcast.297) | data formatting | bytes 10240
  10.2 2.9 %collective-permute-start.4 = (f32[5,16,16]{2,1,0:T(8,128)}, f32[5,16,16]{2,1,0:T(8,128)}, u32[]{:S(2)}, u32[]{:S(2)}) collective-permute-start(f32[5,16,16]{2,1,0:T(8,128)} %reshape.781), channel_id=1, source_target_pairs={{0,1},{1,2},{2,3},{3,4},{4,5},{5,6},{6,7},{7,0},{8,9},{9,10},{10,1... | collective-permute-start | bytes 15368 | tf_op jit(solution)/shard_map/ppermute | solution.py:30
  13.2 3.0 %collective-permute-start.5 = (f32[5,16,16]{2,1,0:T(8,128)}, f32[5,16,16]{2,1,0:T(8,128)}, u32[]{:S(2)}, u32[]{:S(2)}) collective-permute-start(f32[5,16,16]{2,1,0:T(8,128)} %reshape.781), channel_id=1, source_target_pairs={{1,0},{2,1},{3,2},{4,3},{5,4},{6,5},{7,6},{0,7},{9,8},{10,9},{11,1... | collective-permute-start | bytes 15368 | tf_op jit(solution)/shard_map/ppermute | solution.py:32
  18.9 1.3 fusion.58
  20.2 4.7 %collective-permute-start.3 = (f32[2,5,4,4,4,1,8]{6,5,4,3,1,2,0:T(1,128)}, f32[2,5,4,4,4,1,8]{6,5,4,3,1,2,0:T(1,128)}, u32[]{:S(2)}, u32[]{:S(2)}) collective-permute-start(f32[2,5,4,4,4,1,8]{6,5,4,3,1,2,0:T(1,128)} %get-tuple-element.51), channel_id=1, source_target_pairs={{1,0},{2,1},{3,2},{4,3},{5,4},{6,5},{7,6},{0,7},{9,8},{10,9},{11,1... | collective-permute-start | bytes 61448 | tf_op jit(solution)/shard_map/ppermute | solution.py:32
  26.8 4.2 %collective-permute-start = (f32[2,5,4,4,1,32]{5,4,3,1,2,0:T(1,128)}, f32[2,5,4,4,1,32]{5,4,3,1,2,0:T(1,128)}, u32[]{:S(2)}, u32[]{:S(2)}) collective-permute-start(f32[2,5,4,4,1,32]{5,4,3,1,2,0:T(1,128)} %get-tuple-element.54), channel_id=1, source_target_pairs={{0,8},{1,9},{2,10},{3,11},{4,12},{5,13},{6,14},{7,15},{16,24},{17,... | collective-permute-start | bytes 61448 | tf_op jit(solution)/shard_map/ppermute | solution.py:30
  43.6 1.9 %scatter_custom_fusion = f32[5,768]{0,1:T(8,128)S(1)} fusion(s32[256]{0:T(256)} %bitcast.319, f32[256,5]{1,0:T(8,128)} %copy.598, f32[]{:T(128)} %constant.167.clone.1), kind=kCustom, calls=%fused_computation.16 | custom fusion | flops 1280 | bytes 15872 | tf_op jit(solution)/shard_map/scatter-add | solution.py:260
  45.5 2.5 %scatter_fusion = f32[5,768]{0,1:T(8,128)S(1)} fusion(f32[5,768]{0,1:T(8,128)S(1)} %scatter_custom_fusion, s32[256]{0:T(256)} %bitcast.314, f32[256,5]{1,0:T(8,128)} %copy.599), kind=kCustom, calls=%fused_computation.5 | custom fusion | flops 1280 | bytes 16384 | tf_op jit(solution)/shard_map/scatter-add | solution.py:260
  48.0 2.6 %scatter_fusion.1 = f32[5,768]{0,1:T(8,128)S(1)} fusion(f32[5,768]{0,1:T(8,128)S(1)} %scatter_fusion, s32[256]{0:T(256)} %bitcast.313, f32[256,5]{1,0:T(8,128)} %copy.600), kind=kCustom, calls=%fused_computation.6 | custom fusion | flops 1280 | bytes 16384 | tf_op jit(solution)/shard_map/scatter-add | solution.py:260
  50.7 2.5 %scatter_fusion.2 = f32[5,768]{0,1:T(8,128)S(1)} fusion(f32[5,768]{0,1:T(8,128)S(1)} %scatter_fusion.1, s32[256]{0:T(256)S(1)} %bitcast.312, f32[256,5]{1,0:T(8,128)} %copy.601), kind=kCustom, calls=%fused_computation.7 | custom fusion | flops 1280 | bytes 16384 | tf_op jit(solution)/shard_map/scatter-add | solution.py:260
  57.2 1.4 mul.1049
  58.5 1.4 mul.1052
  61.2 1.4 mul.1058
  63.2 1.4 %copy.590 = f32[5,4,4,1,128]{4,2,3,1,0:T(4,128)} copy(f32[5,4,4,1,128]{4,3,0,2,1:T(1,128)} %get-tuple-element.82) | data formatting | bytes 81920 | tf_op jit(solution)/shard_map/add | solution.py:108
  64.6 1.4 %copy.591 = f32[5,4,4,1,128]{4,2,3,1,0:T(4,128)} copy(f32[5,4,4,1,128]{4,3,0,2,1:T(1,128)} %get-tuple-element.83) | data formatting | bytes 81920 | tf_op jit(solution)/shard_map/add | solution.py:108
  68.7 2.0 %pad_maximum_fusion = f32[2,5,4,4,4,6,8]{6,5,4,3,1,2,0:T(8,128)S(1)} fusion(f32[2,5,4,4,4,1,8]{6,5,4,3,1,2,0:T(1,128)} %collective-permute-done.3, f32[2,5,4,4,4,4,8]{6,5,4,3,1,2,0:T(4,128)S(1)} %constant_dynamic-update-slice_fusion.2, f32[2,5,4,4,4,1,8]{6,5,4,3,1,2,0:T(1,128)S(1)} %collective-permute-done.2), kind=kLoop, calls=%fused_computation.8 | loop fusion | flops 61440 | bytes 245760 | tf_op jit(solution)/shard_map/concatenate | solution.py:28
  77.6 3.8 %collective-permute-done.8 = f32[5,16,48]{2,1,0:T(8,128)S(1)} collective-permute-done((f32[5,16,48]{2,1,0:T(8,128)S(1)}, f32[5,16,48]{2,1,0:T(8,128)S(1)}, u32[]{:S(2)}, u32[]{:S(2)}) %collective-permute-start.8) | collective-permute-done | bytes 15392 | tf_op jit(solution)/shard_map/ppermute | solution.py:42
  82.6 2.9 %collective-permute-start.10 = (f32[5,16,16]{2,1,0:T(8,128)S(1)}, f32[5,16,16]{2,1,0:T(8,128)S(1)}, u32[]{:S(2)}, u32[]{:S(2)}) collective-permute-start(f32[5,16,16]{2,1,0:T(8,128)S(1)} %get-tuple-element.111), channel_id=1, source_target_pairs={{0,1},{1,2},{2,3},{3,4},{4,5},{5,6},{6,7},{7,0},{8,9},{9,10},{10,1... | collective-permute-start | bytes 15368 | tf_op jit(solution)/shard_map/ppermute | solution.py:42
  85.5 2.1 %collective-permute-start.11 = (f32[5,16,16]{2,1,0:T(8,128)S(1)}, f32[5,16,16]{2,1,0:T(8,128)S(1)}, u32[]{:S(2)}, u32[]{:S(2)}) collective-permute-start(f32[5,16,16]{2,1,0:T(8,128)S(1)} %get-tuple-element.112), channel_id=1, source_target_pairs={{0,7},{1,0},{2,1},{3,2},{4,3},{5,4},{6,5},{7,6},{8,15},{9,8},{10,9... | collective-permute-start | bytes 15368 | tf_op jit(solution)/shard_map/ppermute | solution.py:42
  87.6 10.6 %gather_fusion = f32[1280]{0:T(1024)S(1)} fusion(f32[5,16,48]{2,1,0:T(8,128)S(1)} %collective-permute-done.9, s32[1280]{0:T(1024)S(1)} %reshape.875), kind=kCustom, calls=%fused_computation.clone | custom fusion | bytes 25600 | tf_op jit(solution)/shard_map/jit(take_along_axis)/gather | solution.py:272
  98.3 10.6 %gather_fusion.1 = f32[1280]{0:T(1024)S(1)} fusion(f32[5,16,48]{2,1,0:T(8,128)S(1)} %collective-permute-done.9, s32[1280]{0:T(1024)S(1)} %reshape.880), kind=kCustom, calls=%fused_computation.1.clone | custom fusion | bytes 25600 | tf_op jit(solution)/shard_map/jit(take_along_axis)/gather | solution.py:272
  109.0 10.6 %gather_fusion.2 = f32[1280]{0:T(1024)S(1)} fusion(f32[5,16,48]{2,1,0:T(8,128)S(1)} %collective-permute-done.9, s32[1280]{0:T(1024)S(1)} %reshape.885), kind=kCustom, calls=%fused_computation.2.clone | custom fusion | bytes 25600 | tf_op jit(solution)/shard_map/jit(take_along_axis)/gather | solution.py:272
  119.9 10.6 %gather_fusion.3 = f32[1280]{0:T(1024)S(1)} fusion(f32[5,16,48]{2,1,0:T(8,128)S(1)} %collective-permute-done.9, s32[1280]{0:T(1024)S(1)} %reshape.890), kind=kCustom, calls=%fused_computation.3.clone | custom fusion | bytes 25600 | tf_op jit(solution)/shard_map/jit(take_along_axis)/gather | solution.py:272
  (274 shorter events, 46.0 us)
Async XLA Ops:
  10.2 43.1 %collective-permute-start.4 = (f32[5,16,16]{2,1,0:T(8,128)}, f32[5,16,16]{2,1,0:T(8,128)}, u32[]{:S(2)}, u32[]{:S(2)}) collective-permute-start(f32[5,16,16]{2,1,0:T(8,128)} %reshape.781), channel_id=1, source_target_pairs={{0,1},{1,2},{2,3},{3,4},{4,5},{5,6},{6,7},{7,0},{8,9},{9,10},{10,1... | collective-permute-start | bytes 15368 | tf_op jit(solution)/shard_map/ppermute | solution.py:30
  13.2 41.5 %collective-permute-start.5 = (f32[5,16,16]{2,1,0:T(8,128)}, f32[5,16,16]{2,1,0:T(8,128)}, u32[]{:S(2)}, u32[]{:S(2)}) collective-permute-start(f32[5,16,16]{2,1,0:T(8,128)} %reshape.781), channel_id=1, source_target_pairs={{1,0},{2,1},{3,2},{4,3},{5,4},{6,5},{7,6},{0,7},{9,8},{10,9},{11,1... | collective-permute-start | bytes 15368 | tf_op jit(solution)/shard_map/ppermute | solution.py:32
  18.9 15.3 %copy-start.26 = (bf16[1,5,4,4,4,128]{5,4,3,2,1,0:T(4,128)(2,1)S(1)}, bf16[1,5,4,4,4,128]{5,4,3,2,1,0:T(4,128)(2,1)}, u32[]{:S(2)}) copy-start(bf16[1,5,4,4,4,128]{5,4,3,2,1,0:T(4,128)(2,1)} %param.9) | copy-start | bytes 245764
  20.2 48.5 %collective-permute-start.2 = (f32[2,5,4,4,4,1,8]{6,5,4,3,1,2,0:T(1,128)}, f32[2,5,4,4,4,1,8]{6,5,4,3,1,2,0:T(1,128)S(1)}, u32[]{:S(2)}, u32[]{:S(2)}) collective-permute-start(f32[2,5,4,4,4,1,8]{6,5,4,3,1,2,0:T(1,128)} %get-tuple-element.50), channel_id=1, source_target_pairs={{0,1},{1,2},{2,3},{3,4},{4,5},{5,6},{6,7},{7,0},{8,9},{9,10},{10,1... | collective-permute-start | bytes 61448 | tf_op jit(solution)/shard_map/ppermute | solution.py:30
  20.2 16.1 %copy-start.49 = (s32[4,256]{1,0:T(4,128)S(1)}, s32[4,256]{1,0:T(4,128)}, u32[]{:S(2)}) copy-start(s32[4,256]{1,0:T(4,128)} %param.11) | copy-start | bytes 12292
  20.2 16.1 %copy-start.57 = (f32[128]{0:T(128)S(1)}, f32[128]{0:T(128)}, u32[]{:S(2)}) copy-start(f32[128]{0:T(128)} %param.12) | copy-start | bytes 1540
  20.2 17.1 %copy-start.47 = (s32[4,256]{1,0:T(4,128)S(1)}, s32[4,256]{1,0:T(4,128)}, u32[]{:S(2)}) copy-start(s32[4,256]{1,0:T(4,128)} %param.10) | copy-start | bytes 12292
  20.2 48.4 %collective-permute-start.3 = (f32[2,5,4,4,4,1,8]{6,5,4,3,1,2,0:T(1,128)}, f32[2,5,4,4,4,1,8]{6,5,4,3,1,2,0:T(1,128)}, u32[]{:S(2)}, u32[]{:S(2)}) collective-permute-start(f32[2,5,4,4,4,1,8]{6,5,4,3,1,2,0:T(1,128)} %get-tuple-element.51), channel_id=1, source_target_pairs={{1,0},{2,1},{3,2},{4,3},{5,4},{6,5},{7,6},{0,7},{9,8},{10,9},{11,1... | collective-permute-start | bytes 61448 | tf_op jit(solution)/shard_map/ppermute | solution.py:32
  26.0 13.2 %copy-start.17 = (f32[5,4,4,1,128]{4,3,0,2,1:T(1,128)S(1)}, f32[5,4,4,1,128]{4,3,0,2,1:T(1,128)}, u32[]{:S(2)}) copy-start(f32[5,4,4,1,128]{4,3,0,2,1:T(1,128)} %get-tuple-element.85) | copy-start | bytes 122884
  26.0 13.2 %copy-start.18 = (f32[5,4,4,1,128]{4,3,0,2,1:T(1,128)S(1)}, f32[5,4,4,1,128]{4,3,0,2,1:T(1,128)}, u32[]{:S(2)}) copy-start(f32[5,4,4,1,128]{4,3,0,2,1:T(1,128)} %get-tuple-element.86) | copy-start | bytes 122884
  26.0 13.2 %copy-start.19 = (f32[5,4,4,1,128]{4,3,0,2,1:T(1,128)S(1)}, f32[5,4,4,1,128]{4,3,0,2,1:T(1,128)}, u32[]{:S(2)}) copy-start(f32[5,4,4,1,128]{4,3,0,2,1:T(1,128)} %get-tuple-element.87) | copy-start | bytes 122884
  26.0 13.2 %copy-start.20 = (f32[5,4,4,1,128]{4,3,0,2,1:T(1,128)S(1)}, f32[5,4,4,1,128]{4,3,0,2,1:T(1,128)}, u32[]{:S(2)}) copy-start(f32[5,4,4,1,128]{4,3,0,2,1:T(1,128)} %get-tuple-element.88) | copy-start | bytes 122884
  26.8 46.4 %collective-permute-start = (f32[2,5,4,4,1,32]{5,4,3,1,2,0:T(1,128)}, f32[2,5,4,4,1,32]{5,4,3,1,2,0:T(1,128)}, u32[]{:S(2)}, u32[]{:S(2)}) collective-permute-start(f32[2,5,4,4,1,32]{5,4,3,1,2,0:T(1,128)} %get-tuple-element.54), channel_id=1, source_target_pairs={{0,8},{1,9},{2,10},{3,11},{4,12},{5,13},{6,14},{7,15},{16,24},{17,... | collective-permute-start | bytes 61448 | tf_op jit(solution)/shard_map/ppermute | solution.py:30
  37.8 15.5 %copy-start.23 = (s32[16,16]{1,0:T(8,128)}, s32[16,16]{1,0:T(8,128)S(1)}, u32[]{:S(2)}) copy-start(s32[16,16]{1,0:T(8,128)S(1)} %get-tuple-element.142) | copy-start | bytes 3076
  39.1 17.0 %copy-start.29 = (s32[16,16]{1,0:T(8,128)}, s32[16,16]{1,0:T(8,128)S(1)}, u32[]{:S(2)}) copy-start(s32[16,16]{1,0:T(8,128)S(1)} %get-tuple-element.148) | copy-start | bytes 3076
  42.0 24.0 %copy-start.16 = (f32[5,4,4,1,128]{4,3,0,2,1:T(1,128)S(1)}, f32[5,4,4,1,128]{4,3,0,2,1:T(1,128)}, u32[]{:S(2)}) copy-start(f32[5,4,4,1,128]{4,3,0,2,1:T(1,128)} %get-tuple-element.84) | copy-start | bytes 122884
  53.3 19.9 %collective-permute-start.1 = (f32[2,5,4,4,1,32]{5,4,3,1,2,0:T(1,128)}, f32[2,5,4,4,1,32]{5,4,3,1,2,0:T(1,128)}, u32[]{:S(2)}, u32[]{:S(2)}) collective-permute-start(f32[2,5,4,4,1,32]{5,4,3,1,2,0:T(1,128)} %get-tuple-element.55), channel_id=1, source_target_pairs={{8,0},{9,1},{10,2},{11,3},{12,4},{13,5},{14,6},{15,7},{24,16},{25,... | collective-permute-start | bytes 61448 | tf_op jit(solution)/shard_map/ppermute | solution.py:32
  55.6 12.5 %collective-permute-start.6 = (f32[5,16,48]{2,1,0:T(8,128)S(1)}, f32[5,16,48]{2,1,0:T(8,128)S(1)}, u32[]{:S(2)}, u32[]{:S(2)}) collective-permute-start(f32[5,16,48]{2,1,0:T(8,128)S(1)} %maximum_select_fusion), channel_id=1, source_target_pairs={{0,1},{1,2},{2,3},{3,4},{4,5},{5,6},{6,7},{7,0},{8,9},{9,10},{10,1... | collective-permute-start | bytes 46088 | tf_op jit(solution)/shard_map/ppermute | solution.py:42
  68.7 6.9 %collective-permute-start.7 = (f32[5,16,48]{2,1,0:T(8,128)}, f32[5,16,48]{2,1,0:T(8,128)}, u32[]{:S(2)}, u32[]{:S(2)}) collective-permute-start(f32[5,16,48]{2,1,0:T(8,128)} %broadcast_select_fusion), channel_id=1, source_target_pairs={{0,2},{1,3},{2,4},{3,5},{4,6},{5,7},{6,0},{7,1},{8,10},{9,11},{10,... | collective-permute-start | bytes 46088 | tf_op jit(solution)/shard_map/ppermute | solution.py:42
  76.4 4.9 %collective-permute-start.8 = (f32[5,16,48]{2,1,0:T(8,128)S(1)}, f32[5,16,48]{2,1,0:T(8,128)S(1)}, u32[]{:S(2)}, u32[]{:S(2)}) collective-permute-start(f32[5,16,48]{2,1,0:T(8,128)S(1)} %broadcast_select_fusion.1), channel_id=1, source_target_pairs={{0,4},{1,5},{2,6},{3,7},{4,0},{5,1},{6,2},{7,3},{8,12},{9,13},{10,... | collective-permute-start | bytes 46088 | tf_op jit(solution)/shard_map/ppermute | solution.py:42
  81.3 1.2 collective-permute-start.9
  82.6 50.2 %collective-permute-start.10 = (f32[5,16,16]{2,1,0:T(8,128)S(1)}, f32[5,16,16]{2,1,0:T(8,128)S(1)}, u32[]{:S(2)}, u32[]{:S(2)}) collective-permute-start(f32[5,16,16]{2,1,0:T(8,128)S(1)} %get-tuple-element.111), channel_id=1, source_target_pairs={{0,1},{1,2},{2,3},{3,4},{4,5},{5,6},{6,7},{7,0},{8,9},{9,10},{10,1... | collective-permute-start | bytes 15368 | tf_op jit(solution)/shard_map/ppermute | solution.py:42
  85.5 47.3 %collective-permute-start.11 = (f32[5,16,16]{2,1,0:T(8,128)S(1)}, f32[5,16,16]{2,1,0:T(8,128)S(1)}, u32[]{:S(2)}, u32[]{:S(2)}) collective-permute-start(f32[5,16,16]{2,1,0:T(8,128)S(1)} %get-tuple-element.112), channel_id=1, source_target_pairs={{0,7},{1,0},{2,1},{3,2},{4,3},{5,4},{6,5},{7,6},{8,15},{9,8},{10,9... | collective-permute-start | bytes 15368 | tf_op jit(solution)/shard_map/ppermute | solution.py:42
  119.7 10.9 %copy-start.24 = (s32[16,16]{1,0:T(8,128)S(1)}, s32[16,16]{1,0:T(8,128)}, u32[]{:S(2)}) copy-start(s32[16,16]{1,0:T(8,128)} %copy-done.23) | copy-start | bytes 3076
  (46 other events, 225.0 us)
where the time goes:
time: 139 us; the launch traced here: 138 us
  local copies, waits for them, and re-layouts  79.8 us (57%)
  other arithmetic  28 us (20%)
  starting transfers between devices  22.4 us (16%)
  waiting for transfers between devices  4.85 us (3%)
  between operations  2.72 us (2%)
    gather x12, local copies, waits for them, and re-layouts, local(): jnp.take_along_axis(crossed, jnp.broadcast_to(inner[None], (5, AP, TP)),...  43.1 us
    scatter-add x4, other arithmetic, local(): contrib.at[:, flat_index]  9.45 us
    ppermute x3, starting transfers between devices, padded(): lax.ppermute(head, axis, [((i + 1) % count, i) for i in range(ends)])  9.04 us
    mul x8, local copies, waits for them, and re-layouts, local(): weights_local[member][None] * own_rows  8.59 us
    ppermute x3, starting transfers between devices, padded(): lax.ppermute(tail, axis, [(i, (i + 1) % count) for i in range(ends)])  7.18 us
    unnamed x124, local copies, waits for them, and re-layouts  6.51 us
    ppermute x5, starting transfers between devices, from_behind(): return lax.ppermute(value, axis, pairs)  6.17 us
    add x8, local copies, waits for them, and re-layouts, face_moment(): running + lax.index_in_dim(adj_field, source, point_dim, keepdims=False)...  4.11 us
  transfers between devices with their start and end apart: 12, of which 2 were waited for; matrix products, arithmetic and copies ran while one was open for 67% of the time, Pallas kernels for 0%

commit v1 on v0

--- a/solution.py
+++ b/solution.py
@@ -17,33 +17,6 @@
 GAMMA = 1.4
 METRIC = 0.1
 SECTION_STEP = 0.5
-
-
-def padded(cells, sides, width, closed):
-    for axis, dim in sides:
-        count = lax.axis_size(axis)
-        ends = count if closed else count - 1
-        head = lax.slice_in_dim(cells, 0, width, axis=dim)
-        tail = lax.slice_in_dim(cells, cells.shape[dim] - width, cells.shape[dim], axis=dim)
-        cells = jnp.concatenate(
-            [
-                lax.ppermute(tail, axis, [(i, (i + 1) % count) for i in range(ends)]),
-                cells,
-                lax.ppermute(head, axis, [((i + 1) % count, i) for i in range(ends)]),
-            ],
-            axis=dim,
-        )
-    return cells
-
-
-def from_behind(value, axis, steps):
-    count = lax.axis_size(axis)
-    pairs = [(source, (source + steps) % count) for source in range(count)]
-    return lax.ppermute(value, axis, pairs)
-
-
-def partner(value, axis, distance):
-    return lax.ppermute(value, axis, [(i, i ^ 1 << distance) for i in range(lax.axis_size(axis))])
 
 
 def gauss_nodes():
@@ -186,59 +159,51 @@
     return rows_vals.reshape(5, axial_elems, 4, azim_elems, 4).transpose(0, 2, 4, 1, 3)
 
 
-def from_next(field, step):
-    filler = jnp.zeros(field.shape[:-1] + (step,), field.dtype)
-    return jnp.concatenate([field[..., step:], filler], axis=-1)
-
-
-def from_prev(field, step):
-    filler = jnp.zeros(field.shape[:-1] + (step,), field.dtype)
-    return jnp.concatenate([filler, field[..., :-step]], axis=-1)
+def shift_sum(window, coefs, lo):
+    total = None
+    for offset, coef in coefs:
+        term = coef[None] * window[:, :, lo + offset : lo + offset + TP]
+        total = term if total is None else total + term
+    return total
 
 
 def local(adjoint, flow_prim, intersection_shift, weight_index, mortar_weights, sector_offset):
     elem_count = EA * ET * ER
+    n_axial = lax.axis_size("axial")
+    n_azim = lax.axis_size("azim")
     adj_field = adjoint[0]
     cons_state = conserved(flow_prim[0].astype(jnp.float32))
     left_moments, right_moments = all_moments(adj_field)
     is_rotor = lax.axis_index("zone") == 0
-    flat_pos = jnp.arange(elem_count, dtype=jnp.int32)
-    radial_pos = flat_pos % ER
-    azim_pos = flat_pos // ER % ET
-    axial_pos = flat_pos // (ET * ER)
-    stacked_axial = jnp.stack([left_moments[0], right_moments[0]]).reshape(2, 5, 4, 4, EA, ET * ER)
-    extended_axial = padded(stacked_axial, (("axial", 4),), 1, False)
-    upper_axial = extended_axial[0][:, :, :, EA + 1 : EA + 2]
-    lower_axial = extended_axial[1][:, :, :, 0:1]
-    stacked_azim = jnp.stack([left_moments[1], right_moments[1]]).reshape(2, 5, 4, 4, EA, ET, ER)
-    extended_azim = padded(stacked_azim, (("azim", 5),), 1, True)
-    upper_azim = extended_azim[0][:, :, :, :, ET + 1 : ET + 2]
-    lower_azim = extended_azim[1][:, :, :, :, 0:1]
-    axial_shape = (5, 4, 4, EA, ET * ER)
-    azim_shape = (5, 4, 4, EA, ET, ER)
-    next_axial = jnp.where(
-        axial_pos == EA - 1,
-        jnp.broadcast_to(upper_axial, axial_shape).reshape(5, 4, 4, elem_count),
-        from_next(left_moments[0], ET * ER),
-    )
-    prev_axial = jnp.where(
-        axial_pos == 0,
-        jnp.broadcast_to(lower_axial, axial_shape).reshape(5, 4, 4, elem_count),
-        from_prev(right_moments[0], ET * ER),
-    )
-    next_azim = jnp.where(
-        azim_pos == ET - 1,
-        jnp.broadcast_to(upper_azim, azim_shape).reshape(5, 4, 4, elem_count),
-        from_next(left_moments[1], ER),
-    )
-    prev_azim = jnp.where(
-        azim_pos == 0,
-        jnp.broadcast_to(lower_azim, azim_shape).reshape(5, 4, 4, elem_count),
-        from_prev(right_moments[1], ER),
-    )
-    outer_radial = right_moments[2].reshape(5, 4, 4, EA, ET, ER)[..., -1]
-    inner_radial = left_moments[2].reshape(5, 4, 4, EA, ET, ER)[..., 0]
-    own_face = jnp.where(is_rotor, outer_radial, inner_radial)
+    face_shape = (5, 4, 4, EA, ET, ER)
+    ax_span = ET * ER
+    upper_axial = lax.ppermute(
+        left_moments[0][..., :ax_span], "axial", [(i + 1, i) for i in range(n_axial - 1)]
+    )
+    lower_axial = lax.ppermute(
+        right_moments[0][..., elem_count - ax_span :],
+        "axial",
+        [(i, i + 1) for i in range(n_axial - 1)],
+    )
+    next_axial = jnp.concatenate([left_moments[0][..., ax_span:], upper_axial], axis=-1)
+    prev_axial = jnp.concatenate([lower_axial, right_moments[0][..., : elem_count - ax_span]], axis=-1)
+    left_az = left_moments[1].reshape(face_shape)
+    right_az = right_moments[1].reshape(face_shape)
+    upper_azim = lax.ppermute(
+        left_az[:, :, :, :, :1], "azim", [((j + 1) % n_azim, j) for j in range(n_azim)]
+    )
+    lower_azim = lax.ppermute(
+        right_az[:, :, :, :, ET - 1 :], "azim", [(j, (j + 1) % n_azim) for j in range(n_azim)]
+    )
+    next_azim = jnp.concatenate([left_az[:, :, :, :, 1:], upper_azim], axis=4).reshape(
+        5, 4, 4, elem_count
+    )
+    prev_azim = jnp.concatenate([lower_azim, right_az[:, :, :, :, : ET - 1]], axis=4).reshape(
+        5, 4, 4, elem_count
+    )
+    left_rad = left_moments[2].reshape(face_shape)
+    right_rad = right_moments[2].reshape(face_shape)
+    own_face = jnp.where(is_rotor, right_rad[..., -1], left_rad[..., 0])
     own_rows = faces_to_rows(own_face)
     shifts_local = intersection_shift.reshape(INTERSECTIONS, AP, TP)
     table_match = weight_index[:, :, None] == jnp.arange(NW, dtype=jnp.int32)[None, None, :]
@@ -246,40 +211,48 @@
         jnp.where(table_match, mortar_weights[None, None, :], 0.0), axis=2
     ).reshape(INTERSECTIONS, AP, TP)
     offset = sector_offset[0]
-    t_local = jnp.arange(TP, dtype=jnp.int32)[None, :]
-    axial_local = jnp.arange(AP, dtype=jnp.int32)[:, None]
-    cycle_size = lax.axis_size("azim")
-    device_turn = (offset + TP // 2) // TP
-    residue = offset - device_turn * TP
-    inner_base = t_local + residue + TP
-    window_rows = padded(own_rows, (("azim", 2),), TP, True)
-    contrib = jnp.zeros((5, AP * 3 * TP), jnp.float32)
-    for member in range(INTERSECTIONS):
-        inner = inner_base + shifts_local[member]
-        flat_index = (axial_local * (3 * TP) + inner).reshape(-1)
-        contrib = contrib.at[:, flat_index].add(
-            (weights_local[member][None] * own_rows).reshape(5, -1)
-        )
-    packet = jnp.where(is_rotor, window_rows, contrib.reshape(5, AP, 3 * TP))
-    amount = jnp.where(is_rotor, -device_turn, device_turn) % cycle_size
-    for bit_pos in range((cycle_size - 1).bit_length()):
-        turned = from_behind(packet, "azim", 2**bit_pos)
-        packet = jnp.where(amount // 2**bit_pos % 2 == 1, turned, packet)
-    crossed = partner(packet, "zone", 0)
-    incoming = jnp.zeros((5, AP, TP), jnp.float32)
-    for member in range(INTERSECTIONS):
-        inner = inner_base + shifts_local[member]
-        picked = jnp.take_along_axis(crossed, jnp.broadcast_to(inner[None], (5, AP, TP)), axis=2)
-        incoming = incoming + weights_local[member][None] * picked
-    from_lower = from_behind(crossed[:, :, 2 * TP :], "azim", 1)
-    from_upper = from_behind(crossed[:, :, :TP], "azim", -1)
-    returned = crossed[:, :, TP : 2 * TP] + from_lower + from_upper
-    outer_face = rows_to_face(jnp.where(is_rotor, returned, 0.0), EA, ET)[..., None]
-    inner_face = rows_to_face(jnp.where(is_rotor, 0.0, incoming), EA, ET)[..., None]
-    outer_full = jnp.broadcast_to(outer_face, azim_shape).reshape(5, 4, 4, elem_count)
-    inner_full = jnp.broadcast_to(inner_face, azim_shape).reshape(5, 4, 4, elem_count)
-    next_radial = jnp.where(radial_pos == ER - 1, outer_full, from_next(left_moments[2], 1))
-    prev_radial = jnp.where(radial_pos == 0, inner_full, from_prev(right_moments[2], 1))
+    turn = (offset + TP // 2) // TP
+    residue = offset - turn * TP
+    offsets_k = residue + shifts_local
+    coefs = []
+    for rel in range(-TP, TP - 1):
+        coef = jnp.where(offsets_k[0] == rel, weights_local[0], 0.0)
+        for member in range(1, INTERSECTIONS):
+            coef = coef + jnp.where(offsets_k[member] == rel, weights_local[member], 0.0)
+        coefs.append((rel, coef))
+    contrib = None
+    for rel, coef in coefs:
+        term = jnp.pad(coef[None] * own_rows, ((0, 0), (0, 0), (TP + rel, TP - rel)))
+        contrib = term if contrib is None else contrib + term
+    received = []
+    for dist in range(n_azim):
+        gap = (dist - turn) % n_azim
+        piece = jnp.where(
+            gap == n_azim - 1,
+            contrib[:, :, :TP],
+            jnp.where(gap == 0, contrib[:, :, TP : 2 * TP], contrib[:, :, 2 * TP :]),
+        )
+        payload = jnp.where(is_rotor, own_rows, piece)
+        pairs = [(j, n_azim + (j - dist) % n_azim) for j in range(n_azim)] + [
+            (n_azim + j, (j + dist) % n_azim) for j in range(n_azim)
+        ]
+        received.append(lax.ppermute(payload, ("zone", "azim"), pairs))
+    stacked = jnp.stack(received)
+    picked = [
+        lax.dynamic_index_in_dim(stacked, (turn + step) % n_azim, 0, keepdims=False)
+        for step in (-1, 0, 1)
+    ]
+    returned = picked[0] + picked[1] + picked[2]
+    window = jnp.concatenate(picked, axis=2)
+    incoming = shift_sum(window, coefs, TP)
+    outer_face = jnp.where(is_rotor, rows_to_face(returned, EA, ET), 0.0)
+    inner_face = jnp.where(is_rotor, 0.0, rows_to_face(incoming, EA, ET))
+    next_radial = jnp.concatenate([left_rad[..., 1:], outer_face[..., None]], axis=5).reshape(
+        5, 4, 4, elem_count
+    )
+    prev_radial = jnp.concatenate([inner_face[..., None], right_rad[..., :-1]], axis=5).reshape(
+        5, 4, 4, elem_count
+    )
     next_left = [next_axial, next_azim, next_radial]
     prev_right = [prev_axial, prev_azim, prev_radial]
     rate_sum = section_rate(

time: 139 us -> 77.2 us (0.56)
  local copies, waits for them, and re-layouts: 79.8 us -> 29.8 us
  other arithmetic: 28 us -> 19.2 us
  waiting for transfers between devices: 4.85 us -> 0.81 us
    gather x12 -> x0, local copies, waits for them, and re-layouts: 43.1 us -> none  [local(): jnp.take_along_axis(crossed, jnp.broadcast_to(inner[None], (5, AP, TP)),...]
    scatter-add x4 -> x0, other arithmetic: 9.45 us -> none  [local(): contrib.at[:, flat_index]]
    mul x8 -> x31, local copies, waits for them, and re-layouts: 8.59 us -> 2.5 us  [local(): coef[None] * own_rows]
    unnamed x124 -> x185, local copies, waits for them, and re-layouts: 6.51 us -> 11.5 us
    ppermute x12, waiting for transfers between devices: 4.85 us -> 0.81 us  [the longest x1 0.45 us: local(): lax.ppermute(right_moments[0][..., elem_count - ax_span:], 'axial', [(i,...]
    slice x14 -> x6, local copies, waits for them, and re-layouts: 5.79 us -> 2.05 us  [the longest x1 0.84 us: local(): right_az[:, :, :, :, ET - 1:]]
    add x7 -> x0, local copies, waits for them, and re-layouts: 3.68 us -> none  [the longest x3 3.44 us: apply_points(): running = running + slab_list[source] * float(matrix[source][target])]
    eq x6 -> x0, other arithmetic: 3.25 us -> none  [the longest x1 0.58 us: local(): radial_pos == ER - 1]
  transfers between devices with their start and end apart: 12 -> 12, of which waited for: 2 -> 2; matrix products, arithmetic and copies ran while one was open for 67% -> 30% of each run, Pallas kernels for 0% -> 0%
where the time goes in v1:
time: 77.2 us; the launch traced here: 76 us
  local copies, waits for them, and re-layouts  29.8 us (39%)
  starting transfers between devices  23.5 us (30%)
  other arithmetic  19.2 us (25%)
  between operations  2.67 us (3%)
  waiting for transfers between devices  0.81 us (1%)
    ppermute x8, starting transfers between devices, local(): received.append(lax.ppermute(payload, ('zone', 'azim'), pairs))  12 us
    unnamed x185, local copies, waits for them, and re-layouts  11.5 us
    add x3, other arithmetic, face_moment(): running + lax.index_in_dim(adj_field, source, point_dim, keepdims=False)...  5.2 us
    ppermute x1, starting transfers between devices, local(): lax.ppermute(left_az[:, :, :, :, :1], 'azim', [((j + 1) % n_azim, j) for...  5.19 us
    add x5, local copies, waits for them, and re-layouts, face_moment(): running + lax.index_in_dim(adj_field, source, point_dim, keepdims=False)...  3.78 us
    ppermute x1, starting transfers between devices, local(): lax.ppermute(right_moments[0][..., elem_count - ax_span:], 'axial', [(i,...  3.43 us
    mul x31, local copies, waits for them, and re-layouts, local(): coef[None] * own_rows  2.5 us
    mul x11, other arithmetic, lift_face(): face_vals * float(vector[target])  2.32 us
  transfers between devices with their start and end apart: 12, of which 2 were waited for; matrix products, arithmetic and copies ran while one was open for 30% of the time, Pallas kernels for 0%

profile of v1, /device:TPU:0, one launch (start us, length us, event | category | flops | bytes accessed | tf_op | source)
XLA Modules:
  0.0 76.0 jit_solution(16079831399558396635)
XLA Ops:
  3.9 3.0 %fusion.215 = (f32[5,4,4,128]{3,2,1,0:T(4,128)S(1)}, f32[5,4,4,1,128]{4,3,2,1,0:T(1,128)}, f32[5,4,4,1,128]{4,3,2,1,0:T(1,128)}, f32[5,4,4,1,128]{4,3,2,1,0:T(1,128)}, f32[5,4,4,1,128]{4,3,2,1,0:T(1,128)}) fusion(f32[]{:T(128)} %broadcast.1614, f32[5,4,4,4,128]{4,3,2,1,0:T(4,128)} %bitcast.165), kind=kLoop, calls=%fused_computation.547 | loop fusion | flops 286720 | bytes 368644 | tf_op jit(solution)/shard_map/add | solution.py:89
  6.9 1.5 %fusion.216 = (f32[5,4,4,128]{3,2,1,0:T(4,128)S(1)}, f32[5,4,4,1,128]{4,3,2,1,0:T(1,128)}, f32[5,4,4,1,128]{4,3,2,1,0:T(1,128)}) fusion(f32[]{:T(128)} %broadcast.1614, f32[5,4,4,4,128]{4,3,2,1,0:T(4,128)S(1)} %bitcast.166), kind=kLoop, calls=%fused_computation.548 | loop fusion | flops 143360 | bytes 286724 | tf_op jit(solution)/shard_map/add | solution.py:89
  10.0 0.8 %add.1232 = f32[5,4,4,4,4,8]{5,4,3,2,1,0:T(4,128)S(1)} reshape(f32[5,4,4,128]{3,2,1,0:T(4,128)S(1)} %get-tuple-element.48) | data formatting | bytes 81920 | tf_op jit(solution)/shard_map/add | solution.py:89
  10.8 1.6 %copy.72 = f32[5,4,4,4,4,1]{0,4,5,3,2,1:T(4,128)S(1)} copy(f32[5,4,4,4,4,1]{5,4,3,2,1,0:T(4,128)S(1)} %bitcast.171) | data formatting | bytes 10240
  13.7 1.6 %copy.71 = f32[5,4,4,4,4,1]{0,4,5,3,2,1:T(4,128)S(1)} copy(f32[5,4,4,4,4,1]{5,4,3,2,1,0:T(4,128)S(1)} %slice.296) | data formatting | bytes 10240
  18.8 3.5 %collective-permute-start.9 = (f32[5,16,16]{2,1,0:T(8,128)S(1)}, f32[5,16,16]{2,1,0:T(8,128)S(1)}, u32[]{:S(2)}, u32[]{:S(2)}) collective-permute-start(f32[5,16,16]{2,1,0:T(8,128)S(1)} %get-tuple-element.104), channel_id=1, source_target_pairs={{0,19},{1,20},{2,21},{3,22},{4,23},{5,16},{6,17},{7,18},{16,5},{17... | collective-permute-start | bytes 15368 | tf_op jit(solution)/shard_map/ppermute | solution.py:239
  22.4 2.7 %collective-permute-start.6 = (f32[5,16,16]{2,1,0:T(8,128)S(1)}, f32[5,16,16]{2,1,0:T(8,128)S(1)}, u32[]{:S(2)}, u32[]{:S(2)}) collective-permute-start(f32[5,16,16]{2,1,0:T(8,128)S(1)} %get-tuple-element.107), channel_id=1, source_target_pairs={{0,22},{1,23},{2,16},{3,17},{4,18},{5,19},{6,20},{7,21},{16,2},{17... | collective-permute-start | bytes 15368 | tf_op jit(solution)/shard_map/ppermute | solution.py:239
  25.3 2.0 %collective-permute-start.5 = (f32[5,16,16]{2,1,0:T(8,128)S(1)}, f32[5,16,16]{2,1,0:T(8,128)S(1)}, u32[]{:S(2)}, u32[]{:S(2)}) collective-permute-start(f32[5,16,16]{2,1,0:T(8,128)S(1)} %get-tuple-element.108), channel_id=1, source_target_pairs={{0,23},{1,16},{2,17},{3,18},{4,19},{5,20},{6,21},{7,22},{16,1},{17... | collective-permute-start | bytes 15368 | tf_op jit(solution)/shard_map/ppermute | solution.py:239
  30.0 1.3 %broadcast_divide_fusion = (f32[3,4,4,4,128]{4,3,2,1,0:T(4,128)}, f32[3,4,4,4,128]{4,3,2,1,0:T(4,128)S(1)}, f32[4,4,4,128]{3,2,1,0:T(4,128)}) fusion(f32[4,4,4,128]{3,2,1,0:T(4,128)S(1)} %get-tuple-element.86, f32[1,5,4,4,4,128]{5,4,3,2,1,0:T(4,128)S(1)} %convert_element_type.66), kind=kLoop, calls=%fused_computation.37 | loop fusion | flops 90112 | bytes 360448 | tf_op jit(solution)/shard_map/jvp()/div | solution.py:111
  31.3 1.5 %slice_bitcast_fusion.2 = f32[5,1,4,4,96]{4,3,2,0,1:T(4,128)} fusion(f32[5,4,4,128]{3,2,1,0:T(4,128)} %bitcast.2), kind=kLoop, calls=%fused_computation.157 | loop fusion | bytes 61440 | tf_op jit(solution)/shard_map/concatenate | solution.py:188
  34.7 0.8 %slice.288 = f32[5,4,4,4,1,8]{5,4,3,2,1,0:T(1,128)} slice(f32[5,4,4,4,4,8]{5,4,3,2,1,0:T(4,128)S(1)} %add.1215), slice={[0:5], [0:4], [0:4], [0:4], [3:4], [0:8]} | slice | bytes 20480 | tf_op jit(solution)/shard_map/slice | solution.py:196
  35.8 2.9 %collective-permute-start.10 = (f32[5,16,16]{2,1,0:T(8,128)S(1)}, f32[5,16,16]{2,1,0:T(8,128)S(1)}, u32[]{:S(2)}, u32[]{:S(2)}) collective-permute-start(f32[5,16,16]{2,1,0:T(8,128)S(1)} %get-tuple-element.103), channel_id=1, source_target_pairs={{0,18},{1,19},{2,20},{3,21},{4,22},{5,23},{6,16},{7,17},{16,6},{17... | collective-permute-start | bytes 15368 | tf_op jit(solution)/shard_map/ppermute | solution.py:239
  38.8 1.5 %collective-permute-start.3 = (f32[5,4,4,4,1,8]{5,4,3,2,1,0:T(1,128)}, f32[5,4,4,4,1,8]{5,4,3,2,1,0:T(1,128)}, u32[]{:S(2)}, u32[]{:S(2)}) collective-permute-start(f32[5,4,4,4,1,8]{5,4,3,2,1,0:T(1,128)} %slice.288), channel_id=1, source_target_pairs={{0,1},{1,2},{2,3},{3,4},{4,5},{5,6},{6,7},{7,0},{8,9},{9,10},{10,1... | collective-permute-start | bytes 30728 | tf_op jit(solution)/shard_map/ppermute | solution.py:195
  40.3 1.5 %collective-permute-start = (f32[5,4,4,32]{3,2,1,0:T(4,128)}, f32[5,4,4,32]{3,2,1,0:T(4,128)}, u32[]{:S(2)}, u32[]{:S(2)}) collective-permute-start(f32[5,4,4,32]{3,2,1,0:T(4,128)} %bitcast.162), channel_id=1, source_target_pairs={{8,0},{9,1},{10,2},{11,3},{12,4},{13,5},{14,6},{15,7},{24,16},{25,... | collective-permute-start | bytes 30728 | tf_op jit(solution)/shard_map/ppermute | solution.py:180
  42.9 2.1 %copy.61 = f32[5,4,4,4,4,1]{5,4,3,2,1,0:T(4,128)S(1)} copy(f32[5,4,4,4,4,1]{2,4,1,3,0,5:T(4,128)S(1)} %bitcast.174) | data formatting | bytes 10240 | tf_op jit(solution)/shard_map/broadcast_in_dim | solution.py:250
  45.8 1.3 %reshape.909 = f32[5,4,4,1,128]{4,3,2,1,0:T(1,128)} reshape(f32[5,4,4,4,4,8]{5,4,3,2,1,0:T(4,128)S(1)} %pad_maximum_fusion.2) | data formatting | bytes 81920 | tf_op jit(solution)/shard_map/reshape | solution.py:250
  48.3 2.1 %copy.63 = f32[5,4,4,4,4,1]{5,4,3,2,1,0:T(4,128)S(1)} copy(f32[5,4,4,4,4,1]{2,4,1,3,0,5:T(4,128)S(1)} %bitcast.175) | data formatting | bytes 10240 | tf_op jit(solution)/shard_map/broadcast_in_dim | solution.py:253
  54.4 1.3 %pad_maximum_fusion.1 = f32[5,4,4,4,4,8]{5,4,3,2,1,0:T(4,128)S(1)} fusion(f32[5,4,4,4,3,8]{5,4,3,2,1,0:T(4,128)S(1)} %bitcast.173, f32[5,4,4,4,1,8]{5,4,3,2,1,0:T(1,128)} %collective-permute-done.3), kind=kLoop, calls=%fused_computation.1 | loop fusion | flops 10240 | bytes 81920 | tf_op jit(solution)/shard_map/concatenate | solution.py:201
  57.4 5.2 %collective-permute-start.2 = (f32[5,4,4,4,1,8]{5,4,3,2,1,0:T(1,128)S(1)}, f32[5,4,4,4,1,8]{5,4,3,2,1,0:T(1,128)S(1)}, u32[]{:S(2)}, u32[]{:S(2)}) collective-permute-start(f32[5,4,4,4,1,8]{5,4,3,2,1,0:T(1,128)S(1)} %slice.287), channel_id=1, source_target_pairs={{1,0},{2,1},{3,2},{4,3},{5,4},{6,5},{7,6},{0,7},{9,8},{10,9},{11,1... | collective-permute-start | bytes 30728 | tf_op jit(solution)/shard_map/ppermute | solution.py:192
  63.3 0.9 %broadcast_multiply_fusion.54 = (f32[5,1,4,4,128]{4,3,2,0,1:T(4,128)S(1)}, f32[5,1,4,4,128]{4,3,2,0,1:T(4,128)S(1)}, f32[5,1,4,4,128]{4,3,2,1,0:T(4,128)S(1)}, f32[5,1,4,4,128]{4,3,2,0,1:T(4,128)S(1)}) fusion(f32[5,1,4,4,32]{4,3,2,0,1:T(4,128)} %bitcast.4, f32[5,1,4,4,96]{4,3,2,0,1:T(4,128)S(1)} %copy-done.19, f32[5,4,4,4,128]{4,3,2,1,0:T(4,128)S(1)} %bitcast.170), kind=kLoop, calls=%fused_computation.297 | loop fusion | flops 174080 | bytes 368640 | tf_op jit(solution)/shard_map/mul | solution.py:96
  64.3 3.4 %collective-permute-start.1 = (f32[5,4,4,32]{3,2,1,0:T(4,128)S(1)}, f32[5,4,4,32]{3,2,1,0:T(4,128)S(1)}, u32[]{:S(2)}, u32[]{:S(2)}) collective-permute-start(f32[5,4,4,32]{3,2,1,0:T(4,128)S(1)} %slice.272), channel_id=1, source_target_pairs={{0,8},{1,9},{2,10},{3,11},{4,12},{5,13},{6,14},{7,15},{16,24},{17,... | collective-permute-start | bytes 30728 | tf_op jit(solution)/shard_map/ppermute | solution.py:183
  69.7 0.9 %broadcast_multiply_fusion.47 = (f32[5,1,4,4,128]{4,3,2,0,1:T(4,128)S(1)}, f32[5,1,4,4,128]{4,3,2,0,1:T(4,128)S(1)}) fusion(f32[5,1,4,4,128]{4,3,2,0,1:T(4,128)} %get-tuple-element.89, f32[5,1,4,4,96]{4,3,2,0,1:T(4,128)S(1)} %slice_bitcast_fusion.1, f32[5,1,4,4,32]{4,3,2,0,1:T(4,128)S(1)} %bitcast.179), kind=kLoop, calls=%fused_computation.290 | loop fusion | flops 30720 | bytes 163840 | tf_op jit(solution)/shard_map/mul | solution.py:96
  73.1 0.8 %multiply_add_fusion.16 = (f32[1,4,4,4,128]{4,3,2,1,0:T(4,128)S(1)}, f32[1,4,4,4,128]{4,3,2,1,0:T(4,128)S(1)}) fusion(f32[5,4,4,4,128]{4,3,2,1,0:T(4,128)S(1)} %fusion, f32[3,4,4,4,128]{4,3,2,1,0:T(4,128)S(1)} %get-tuple-element.53, f32[4,4,4,128]{3,2,1,0:T(4,128)S(1)} %copy-done.23, f32[4,4,4,128]{3,2,1,0:T(4,128)S(1)} %copy-done.24, ...), kind=kLoop, calls=%fused_computation.221 | loop fusion | flops 122880 | bytes 425984 | tf_op jit(solution)/shard_map/transpose(jvp())/add_any | solution.py:119
  75.1 0.9 %bitcast_add_fusion = (f32[1,5,4,4,4,128]{5,4,3,2,1,0:T(4,128)}, f32[5,4,4,4,128]{4,3,2,1,0:T(4,128)}) fusion(f32[1,5,4,4,4,128]{5,4,3,2,1,0:T(4,128)S(1)} %copy-done, f32[1,4,4,4,128]{4,3,2,1,0:T(4,128)S(1)} %negate_bitcast_fusion, f32[3,4,4,4,128]{4,3,2,1,0:T(4,128)S(1)} %get-tuple-element.99, f32[1,4,4,4,128]{4,3,2,1,0:T(4,128)S(1)} %get-tuple-element.73, ...), kind=kLoop, calls=%fused_computation.17 | loop fusion | flops 573440 | bytes 983040 | tf_op jit(solution)/shard_map/add | solution.py:262
  (296 shorter events, 28.3 us)
Async XLA Ops:
  8.7 9.0 %copy-start.26 = (f32[16,16]{1,0:T(8,128)}, f32[16,16]{1,0:T(8,128)S(1)}, u32[]{:S(2)}) copy-start(f32[16,16]{1,0:T(8,128)S(1)} %mul.1447) | copy-start | bytes 3076
  8.8 8.9 %copy-start.28 = (f32[16,16]{1,0:T(8,128)}, f32[16,16]{1,0:T(8,128)S(1)}, u32[]{:S(2)}) copy-start(f32[16,16]{1,0:T(8,128)S(1)} %mul.1450) | copy-start | bytes 3076
  8.9 8.8 %copy-start.30 = (f32[16,16]{1,0:T(8,128)}, f32[16,16]{1,0:T(8,128)S(1)}, u32[]{:S(2)}) copy-start(f32[16,16]{1,0:T(8,128)S(1)} %mul.1453) | copy-start | bytes 3076
  9.0 8.7 %copy-start.32 = (f32[16,16]{1,0:T(8,128)}, f32[16,16]{1,0:T(8,128)S(1)}, u32[]{:S(2)}) copy-start(f32[16,16]{1,0:T(8,128)S(1)} %mul.1456) | copy-start | bytes 3076
  9.1 8.7 %copy-start.34 = (f32[16,16]{1,0:T(8,128)}, f32[16,16]{1,0:T(8,128)S(1)}, u32[]{:S(2)}) copy-start(f32[16,16]{1,0:T(8,128)S(1)} %mul.1459) | copy-start | bytes 3076
  9.1 8.6 %copy-start.36 = (f32[16,16]{1,0:T(8,128)}, f32[16,16]{1,0:T(8,128)S(1)}, u32[]{:S(2)}) copy-start(f32[16,16]{1,0:T(8,128)S(1)} %mul.1462) | copy-start | bytes 3076
  9.2 8.5 %copy-start.38 = (f32[16,16]{1,0:T(8,128)}, f32[16,16]{1,0:T(8,128)S(1)}, u32[]{:S(2)}) copy-start(f32[16,16]{1,0:T(8,128)S(1)} %mul.1465) | copy-start | bytes 3076
  9.3 8.4 %copy-start.40 = (f32[16,16]{1,0:T(8,128)}, f32[16,16]{1,0:T(8,128)S(1)}, u32[]{:S(2)}) copy-start(f32[16,16]{1,0:T(8,128)S(1)} %mul.1468) | copy-start | bytes 3076
  9.4 8.4 %copy-start.42 = (f32[16,16]{1,0:T(8,128)}, f32[16,16]{1,0:T(8,128)S(1)}, u32[]{:S(2)}) copy-start(f32[16,16]{1,0:T(8,128)S(1)} %mul.1471) | copy-start | bytes 3076
  9.5 8.3 %copy-start.44 = (f32[16,16]{1,0:T(8,128)}, f32[16,16]{1,0:T(8,128)S(1)}, u32[]{:S(2)}) copy-start(f32[16,16]{1,0:T(8,128)S(1)} %mul.1474) | copy-start | bytes 3076
  9.6 8.2 %copy-start.46 = (f32[16,16]{1,0:T(8,128)}, f32[16,16]{1,0:T(8,128)S(1)}, u32[]{:S(2)}) copy-start(f32[16,16]{1,0:T(8,128)S(1)} %mul.1477) | copy-start | bytes 3076
  9.7 8.2 %copy-start.48 = (f32[16,16]{1,0:T(8,128)}, f32[16,16]{1,0:T(8,128)S(1)}, u32[]{:S(2)}) copy-start(f32[16,16]{1,0:T(8,128)S(1)} %mul.1480) | copy-start | bytes 3076
  18.8 22.9 %collective-permute-start.9 = (f32[5,16,16]{2,1,0:T(8,128)S(1)}, f32[5,16,16]{2,1,0:T(8,128)S(1)}, u32[]{:S(2)}, u32[]{:S(2)}) collective-permute-start(f32[5,16,16]{2,1,0:T(8,128)S(1)} %get-tuple-element.104), channel_id=1, source_target_pairs={{0,19},{1,20},{2,21},{3,22},{4,23},{5,16},{6,17},{7,18},{16,5},{17... | collective-permute-start | bytes 15368 | tf_op jit(solution)/shard_map/ppermute | solution.py:239
  22.4 16.3 %collective-permute-start.6 = (f32[5,16,16]{2,1,0:T(8,128)S(1)}, f32[5,16,16]{2,1,0:T(8,128)S(1)}, u32[]{:S(2)}, u32[]{:S(2)}) collective-permute-start(f32[5,16,16]{2,1,0:T(8,128)S(1)} %get-tuple-element.107), channel_id=1, source_target_pairs={{0,22},{1,23},{2,16},{3,17},{4,18},{5,19},{6,20},{7,21},{16,2},{17... | collective-permute-start | bytes 15368 | tf_op jit(solution)/shard_map/ppermute | solution.py:239
  25.2 10.3 %collective-permute-start.4 = (f32[5,16,16]{2,1,0:T(8,128)S(1)}, f32[5,16,16]{2,1,0:T(8,128)S(1)}, u32[]{:S(2)}, u32[]{:S(2)}) collective-permute-start(f32[5,16,16]{2,1,0:T(8,128)S(1)} %get-tuple-element.109), channel_id=1, source_target_pairs={{0,16},{1,17},{2,18},{3,19},{4,20},{5,21},{6,22},{7,23},{16,0},{17... | collective-permute-start | bytes 15368 | tf_op jit(solution)/shard_map/ppermute | solution.py:239
  25.3 10.5 %collective-permute-start.5 = (f32[5,16,16]{2,1,0:T(8,128)S(1)}, f32[5,16,16]{2,1,0:T(8,128)S(1)}, u32[]{:S(2)}, u32[]{:S(2)}) collective-permute-start(f32[5,16,16]{2,1,0:T(8,128)S(1)} %get-tuple-element.108), channel_id=1, source_target_pairs={{0,23},{1,16},{2,17},{3,18},{4,19},{5,20},{6,21},{7,22},{16,1},{17... | collective-permute-start | bytes 15368 | tf_op jit(solution)/shard_map/ppermute | solution.py:239
  27.2 11.6 %collective-permute-start.7 = (f32[5,16,16]{2,1,0:T(8,128)S(1)}, f32[5,16,16]{2,1,0:T(8,128)S(1)}, u32[]{:S(2)}, u32[]{:S(2)}) collective-permute-start(f32[5,16,16]{2,1,0:T(8,128)S(1)} %get-tuple-element.106), channel_id=1, source_target_pairs={{0,21},{1,22},{2,23},{3,16},{4,17},{5,18},{6,19},{7,20},{16,3},{17... | collective-permute-start | bytes 15368 | tf_op jit(solution)/shard_map/ppermute | solution.py:239
  35.5 4.7 %collective-permute-start.8 = (f32[5,16,16]{2,1,0:T(8,128)S(1)}, f32[5,16,16]{2,1,0:T(8,128)S(1)}, u32[]{:S(2)}, u32[]{:S(2)}) collective-permute-start(f32[5,16,16]{2,1,0:T(8,128)S(1)} %get-tuple-element.105), channel_id=1, source_target_pairs={{0,20},{1,21},{2,22},{3,23},{4,16},{5,17},{6,18},{7,19},{16,4},{17... | collective-permute-start | bytes 15368 | tf_op jit(solution)/shard_map/ppermute | solution.py:239
  35.8 6.0 %collective-permute-start.10 = (f32[5,16,16]{2,1,0:T(8,128)S(1)}, f32[5,16,16]{2,1,0:T(8,128)S(1)}, u32[]{:S(2)}, u32[]{:S(2)}) collective-permute-start(f32[5,16,16]{2,1,0:T(8,128)S(1)} %get-tuple-element.103), channel_id=1, source_target_pairs={{0,18},{1,19},{2,20},{3,21},{4,22},{5,23},{6,16},{7,17},{16,6},{17... | collective-permute-start | bytes 15368 | tf_op jit(solution)/shard_map/ppermute | solution.py:239
  38.6 3.5 %collective-permute-start.11 = (f32[5,16,16]{2,1,0:T(8,128)S(1)}, f32[5,16,16]{2,1,0:T(8,128)S(1)}, u32[]{:S(2)}, u32[]{:S(2)}) collective-permute-start(f32[5,16,16]{2,1,0:T(8,128)S(1)} %get-tuple-element.102), channel_id=1, source_target_pairs={{0,17},{1,18},{2,19},{3,20},{4,21},{5,22},{6,23},{7,16},{16,7},{17... | collective-permute-start | bytes 15368 | tf_op jit(solution)/shard_map/ppermute | solution.py:239
  38.8 15.6 %collective-permute-start.3 = (f32[5,4,4,4,1,8]{5,4,3,2,1,0:T(1,128)}, f32[5,4,4,4,1,8]{5,4,3,2,1,0:T(1,128)}, u32[]{:S(2)}, u32[]{:S(2)}) collective-permute-start(f32[5,4,4,4,1,8]{5,4,3,2,1,0:T(1,128)} %slice.288), channel_id=1, source_target_pairs={{0,1},{1,2},{2,3},{3,4},{4,5},{5,6},{6,7},{7,0},{8,9},{9,10},{10,1... | collective-permute-start | bytes 30728 | tf_op jit(solution)/shard_map/ppermute | solution.py:195
  40.3 22.3 %collective-permute-start = (f32[5,4,4,32]{3,2,1,0:T(4,128)}, f32[5,4,4,32]{3,2,1,0:T(4,128)}, u32[]{:S(2)}, u32[]{:S(2)}) collective-permute-start(f32[5,4,4,32]{3,2,1,0:T(4,128)} %bitcast.162), channel_id=1, source_target_pairs={{8,0},{9,1},{10,2},{11,3},{12,4},{13,5},{14,6},{15,7},{24,16},{25,... | collective-permute-start | bytes 30728 | tf_op jit(solution)/shard_map/ppermute | solution.py:180
  57.4 10.6 %collective-permute-start.2 = (f32[5,4,4,4,1,8]{5,4,3,2,1,0:T(1,128)S(1)}, f32[5,4,4,4,1,8]{5,4,3,2,1,0:T(1,128)S(1)}, u32[]{:S(2)}, u32[]{:S(2)}) collective-permute-start(f32[5,4,4,4,1,8]{5,4,3,2,1,0:T(1,128)S(1)} %slice.287), channel_id=1, source_target_pairs={{1,0},{2,1},{3,2},{4,3},{5,4},{6,5},{7,6},{0,7},{9,8},{10,9},{11,1... | collective-permute-start | bytes 30728 | tf_op jit(solution)/shard_map/ppermute | solution.py:192
  64.3 5.4 %collective-permute-start.1 = (f32[5,4,4,32]{3,2,1,0:T(4,128)S(1)}, f32[5,4,4,32]{3,2,1,0:T(4,128)S(1)}, u32[]{:S(2)}, u32[]{:S(2)}) collective-permute-start(f32[5,4,4,32]{3,2,1,0:T(4,128)S(1)} %slice.272), channel_id=1, source_target_pairs={{0,8},{1,9},{2,10},{3,11},{4,12},{5,13},{6,14},{7,15},{16,24},{17,... | collective-permute-start | bytes 30728 | tf_op jit(solution)/shard_map/ppermute | solution.py:183
  (76 other events, 123.5 us)

commit v2 on v1

--- a/solution.py
+++ b/solution.py
@@ -3,6 +3,8 @@
 import jax
 import jax.numpy as jnp
 from jax import lax
+from jax.experimental import pallas as pl
+from jax.experimental.pallas import tpu as pltpu
 from jax.sharding import PartitionSpec as P
 
 EA = 4
@@ -167,44 +169,129 @@
     return total
 
 
+def lane_roll(value, shift):
+    return pltpu.roll(value, shift % 128, value.ndim - 1)
+
+
+def sweep(field, weights, pick):
+    total = field[pick(0)] * float(weights[0])
+    for source in range(1, 4):
+        total = total + field[pick(source)] * float(weights[source])
+    return total
+
+
+def column(values, shape):
+    rows = lax.broadcasted_iota(jnp.int32, shape, 2)
+    out = jnp.full(shape, float(values[3]), jnp.float32)
+    for index in range(3):
+        out = jnp.where(rows == index, float(values[index]), out)
+    return out
+
+
+def rate_kernel(
+    adj_ref, flow_ref, up_ax_ref, down_ax_ref, up_az_ref, down_az_ref, outer_ref, inner_ref,
+    rate_ref, next_ref,
+):
+    derivs, left_vals, right_vals, left_corr, right_corr = basis_tables()
+    shape = (4, 4, 4, 128)
+    lane = lax.broadcasted_iota(jnp.int32, shape, 3)
+    flat_lane = lax.broadcasted_iota(jnp.int32, (4, 4, 128), 2)
+    az_flat = flat_lane // ER % ET
+    radial_lane = lane % ER
+    brackets = [[None] * 5 for _ in range(3)]
+    for chan in range(5):
+        field = adj_ref[0, chan]
+        left0 = sweep(field, left_corr, lambda i: (i,))
+        right0 = sweep(field, right_corr, lambda i: (i,))
+        next0 = lane_roll(jnp.where(flat_lane < ET * ER, up_ax_ref[chan], left0), -ET * ER)
+        prev0 = lane_roll(jnp.where(flat_lane >= (EA - 1) * ET * ER, down_ax_ref[chan], right0), ET * ER)
+        jump_r = 0.5 * (next0 - right0)
+        jump_l = 0.5 * (prev0 - left0)
+        slabs = []
+        for target in range(4):
+            slab = sweep(field, [derivs[i][target] for i in range(4)], lambda i: (i,))
+            slabs.append(slab + jump_r * float(right_vals[target]) + jump_l * float(left_vals[target]))
+        brackets[0][chan] = jnp.stack(slabs, axis=0)
+        pick1 = lambda i: (slice(None), i)
+        left1 = sweep(field, left_corr, pick1)
+        right1 = sweep(field, right_corr, pick1)
+        next1 = lane_roll(
+            jnp.where(az_flat == 0, lane_roll(up_az_ref[chan], ET * ER), left1), -ER
+        )
+        prev1 = lane_roll(
+            jnp.where(az_flat == ET - 1, lane_roll(down_az_ref[chan], -ET * ER), right1), ER
+        )
+        jump_r = 0.5 * (next1 - right1)
+        jump_l = 0.5 * (prev1 - left1)
+        slabs = []
+        for target in range(4):
+            slab = sweep(field, [derivs[i][target] for i in range(4)], pick1)
+            slabs.append(slab + jump_r * float(right_vals[target]) + jump_l * float(left_vals[target]))
+        brackets[1][chan] = jnp.stack(slabs, axis=1)
+        points = [jnp.broadcast_to(field[:, :, i : i + 1, :], shape) for i in range(4)]
+        left2 = sweep(points, left_corr, lambda i: i)
+        right2 = sweep(points, right_corr, lambda i: i)
+        next2 = jnp.where(radial_lane == ER - 1, outer_ref[chan], lane_roll(left2, -1))
+        prev2 = jnp.where(radial_lane == 0, inner_ref[chan], lane_roll(right2, 1))
+        bracket = 0.5 * (next2 - right2) * column(right_vals, shape)
+        bracket = bracket + 0.5 * (prev2 - left2) * column(left_vals, shape)
+        for source in range(4):
+            bracket = bracket + points[source] * column(derivs[source], shape)
+        brackets[2][chan] = bracket
+    prim = [flow_ref[0, chan].astype(jnp.float32) for chan in range(5)]
+    density = prim[0]
+    speed_sq = prim[1] * prim[1] + prim[2] * prim[2] + prim[3] * prim[3]
+    energy = prim[4] / (GAMMA - 1.0) + 0.5 * density * speed_sq
+    momentum = [density * prim[1 + k] for k in range(3)]
+    velocity = [momentum[k] / density for k in range(3)]
+    kinetic = momentum[0] * velocity[0] + momentum[1] * velocity[1] + momentum[2] * velocity[2]
+    pressure = (GAMMA - 1.0) * (energy - 0.5 * kinetic)
+    enthalpy = (energy + pressure) / density
+    vel_sq = velocity[0] * velocity[0] + velocity[1] * velocity[1] + velocity[2] * velocity[2]
+    grad = [None] * 5
+    for direction in range(3):
+        cot = brackets[direction]
+        normal = velocity[direction]
+        dotted = cot[1] * velocity[0] + cot[2] * velocity[1] + cot[3] * velocity[2] + cot[4] * enthalpy
+        weight = cot[1 + direction] + cot[4] * normal
+        terms = [
+            0.5 * (GAMMA - 1.0) * vel_sq * weight - dotted * normal,
+            None,
+            None,
+            None,
+            (GAMMA - 1.0) * weight + cot[4] * normal,
+        ]
+        for k in range(3):
+            term = cot[1 + k] * normal - (GAMMA - 1.0) * weight * velocity[k]
+            if k == direction:
+                term = term + (cot[0] + dotted)
+            terms[1 + k] = term
+        for chan in range(5):
+            grad[chan] = terms[chan] if grad[chan] is None else grad[chan] + terms[chan]
+    for chan in range(5):
+        rate = -METRIC * grad[chan]
+        rate_ref[0, chan] = rate
+        next_ref[0, chan] = adj_ref[0, chan] + SECTION_STEP * rate
+
+
 def local(adjoint, flow_prim, intersection_shift, weight_index, mortar_weights, sector_offset):
-    elem_count = EA * ET * ER
     n_axial = lax.axis_size("axial")
     n_azim = lax.axis_size("azim")
     adj_field = adjoint[0]
-    cons_state = conserved(flow_prim[0].astype(jnp.float32))
-    left_moments, right_moments = all_moments(adj_field)
+    derivs, left_vals, right_vals, left_corr, right_corr = basis_tables()
+    left_ax = face_moment(adj_field, left_corr, 1)
+    right_ax = face_moment(adj_field, right_corr, 1)
+    left_az = face_moment(adj_field, left_corr, 2)
+    right_az = face_moment(adj_field, right_corr, 2)
     is_rotor = lax.axis_index("zone") == 0
+    up_ax = lax.ppermute(left_ax, "axial", [(i + 1, i) for i in range(n_axial - 1)])
+    down_ax = lax.ppermute(right_ax, "axial", [(i, i + 1) for i in range(n_axial - 1)])
+    up_az = lax.ppermute(left_az, "azim", [((j + 1) % n_azim, j) for j in range(n_azim)])
+    down_az = lax.ppermute(right_az, "azim", [(j, (j + 1) % n_azim) for j in range(n_azim)])
     face_shape = (5, 4, 4, EA, ET, ER)
-    ax_span = ET * ER
-    upper_axial = lax.ppermute(
-        left_moments[0][..., :ax_span], "axial", [(i + 1, i) for i in range(n_axial - 1)]
-    )
-    lower_axial = lax.ppermute(
-        right_moments[0][..., elem_count - ax_span :],
-        "axial",
-        [(i, i + 1) for i in range(n_axial - 1)],
-    )
-    next_axial = jnp.concatenate([left_moments[0][..., ax_span:], upper_axial], axis=-1)
-    prev_axial = jnp.concatenate([lower_axial, right_moments[0][..., : elem_count - ax_span]], axis=-1)
-    left_az = left_moments[1].reshape(face_shape)
-    right_az = right_moments[1].reshape(face_shape)
-    upper_azim = lax.ppermute(
-        left_az[:, :, :, :, :1], "azim", [((j + 1) % n_azim, j) for j in range(n_azim)]
-    )
-    lower_azim = lax.ppermute(
-        right_az[:, :, :, :, ET - 1 :], "azim", [(j, (j + 1) % n_azim) for j in range(n_azim)]
-    )
-    next_azim = jnp.concatenate([left_az[:, :, :, :, 1:], upper_azim], axis=4).reshape(
-        5, 4, 4, elem_count
-    )
-    prev_azim = jnp.concatenate([lower_azim, right_az[:, :, :, :, : ET - 1]], axis=4).reshape(
-        5, 4, 4, elem_count
-    )
-    left_rad = left_moments[2].reshape(face_shape)
-    right_rad = right_moments[2].reshape(face_shape)
-    own_face = jnp.where(is_rotor, right_rad[..., -1], left_rad[..., 0])
-    own_rows = faces_to_rows(own_face)
+    outer_moment = face_moment(adj_field, right_corr, 3).reshape(face_shape)[..., ER - 1]
+    inner_moment = face_moment(adj_field, left_corr, 3).reshape(face_shape)[..., 0]
+    own_rows = faces_to_rows(jnp.where(is_rotor, outer_moment, inner_moment))
     shifts_local = intersection_shift.reshape(INTERSECTIONS, AP, TP)
     table_match = weight_index[:, :, None] == jnp.arange(NW, dtype=jnp.int32)[None, None, :]
     weights_local = jnp.sum(
@@ -245,21 +332,16 @@
     returned = picked[0] + picked[1] + picked[2]
     window = jnp.concatenate(picked, axis=2)
     incoming = shift_sum(window, coefs, TP)
-    outer_face = jnp.where(is_rotor, rows_to_face(returned, EA, ET), 0.0)
-    inner_face = jnp.where(is_rotor, 0.0, rows_to_face(incoming, EA, ET))
-    next_radial = jnp.concatenate([left_rad[..., 1:], outer_face[..., None]], axis=5).reshape(
-        5, 4, 4, elem_count
-    )
-    prev_radial = jnp.concatenate([inner_face[..., None], right_rad[..., :-1]], axis=5).reshape(
-        5, 4, 4, elem_count
-    )
-    next_left = [next_axial, next_azim, next_radial]
-    prev_right = [prev_axial, prev_azim, prev_radial]
-    rate_sum = section_rate(
-        adj_field, cons_state, left_moments, right_moments, next_left, prev_right
-    )
-    adjoint_rate = rate_sum.reshape(1, 5, 4, 4, 4, elem_count)
-    next_adjoint = adjoint + SECTION_STEP * adjoint_rate
+    iface = rows_to_face(jnp.where(is_rotor, returned, incoming), EA, ET)
+    iface = jnp.broadcast_to(
+        iface[:, :, :, None, :, :, None], (5, 4, 4, 4, EA, ET, ER)
+    ).reshape(5, 4, 4, 4, EA * ET * ER)
+    outer = jnp.where(is_rotor, iface, 0.0)
+    inner = jnp.where(is_rotor, 0.0, iface)
+    field_shape = jax.ShapeDtypeStruct(adjoint.shape, jnp.float32)
+    adjoint_rate, next_adjoint = pl.pallas_call(
+        rate_kernel, out_shape=(field_shape, field_shape)
+    )(adjoint, flow_prim, up_ax, down_ax, up_az, down_az, outer, inner)
     return (adjoint_rate, next_adjoint)
 
 

time: 77.2 us -> 47.9 us (0.62); the launches traced: 76 us -> 47.6 us
  other arithmetic: 19.2 us -> 2.82 us
  local copies, waits for them, and re-layouts: 29.8 us -> 16.1 us
  starting transfers between devices: 23.5 us -> 17.2 us
  waiting for transfers between devices: 0.81 us -> 6.46 us
  Pallas kernels: 0 us -> 3.15 us
  between operations: 2.67 us -> 1.82 us
    unnamed x185 -> x22, local copies, waits for them, and re-layouts: 11.5 us -> 4.76 us
    ppermute x8, waiting for transfers between devices: 0.35 us -> 5.39 us  [local(): received.append(lax.ppermute(payload, ('zone', 'azim'), pairs))]
    add x3, other arithmetic: 5.2 us -> 0.52 us  [face_moment(): running + lax.index_in_dim(adj_field, source, point_dim, keepdims=False)...]
    ppermute x4, starting transfers between devices: 11.6 us -> 8.16 us  [the longest x1 4.55 us: local(): lax.ppermute(right_ax, 'axial', [(i, i + 1) for i in range(n_axial - 1)])]
    reshape x4 -> x0, local copies, waits for them, and re-layouts: 3.3 us -> none  [the longest x1 1.3 us: local(): jnp.concatenate([left_rad[..., 1:], outer_face[..., None]], axis=5)]
    pallas_call x0 -> x1, Pallas kernels: none -> 3.15 us  [local(): pl.pallas_call(rate_kernel, out_shape=(field_shape, field_shape))]
    mul x12 -> x0, other arithmetic: 2.98 us -> none  [the longest x11 2.32 us: lift_face(): face_vals * float(vector[target])]
    ppermute x8, starting transfers between devices: 12 us -> 9.09 us  [local(): received.append(lax.ppermute(payload, ('zone', 'azim'), pairs))]
  transfers between devices with their start and end apart: 12 -> 12, of which waited for: 2 -> 3; matrix products, arithmetic and copies ran while one was open for 30% -> 12% of each run, Pallas kernels for 0% -> 0%
where the time goes in v2:
time: 47.9 us; the launch traced here: 47.6 us
  starting transfers between devices  17.2 us (36%)
  local copies, waits for them, and re-layouts  16.1 us (34%)
  waiting for transfers between devices  6.46 us (13%)
  Pallas kernels  3.15 us (7%)
  other arithmetic  2.82 us (6%)
  between operations  1.82 us (4%)
    ppermute x8, starting transfers between devices, local(): received.append(lax.ppermute(payload, ('zone', 'azim'), pairs))  9.09 us
    ppermute x8, waiting for transfers between devices, local(): received.append(lax.ppermute(payload, ('zone', 'azim'), pairs))  5.39 us
    unnamed x22, local copies, waits for them, and re-layouts  4.76 us
    ppermute x1, starting transfers between devices, local(): lax.ppermute(right_ax, 'axial', [(i, i + 1) for i in range(n_axial - 1)])  4.55 us
    pallas_call x1, Pallas kernels, local(): pl.pallas_call(rate_kernel, out_shape=(field_shape, field_shape))  3.15 us
    mul x31, local copies, waits for them, and re-layouts, local(): coef[None] * own_rows  2.38 us
    ppermute x1, starting transfers between devices, local(): lax.ppermute(left_az, 'azim', [((j + 1) % n_azim, j) for j in range(n_azi...  2.28 us
    broadcast_in_dim x4, local copies, waits for them, and re-layouts, local(): jnp.broadcast_to(iface[:, :, :, None, :, :, None], (5, 4, 4, 4, EA, ET, ER))  2.19 us
  transfers between devices with their start and end apart: 12, of which 3 were waited for; matrix products, arithmetic and copies ran while one was open for 12% of the time, Pallas kernels for 0%

profile of v2, /device:TPU:0, one launch (start us, length us, event | category | flops | bytes accessed | tf_op | source)
XLA Modules:
  0.0 47.6 jit_solution(5531164978997661715)
XLA Ops:
  1.3 0.7 %copy-done.3 = s32[4,256]{1,0:T(4,128)S(1)} copy-done((s32[4,256]{1,0:T(4,128)S(1)}, s32[4,256]{1,0:T(4,128)}, u32[]{:S(2)}) %copy-start.3) | copy-done | bytes 4120
  2.0 0.7 %copy-done.4 = s32[4,256]{1,0:T(4,128)S(1)} copy-done((s32[4,256]{1,0:T(4,128)S(1)}, s32[4,256]{1,0:T(4,128)}, u32[]{:S(2)}) %copy-start.4) | copy-done | bytes 4120
  5.0 0.8 %add.883 = f32[5,4,4,4,4,8]{5,4,3,1,0,2:T(4,128)S(1)} reshape(f32[5,4,4,128]{3,1,0,2:T(4,128)S(1)} %get-tuple-element.3) | data formatting | bytes 81920 | tf_op jit(solution)/shard_map/add | solution.py:91
  6.2 1.6 %copy.27 = f32[5,4,4,4,4,1]{0,4,5,3,2,1:T(4,128)S(1)} copy(f32[5,4,4,4,4,1]{5,4,3,1,0,2:T(4,128)S(1)} %slice.211) | data formatting | bytes 10240
  7.8 0.8 %add.887 = f32[5,4,4,4,4,8]{5,4,3,1,0,2:T(4,128)S(1)} reshape(f32[5,4,4,128]{3,1,0,2:T(4,128)S(1)} %get-tuple-element.2) | data formatting | bytes 81920 | tf_op jit(solution)/shard_map/add | solution.py:91
  8.7 1.6 %copy.28 = f32[5,4,4,4,4,1]{0,4,5,3,2,1:T(4,128)S(1)} copy(f32[5,4,4,4,4,1]{5,4,3,1,0,2:T(4,128)S(1)} %bitcast.47) | data formatting | bytes 10240
  10.3 0.6 %copy.22 = f32[5,4,4,4,4]{4,3,2,1,0:T(4,128)S(1)} copy(f32[5,4,4,4,4]{0,3,1,4,2:T(4,128)S(1)} %select_bitcast_fusion) | data formatting | bytes 10240 | tf_op jit(solution)/shard_map/transpose | solution.py:157
  13.2 3.5 %collective-permute-start.9 = (f32[5,16,16]{2,1,0:T(8,128)S(1)}, f32[5,16,16]{2,1,0:T(8,128)S(1)}, u32[]{:S(2)}, u32[]{:S(2)}) collective-permute-start(f32[5,16,16]{2,1,0:T(8,128)S(1)} %get-tuple-element.45), channel_id=1, source_target_pairs={{0,19},{1,20},{2,21},{3,22},{4,23},{5,16},{6,17},{7,18},{16,5},{17... | collective-permute-start | bytes 15368 | tf_op jit(solution)/shard_map/ppermute | solution.py:326
  16.8 2.7 %collective-permute-start.6 = (f32[5,16,16]{2,1,0:T(8,128)S(1)}, f32[5,16,16]{2,1,0:T(8,128)S(1)}, u32[]{:S(2)}, u32[]{:S(2)}) collective-permute-start(f32[5,16,16]{2,1,0:T(8,128)S(1)} %get-tuple-element.48), channel_id=1, source_target_pairs={{0,22},{1,23},{2,16},{3,17},{4,18},{5,19},{6,20},{7,21},{16,2},{17... | collective-permute-start | bytes 15368 | tf_op jit(solution)/shard_map/ppermute | solution.py:326
  19.7 2.0 %collective-permute-start.5 = (f32[5,16,16]{2,1,0:T(8,128)S(1)}, f32[5,16,16]{2,1,0:T(8,128)S(1)}, u32[]{:S(2)}, u32[]{:S(2)}) collective-permute-start(f32[5,16,16]{2,1,0:T(8,128)S(1)} %get-tuple-element.49), channel_id=1, source_target_pairs={{0,23},{1,16},{2,17},{3,18},{4,19},{5,20},{6,21},{7,22},{16,1},{17... | collective-permute-start | bytes 15368 | tf_op jit(solution)/shard_map/ppermute | solution.py:326
  22.6 3.7 %collective-permute-done.5 = f32[5,16,16]{2,1,0:T(8,128)S(1)} collective-permute-done((f32[5,16,16]{2,1,0:T(8,128)S(1)}, f32[5,16,16]{2,1,0:T(8,128)S(1)}, u32[]{:S(2)}, u32[]{:S(2)}) %collective-permute-start.5) | collective-permute-done | bytes 5152 | tf_op jit(solution)/shard_map/ppermute | solution.py:326
  26.4 1.7 %collective-permute-done.7 = f32[5,16,16]{2,1,0:T(8,128)S(1)} collective-permute-done((f32[5,16,16]{2,1,0:T(8,128)S(1)}, f32[5,16,16]{2,1,0:T(8,128)S(1)}, u32[]{:S(2)}, u32[]{:S(2)}) %collective-permute-start.7) | collective-permute-done | bytes 5152 | tf_op jit(solution)/shard_map/ppermute | solution.py:326
  28.1 1.3 %collective-permute-start = (f32[5,4,4,128]{3,2,0,1:T(4,128)S(1)}, f32[5,4,4,128]{3,2,0,1:T(4,128)S(1)}, u32[]{:S(2)}, u32[]{:S(2)}) collective-permute-start(f32[5,4,4,128]{3,2,0,1:T(4,128)S(1)} %get-tuple-element.42), channel_id=1, source_target_pairs={{8,0},{9,1},{10,2},{11,3},{12,4},{13,5},{14,6},{15,7},{24,16},{25,... | collective-permute-start | bytes 122888 | tf_op jit(solution)/shard_map/ppermute | solution.py:287
  29.4 4.5 %collective-permute-start.1 = (f32[5,4,4,128]{3,2,0,1:T(4,128)S(1)}, f32[5,4,4,128]{3,2,0,1:T(4,128)S(1)}, u32[]{:S(2)}, u32[]{:S(2)}) collective-permute-start(f32[5,4,4,128]{3,2,0,1:T(4,128)S(1)} %get-tuple-element.41), channel_id=1, source_target_pairs={{0,8},{1,9},{2,10},{3,11},{4,12},{5,13},{6,14},{7,15},{16,24},{17,... | collective-permute-start | bytes 122888 | tf_op jit(solution)/shard_map/ppermute | solution.py:288
  34.0 2.3 %collective-permute-start.2 = (f32[5,4,4,128]{3,2,1,0:T(4,128)S(1)}, f32[5,4,4,128]{3,2,1,0:T(4,128)S(1)}, u32[]{:S(2)}, u32[]{:S(2)}) collective-permute-start(f32[5,4,4,128]{3,2,1,0:T(4,128)S(1)} %get-tuple-element.40), channel_id=1, source_target_pairs={{1,0},{2,1},{3,2},{4,3},{5,4},{6,5},{7,6},{0,7},{9,8},{10,9},{11,1... | collective-permute-start | bytes 122888 | tf_op jit(solution)/shard_map/ppermute | solution.py:289
  36.4 0.7 %broadcast_select_fusion = (f32[5,16,16]{2,1,0:T(8,128)S(1)}, f32[5,16,16]{2,1,0:T(8,128)S(1)}) fusion(pred[]{:T(512)S(6)} %eq.696, f32[5,16,16]{2,1,0:T(8,128)S(1)} %get-tuple-element.37, f32[5,16,16]{2,1,0:T(8,128)S(1)} %get-tuple-element.38, f32[16,16]{1,0:T(8,128)S(1)} %mul.718, f32[16,16]{1,0:T(8,128)S(1)} %mul.715, f32[16,16]{1,0:T(8,128)S(1)} %mul.712, ...), kind=kLoop, calls=%fused_computation.148 | loop fusion | flops 120320 | bytes 57345 | tf_op jit(solution)/shard_map/jit(_where)/select_n | solution.py:340
  38.3 0.6 %select_n.1231 = f32[5,4,4,128]{3,2,1,0:T(4,128)S(1)} reshape(f32[5,4,4,4,4,8]{5,4,3,2,1,0:T(4,128)S(1)} %broadcast_in_dim.226) | data formatting | bytes 81920 | tf_op jit(solution)/shard_map/jit(_where)/select_n | solution.py:339
  40.1 0.6 %select_n.1235 = f32[5,4,4,128]{3,2,1,0:T(4,128)S(1)} reshape(f32[5,4,4,4,4,8]{5,4,3,2,1,0:T(4,128)S(1)} %broadcast_in_dim.228) | data formatting | bytes 81920 | tf_op jit(solution)/shard_map/jit(_where)/select_n | solution.py:340
  40.8 0.6 %copy.25.up_ax_ref = f32[5,4,4,128]{3,2,1,0:T(4,128)} copy(f32[5,4,4,128]{3,2,0,1:T(4,128)S(1)} %collective-permute-done) | data formatting | bytes 81920 | tf_op jit(solution)/shard_map/ppermute | solution.py:287
  41.4 0.6 %copy.26.down_ax_ref = f32[5,4,4,128]{3,2,1,0:T(4,128)} copy(f32[5,4,4,128]{3,2,0,1:T(4,128)S(1)} %collective-permute-done.1) | data formatting | bytes 81920 | tf_op jit(solution)/shard_map/ppermute | solution.py:288
  42.0 1.1 %collective-permute-done.3.down_az_ref = f32[5,4,4,128]{3,2,1,0:T(4,128)S(1)} collective-permute-done((f32[5,4,4,128]{3,2,1,0:T(4,128)S(1)}, f32[5,4,4,128]{3,2,1,0:T(4,128)S(1)}, u32[]{:S(2)}, u32[]{:S(2)}) %collective-permute-start.3) | collective-permute-done | bytes 40992 | tf_op jit(solution)/shard_map/ppermute | solution.py:290
  43.1 0.7 %broadcast_in_dim.227.outer_ref = f32[5,4,4,4,128]{4,3,2,1,0:T(4,128)} broadcast(f32[5,4,4,128]{3,2,1,0:T(4,128)S(1)} %select_n.1231), dimensions={0,1,2,4} | broadcast | bytes 204800 | tf_op jit(solution)/shard_map/broadcast_in_dim | solution.py:336
  43.7 0.7 %broadcast_in_dim.229.inner_ref = f32[5,4,4,4,128]{4,3,2,1,0:T(4,128)} broadcast(f32[5,4,4,128]{3,2,1,0:T(4,128)S(1)} %select_n.1235), dimensions={0,1,2,4} | broadcast | bytes 204800 | tf_op jit(solution)/shard_map/broadcast_in_dim | solution.py:336
  44.4 3.1 %shard_map.77 = (f32[1,5,4,4,4,128]{5,4,3,2,1,0:T(4,128)}, f32[1,5,4,4,4,128]{5,4,3,2,1,0:T(4,128)}) custom-call(f32[1,5,4,4,4,128]{5,4,3,2,1,0:T(4,128)} %adj_ref.1, bf16[1,5,4,4,4,128]{5,4,3,2,1,0:T(4,128)(2,1)} %flow_ref.1, f32[5,4,4,128]{3,2,1,0:T(4,128)} %copy.25.up_ax_ref, f32[5,4,4,128]{3,2,1,0:T(4,128)} %copy.26.down_ax_ref, ...), custom_call_target="tpu_custom_call" | custom-call | tf_op jit(solution)/shard_map/pallas_call | solution.py:342
  (95 shorter events, 8.5 us)
Async XLA Ops:
  1.3 0.7 %copy-start.3 = (s32[4,256]{1,0:T(4,128)S(1)}, s32[4,256]{1,0:T(4,128)}, u32[]{:S(2)}) copy-start(s32[4,256]{1,0:T(4,128)} %param.8) | copy-start | bytes 12292
  2.0 0.7 %copy-start.4 = (s32[4,256]{1,0:T(4,128)S(1)}, s32[4,256]{1,0:T(4,128)}, u32[]{:S(2)}) copy-start(s32[4,256]{1,0:T(4,128)} %param.9) | copy-start | bytes 12292
  2.0 0.7 %copy-start.5 = (f32[128]{0:T(128)S(1)}, f32[128]{0:T(128)}, u32[]{:S(2)}) copy-start(f32[128]{0:T(128)} %param.10) | copy-start | bytes 1540
  3.1 1.4 %copy-start = (f32[1,5,4,4,4,128]{5,4,3,2,1,0:T(4,128)S(1)}, f32[1,5,4,4,4,128]{5,4,3,2,1,0:T(4,128)}, u32[]{:S(2)}) copy-start(f32[1,5,4,4,4,128]{5,4,3,2,1,0:T(4,128)} %adj_ref.1) | copy-start | bytes 491524
  13.2 20.8 %collective-permute-start.9 = (f32[5,16,16]{2,1,0:T(8,128)S(1)}, f32[5,16,16]{2,1,0:T(8,128)S(1)}, u32[]{:S(2)}, u32[]{:S(2)}) collective-permute-start(f32[5,16,16]{2,1,0:T(8,128)S(1)} %get-tuple-element.45), channel_id=1, source_target_pairs={{0,19},{1,20},{2,21},{3,22},{4,23},{5,16},{6,17},{7,18},{16,5},{17... | collective-permute-start | bytes 15368 | tf_op jit(solution)/shard_map/ppermute | solution.py:326
  16.8 9.6 %collective-permute-start.6 = (f32[5,16,16]{2,1,0:T(8,128)S(1)}, f32[5,16,16]{2,1,0:T(8,128)S(1)}, u32[]{:S(2)}, u32[]{:S(2)}) collective-permute-start(f32[5,16,16]{2,1,0:T(8,128)S(1)} %get-tuple-element.48), channel_id=1, source_target_pairs={{0,22},{1,23},{2,16},{3,17},{4,18},{5,19},{6,20},{7,21},{16,2},{17... | collective-permute-start | bytes 15368 | tf_op jit(solution)/shard_map/ppermute | solution.py:326
  19.6 2.7 %collective-permute-start.4 = (f32[5,16,16]{2,1,0:T(8,128)S(1)}, f32[5,16,16]{2,1,0:T(8,128)S(1)}, u32[]{:S(2)}, u32[]{:S(2)}) collective-permute-start(f32[5,16,16]{2,1,0:T(8,128)S(1)} %get-tuple-element.50), channel_id=1, source_target_pairs={{0,16},{1,17},{2,18},{3,19},{4,20},{5,21},{6,22},{7,23},{16,0},{17... | collective-permute-start | bytes 15368 | tf_op jit(solution)/shard_map/ppermute | solution.py:326
  19.7 6.7 %collective-permute-start.5 = (f32[5,16,16]{2,1,0:T(8,128)S(1)}, f32[5,16,16]{2,1,0:T(8,128)S(1)}, u32[]{:S(2)}, u32[]{:S(2)}) collective-permute-start(f32[5,16,16]{2,1,0:T(8,128)S(1)} %get-tuple-element.49), channel_id=1, source_target_pairs={{0,23},{1,16},{2,17},{3,18},{4,19},{5,20},{6,21},{7,22},{16,1},{17... | collective-permute-start | bytes 15368 | tf_op jit(solution)/shard_map/ppermute | solution.py:326
  21.6 6.5 %collective-permute-start.7 = (f32[5,16,16]{2,1,0:T(8,128)S(1)}, f32[5,16,16]{2,1,0:T(8,128)S(1)}, u32[]{:S(2)}, u32[]{:S(2)}) collective-permute-start(f32[5,16,16]{2,1,0:T(8,128)S(1)} %get-tuple-element.47), channel_id=1, source_target_pairs={{0,21},{1,22},{2,23},{3,16},{4,17},{5,18},{6,19},{7,20},{16,3},{17... | collective-permute-start | bytes 15368 | tf_op jit(solution)/shard_map/ppermute | solution.py:326
  22.3 7.1 %collective-permute-start.8 = (f32[5,16,16]{2,1,0:T(8,128)S(1)}, f32[5,16,16]{2,1,0:T(8,128)S(1)}, u32[]{:S(2)}, u32[]{:S(2)}) collective-permute-start(f32[5,16,16]{2,1,0:T(8,128)S(1)} %get-tuple-element.46), channel_id=1, source_target_pairs={{0,20},{1,21},{2,22},{3,23},{4,16},{5,17},{6,18},{7,19},{16,4},{17... | collective-permute-start | bytes 15368 | tf_op jit(solution)/shard_map/ppermute | solution.py:326
  26.3 10.0 %collective-permute-start.10 = (f32[5,16,16]{2,1,0:T(8,128)S(1)}, f32[5,16,16]{2,1,0:T(8,128)S(1)}, u32[]{:S(2)}, u32[]{:S(2)}) collective-permute-start(f32[5,16,16]{2,1,0:T(8,128)S(1)} %get-tuple-element.44), channel_id=1, source_target_pairs={{0,18},{1,19},{2,20},{3,21},{4,22},{5,23},{6,16},{7,17},{16,6},{17... | collective-permute-start | bytes 15368 | tf_op jit(solution)/shard_map/ppermute | solution.py:326
  26.4 10.0 %collective-permute-start.11 = (f32[5,16,16]{2,1,0:T(8,128)S(1)}, f32[5,16,16]{2,1,0:T(8,128)S(1)}, u32[]{:S(2)}, u32[]{:S(2)}) collective-permute-start(f32[5,16,16]{2,1,0:T(8,128)S(1)} %get-tuple-element.43), channel_id=1, source_target_pairs={{0,17},{1,18},{2,19},{3,20},{4,21},{5,22},{6,23},{7,16},{16,7},{17... | collective-permute-start | bytes 15368 | tf_op jit(solution)/shard_map/ppermute | solution.py:326
  28.1 12.6 %collective-permute-start = (f32[5,4,4,128]{3,2,0,1:T(4,128)S(1)}, f32[5,4,4,128]{3,2,0,1:T(4,128)S(1)}, u32[]{:S(2)}, u32[]{:S(2)}) collective-permute-start(f32[5,4,4,128]{3,2,0,1:T(4,128)S(1)} %get-tuple-element.42), channel_id=1, source_target_pairs={{8,0},{9,1},{10,2},{11,3},{12,4},{13,5},{14,6},{15,7},{24,16},{25,... | collective-permute-start | bytes 122888 | tf_op jit(solution)/shard_map/ppermute | solution.py:287
  29.4 11.9 %collective-permute-start.1 = (f32[5,4,4,128]{3,2,0,1:T(4,128)S(1)}, f32[5,4,4,128]{3,2,0,1:T(4,128)S(1)}, u32[]{:S(2)}, u32[]{:S(2)}) collective-permute-start(f32[5,4,4,128]{3,2,0,1:T(4,128)S(1)} %get-tuple-element.41), channel_id=1, source_target_pairs={{0,8},{1,9},{2,10},{3,11},{4,12},{5,13},{6,14},{7,15},{16,24},{17,... | collective-permute-start | bytes 122888 | tf_op jit(solution)/shard_map/ppermute | solution.py:288
  34.0 8.0 %collective-permute-start.2 = (f32[5,4,4,128]{3,2,1,0:T(4,128)S(1)}, f32[5,4,4,128]{3,2,1,0:T(4,128)S(1)}, u32[]{:S(2)}, u32[]{:S(2)}) collective-permute-start(f32[5,4,4,128]{3,2,1,0:T(4,128)S(1)} %get-tuple-element.40), channel_id=1, source_target_pairs={{1,0},{2,1},{3,2},{4,3},{5,4},{6,5},{7,6},{0,7},{9,8},{10,9},{11,1... | collective-permute-start | bytes 122888 | tf_op jit(solution)/shard_map/ppermute | solution.py:289
  36.3 6.7 %collective-permute-start.3 = (f32[5,4,4,128]{3,2,1,0:T(4,128)S(1)}, f32[5,4,4,128]{3,2,1,0:T(4,128)S(1)}, u32[]{:S(2)}, u32[]{:S(2)}) collective-permute-start(f32[5,4,4,128]{3,2,1,0:T(4,128)S(1)} %get-tuple-element.39), channel_id=1, source_target_pairs={{0,1},{1,2},{2,3},{3,4},{4,5},{5,6},{6,7},{7,0},{8,9},{9,10},{10,1... | collective-permute-start | bytes 122888 | tf_op jit(solution)/shard_map/ppermute | solution.py:290
  42.0 1.7 %copy-start.1 = (f32[5,4,4,128]{3,2,1,0:T(4,128)}, f32[5,4,4,128]{3,2,1,0:T(4,128)S(1)}, u32[]{:S(2)}) copy-start(f32[5,4,4,128]{3,2,1,0:T(4,128)S(1)} %collective-permute-done.2.up_az_ref) | copy-start | bytes 122884
  43.1 0.7 %copy-start.2 = (f32[5,4,4,128]{3,2,1,0:T(4,128)}, f32[5,4,4,128]{3,2,1,0:T(4,128)S(1)}, u32[]{:S(2)}) copy-start(f32[5,4,4,128]{3,2,1,0:T(4,128)S(1)} %collective-permute-done.3.down_az_ref) | copy-start | bytes 122884

commit v3 on v2

--- a/solution.py
+++ b/solution.py
@@ -286,8 +286,6 @@
     is_rotor = lax.axis_index("zone") == 0
     up_ax = lax.ppermute(left_ax, "axial", [(i + 1, i) for i in range(n_axial - 1)])
     down_ax = lax.ppermute(right_ax, "axial", [(i, i + 1) for i in range(n_axial - 1)])
-    up_az = lax.ppermute(left_az, "azim", [((j + 1) % n_azim, j) for j in range(n_azim)])
-    down_az = lax.ppermute(right_az, "azim", [(j, (j + 1) % n_azim) for j in range(n_azim)])
     face_shape = (5, 4, 4, EA, ET, ER)
     outer_moment = face_moment(adj_field, right_corr, 3).reshape(face_shape)[..., ER - 1]
     inner_moment = face_moment(adj_field, left_corr, 3).reshape(face_shape)[..., 0]
@@ -311,22 +309,43 @@
     for rel, coef in coefs:
         term = jnp.pad(coef[None] * own_rows, ((0, 0), (0, 0), (TP + rel, TP - rel)))
         contrib = term if contrib is None else contrib + term
-    received = []
-    for dist in range(n_azim):
-        gap = (dist - turn) % n_azim
-        piece = jnp.where(
-            gap == n_azim - 1,
-            contrib[:, :, :TP],
-            jnp.where(gap == 0, contrib[:, :, TP : 2 * TP], contrib[:, :, 2 * TP :]),
-        )
-        payload = jnp.where(is_rotor, own_rows, piece)
-        pairs = [(j, n_azim + (j - dist) % n_azim) for j in range(n_azim)] + [
-            (n_azim + j, (j + dist) % n_azim) for j in range(n_azim)
-        ]
-        received.append(lax.ppermute(payload, ("zone", "azim"), pairs))
-    stacked = jnp.stack(received)
+    zone = lax.axis_index("zone")
+    azim = lax.axis_index("azim")
+    dest = jnp.arange(2 * n_azim, dtype=jnp.int32)
+    dest_azim = dest % n_azim
+    gap = ((dest_azim - azim) % n_azim - turn) % n_azim
+    gap = gap[:, None, None, None]
+    pieces = jnp.where(
+        gap == n_azim - 1,
+        contrib[None, :, :, :TP],
+        jnp.where(gap == 0, contrib[None, :, :, TP : 2 * TP], contrib[None, :, :, 2 * TP :]),
+    )
+    iface_out = jnp.where(is_rotor, jnp.broadcast_to(own_rows[None], pieces.shape), pieces)
+    iface_out = jnp.pad(iface_out.reshape(2 * n_azim, 5, 2, 128), ((0, 0), (0, 0), (0, 2), (0, 0)))
+    split = (5, 4, 4, EA, ET, ER)
+    upper_face = left_az.reshape(split)[:, :, :, :, 0, :].reshape(5, 4, 128)
+    lower_face = right_az.reshape(split)[:, :, :, :, ET - 1, :].reshape(5, 4, 128)
+    same_zone = dest // n_azim == zone
+    to_prev = (same_zone & (dest_azim == (azim - 1) % n_azim))[:, None, None, None]
+    to_next = (same_zone & (dest_azim == (azim + 1) % n_azim))[:, None, None, None]
+    chunks = jnp.where(
+        to_prev, upper_face[None], jnp.where(to_next, lower_face[None], jnp.where(same_zone[:, None, None, None], 0.0, iface_out))
+    )
+    got = lax.all_to_all(chunks, ("zone", "azim"), 0, 0)
+    base = (1 - zone) * n_azim
+    up_compact = lax.dynamic_index_in_dim(got, zone * n_azim + (azim + 1) % n_azim, 0, keepdims=False)
+    down_compact = lax.dynamic_index_in_dim(got, zone * n_azim + (azim - 1) % n_azim, 0, keepdims=False)
+    up_az = jnp.pad(
+        up_compact.reshape(5, 4, 4, EA, 1, ER), ((0, 0),) * 4 + ((0, ET - 1), (0, 0))
+    ).reshape(5, 4, 4, EA * ET * ER)
+    down_az = jnp.pad(
+        down_compact.reshape(5, 4, 4, EA, 1, ER), ((0, 0),) * 4 + ((ET - 1, 0), (0, 0))
+    ).reshape(5, 4, 4, EA * ET * ER)
+    direction = jnp.where(is_rotor, -1, 1)
     picked = [
-        lax.dynamic_index_in_dim(stacked, (turn + step) % n_azim, 0, keepdims=False)
+        lax.dynamic_index_in_dim(
+            got, base + (azim + direction * (turn + step)) % n_azim, 0, keepdims=False
+        )[:, :2].reshape(5, AP, TP)
         for step in (-1, 0, 1)
     ]
     returned = picked[0] + picked[1] + picked[2]

time: 47.9 us -> 46.3 us (0.967)
  waiting for transfers between devices: 6.46 us -> 1.95 us
  local copies, waits for them, and re-layouts: 16.1 us -> 20.6 us
  starting transfers between devices: 17.2 us -> 13.4 us
  other arithmetic: 2.82 us -> 4.9 us
    ppermute x10 -> x0, starting transfers between devices: 11.4 us -> none  [the longest x8 9.09 us: local(): received.append(lax.ppermute(payload, ('zone', 'azim'), pairs))]
    all_to_all x0 -> x1, starting transfers between devices: none -> 7.36 us  [local(): got = lax.all_to_all(chunks, ('zone', 'azim'), 0, 0)]
    ppermute x10 -> x0, waiting for transfers between devices: 6.45 us -> none  [the longest x8 5.39 us: local(): received.append(lax.ppermute(payload, ('zone', 'azim'), pairs))]
    reshape x0 -> x7, local copies, waits for them, and re-layouts: none -> 3.32 us  [the longest x1 1.27 us: local(): up_az = jnp.pad(up_compact.reshape(5, 4, 4, EA, 1, ER), ((0, 0),) * 4 + (...]
    all_to_all x0 -> x1, waiting for transfers between devices: none -> 1.94 us  [local(): got = lax.all_to_all(chunks, ('zone', 'azim'), 0, 0)]
    add x2 -> x4, local copies, waits for them, and re-layouts: 1.63 us -> 3.25 us  [face_moment(): running + lax.index_in_dim(adj_field, source, point_dim, keepdims=False)...]
    unnamed x22 -> x9, local copies, waits for them, and re-layouts: 4.76 us -> 3.29 us
    ppermute x2 -> x0, local copies, waits for them, and re-layouts: 1.24 us -> none  [the longest x1 0.62 us: local(): lax.ppermute(left_ax, 'axial', [(i + 1, i) for i in range(n_axial - 1)])]
  transfers between devices with their start and end apart: 12 -> 3, of which waited for: 3 -> 1; matrix products, arithmetic and copies ran while one was open for 12% -> 17% of each run, Pallas kernels for 0% -> 0%
where the time goes in v3:
time: 46.3 us; the launch traced here: 45.9 us
  local copies, waits for them, and re-layouts  20.6 us (44%)
  starting transfers between devices  13.4 us (29%)
  other arithmetic  4.9 us (11%)
  Pallas kernels  3.15 us (7%)
  between operations  1.97 us (4%)
  waiting for transfers between devices  1.95 us (4%)
    all_to_all x1, starting transfers between devices, local(): got = lax.all_to_all(chunks, ('zone', 'azim'), 0, 0)  7.36 us
    ppermute x1, starting transfers between devices, local(): lax.ppermute(right_ax, 'axial', [(i, i + 1) for i in range(n_axial - 1)])  4.73 us
    unnamed x9, local copies, waits for them, and re-layouts  3.29 us
    add x4, local copies, waits for them, and re-layouts, face_moment(): running + lax.index_in_dim(adj_field, source, point_dim, keepdims=False)...  3.25 us
    pallas_call x1, Pallas kernels, local(): pl.pallas_call(rate_kernel, out_shape=(field_shape, field_shape))  3.15 us
    mul x31, local copies, waits for them, and re-layouts, local(): coef[None] * own_rows  2.39 us
    broadcast_in_dim x4, local copies, waits for them, and re-layouts, local(): jnp.broadcast_to(iface[:, :, :, None, :, :, None], (5, 4, 4, 4, EA, ET, ER))  2.19 us
    all_to_all x1, waiting for transfers between devices, local(): got = lax.all_to_all(chunks, ('zone', 'azim'), 0, 0)  1.94 us
  transfers between devices with their start and end apart: 3, of which 1 were waited for; matrix products, arithmetic and copies ran while one was open for 17% of the time, Pallas kernels for 0%

profile of v3, /device:TPU:0, one launch (start us, length us, event | category | flops | bytes accessed | tf_op | source)
XLA Modules:
  0.0 45.9 jit_solution(4537759994919484466)
XLA Ops:
  1.4 1.1 %select_reduce_fusion = f32[4,256]{1,0:T(4,128)S(1)} fusion(f32[128]{0:T(128)} %param.10, s32[4,256]{1,0:T(4,128)} %param.9), kind=kLoop, calls=%fused_computation | loop fusion | flops 392192 | bytes 8704 | tf_op jit(solution)/shard_map/reduce_sum | solution.py:295
  2.5 0.7 %broadcast_add_fusion = s32[4,256]{1,0:T(4,128)S(1)} fusion(s32[4,256]{1,0:T(4,128)} %param.8, s32[]{:T(128)S(6)} %sub.51), kind=kLoop, calls=%fused_computation.297 | loop fusion | flops 1024 | bytes 8196 | tf_op jit(solution)/shard_map/add | solution.py:301
  3.9 0.8 %add.974 = f32[5,4,4,4,4,8]{5,4,3,2,0,1:T(4,128)S(1)} reshape(f32[5,4,4,128]{3,2,0,1:T(4,128)S(1)} %get-tuple-element.3) | data formatting | bytes 81920 | tf_op jit(solution)/shard_map/add | solution.py:91
  5.2 1.6 %copy.31 = f32[5,4,4,4,4,1]{0,4,5,3,2,1:T(4,128)S(1)} copy(f32[5,4,4,4,4,1]{5,4,3,2,0,1:T(4,128)S(1)} %slice.228) | data formatting | bytes 10240
  6.8 0.8 %add.978 = f32[5,4,4,4,4,8]{5,4,3,2,0,1:T(4,128)S(1)} reshape(f32[5,4,4,128]{3,2,0,1:T(4,128)S(1)} %get-tuple-element.2) | data formatting | bytes 81920 | tf_op jit(solution)/shard_map/add | solution.py:91
  7.6 1.6 %copy.32 = f32[5,4,4,4,4,1]{0,4,5,3,2,1:T(4,128)S(1)} copy(f32[5,4,4,4,4,1]{5,4,3,2,0,1:T(4,128)S(1)} %bitcast.35) | data formatting | bytes 10240
  9.3 0.6 %copy.25 = f32[5,4,4,4,4]{4,3,2,1,0:T(4,128)S(1)} copy(f32[5,4,4,4,4]{0,3,1,4,2:T(4,128)S(1)} %select_bitcast_fusion) | data formatting | bytes 10240 | tf_op jit(solution)/shard_map/transpose | solution.py:157
  13.8 0.8 %add.970 = f32[5,4,4,4,4,8]{5,4,3,2,0,1:T(4,128)S(1)} reshape(f32[5,4,1,4,128]{4,3,2,0,1:T(4,128)S(1)} %get-tuple-element.42) | data formatting | bytes 81920 | tf_op jit(solution)/shard_map/add | solution.py:91
  14.6 0.8 %add.964 = f32[5,4,4,4,4,8]{5,4,3,2,0,1:T(4,128)S(1)} reshape(f32[5,4,1,4,128]{4,3,2,0,1:T(4,128)S(1)} %get-tuple-element.41) | data formatting | bytes 81920 | tf_op jit(solution)/shard_map/add | solution.py:91
  15.4 1.0 %slice_reduce_fusion = (f32[5,4,4,4,8]{4,3,2,0,1:T(4,128)S(1)}, f32[5,4,4,4,8]{4,3,2,0,1:T(4,128)S(1)}) fusion(f32[5,4,4,4,4,8]{5,4,3,2,0,1:T(4,128)S(1)} %add.970, f32[5,4,4,4,4,8]{5,4,3,2,0,1:T(4,128)S(1)} %add.964), kind=kLoop, calls=%fused_computation.2 | loop fusion | bytes 40960 | tf_op jit(solution)/shard_map/slice | solution.py:327
  17.0 0.8 %select_select_fusion = f32[16,5,4,128]{3,2,1,0:T(4,128)} fusion(f32[16,5,2,128]{3,2,1,0:T(2,128)S(1)} %select_select_fusion.1, f32[5,4,128]{2,1,0:T(4,128)S(1)} %copy.34, f32[5,4,128]{2,1,0:T(4,128)S(1)} %copy.33, pred[16]{0:T(512)(128)(4,1)S(1)} %get-tuple-element.96, pred[16]{0:T(512)(128)(4,1)S(1)} %get-tuple-element.94, ...), kind=kLoop, calls=%fused_computation.5 | loop fusion | flops 122880 | bytes 266288 | tf_op jit(solution)/shard_map/jit(_where)/select_n | solution.py:331
  17.8 7.4 %all-to-all-start = ((f32[16,5,4,128]{3,2,1,0:T(4,128)}), f32[16,5,4,128]{3,2,1,0:T(4,128)S(1)}, u32[]{:S(2)}, u32[]{:S(2)}) async-start(f32[16,5,4,128]{3,2,1,0:T(4,128)} %select_select_fusion), calls=%async_computation | async-start | bytes 327680 | tf_op jit(solution)/shard_map/all_to_all | solution.py:334
  25.2 1.3 %collective-permute-start = (f32[5,4,4,128]{3,2,1,0:T(4,128)S(1)}, f32[5,4,4,128]{3,2,1,0:T(4,128)S(1)}, u32[]{:S(2)}, u32[]{:S(2)}) collective-permute-start(f32[5,4,4,128]{3,2,1,0:T(4,128)S(1)} %get-tuple-element.44), channel_id=1, source_target_pairs={{8,0},{9,1},{10,2},{11,3},{12,4},{13,5},{14,6},{15,7},{24,16},{25,... | collective-permute-start | bytes 122888 | tf_op jit(solution)/shard_map/ppermute | solution.py:287
  26.5 4.7 %collective-permute-start.1 = (f32[5,4,4,128]{3,2,1,0:T(4,128)S(1)}, f32[5,4,4,128]{3,2,1,0:T(4,128)S(1)}, u32[]{:S(2)}, u32[]{:S(2)}) collective-permute-start(f32[5,4,4,128]{3,2,1,0:T(4,128)S(1)} %get-tuple-element.43), channel_id=1, source_target_pairs={{0,8},{1,9},{2,10},{3,11},{4,12},{5,13},{6,14},{7,15},{16,24},{17,... | collective-permute-start | bytes 122888 | tf_op jit(solution)/shard_map/ppermute | solution.py:288
  31.3 1.9 %all-to-all-done = f32[16,5,4,128]{3,2,1,0:T(4,128)S(1)} async-done(((f32[16,5,4,128]{3,2,1,0:T(4,128)}), f32[16,5,4,128]{3,2,1,0:T(4,128)S(1)}, u32[]{:S(2)}, u32[]{:S(2)}) %all-to-all-start) | async-done | bytes 163872 | tf_op jit(solution)/shard_map/all_to_all | solution.py:334
  33.6 0.7 %broadcast_select_fusion = (f32[5,16,16]{2,1,0:T(8,128)S(1)}, f32[5,16,16]{2,1,0:T(8,128)S(1)}) fusion(pred[]{:T(512)S(6)} %eq.706, f32[5,16,16]{2,1,0:T(8,128)S(1)} %reshape.886, f32[5,16,16]{2,1,0:T(8,128)S(1)} %reshape.885, f32[16,16]{1,0:T(8,128)S(1)} %mul.742, f32[16,16]{1,0:T(8,128)S(1)} %mul.739, f32[16,16]{1,0:T(8,128)S(1)} %mul.736, ...), kind=kLoop, calls=%fused_computation.133 | loop fusion | flops 120320 | bytes 57345 | tf_op jit(solution)/shard_map/jit(_where)/select_n | solution.py:359
  34.8 1.3 %reshape.881.up_az_ref = f32[5,4,4,128]{3,2,1,0:T(4,128)} reshape(f32[5,4,4,4,4,8]{5,4,3,2,1,0:T(4,128)S(1)} %pad.168) | data formatting | bytes 81920 | tf_op jit(solution)/shard_map/reshape | solution.py:340
  36.5 1.3 %reshape.883.down_az_ref = f32[5,4,4,128]{3,2,1,0:T(4,128)} reshape(f32[5,4,4,4,4,8]{5,4,3,2,1,0:T(4,128)S(1)} %pad.169) | data formatting | bytes 81920 | tf_op jit(solution)/shard_map/reshape | solution.py:343
  37.9 0.6 %copy.27 = f32[5,4,4,4,4]{4,3,2,1,0:T(4,128)S(1)} copy(f32[5,4,4,4,4]{2,4,1,3,0:T(4,128)S(1)} %bitcast.39) | data formatting | bytes 10240 | tf_op jit(solution)/shard_map/jit(_where)/select_n | solution.py:358
  38.9 0.6 %select_n.1151 = f32[5,4,4,128]{3,2,1,0:T(4,128)S(1)} reshape(f32[5,4,4,4,4,8]{5,4,3,2,1,0:T(4,128)S(1)} %broadcast_in_dim.346) | data formatting | bytes 81920 | tf_op jit(solution)/shard_map/jit(_where)/select_n | solution.py:358
  40.7 0.6 %select_n.1155 = f32[5,4,4,128]{3,2,1,0:T(4,128)S(1)} reshape(f32[5,4,4,4,4,8]{5,4,3,2,1,0:T(4,128)S(1)} %broadcast_in_dim.348) | data formatting | bytes 81920 | tf_op jit(solution)/shard_map/jit(_where)/select_n | solution.py:359
  41.4 0.7 %broadcast_in_dim.347.outer_ref = f32[5,4,4,4,128]{4,3,2,1,0:T(4,128)} broadcast(f32[5,4,4,128]{3,2,1,0:T(4,128)S(1)} %select_n.1151), dimensions={0,1,2,4} | broadcast | bytes 204800 | tf_op jit(solution)/shard_map/broadcast_in_dim | solution.py:355
  42.1 0.7 %broadcast_in_dim.349.inner_ref = f32[5,4,4,4,128]{4,3,2,1,0:T(4,128)} broadcast(f32[5,4,4,128]{3,2,1,0:T(4,128)S(1)} %select_n.1155), dimensions={0,1,2,4} | broadcast | bytes 204800 | tf_op jit(solution)/shard_map/broadcast_in_dim | solution.py:355
  42.8 3.1 %shard_map.77 = (f32[1,5,4,4,4,128]{5,4,3,2,1,0:T(4,128)}, f32[1,5,4,4,4,128]{5,4,3,2,1,0:T(4,128)}) custom-call(f32[1,5,4,4,4,128]{5,4,3,2,1,0:T(4,128)} %adj_ref.1, bf16[1,5,4,4,4,128]{5,4,3,2,1,0:T(4,128)(2,1)} %flow_ref.1, f32[5,4,4,128]{3,2,1,0:T(4,128)} %copy-done.1, f32[5,4,4,128]{3,2,1,0:T(4,128)} %copy-done.2, f32[5,4,4,128]{3,2,1,0:T(4,128)} %reshape.881.up_az_ref, ...), custom_call_target="tpu_custom_call" | custom-call | tf_op jit(solution)/shard_map/pallas_call | solution.py:361
  (87 shorter events, 8.3 us)
Async XLA Ops:
  0.6 2.9 %copy-start = (f32[1,5,4,4,4,128]{5,4,3,2,1,0:T(4,128)S(1)}, f32[1,5,4,4,4,128]{5,4,3,2,1,0:T(4,128)}, u32[]{:S(2)}) copy-start(f32[1,5,4,4,4,128]{5,4,3,2,1,0:T(4,128)} %adj_ref.1) | copy-start | bytes 491524
  17.8 15.5 %all-to-all-start = ((f32[16,5,4,128]{3,2,1,0:T(4,128)}), f32[16,5,4,128]{3,2,1,0:T(4,128)S(1)}, u32[]{:S(2)}, u32[]{:S(2)}) async-start(f32[16,5,4,128]{3,2,1,0:T(4,128)} %select_select_fusion), calls=%async_computation | async-start | bytes 327680 | tf_op jit(solution)/shard_map/all_to_all | solution.py:334
  25.2 16.2 %collective-permute-start = (f32[5,4,4,128]{3,2,1,0:T(4,128)S(1)}, f32[5,4,4,128]{3,2,1,0:T(4,128)S(1)}, u32[]{:S(2)}, u32[]{:S(2)}) collective-permute-start(f32[5,4,4,128]{3,2,1,0:T(4,128)S(1)} %get-tuple-element.44), channel_id=1, source_target_pairs={{8,0},{9,1},{10,2},{11,3},{12,4},{13,5},{14,6},{15,7},{24,16},{25,... | collective-permute-start | bytes 122888 | tf_op jit(solution)/shard_map/ppermute | solution.py:287
  26.5 14.9 %collective-permute-start.1 = (f32[5,4,4,128]{3,2,1,0:T(4,128)S(1)}, f32[5,4,4,128]{3,2,1,0:T(4,128)S(1)}, u32[]{:S(2)}, u32[]{:S(2)}) collective-permute-start(f32[5,4,4,128]{3,2,1,0:T(4,128)S(1)} %get-tuple-element.43), channel_id=1, source_target_pairs={{0,8},{1,9},{2,10},{3,11},{4,12},{5,13},{6,14},{7,15},{16,24},{17,... | collective-permute-start | bytes 122888 | tf_op jit(solution)/shard_map/ppermute | solution.py:288
  41.4 0.7 %copy-start.1 = (f32[5,4,4,128]{3,2,1,0:T(4,128)}, f32[5,4,4,128]{3,2,1,0:T(4,128)S(1)}, u32[]{:S(2)}) copy-start(f32[5,4,4,128]{3,2,1,0:T(4,128)S(1)} %collective-permute-done.up_ax_ref) | copy-start | bytes 122884
  41.4 0.7 %copy-start.2 = (f32[5,4,4,128]{3,2,1,0:T(4,128)}, f32[5,4,4,128]{3,2,1,0:T(4,128)S(1)}, u32[]{:S(2)}) copy-start(f32[5,4,4,128]{3,2,1,0:T(4,128)S(1)} %collective-permute-done.1.down_ax_ref) | copy-start | bytes 122884

commit v4 on v3

--- a/solution.py
+++ b/solution.py
@@ -188,8 +188,52 @@
     return out
 
 
+def compact_face(face, part):
+    lane = lax.broadcasted_iota(jnp.int32, (4, 128), 1)
+    out = jnp.zeros((4, 128), jnp.float32)
+    for block in range(4):
+        for group in range(EA):
+            shift = block * ET * ER - group * (ET - 1) * ER - part * ER
+            start = block * ET * ER + group * ER
+            mask = (lane >= start) & (lane < start + ER)
+            out = jnp.where(mask, lane_roll(face[block], shift), out)
+    return out
+
+
+def expand_face(chunk, part):
+    lane = lax.broadcasted_iota(jnp.int32, (4, 128), 1)
+    group_of = lane // (ET * ER)
+    in_part = lane // ER % ET == part
+    blocks = []
+    for block in range(4):
+        out = jnp.zeros((4, 128), jnp.float32)
+        for group in range(EA):
+            shift = block * ET * ER - group * (ET - 1) * ER - part * ER
+            out = jnp.where(in_part & (group_of == group), lane_roll(chunk, -shift), out)
+        blocks.append(out)
+    return jnp.stack(blocks, axis=0)
+
+
+def moment_kernel(adj_ref, left_ax_ref, right_ax_ref, up_ref, down_ref, outer_ref, inner_ref):
+    derivs, left_vals, right_vals, left_corr, right_corr = basis_tables()
+    for chan in range(5):
+        field = adj_ref[0, chan]
+        left_ax_ref[chan] = sweep(field, left_corr, lambda i: (i,))
+        right_ax_ref[chan] = sweep(field, right_corr, lambda i: (i,))
+        pick1 = lambda i: (slice(None), i)
+        up_ref[chan] = compact_face(sweep(field, left_corr, pick1), 0)
+        down_ref[chan] = compact_face(sweep(field, right_corr, pick1), ET - 1)
+        pick2 = lambda i: (slice(None), slice(None), slice(i, i + 1))
+        outer = sweep(field, right_corr, pick2)
+        inner = sweep(field, left_corr, pick2)
+        for axial in range(4):
+            for azim in range(4):
+                outer_ref[chan, axial, azim : azim + 1] = outer[axial, azim]
+                inner_ref[chan, axial, azim : azim + 1] = inner[axial, azim]
+
+
 def rate_kernel(
-    adj_ref, flow_ref, up_ax_ref, down_ax_ref, up_az_ref, down_az_ref, outer_ref, inner_ref,
+    adj_ref, flow_ref, up_ax_ref, down_ax_ref, up_az_ref, down_az_ref, iface_ref, flag_ref,
     rate_ref, next_ref,
 ):
     derivs, left_vals, right_vals, left_corr, right_corr = basis_tables()
@@ -199,8 +243,23 @@
     az_flat = flat_lane // ER % ET
     radial_lane = lane % ER
     brackets = [[None] * 5 for _ in range(3)]
+    rotor = jnp.broadcast_to(flag_ref[0:1, :], shape) > 0.5
     for chan in range(5):
         field = adj_ref[0, chan]
+        face = jnp.stack(
+            [
+                jnp.stack(
+                    [jnp.broadcast_to(iface_ref[chan, axial, azim : azim + 1], (4, 128)) for azim in range(4)],
+                    axis=0,
+                )
+                for axial in range(4)
+            ],
+            axis=0,
+        )
+        outer_face = jnp.where(rotor, face, 0.0)
+        inner_face = jnp.where(rotor, 0.0, face)
+        up_az = expand_face(up_az_ref[chan], 0)
+        down_az = expand_face(down_az_ref[chan], ET - 1)
         left0 = sweep(field, left_corr, lambda i: (i,))
         right0 = sweep(field, right_corr, lambda i: (i,))
         next0 = lane_roll(jnp.where(flat_lane < ET * ER, up_ax_ref[chan], left0), -ET * ER)
@@ -216,10 +275,10 @@
         left1 = sweep(field, left_corr, pick1)
         right1 = sweep(field, right_corr, pick1)
         next1 = lane_roll(
-            jnp.where(az_flat == 0, lane_roll(up_az_ref[chan], ET * ER), left1), -ER
+            jnp.where(az_flat == 0, lane_roll(up_az, ET * ER), left1), -ER
         )
         prev1 = lane_roll(
-            jnp.where(az_flat == ET - 1, lane_roll(down_az_ref[chan], -ET * ER), right1), ER
+            jnp.where(az_flat == ET - 1, lane_roll(down_az, -ET * ER), right1), ER
         )
         jump_r = 0.5 * (next1 - right1)
         jump_l = 0.5 * (prev1 - left1)
@@ -231,8 +290,8 @@
         points = [jnp.broadcast_to(field[:, :, i : i + 1, :], shape) for i in range(4)]
         left2 = sweep(points, left_corr, lambda i: i)
         right2 = sweep(points, right_corr, lambda i: i)
-        next2 = jnp.where(radial_lane == ER - 1, outer_ref[chan], lane_roll(left2, -1))
-        prev2 = jnp.where(radial_lane == 0, inner_ref[chan], lane_roll(right2, 1))
+        next2 = jnp.where(radial_lane == ER - 1, outer_face, lane_roll(left2, -1))
+        prev2 = jnp.where(radial_lane == 0, inner_face, lane_roll(right2, 1))
         bracket = 0.5 * (next2 - right2) * column(right_vals, shape)
         bracket = bracket + 0.5 * (prev2 - left2) * column(left_vals, shape)
         for source in range(4):
@@ -277,19 +336,19 @@
 def local(adjoint, flow_prim, intersection_shift, weight_index, mortar_weights, sector_offset):
     n_axial = lax.axis_size("axial")
     n_azim = lax.axis_size("azim")
-    adj_field = adjoint[0]
-    derivs, left_vals, right_vals, left_corr, right_corr = basis_tables()
-    left_ax = face_moment(adj_field, left_corr, 1)
-    right_ax = face_moment(adj_field, right_corr, 1)
-    left_az = face_moment(adj_field, left_corr, 2)
-    right_az = face_moment(adj_field, right_corr, 2)
+    face4 = jax.ShapeDtypeStruct((5, 4, 4, 128), jnp.float32)
+    chunk = jax.ShapeDtypeStruct((5, 4, 128), jnp.float32)
+    left_ax, right_ax, upper_face, lower_face, outer_moment, inner_moment = pl.pallas_call(
+        moment_kernel, out_shape=(face4, face4, chunk, chunk, face4, face4)
+    )(adjoint)
     is_rotor = lax.axis_index("zone") == 0
     up_ax = lax.ppermute(left_ax, "axial", [(i + 1, i) for i in range(n_axial - 1)])
     down_ax = lax.ppermute(right_ax, "axial", [(i, i + 1) for i in range(n_axial - 1)])
     face_shape = (5, 4, 4, EA, ET, ER)
-    outer_moment = face_moment(adj_field, right_corr, 3).reshape(face_shape)[..., ER - 1]
-    inner_moment = face_moment(adj_field, left_corr, 3).reshape(face_shape)[..., 0]
-    own_rows = faces_to_rows(jnp.where(is_rotor, outer_moment, inner_moment))
+    own_face = jnp.where(
+        is_rotor, outer_moment.reshape(face_shape)[..., ER - 1], inner_moment.reshape(face_shape)[..., 0]
+    )
+    own_rows = faces_to_rows(own_face)
     shifts_local = intersection_shift.reshape(INTERSECTIONS, AP, TP)
     table_match = weight_index[:, :, None] == jnp.arange(NW, dtype=jnp.int32)[None, None, :]
     weights_local = jnp.sum(
@@ -322,9 +381,6 @@
     )
     iface_out = jnp.where(is_rotor, jnp.broadcast_to(own_rows[None], pieces.shape), pieces)
     iface_out = jnp.pad(iface_out.reshape(2 * n_azim, 5, 2, 128), ((0, 0), (0, 0), (0, 2), (0, 0)))
-    split = (5, 4, 4, EA, ET, ER)
-    upper_face = left_az.reshape(split)[:, :, :, :, 0, :].reshape(5, 4, 128)
-    lower_face = right_az.reshape(split)[:, :, :, :, ET - 1, :].reshape(5, 4, 128)
     same_zone = dest // n_azim == zone
     to_prev = (same_zone & (dest_azim == (azim - 1) % n_azim))[:, None, None, None]
     to_next = (same_zone & (dest_azim == (azim + 1) % n_azim))[:, None, None, None]
@@ -333,14 +389,8 @@
     )
     got = lax.all_to_all(chunks, ("zone", "azim"), 0, 0)
     base = (1 - zone) * n_azim
-    up_compact = lax.dynamic_index_in_dim(got, zone * n_azim + (azim + 1) % n_azim, 0, keepdims=False)
-    down_compact = lax.dynamic_index_in_dim(got, zone * n_azim + (azim - 1) % n_azim, 0, keepdims=False)
-    up_az = jnp.pad(
-        up_compact.reshape(5, 4, 4, EA, 1, ER), ((0, 0),) * 4 + ((0, ET - 1), (0, 0))
-    ).reshape(5, 4, 4, EA * ET * ER)
-    down_az = jnp.pad(
-        down_compact.reshape(5, 4, 4, EA, 1, ER), ((0, 0),) * 4 + ((ET - 1, 0), (0, 0))
-    ).reshape(5, 4, 4, EA * ET * ER)
+    up_az = lax.dynamic_index_in_dim(got, zone * n_azim + (azim + 1) % n_azim, 0, keepdims=False)
+    down_az = lax.dynamic_index_in_dim(got, zone * n_azim + (azim - 1) % n_azim, 0, keepdims=False)
     direction = jnp.where(is_rotor, -1, 1)
     picked = [
         lax.dynamic_index_in_dim(
@@ -352,15 +402,12 @@
     window = jnp.concatenate(picked, axis=2)
     incoming = shift_sum(window, coefs, TP)
     iface = rows_to_face(jnp.where(is_rotor, returned, incoming), EA, ET)
-    iface = jnp.broadcast_to(
-        iface[:, :, :, None, :, :, None], (5, 4, 4, 4, EA, ET, ER)
-    ).reshape(5, 4, 4, 4, EA * ET * ER)
-    outer = jnp.where(is_rotor, iface, 0.0)
-    inner = jnp.where(is_rotor, 0.0, iface)
+    iface = jnp.broadcast_to(iface[..., None], (5, 4, 4, EA, ET, ER)).reshape(5, 4, 4, EA * ET * ER)
+    flag = jnp.broadcast_to(jnp.where(is_rotor, 1.0, 0.0), (8, 128))
     field_shape = jax.ShapeDtypeStruct(adjoint.shape, jnp.float32)
     adjoint_rate, next_adjoint = pl.pallas_call(
         rate_kernel, out_shape=(field_shape, field_shape)
-    )(adjoint, flow_prim, up_ax, down_ax, up_az, down_az, outer, inner)
+    )(adjoint, flow_prim, up_ax, down_ax, up_az, down_az, iface, flag)
     return (adjoint_rate, next_adjoint)
 
 

time: 46.3 us -> 41.4 us (0.89)
  local copies, waits for them, and re-layouts: 20.6 us -> 15.5 us
  other arithmetic: 4.9 us -> 2.99 us
  Pallas kernels: 3.15 us -> 5.06 us
    add x4 -> x0, local copies, waits for them, and re-layouts: 3.25 us -> none  [face_moment(): running + lax.index_in_dim(adj_field, source, point_dim, keepdims=False)...]
    select_n x6 -> x0, local copies, waits for them, and re-layouts: 2.73 us -> none  [the longest x3 1.37 us: local(): inner = jnp.where(is_rotor, 0.0, iface)]
    pallas_call x0 -> x1, Pallas kernels: none -> 1.9 us  [local(): pl.pallas_call(moment_kernel, out_shape=(face4, face4, chunk, chunk, face...]
    unnamed x9 -> x22, local copies, waits for them, and re-layouts: 3.29 us -> 5.19 us
    broadcast_in_dim x8 -> x2, local copies, waits for them, and re-layouts: 2.55 us -> 1.03 us  [the longest x1 0.62 us: local(): flag = jnp.broadcast_to(jnp.where(is_rotor, 1.0, 0.0), (8, 128))]
    slice x2 -> x1, local copies, waits for them, and re-layouts: 1.4 us -> 0.4 us  [local(): outer_moment.reshape(face_shape)[..., ER - 1]]
    reshape x4, local copies, waits for them, and re-layouts: 3.08 us -> 3.8 us  [the longest x1 1.58 us: local(): outer_moment.reshape(face_shape)[..., ER - 1]]
    reduce_sum x1, other arithmetic: 1.08 us -> 0.38 us  [local(): jnp.sum(jnp.where(table_match, mortar_weights[None, None, :], 0.0), axis=2)]
  transfers between devices with their start and end apart: 3 -> 3, of which waited for: 1 -> 1; matrix products, arithmetic and copies ran while one was open for 17% -> 10% of each run, Pallas kernels for 0% -> 0%
where the time goes in v4:
time: 41.4 us; the launch traced here: 40.9 us
  local copies, waits for them, and re-layouts  15.5 us (37%)
  starting transfers between devices  13.3 us (32%)
  Pallas kernels  5.06 us (12%)
  other arithmetic  2.99 us (7%)
  waiting for transfers between devices  2.16 us (5%)
  between operations  1.82 us (4%)
    all_to_all x1, starting transfers between devices, local(): got = lax.all_to_all(chunks, ('zone', 'azim'), 0, 0)  7.49 us
    unnamed x22, local copies, waits for them, and re-layouts  5.19 us
    ppermute x1, starting transfers between devices, local(): lax.ppermute(right_ax, 'axial', [(i, i + 1) for i in range(n_axial - 1)])  4.55 us
    pallas_call x1, Pallas kernels, local(): pl.pallas_call(rate_kernel, out_shape=(field_shape, field_shape))  3.16 us
    mul x31, local copies, waits for them, and re-layouts, local(): coef[None] * own_rows  2.39 us
    all_to_all x1, waiting for transfers between devices, local(): got = lax.all_to_all(chunks, ('zone', 'azim'), 0, 0)  2.16 us
    pallas_call x1, Pallas kernels, local(): pl.pallas_call(moment_kernel, out_shape=(face4, face4, chunk, chunk, face...  1.9 us
    reshape x1, local copies, waits for them, and re-layouts, local(): outer_moment.reshape(face_shape)[..., ER - 1]  1.58 us
  transfers between devices with their start and end apart: 3, of which 1 were waited for; matrix products, arithmetic and copies ran while one was open for 10% of the time, Pallas kernels for 0%

profile of v4, /device:TPU:0, one launch (start us, length us, event | category | flops | bytes accessed | tf_op | source)
XLA Modules:
  0.0 40.9 jit_solution(6876515353877200792)
XLA Ops:
  1.4 0.6 %copy-done.5 = s32[4,256]{1,0:T(4,128)S(1)} copy-done((s32[4,256]{1,0:T(4,128)S(1)}, s32[4,256]{1,0:T(4,128)}, u32[]{:S(2)}) %copy-start.5) | copy-done | bytes 4120
  2.0 0.7 %copy-done.6 = s32[4,256]{1,0:T(4,128)S(1)} copy-done((s32[4,256]{1,0:T(4,128)S(1)}, s32[4,256]{1,0:T(4,128)}, u32[]{:S(2)}) %copy-start.6) | copy-done | bytes 4120
  2.7 0.4 select_reduce_fusion
  3.4 1.9 %shard_map.77 = (f32[5,4,4,128]{3,2,1,0:T(4,128)}, f32[5,4,4,128]{3,2,1,0:T(4,128)}, f32[5,4,128]{2,1,0:T(4,128)}, f32[5,4,128]{2,1,0:T(4,128)}, f32[5,4,4,128]{3,2,1,0:T(4,128)}, /*index=5*/f32[5,4,4,128]{3,2,1,0:T(4,128)}) custom-call(f32[1,5,4,4,4,128]{5,4,3,2,1,0:T(4,128)} %adj_ref.3), custom_call_target="tpu_custom_call" | custom-call | tf_op jit(solution)/shard_map/pallas_call | solution.py:341
  5.3 1.6 %reshape.776 = f32[5,4,4,4,4,8]{5,4,3,2,1,0:T(4,128)S(1)} reshape(f32[5,4,4,128]{3,2,1,0:T(4,128)} %get-tuple-element.12) | data formatting | bytes 81920 | tf_op jit(solution)/shard_map/reshape | solution.py:349
  6.9 0.4 slice.172
  7.3 1.6 %copy.18 = f32[5,4,4,4,4,1]{0,4,5,3,2,1:T(4,128)S(1)} copy(f32[5,4,4,4,4,1]{5,4,3,2,1,0:T(4,128)S(1)} %slice.172) | data formatting | bytes 10240
  9.0 0.8 %reshape.777 = f32[5,4,4,4,4,8]{5,4,3,2,1,0:T(4,128)S(1)} reshape(f32[5,4,4,128]{3,2,1,0:T(4,128)S(1)} %copy-done.2) | data formatting | bytes 81920 | tf_op jit(solution)/shard_map/reshape | solution.py:349
  9.8 1.6 %copy.19 = f32[5,4,4,4,4,1]{0,4,5,3,2,1:T(4,128)S(1)} copy(f32[5,4,4,4,4,1]{5,4,3,2,1,0:T(4,128)S(1)} %bitcast.19) | data formatting | bytes 10240
  11.5 0.6 %copy.15 = f32[5,4,4,4,4]{4,3,2,1,0:T(4,128)S(1)} copy(f32[5,4,4,4,4]{0,3,1,4,2:T(4,128)S(1)} %select_bitcast_fusion) | data formatting | bytes 10240 | tf_op jit(solution)/shard_map/transpose | solution.py:157
  15.1 0.4 %pad_add_fusion = f32[5,16,48]{2,1,0:T(8,128)S(1)} fusion(f32[5,16,16]{2,1,0:T(8,128)S(1)} %get-tuple-element.53, f32[5,16,16]{2,1,0:T(8,128)S(1)} %get-tuple-element.54, f32[5,16,16]{2,1,0:T(8,128)S(1)} %get-tuple-element.55, f32[5,16,16]{2,1,0:T(8,128)S(1)} %get-tuple-element.56, f32[5,16,16]{2,1,0:T(8,128)S(1)} %get-tuple-element.57, ...), kind=kLoop, calls=%fused_computation.123 | loop fusion | flops 115200 | bytes 174080 | tf_op jit(solution)/shard_map/add | solution.py:370
  16.1 0.6 %copy-done.3 = f32[5,4,128]{2,1,0:T(4,128)S(1)} copy-done((f32[5,4,128]{2,1,0:T(4,128)S(1)}, f32[5,4,128]{2,1,0:T(4,128)}, u32[]{:S(2)}) %copy-start.3) | copy-done | bytes 10264
  16.7 0.8 %select_select_fusion = f32[16,5,4,128]{3,2,1,0:T(4,128)} fusion(f32[16,5,2,128]{3,2,1,0:T(2,128)S(1)} %select_select_fusion.1, f32[5,4,128]{2,1,0:T(4,128)S(1)} %copy-done.4, f32[5,4,128]{2,1,0:T(4,128)S(1)} %copy-done.3, pred[16]{0:T(512)(128)(4,1)S(1)} %get-tuple-element.100, pred[16]{0:T(512)(128)(4,1)S(1)} %get-tuple-element.98, ...), kind=kLoop, calls=%fused_computation.2 | loop fusion | flops 122880 | bytes 266288 | tf_op jit(solution)/shard_map/jit(_where)/select_n | solution.py:387
  17.5 7.5 %all-to-all-start = ((f32[16,5,4,128]{3,2,1,0:T(4,128)}), f32[16,5,4,128]{3,2,1,0:T(4,128)S(1)}, u32[]{:S(2)}, u32[]{:S(2)}) async-start(f32[16,5,4,128]{3,2,1,0:T(4,128)} %select_select_fusion), calls=%async_computation | async-start | bytes 327680 | tf_op jit(solution)/shard_map/all_to_all | solution.py:390
  25.0 1.3 %collective-permute-start = (f32[5,4,4,128]{3,2,1,0:T(4,128)S(1)}, f32[5,4,4,128]{3,2,1,0:T(4,128)S(1)}, u32[]{:S(2)}, u32[]{:S(2)}) collective-permute-start(f32[5,4,4,128]{3,2,1,0:T(4,128)S(1)} %copy-done.9), channel_id=1, source_target_pairs={{8,0},{9,1},{10,2},{11,3},{12,4},{13,5},{14,6},{15,7},{24,16},{25,... | collective-permute-start | bytes 122888 | tf_op jit(solution)/shard_map/ppermute | solution.py:345
  26.3 4.5 %collective-permute-start.1 = (f32[5,4,4,128]{3,2,1,0:T(4,128)S(1)}, f32[5,4,4,128]{3,2,1,0:T(4,128)S(1)}, u32[]{:S(2)}, u32[]{:S(2)}) collective-permute-start(f32[5,4,4,128]{3,2,1,0:T(4,128)S(1)} %copy-done.8), channel_id=1, source_target_pairs={{0,8},{1,9},{2,10},{3,11},{4,12},{5,13},{6,14},{7,15},{16,24},{17,... | collective-permute-start | bytes 122888 | tf_op jit(solution)/shard_map/ppermute | solution.py:346
  30.9 2.2 %all-to-all-done = f32[16,5,4,128]{3,2,1,0:T(4,128)S(1)} async-done(((f32[16,5,4,128]{3,2,1,0:T(4,128)}), f32[16,5,4,128]{3,2,1,0:T(4,128)S(1)}, u32[]{:S(2)}, u32[]{:S(2)}) %all-to-all-start) | async-done | bytes 163872 | tf_op jit(solution)/shard_map/all_to_all | solution.py:390
  33.1 0.6 %dynamic-slice_bitcast_fusion.2 = (f32[5,4,128]{2,1,0:T(4,128)S(1)}, f32[5,4,128]{2,1,0:T(4,128)S(1)}, f32[5,4,128]{2,1,0:T(4,128)S(1)}, f32[5,4,128]{2,1,0:T(4,128)}, f32[5,4,128]{2,1,0:T(4,128)}) fusion(f32[16,5,4,128]{3,2,1,0:T(4,128)S(1)} %all-to-all-done, s32[]{:T(128)S(6)} %select_n.1122, s32[]{:T(128)S(6)} %select_n.1126, s32[]{:T(128)S(6)} %select_n.1124, ...), kind=kLoop, calls=%fused_computation.157 | loop fusion | bytes 102420 | tf_op jit(solution)/shard_map/jit(dynamic_index_in_dim)/squeeze | solution.py:396
  34.0 0.7 %fusion.2 = f32[5,16,16]{2,1,0:T(8,128)S(1)} fusion(f32[5,16,16]{2,1,0:T(8,128)S(1)} %reshape.781, f32[5,16,16]{2,1,0:T(8,128)S(1)} %reshape.780, f32[5,16,16]{2,1,0:T(8,128)S(1)} %reshape.779, f32[16,16]{1,0:T(8,128)S(1)} %mul.606, f32[16,16]{1,0:T(8,128)S(1)} %mul.603, f32[16,16]{1,0:T(8,128)S(1)} %mul.600, f32[16,16]{1,0:T(8,128)S(1)} %mul.597, ...), kind=kLoop, calls=%fused_computation.8 | loop fusion | flops 119040 | bytes 52225 | tf_op jit(solution)/shard_map/jit(_where)/select_n | solution.py:404
  34.8 0.6 %copy.17 = f32[5,4,4,4,4]{4,3,2,1,0:T(4,128)S(1)} copy(f32[5,4,4,4,4]{2,4,1,3,0:T(4,128)S(1)} %bitcast.20) | data formatting | bytes 10240 | tf_op jit(solution)/shard_map/transpose | solution.py:161
  35.4 0.4 %broadcast_in_dim.332 = f32[5,4,4,4,4,8]{5,4,3,2,1,0:T(4,128)S(1)} broadcast(f32[5,4,4,4,4]{4,3,2,1,0:T(4,128)S(1)} %copy.17), dimensions={0,1,2,3,4} | broadcast | bytes 46080 | tf_op jit(solution)/shard_map/broadcast_in_dim | solution.py:405
  35.8 1.3 %reshape.783.iface_ref = f32[5,4,4,128]{3,2,1,0:T(4,128)} reshape(f32[5,4,4,4,4,8]{5,4,3,2,1,0:T(4,128)S(1)} %broadcast_in_dim.332) | data formatting | bytes 81920 | tf_op jit(solution)/shard_map/reshape | solution.py:405
  37.1 0.6 %broadcast_in_dim.333.flag_ref = f32[8,128]{1,0:T(8,128)} broadcast(f32[]{:T(128)S(6)} %select_n.1128), dimensions={} | broadcast | bytes 4100 | tf_op jit(solution)/shard_map/broadcast_in_dim | solution.py:406
  37.7 3.2 %shard_map.78 = (f32[1,5,4,4,4,128]{5,4,3,2,1,0:T(4,128)}, f32[1,5,4,4,4,128]{5,4,3,2,1,0:T(4,128)}) custom-call(f32[1,5,4,4,4,128]{5,4,3,2,1,0:T(4,128)} %adj_ref.3, bf16[1,5,4,4,4,128]{5,4,3,2,1,0:T(4,128)(2,1)} %flow_ref.1, f32[5,4,4,128]{3,2,1,0:T(4,128)} %copy-done, f32[5,4,4,128]{3,2,1,0:T(4,128)} %copy-done.1, ...), custom_call_target="tpu_custom_call" | custom-call | tf_op jit(solution)/shard_map/pallas_call | solution.py:408
  (79 shorter events, 4.2 us)
Async XLA Ops:
  1.4 0.7 %copy-start.5 = (s32[4,256]{1,0:T(4,128)S(1)}, s32[4,256]{1,0:T(4,128)}, u32[]{:S(2)}) copy-start(s32[4,256]{1,0:T(4,128)} %param.8) | copy-start | bytes 12292
  2.0 0.7 %copy-start.6 = (s32[4,256]{1,0:T(4,128)S(1)}, s32[4,256]{1,0:T(4,128)}, u32[]{:S(2)}) copy-start(s32[4,256]{1,0:T(4,128)} %param.9) | copy-start | bytes 12292
  2.0 0.7 %copy-start.7 = (f32[128]{0:T(128)S(1)}, f32[128]{0:T(128)}, u32[]{:S(2)}) copy-start(f32[128]{0:T(128)} %param.10) | copy-start | bytes 1540
  7.3 1.6 %copy-start.2 = (f32[5,4,4,128]{3,2,1,0:T(4,128)S(1)}, f32[5,4,4,128]{3,2,1,0:T(4,128)}, u32[]{:S(2)}) copy-start(f32[5,4,4,128]{3,2,1,0:T(4,128)} %get-tuple-element.13) | copy-start | bytes 122884
  15.9 0.7 %copy-start.3 = (f32[5,4,128]{2,1,0:T(4,128)S(1)}, f32[5,4,128]{2,1,0:T(4,128)}, u32[]{:S(2)}) copy-start(f32[5,4,128]{2,1,0:T(4,128)} %get-tuple-element.10) | copy-start | bytes 30724
  15.9 0.7 %copy-start.4 = (f32[5,4,128]{2,1,0:T(4,128)S(1)}, f32[5,4,128]{2,1,0:T(4,128)}, u32[]{:S(2)}) copy-start(f32[5,4,128]{2,1,0:T(4,128)} %get-tuple-element.11) | copy-start | bytes 30724
  17.4 7.5 %copy-start.9 = (f32[5,4,4,128]{3,2,1,0:T(4,128)S(1)}, f32[5,4,4,128]{3,2,1,0:T(4,128)}, u32[]{:S(2)}) copy-start(f32[5,4,4,128]{3,2,1,0:T(4,128)} %get-tuple-element.8) | copy-start | bytes 122884
  17.4 8.8 %copy-start.8 = (f32[5,4,4,128]{3,2,1,0:T(4,128)S(1)}, f32[5,4,4,128]{3,2,1,0:T(4,128)}, u32[]{:S(2)}) copy-start(f32[5,4,4,128]{3,2,1,0:T(4,128)} %get-tuple-element.9) | copy-start | bytes 122884
  17.5 15.6 %all-to-all-start = ((f32[16,5,4,128]{3,2,1,0:T(4,128)}), f32[16,5,4,128]{3,2,1,0:T(4,128)S(1)}, u32[]{:S(2)}, u32[]{:S(2)}) async-start(f32[16,5,4,128]{3,2,1,0:T(4,128)} %select_select_fusion), calls=%async_computation | async-start | bytes 327680 | tf_op jit(solution)/shard_map/all_to_all | solution.py:390
  25.0 12.1 %collective-permute-start = (f32[5,4,4,128]{3,2,1,0:T(4,128)S(1)}, f32[5,4,4,128]{3,2,1,0:T(4,128)S(1)}, u32[]{:S(2)}, u32[]{:S(2)}) collective-permute-start(f32[5,4,4,128]{3,2,1,0:T(4,128)S(1)} %copy-done.9), channel_id=1, source_target_pairs={{8,0},{9,1},{10,2},{11,3},{12,4},{13,5},{14,6},{15,7},{24,16},{25,... | collective-permute-start | bytes 122888 | tf_op jit(solution)/shard_map/ppermute | solution.py:345
  26.3 10.8 %collective-permute-start.1 = (f32[5,4,4,128]{3,2,1,0:T(4,128)S(1)}, f32[5,4,4,128]{3,2,1,0:T(4,128)S(1)}, u32[]{:S(2)}, u32[]{:S(2)}) collective-permute-start(f32[5,4,4,128]{3,2,1,0:T(4,128)S(1)} %copy-done.8), channel_id=1, source_target_pairs={{0,8},{1,9},{2,10},{3,11},{4,12},{5,13},{6,14},{7,15},{16,24},{17,... | collective-permute-start | bytes 122888 | tf_op jit(solution)/shard_map/ppermute | solution.py:346
  37.1 0.6 %copy-start = (f32[5,4,4,128]{3,2,1,0:T(4,128)}, f32[5,4,4,128]{3,2,1,0:T(4,128)S(1)}, u32[]{:S(2)}) copy-start(f32[5,4,4,128]{3,2,1,0:T(4,128)S(1)} %collective-permute-done.up_ax_ref) | copy-start | bytes 122884
  37.1 0.6 %copy-start.1 = (f32[5,4,4,128]{3,2,1,0:T(4,128)}, f32[5,4,4,128]{3,2,1,0:T(4,128)S(1)}, u32[]{:S(2)}) copy-start(f32[5,4,4,128]{3,2,1,0:T(4,128)S(1)} %collective-permute-done.1.down_ax_ref) | copy-start | bytes 122884

commit v5 on v4

--- a/solution.py
+++ b/solution.py
@@ -214,8 +214,24 @@
     return jnp.stack(blocks, axis=0)
 
 
-def moment_kernel(adj_ref, left_ax_ref, right_ax_ref, up_ref, down_ref, outer_ref, inner_ref):
+def selector(rows, cols, lane_of, use_rows):
+    row = lax.broadcasted_iota(jnp.int32, (rows, cols), 0)
+    col = lax.broadcasted_iota(jnp.int32, (rows, cols), 1)
+    if use_rows:
+        hit = (row == lane_of(col)) & (row < EA * ET)
+    else:
+        hit = (row == lane_of(col)) & (col < EA * ET)
+    return jnp.where(hit, 1.0, 0.0)
+
+
+def exact_dot(left, right):
+    return jnp.dot(left, right, precision=lax.Precision.HIGHEST, preferred_element_type=jnp.float32)
+
+
+def moment_kernel(adj_ref, left_ax_ref, right_ax_ref, up_ref, down_ref, outer_ref, inner_ref, scratch_ref):
     derivs, left_vals, right_vals, left_corr, right_corr = basis_tables()
+    pick_outer = selector(128, 128, lambda k: k // ET * ET * ER + k % ET * ER + ER - 1, False)
+    pick_inner = selector(128, 128, lambda k: k // ET * ET * ER + k % ET * ER, False)
     for chan in range(5):
         field = adj_ref[0, chan]
         left_ax_ref[chan] = sweep(field, left_corr, lambda i: (i,))
@@ -228,12 +244,15 @@
         inner = sweep(field, left_corr, pick2)
         for axial in range(4):
             for azim in range(4):
-                outer_ref[chan, axial, azim : azim + 1] = outer[axial, azim]
-                inner_ref[chan, axial, azim : azim + 1] = inner[axial, azim]
+                row = axial * 4 + azim
+                scratch_ref[0, row : row + 1] = outer[axial, azim]
+                scratch_ref[1, row : row + 1] = inner[axial, azim]
+        outer_ref[chan] = exact_dot(scratch_ref[0], pick_outer)
+        inner_ref[chan] = exact_dot(scratch_ref[1], pick_inner)
 
 
 def rate_kernel(
-    adj_ref, flow_ref, up_ax_ref, down_ax_ref, up_az_ref, down_az_ref, iface_ref, flag_ref,
+    adj_ref, flow_ref, up_ax_ref, down_ax_ref, up_az_ref, down_az_ref, outer_ref, inner_ref,
     rate_ref, next_ref,
 ):
     derivs, left_vals, right_vals, left_corr, right_corr = basis_tables()
@@ -243,21 +262,31 @@
     az_flat = flat_lane // ER % ET
     radial_lane = lane % ER
     brackets = [[None] * 5 for _ in range(3)]
-    rotor = jnp.broadcast_to(flag_ref[0:1, :], shape) > 0.5
+    spread = selector(128, 128, lambda k: k // (ET * ER) * ET + k // ER % ET, True)
     for chan in range(5):
         field = adj_ref[0, chan]
-        face = jnp.stack(
+        outer_lanes = exact_dot(outer_ref[chan], spread)
+        inner_lanes = exact_dot(inner_ref[chan], spread)
+        outer_face = jnp.stack(
             [
                 jnp.stack(
-                    [jnp.broadcast_to(iface_ref[chan, axial, azim : azim + 1], (4, 128)) for azim in range(4)],
+                    [jnp.broadcast_to(outer_lanes[axial * 4 + azim : axial * 4 + azim + 1], (4, 128)) for azim in range(4)],
                     axis=0,
                 )
                 for axial in range(4)
             ],
             axis=0,
         )
-        outer_face = jnp.where(rotor, face, 0.0)
-        inner_face = jnp.where(rotor, 0.0, face)
+        inner_face = jnp.stack(
+            [
+                jnp.stack(
+                    [jnp.broadcast_to(inner_lanes[axial * 4 + azim : axial * 4 + azim + 1], (4, 128)) for azim in range(4)],
+                    axis=0,
+                )
+                for axial in range(4)
+            ],
+            axis=0,
+        )
         up_az = expand_face(up_az_ref[chan], 0)
         down_az = expand_face(down_az_ref[chan], ET - 1)
         left0 = sweep(field, left_corr, lambda i: (i,))
@@ -338,17 +367,17 @@
     n_azim = lax.axis_size("azim")
     face4 = jax.ShapeDtypeStruct((5, 4, 4, 128), jnp.float32)
     chunk = jax.ShapeDtypeStruct((5, 4, 128), jnp.float32)
+    rows16 = jax.ShapeDtypeStruct((5, 16, 128), jnp.float32)
     left_ax, right_ax, upper_face, lower_face, outer_moment, inner_moment = pl.pallas_call(
-        moment_kernel, out_shape=(face4, face4, chunk, chunk, face4, face4)
+        moment_kernel,
+        out_shape=(face4, face4, chunk, chunk, rows16, rows16),
+        scratch_shapes=[pltpu.VMEM((2, 16, 128), jnp.float32)],
     )(adjoint)
     is_rotor = lax.axis_index("zone") == 0
     up_ax = lax.ppermute(left_ax, "axial", [(i + 1, i) for i in range(n_axial - 1)])
     down_ax = lax.ppermute(right_ax, "axial", [(i, i + 1) for i in range(n_axial - 1)])
-    face_shape = (5, 4, 4, EA, ET, ER)
-    own_face = jnp.where(
-        is_rotor, outer_moment.reshape(face_shape)[..., ER - 1], inner_moment.reshape(face_shape)[..., 0]
-    )
-    own_rows = faces_to_rows(own_face)
+    own_face = jnp.where(is_rotor, outer_moment, inner_moment)[:, :, : EA * ET]
+    own_rows = own_face.reshape(5, 4, 4, EA, ET).transpose(0, 3, 1, 4, 2).reshape(5, AP, TP)
     shifts_local = intersection_shift.reshape(INTERSECTIONS, AP, TP)
     table_match = weight_index[:, :, None] == jnp.arange(NW, dtype=jnp.int32)[None, None, :]
     weights_local = jnp.sum(
@@ -401,13 +430,16 @@
     returned = picked[0] + picked[1] + picked[2]
     window = jnp.concatenate(picked, axis=2)
     incoming = shift_sum(window, coefs, TP)
-    iface = rows_to_face(jnp.where(is_rotor, returned, incoming), EA, ET)
-    iface = jnp.broadcast_to(iface[..., None], (5, 4, 4, EA, ET, ER)).reshape(5, 4, 4, EA * ET * ER)
-    flag = jnp.broadcast_to(jnp.where(is_rotor, 1.0, 0.0), (8, 128))
+    def to_lanes(rows_vals):
+        face = rows_vals.reshape(5, EA, 4, ET, 4).transpose(0, 2, 4, 1, 3).reshape(5, 16, EA * ET)
+        return jnp.pad(face, ((0, 0), (0, 0), (0, 128 - EA * ET)))
+
+    outer = to_lanes(jnp.where(is_rotor, returned, 0.0))
+    inner = to_lanes(jnp.where(is_rotor, 0.0, incoming))
     field_shape = jax.ShapeDtypeStruct(adjoint.shape, jnp.float32)
     adjoint_rate, next_adjoint = pl.pallas_call(
         rate_kernel, out_shape=(field_shape, field_shape)
-    )(adjoint, flow_prim, up_ax, down_ax, up_az, down_az, iface, flag)
+    )(adjoint, flow_prim, up_ax, down_ax, up_az, down_az, outer, inner)
     return (adjoint_rate, next_adjoint)
 
 

time: 41.4 us -> 37.2 us (0.90)
  local copies, waits for them, and re-layouts: 15.5 us -> 10.2 us
  other arithmetic: 2.99 us -> 3.76 us
    reshape x5, local copies, waits for them, and re-layouts: 3.93 us -> 0.67 us  [the longest x3 0.41 us: to_lanes(): rows_vals.reshape(5, EA, 4, ET, 4).transpose(0, 2, 4, 1, 3)]
    unnamed x22 -> x18, local copies, waits for them, and re-layouts: 5.19 us -> 2.53 us
    pad x0 -> x2, local copies, waits for them, and re-layouts: none -> 1.23 us  [to_lanes(): return jnp.pad(face, ((0, 0), (0, 0), (0, 128 - EA * ET)))]
    broadcast_in_dim x2 -> x0, local copies, waits for them, and re-layouts: 1.03 us -> none  [the longest x1 0.62 us: local(): flag = jnp.broadcast_to(jnp.where(is_rotor, 1.0, 0.0), (8, 128))]
    select_n x1 -> x2, other arithmetic: 0.7 us -> 1.51 us  [the longest x1 0.81 us: local(): own_face = jnp.where(is_rotor, outer_moment, inner_moment)[:, :, :EA * ET]]
    transpose x2 -> x3, local copies, waits for them, and re-layouts: 1.18 us -> 1.77 us  [the longest x2 1.18 us: to_lanes(): rows_vals.reshape(5, EA, 4, ET, 4).transpose(0, 2, 4, 1, 3)]
  transfers between devices with their start and end apart: 3 -> 3, of which waited for: 1 -> 1; matrix products, arithmetic and copies ran while one was open for 10% -> 13% of each run, Pallas kernels for 0% -> 0%
where the time goes in v5:
time: 37.2 us; the launch traced here: 36.7 us
  starting transfers between devices  13.3 us (36%)
  local copies, waits for them, and re-layouts  10.2 us (27%)
  Pallas kernels  5.44 us (15%)
  other arithmetic  3.76 us (10%)
  waiting for transfers between devices  2.17 us (6%)
  between operations  1.8 us (5%)
    all_to_all x1, starting transfers between devices, local(): got = lax.all_to_all(chunks, ('zone', 'azim'), 0, 0)  7.49 us
    ppermute x1, starting transfers between devices, local(): lax.ppermute(right_ax, 'axial', [(i, i + 1) for i in range(n_axial - 1)])  4.55 us
    pallas_call x1, Pallas kernels, local(): pl.pallas_call(rate_kernel, out_shape=(field_shape, field_shape))  3.17 us
    unnamed x18, local copies, waits for them, and re-layouts  2.53 us
    mul x31, local copies, waits for them, and re-layouts, local(): coef[None] * own_rows  2.39 us
    pallas_call x1, Pallas kernels, local(): pl.pallas_call(moment_kernel, out_shape=(face4, face4, chunk, chunk, rows...  2.27 us
    all_to_all x1, waiting for transfers between devices, local(): got = lax.all_to_all(chunks, ('zone', 'azim'), 0, 0)  2.16 us
    ppermute x1, starting transfers between devices, local(): lax.ppermute(left_ax, 'axial', [(i + 1, i) for i in range(n_axial - 1)])  1.29 us
  transfers between devices with their start and end apart: 3, of which 1 were waited for; matrix products, arithmetic and copies ran while one was open for 13% of the time, Pallas kernels for 0%

profile of v5, /device:TPU:0, one launch (start us, length us, event | category | flops | bytes accessed | tf_op | source)
XLA Modules:
  0.0 36.7 jit_solution(8385675541726370381)
XLA Ops:
  1.4 0.6 %copy-done.4 = s32[4,256]{1,0:T(4,128)S(1)} copy-done((s32[4,256]{1,0:T(4,128)S(1)}, s32[4,256]{1,0:T(4,128)}, u32[]{:S(2)}) %copy-start.4) | copy-done | bytes 4120
  2.0 0.7 %copy-done.5 = s32[4,256]{1,0:T(4,128)S(1)} copy-done((s32[4,256]{1,0:T(4,128)S(1)}, s32[4,256]{1,0:T(4,128)}, u32[]{:S(2)}) %copy-start.5) | copy-done | bytes 4120
  2.7 0.4 %select_reduce_fusion = f32[4,256]{1,0:T(4,128)S(1)} fusion(f32[128]{0:T(128)S(1)} %copy-done.6, s32[4,256]{1,0:T(4,128)S(1)} %copy-done.5), kind=kLoop, calls=%fused_computation | loop fusion | flops 392192 | bytes 8704 | tf_op jit(solution)/shard_map/reduce_sum | solution.py:383
  3.4 2.3 %shard_map.77 = (f32[5,4,4,128]{3,2,1,0:T(4,128)}, f32[5,4,4,128]{3,2,1,0:T(4,128)}, f32[5,4,128]{2,1,0:T(4,128)}, f32[5,4,128]{2,1,0:T(4,128)}, f32[5,16,128]{2,1,0:T(8,128)}, /*index=5*/f32[5,16,128]{2,1,0:T(8,128)}) custom-call(f32[1,5,4,4,4,128]{5,4,3,2,1,0:T(4,128)} %adj_ref.3), custom_call_target="tpu_custom_call" | custom-call | tf_op jit(solution)/shard_map/pallas_call | solution.py:371
  5.7 0.8 %slice_select_fusion = f32[5,16,16]{2,1,0:T(8,128)S(1)} fusion(f32[5,16,128]{2,1,0:T(8,128)} %get-tuple-element.13, f32[5,16,128]{2,1,0:T(8,128)} %get-tuple-element.12, pred[]{:T(512)S(6)} %eq.706), kind=kLoop, calls=%fused_computation.122 | loop fusion | flops 1280 | bytes 15361 | tf_op jit(solution)/shard_map/jit(_where)/select_n | solution.py:379
  6.6 0.6 %copy.12 = f32[5,4,4,4,4]{4,3,2,1,0:T(4,128)S(1)} copy(f32[5,4,4,4,4]{3,1,4,2,0:T(4,128)S(1)} %bitcast.16) | data formatting | bytes 10240 | tf_op jit(solution)/shard_map/transpose | solution.py:380
  7.2 0.2 broadcast_in_dim.318
  10.3 0.4 %pad_add_fusion = f32[5,16,48]{2,1,0:T(8,128)S(1)} fusion(f32[5,16,16]{2,1,0:T(8,128)S(1)} %get-tuple-element.53, f32[5,16,16]{2,1,0:T(8,128)S(1)} %get-tuple-element.54, f32[5,16,16]{2,1,0:T(8,128)S(1)} %get-tuple-element.55, f32[5,16,16]{2,1,0:T(8,128)S(1)} %get-tuple-element.56, f32[5,16,16]{2,1,0:T(8,128)S(1)} %get-tuple-element.57, ...), kind=kLoop, calls=%fused_computation.123 | loop fusion | flops 115200 | bytes 174080 | tf_op jit(solution)/shard_map/add | solution.py:399
  11.2 0.6 %copy-done.2 = f32[5,4,128]{2,1,0:T(4,128)S(1)} copy-done((f32[5,4,128]{2,1,0:T(4,128)S(1)}, f32[5,4,128]{2,1,0:T(4,128)}, u32[]{:S(2)}) %copy-start.2) | copy-done | bytes 10264
  11.8 0.8 %select_select_fusion = f32[16,5,4,128]{3,2,1,0:T(4,128)} fusion(f32[16,5,2,128]{3,2,1,0:T(2,128)S(1)} %select_select_fusion.1, f32[5,4,128]{2,1,0:T(4,128)S(1)} %copy-done.3, f32[5,4,128]{2,1,0:T(4,128)S(1)} %copy-done.2, pred[16]{0:T(512)(128)(4,1)S(1)} %get-tuple-element.104, pred[16]{0:T(512)(128)(4,1)S(1)} %get-tuple-element.102, ...), kind=kLoop, calls=%fused_computation.2 | loop fusion | flops 122880 | bytes 266288 | tf_op jit(solution)/shard_map/jit(_where)/select_n | solution.py:416
  12.6 7.5 %all-to-all-start = ((f32[16,5,4,128]{3,2,1,0:T(4,128)}), f32[16,5,4,128]{3,2,1,0:T(4,128)S(1)}, u32[]{:S(2)}, u32[]{:S(2)}) async-start(f32[16,5,4,128]{3,2,1,0:T(4,128)} %select_select_fusion), calls=%async_computation | async-start | bytes 327680 | tf_op jit(solution)/shard_map/all_to_all | solution.py:419
  20.1 1.3 %collective-permute-start = (f32[5,4,4,128]{3,2,1,0:T(4,128)S(1)}, f32[5,4,4,128]{3,2,1,0:T(4,128)S(1)}, u32[]{:S(2)}, u32[]{:S(2)}) collective-permute-start(f32[5,4,4,128]{3,2,1,0:T(4,128)S(1)} %copy-done.8), channel_id=1, source_target_pairs={{8,0},{9,1},{10,2},{11,3},{12,4},{13,5},{14,6},{15,7},{24,16},{25,... | collective-permute-start | bytes 122888 | tf_op jit(solution)/shard_map/ppermute | solution.py:377
  21.4 4.5 %collective-permute-start.1 = (f32[5,4,4,128]{3,2,1,0:T(4,128)S(1)}, f32[5,4,4,128]{3,2,1,0:T(4,128)S(1)}, u32[]{:S(2)}, u32[]{:S(2)}) collective-permute-start(f32[5,4,4,128]{3,2,1,0:T(4,128)S(1)} %copy-done.7), channel_id=1, source_target_pairs={{0,8},{1,9},{2,10},{3,11},{4,12},{5,13},{6,14},{7,15},{16,24},{17,... | collective-permute-start | bytes 122888 | tf_op jit(solution)/shard_map/ppermute | solution.py:378
  26.1 2.2 %all-to-all-done = f32[16,5,4,128]{3,2,1,0:T(4,128)S(1)} async-done(((f32[16,5,4,128]{3,2,1,0:T(4,128)}), f32[16,5,4,128]{3,2,1,0:T(4,128)S(1)}, u32[]{:S(2)}, u32[]{:S(2)}) %all-to-all-start) | async-done | bytes 163872 | tf_op jit(solution)/shard_map/all_to_all | solution.py:419
  28.2 0.6 %dynamic-slice_bitcast_fusion.2 = (f32[5,4,128]{2,1,0:T(4,128)S(1)}, f32[5,4,128]{2,1,0:T(4,128)S(1)}, f32[5,4,128]{2,1,0:T(4,128)S(1)}, f32[5,4,128]{2,1,0:T(4,128)}, f32[5,4,128]{2,1,0:T(4,128)}) fusion(f32[16,5,4,128]{3,2,1,0:T(4,128)S(1)} %all-to-all-done, s32[]{:T(128)S(6)} %select_n.1126, s32[]{:T(128)S(6)} %select_n.1130, s32[]{:T(128)S(6)} %select_n.1128, ...), kind=kLoop, calls=%fused_computation.157 | loop fusion | bytes 102420 | tf_op jit(solution)/shard_map/jit(dynamic_index_in_dim)/squeeze | solution.py:425
  29.1 0.7 %fusion.2 = f32[5,16,16]{2,1,0:T(8,128)S(1)} fusion(f32[5,16,16]{2,1,0:T(8,128)S(1)} %reshape.787, f32[5,16,16]{2,1,0:T(8,128)S(1)} %reshape.786, f32[5,16,16]{2,1,0:T(8,128)S(1)} %reshape.785, f32[16,16]{1,0:T(8,128)S(1)} %mul.606, f32[16,16]{1,0:T(8,128)S(1)} %mul.603, f32[16,16]{1,0:T(8,128)S(1)} %mul.600, f32[16,16]{1,0:T(8,128)S(1)} %mul.597, ...), kind=kLoop, calls=%fused_computation.7 | loop fusion | flops 116480 | bytes 52225 | tf_op jit(solution)/shard_map/jit(_where)/select_n | solution.py:438
  29.9 0.6 %copy.15 = f32[5,4,4,4,4]{4,3,2,1,0:T(4,128)S(1)} copy(f32[5,4,4,4,4]{2,4,1,3,0:T(4,128)S(1)} %bitcast.17) | data formatting | bytes 10240 | tf_op jit(solution)/shard_map/transpose | solution.py:434
  30.7 0.2 select_n.1132
  30.9 0.6 %copy.14 = f32[5,4,4,4,4]{4,3,2,1,0:T(4,128)S(1)} copy(f32[5,4,4,4,4]{2,4,1,3,0:T(4,128)S(1)} %bitcast.18) | data formatting | bytes 10240 | tf_op jit(solution)/shard_map/transpose | solution.py:434
  31.5 0.1 reshape.784
  31.7 0.6 %pad.168.inner_ref = f32[5,16,128]{2,1,0:T(8,128)} pad(f32[5,16,16]{2,1,0:T(8,128)S(1)} %reshape.789, f32[]{:T(128)} %constant.143.clone.1), padding=0_0x0_0x0_112 | pad | bytes 46084 | tf_op jit(solution)/shard_map/jit(_pad)/pad | solution.py:435
  32.3 0.6 %pad.167.outer_ref = f32[5,16,128]{2,1,0:T(8,128)} pad(f32[5,16,16]{2,1,0:T(8,128)S(1)} %reshape.784, f32[]{:T(128)} %constant.143.clone.1), padding=0_0x0_0x0_112 | pad | bytes 46084 | tf_op jit(solution)/shard_map/jit(_pad)/pad | solution.py:435
  32.9 0.6 %copy-done = f32[5,4,4,128]{3,2,1,0:T(4,128)} copy-done((f32[5,4,4,128]{3,2,1,0:T(4,128)}, f32[5,4,4,128]{3,2,1,0:T(4,128)S(1)}, u32[]{:S(2)}) %copy-start) | copy-done | bytes 40984
  33.5 3.2 %shard_map.78 = (f32[1,5,4,4,4,128]{5,4,3,2,1,0:T(4,128)}, f32[1,5,4,4,4,128]{5,4,3,2,1,0:T(4,128)}) custom-call(f32[1,5,4,4,4,128]{5,4,3,2,1,0:T(4,128)} %adj_ref.3, bf16[1,5,4,4,4,128]{5,4,3,2,1,0:T(4,128)(2,1)} %flow_ref.1, f32[5,4,4,128]{3,2,1,0:T(4,128)} %copy-done, f32[5,4,4,128]{3,2,1,0:T(4,128)} %copy-done.1, ...), custom_call_target="tpu_custom_call" | custom-call | tf_op jit(solution)/shard_map/pallas_call | solution.py:440
  (74 shorter events, 4.2 us)
Async XLA Ops:
  1.4 0.7 %copy-start.4 = (s32[4,256]{1,0:T(4,128)S(1)}, s32[4,256]{1,0:T(4,128)}, u32[]{:S(2)}) copy-start(s32[4,256]{1,0:T(4,128)} %param.8) | copy-start | bytes 12292
  2.0 0.7 %copy-start.5 = (s32[4,256]{1,0:T(4,128)S(1)}, s32[4,256]{1,0:T(4,128)}, u32[]{:S(2)}) copy-start(s32[4,256]{1,0:T(4,128)} %param.9) | copy-start | bytes 12292
  2.0 0.7 %copy-start.6 = (f32[128]{0:T(128)S(1)}, f32[128]{0:T(128)}, u32[]{:S(2)}) copy-start(f32[128]{0:T(128)} %param.10) | copy-start | bytes 1540
  11.1 0.7 %copy-start.2 = (f32[5,4,128]{2,1,0:T(4,128)S(1)}, f32[5,4,128]{2,1,0:T(4,128)}, u32[]{:S(2)}) copy-start(f32[5,4,128]{2,1,0:T(4,128)} %get-tuple-element.10) | copy-start | bytes 30724
  11.1 0.7 %copy-start.3 = (f32[5,4,128]{2,1,0:T(4,128)S(1)}, f32[5,4,128]{2,1,0:T(4,128)}, u32[]{:S(2)}) copy-start(f32[5,4,128]{2,1,0:T(4,128)} %get-tuple-element.11) | copy-start | bytes 30724
  12.6 7.5 %copy-start.8 = (f32[5,4,4,128]{3,2,1,0:T(4,128)S(1)}, f32[5,4,4,128]{3,2,1,0:T(4,128)}, u32[]{:S(2)}) copy-start(f32[5,4,4,128]{3,2,1,0:T(4,128)} %get-tuple-element.8) | copy-start | bytes 122884
  12.6 8.8 %copy-start.7 = (f32[5,4,4,128]{3,2,1,0:T(4,128)S(1)}, f32[5,4,4,128]{3,2,1,0:T(4,128)}, u32[]{:S(2)}) copy-start(f32[5,4,4,128]{3,2,1,0:T(4,128)} %get-tuple-element.9) | copy-start | bytes 122884
  12.6 15.6 %all-to-all-start = ((f32[16,5,4,128]{3,2,1,0:T(4,128)}), f32[16,5,4,128]{3,2,1,0:T(4,128)S(1)}, u32[]{:S(2)}, u32[]{:S(2)}) async-start(f32[16,5,4,128]{3,2,1,0:T(4,128)} %select_select_fusion), calls=%async_computation | async-start | bytes 327680 | tf_op jit(solution)/shard_map/all_to_all | solution.py:419
  20.1 12.8 %collective-permute-start = (f32[5,4,4,128]{3,2,1,0:T(4,128)S(1)}, f32[5,4,4,128]{3,2,1,0:T(4,128)S(1)}, u32[]{:S(2)}, u32[]{:S(2)}) collective-permute-start(f32[5,4,4,128]{3,2,1,0:T(4,128)S(1)} %copy-done.8), channel_id=1, source_target_pairs={{8,0},{9,1},{10,2},{11,3},{12,4},{13,5},{14,6},{15,7},{24,16},{25,... | collective-permute-start | bytes 122888 | tf_op jit(solution)/shard_map/ppermute | solution.py:377
  21.4 11.5 %collective-permute-start.1 = (f32[5,4,4,128]{3,2,1,0:T(4,128)S(1)}, f32[5,4,4,128]{3,2,1,0:T(4,128)S(1)}, u32[]{:S(2)}, u32[]{:S(2)}) collective-permute-start(f32[5,4,4,128]{3,2,1,0:T(4,128)S(1)} %copy-done.7), channel_id=1, source_target_pairs={{0,8},{1,9},{2,10},{3,11},{4,12},{5,13},{6,14},{7,15},{16,24},{17,... | collective-permute-start | bytes 122888 | tf_op jit(solution)/shard_map/ppermute | solution.py:378
  32.9 0.6 %copy-start = (f32[5,4,4,128]{3,2,1,0:T(4,128)}, f32[5,4,4,128]{3,2,1,0:T(4,128)S(1)}, u32[]{:S(2)}) copy-start(f32[5,4,4,128]{3,2,1,0:T(4,128)S(1)} %collective-permute-done.up_ax_ref) | copy-start | bytes 122884
  32.9 0.6 %copy-start.1 = (f32[5,4,4,128]{3,2,1,0:T(4,128)}, f32[5,4,4,128]{3,2,1,0:T(4,128)S(1)}, u32[]{:S(2)}) copy-start(f32[5,4,4,128]{3,2,1,0:T(4,128)S(1)} %collective-permute-done.1.down_ax_ref) | copy-start | bytes 122884

commit v6 on v5

--- a/solution.py
+++ b/solution.py
@@ -416,6 +416,7 @@
     chunks = jnp.where(
         to_prev, upper_face[None], jnp.where(to_next, lower_face[None], jnp.where(same_zone[:, None, None, None], 0.0, iface_out))
     )
+    up_ax, down_ax, chunks = lax.optimization_barrier((up_ax, down_ax, chunks))
     got = lax.all_to_all(chunks, ("zone", "azim"), 0, 0)
     base = (1 - zone) * n_azim
     up_az = lax.dynamic_index_in_dim(got, zone * n_azim + (azim + 1) % n_azim, 0, keepdims=False)

time: 37.2 us -> 42.6 us (1.15)
  waiting for transfers between devices: 2.17 us -> 8.04 us
  other arithmetic: 3.76 us -> 2.94 us
  local copies, waits for them, and re-layouts: 10.2 us -> 10.7 us
    all_to_all x1, waiting for transfers between devices: 2.16 us -> 8.04 us  [local(): got = lax.all_to_all(chunks, ('zone', 'azim'), 0, 0)]
    select_n x1, other arithmetic: 0.81 us -> 0.01 us  [local(): own_face = jnp.where(is_rotor, outer_moment, inner_moment)[:, :, :EA * ET]]
    unnamed x18, local copies, waits for them, and re-layouts: 2.53 us -> 3.06 us
    all_to_all x1, starting transfers between devices: 7.49 us -> 7.03 us  [local(): got = lax.all_to_all(chunks, ('zone', 'azim'), 0, 0)]
  transfers between devices with their start and end apart: 3 -> 3, of which waited for: 1 -> 1; matrix products, arithmetic and copies ran while one was open for 13% -> 14% of each run, Pallas kernels for 0% -> 0%
where the time goes in v6:
time: 42.6 us; the launch traced here: 42.2 us
  starting transfers between devices  13.2 us (31%)
  local copies, waits for them, and re-layouts  10.7 us (25%)
  waiting for transfers between devices  8.04 us (19%)
  Pallas kernels  5.44 us (13%)
  other arithmetic  2.94 us (7%)
  between operations  1.82 us (4%)
    all_to_all x1, waiting for transfers between devices, local(): got = lax.all_to_all(chunks, ('zone', 'azim'), 0, 0)  8.04 us
    all_to_all x1, starting transfers between devices, local(): got = lax.all_to_all(chunks, ('zone', 'azim'), 0, 0)  7.03 us
    ppermute x1, starting transfers between devices, local(): lax.ppermute(right_ax, 'axial', [(i, i + 1) for i in range(n_axial - 1)])  4.87 us
    pallas_call x1, Pallas kernels, local(): pl.pallas_call(rate_kernel, out_shape=(field_shape, field_shape))  3.17 us
    unnamed x18, local copies, waits for them, and re-layouts  3.06 us
    mul x31, local copies, waits for them, and re-layouts, local(): coef[None] * own_rows  2.39 us
    pallas_call x1, Pallas kernels, local(): pl.pallas_call(moment_kernel, out_shape=(face4, face4, chunk, chunk, rows...  2.27 us
    ppermute x1, starting transfers between devices, local(): lax.ppermute(left_ax, 'axial', [(i + 1, i) for i in range(n_axial - 1)])  1.28 us
  transfers between devices with their start and end apart: 3, of which 1 were waited for; matrix products, arithmetic and copies ran while one was open for 14% of the time, Pallas kernels for 0%

profile of v6, /device:TPU:0, one launch (start us, length us, event | category | flops | bytes accessed | tf_op | source)
XLA Modules:
  0.0 42.2 jit_solution(4040377612737218401)
XLA Ops:
  0.6 2.3 %shard_map.77 = (f32[5,4,4,128]{3,2,1,0:T(4,128)}, f32[5,4,4,128]{3,2,1,0:T(4,128)}, f32[5,4,128]{2,1,0:T(4,128)}, f32[5,4,128]{2,1,0:T(4,128)}, f32[5,16,128]{2,1,0:T(8,128)}, /*index=5*/f32[5,16,128]{2,1,0:T(8,128)}) custom-call(f32[1,5,4,4,4,128]{5,4,3,2,1,0:T(4,128)} %adj_ref.3), custom_call_target="tpu_custom_call" | custom-call | tf_op jit(solution)/shard_map/pallas_call | solution.py:371
  2.9 1.3 %collective-permute-start = (f32[5,4,4,128]{3,2,1,0:T(4,128)}, f32[5,4,4,128]{3,2,1,0:T(4,128)S(1)}, u32[]{:S(2)}, u32[]{:S(2)}) collective-permute-start(f32[5,4,4,128]{3,2,1,0:T(4,128)} %get-tuple-element.11), channel_id=1, source_target_pairs={{8,0},{9,1},{10,2},{11,3},{12,4},{13,5},{14,6},{15,7},{24,16},{25,... | collective-permute-start | bytes 122888 | tf_op jit(solution)/shard_map/ppermute | solution.py:377
  4.2 4.9 %collective-permute-start.1 = (f32[5,4,4,128]{3,2,1,0:T(4,128)}, f32[5,4,4,128]{3,2,1,0:T(4,128)S(1)}, u32[]{:S(2)}, u32[]{:S(2)}) collective-permute-start(f32[5,4,4,128]{3,2,1,0:T(4,128)} %get-tuple-element.12), channel_id=1, source_target_pairs={{0,8},{1,9},{2,10},{3,11},{4,12},{5,13},{6,14},{7,15},{16,24},{17,... | collective-permute-start | bytes 122888 | tf_op jit(solution)/shard_map/ppermute | solution.py:378
  9.8 0.6 %copy-done.6 = s32[4,256]{1,0:T(4,128)S(1)} copy-done((s32[4,256]{1,0:T(4,128)S(1)}, s32[4,256]{1,0:T(4,128)}, u32[]{:S(2)}) %copy-start.6) | copy-done | bytes 4120
  10.5 0.7 %copy-done.7 = s32[4,256]{1,0:T(4,128)S(1)} copy-done((s32[4,256]{1,0:T(4,128)S(1)}, s32[4,256]{1,0:T(4,128)}, u32[]{:S(2)}) %copy-start.7) | copy-done | bytes 4120
  11.2 0.4 select_reduce_fusion
  11.9 0.5 %copy-done.1 = f32[5,16,128]{2,1,0:T(8,128)S(1)} copy-done((f32[5,16,128]{2,1,0:T(8,128)S(1)}, f32[5,16,128]{2,1,0:T(8,128)}, u32[]{:S(2)}) %copy-start.1) | copy-done | bytes 40984
  12.6 0.6 %copy.12 = f32[5,4,4,4,4]{4,3,2,1,0:T(4,128)S(1)} copy(f32[5,4,4,4,4]{3,1,4,2,0:T(4,128)S(1)} %bitcast.16) | data formatting | bytes 10240 | tf_op jit(solution)/shard_map/transpose | solution.py:380
  13.2 0.2 broadcast_in_dim.318
  16.2 0.4 pad_add_fusion
  17.1 0.6 %copy-done.4 = f32[5,4,128]{2,1,0:T(4,128)S(1)} copy-done((f32[5,4,128]{2,1,0:T(4,128)S(1)}, f32[5,4,128]{2,1,0:T(4,128)}, u32[]{:S(2)}) %copy-start.4) | copy-done | bytes 10264
  17.7 0.8 %select_select_fusion = f32[16,5,4,128]{3,2,1,0:T(4,128)} fusion(f32[16,5,2,128]{3,2,1,0:T(2,128)S(1)} %select_select_fusion.1, f32[5,4,128]{2,1,0:T(4,128)S(1)} %copy-done.5, f32[5,4,128]{2,1,0:T(4,128)S(1)} %copy-done.4, pred[16]{0:T(512)(128)(4,1)S(1)} %fusion.197, pred[16]{0:T(512)(128)(4,1)S(1)} %get-tuple-element.108, ...), kind=kLoop, calls=%fused_computation.2 | loop fusion | flops 122880 | bytes 266288 | tf_op jit(solution)/shard_map/jit(_where)/select_n | solution.py:416
  18.5 0.6 %copy-done.2 = f32[5,4,4,128]{3,2,1,0:T(4,128)} copy-done((f32[5,4,4,128]{3,2,1,0:T(4,128)}, f32[5,4,4,128]{3,2,1,0:T(4,128)S(1)}, u32[]{:S(2)}) %copy-start.2) | copy-done | bytes 40984
  19.1 7.0 %all-to-all-start = ((f32[16,5,4,128]{3,2,1,0:T(4,128)}), f32[16,5,4,128]{3,2,1,0:T(4,128)S(1)}, u32[]{:S(2)}, u32[]{:S(2)}) async-start(f32[16,5,4,128]{3,2,1,0:T(4,128)} %select_select_fusion), calls=%async_computation | async-start | bytes 327680 | tf_op jit(solution)/shard_map/all_to_all | solution.py:420
  26.3 8.0 %all-to-all-done = f32[16,5,4,128]{3,2,1,0:T(4,128)S(1)} async-done(((f32[16,5,4,128]{3,2,1,0:T(4,128)}), f32[16,5,4,128]{3,2,1,0:T(4,128)S(1)}, u32[]{:S(2)}, u32[]{:S(2)}) %all-to-all-start) | async-done | bytes 163872 | tf_op jit(solution)/shard_map/all_to_all | solution.py:420
  34.3 0.6 %dynamic-slice_bitcast_fusion.2 = (f32[5,4,128]{2,1,0:T(4,128)S(1)}, f32[5,4,128]{2,1,0:T(4,128)S(1)}, f32[5,4,128]{2,1,0:T(4,128)S(1)}, f32[5,4,128]{2,1,0:T(4,128)}, f32[5,4,128]{2,1,0:T(4,128)}) fusion(f32[16,5,4,128]{3,2,1,0:T(4,128)S(1)} %all-to-all-done, s32[]{:T(128)S(6)} %select_n.1126, s32[]{:T(128)S(6)} %select_n.1130, s32[]{:T(128)S(6)} %select_n.1128, ...), kind=kLoop, calls=%fused_computation.157 | loop fusion | bytes 102420 | tf_op jit(solution)/shard_map/jit(dynamic_index_in_dim)/squeeze | solution.py:426
  35.2 0.7 %fusion.2 = f32[5,16,16]{2,1,0:T(8,128)S(1)} fusion(f32[5,16,16]{2,1,0:T(8,128)S(1)} %reshape.787, f32[5,16,16]{2,1,0:T(8,128)S(1)} %reshape.786, f32[5,16,16]{2,1,0:T(8,128)S(1)} %reshape.785, f32[16,16]{1,0:T(8,128)S(1)} %mul.606, f32[16,16]{1,0:T(8,128)S(1)} %mul.603, f32[16,16]{1,0:T(8,128)S(1)} %mul.600, f32[16,16]{1,0:T(8,128)S(1)} %mul.597, ...), kind=kLoop, calls=%fused_computation.7 | loop fusion | flops 116480 | bytes 52225 | tf_op jit(solution)/shard_map/jit(_where)/select_n | solution.py:439
  36.0 0.6 %copy.15 = f32[5,4,4,4,4]{4,3,2,1,0:T(4,128)S(1)} copy(f32[5,4,4,4,4]{2,4,1,3,0:T(4,128)S(1)} %bitcast.17) | data formatting | bytes 10240 | tf_op jit(solution)/shard_map/transpose | solution.py:435
  36.8 0.2 select_n.1132
  37.0 0.6 %copy.14 = f32[5,4,4,4,4]{4,3,2,1,0:T(4,128)S(1)} copy(f32[5,4,4,4,4]{2,4,1,3,0:T(4,128)S(1)} %bitcast.18) | data formatting | bytes 10240 | tf_op jit(solution)/shard_map/transpose | solution.py:435
  37.6 0.1 reshape.784
  37.8 0.6 %pad.168.inner_ref = f32[5,16,128]{2,1,0:T(8,128)} pad(f32[5,16,16]{2,1,0:T(8,128)S(1)} %reshape.789, f32[]{:T(128)} %constant.143.clone.1), padding=0_0x0_0x0_112 | pad | bytes 46084 | tf_op jit(solution)/shard_map/jit(_pad)/pad | solution.py:436
  38.4 0.6 %pad.167.outer_ref = f32[5,16,128]{2,1,0:T(8,128)} pad(f32[5,16,16]{2,1,0:T(8,128)S(1)} %reshape.784, f32[]{:T(128)} %constant.143.clone.1), padding=0_0x0_0x0_112 | pad | bytes 46084 | tf_op jit(solution)/shard_map/jit(_pad)/pad | solution.py:436
  39.0 3.2 %shard_map.78 = (f32[1,5,4,4,4,128]{5,4,3,2,1,0:T(4,128)}, f32[1,5,4,4,4,128]{5,4,3,2,1,0:T(4,128)}) custom-call(f32[1,5,4,4,4,128]{5,4,3,2,1,0:T(4,128)} %adj_ref.3, bf16[1,5,4,4,4,128]{5,4,3,2,1,0:T(4,128)(2,1)} %flow_ref.1, f32[5,4,4,128]{3,2,1,0:T(4,128)} %copy-done.2, f32[5,4,4,128]{3,2,1,0:T(4,128)} %copy-done.3, ...), custom_call_target="tpu_custom_call" | custom-call | tf_op jit(solution)/shard_map/pallas_call | solution.py:441
  (74 shorter events, 4.3 us)
Async XLA Ops:
  2.9 15.6 %collective-permute-start = (f32[5,4,4,128]{3,2,1,0:T(4,128)}, f32[5,4,4,128]{3,2,1,0:T(4,128)S(1)}, u32[]{:S(2)}, u32[]{:S(2)}) collective-permute-start(f32[5,4,4,128]{3,2,1,0:T(4,128)} %get-tuple-element.11), channel_id=1, source_target_pairs={{8,0},{9,1},{10,2},{11,3},{12,4},{13,5},{14,6},{15,7},{24,16},{25,... | collective-permute-start | bytes 122888 | tf_op jit(solution)/shard_map/ppermute | solution.py:377
  4.2 14.3 %collective-permute-start.1 = (f32[5,4,4,128]{3,2,1,0:T(4,128)}, f32[5,4,4,128]{3,2,1,0:T(4,128)S(1)}, u32[]{:S(2)}, u32[]{:S(2)}) collective-permute-start(f32[5,4,4,128]{3,2,1,0:T(4,128)} %get-tuple-element.12), channel_id=1, source_target_pairs={{0,8},{1,9},{2,10},{3,11},{4,12},{5,13},{6,14},{7,15},{16,24},{17,... | collective-permute-start | bytes 122888 | tf_op jit(solution)/shard_map/ppermute | solution.py:378
  9.8 0.7 %copy-start.6 = (s32[4,256]{1,0:T(4,128)S(1)}, s32[4,256]{1,0:T(4,128)}, u32[]{:S(2)}) copy-start(s32[4,256]{1,0:T(4,128)} %param.8) | copy-start | bytes 12292
  10.5 0.7 %copy-start.7 = (s32[4,256]{1,0:T(4,128)S(1)}, s32[4,256]{1,0:T(4,128)}, u32[]{:S(2)}) copy-start(s32[4,256]{1,0:T(4,128)} %param.9) | copy-start | bytes 12292
  10.5 0.7 %copy-start.8 = (f32[128]{0:T(128)S(1)}, f32[128]{0:T(128)}, u32[]{:S(2)}) copy-start(f32[128]{0:T(128)} %param.10) | copy-start | bytes 1540
  11.6 0.8 %copy-start.1 = (f32[5,16,128]{2,1,0:T(8,128)S(1)}, f32[5,16,128]{2,1,0:T(8,128)}, u32[]{:S(2)}) copy-start(f32[5,16,128]{2,1,0:T(8,128)} %get-tuple-element.16) | copy-start | bytes 122884
  11.6 0.8 %copy-start = (f32[5,16,128]{2,1,0:T(8,128)S(1)}, f32[5,16,128]{2,1,0:T(8,128)}, u32[]{:S(2)}) copy-start(f32[5,16,128]{2,1,0:T(8,128)} %get-tuple-element.15) | copy-start | bytes 122884
  17.0 0.7 %copy-start.4 = (f32[5,4,128]{2,1,0:T(4,128)S(1)}, f32[5,4,128]{2,1,0:T(4,128)}, u32[]{:S(2)}) copy-start(f32[5,4,128]{2,1,0:T(4,128)} %get-tuple-element.13) | copy-start | bytes 30724
  17.0 0.7 %copy-start.5 = (f32[5,4,128]{2,1,0:T(4,128)S(1)}, f32[5,4,128]{2,1,0:T(4,128)}, u32[]{:S(2)}) copy-start(f32[5,4,128]{2,1,0:T(4,128)} %get-tuple-element.14) | copy-start | bytes 30724
  18.5 0.6 %copy-start.2 = (f32[5,4,4,128]{3,2,1,0:T(4,128)}, f32[5,4,4,128]{3,2,1,0:T(4,128)S(1)}, u32[]{:S(2)}) copy-start(f32[5,4,4,128]{3,2,1,0:T(4,128)S(1)} %collective-permute-done.up_ax_ref) | copy-start | bytes 122884
  18.5 0.6 %copy-start.3 = (f32[5,4,4,128]{3,2,1,0:T(4,128)}, f32[5,4,4,128]{3,2,1,0:T(4,128)S(1)}, u32[]{:S(2)}) copy-start(f32[5,4,4,128]{3,2,1,0:T(4,128)S(1)} %collective-permute-done.1.down_ax_ref) | copy-start | bytes 122884
  19.1 15.2 %all-to-all-start = ((f32[16,5,4,128]{3,2,1,0:T(4,128)}), f32[16,5,4,128]{3,2,1,0:T(4,128)S(1)}, u32[]{:S(2)}, u32[]{:S(2)}) async-start(f32[16,5,4,128]{3,2,1,0:T(4,128)} %select_select_fusion), calls=%async_computation | async-start | bytes 327680 | tf_op jit(solution)/shard_map/all_to_all | solution.py:420

commit v7 on v5

--- a/solution.py
+++ b/solution.py
@@ -228,14 +228,29 @@
     return jnp.dot(left, right, precision=lax.Precision.HIGHEST, preferred_element_type=jnp.float32)
 
 
+def compact_axial(face, part):
+    lane = lax.broadcasted_iota(jnp.int32, (4, 128), 1)
+    span = ET * ER
+    out = jnp.zeros((4, 128), jnp.float32)
+    for block in range(4):
+        mask = (lane >= block * span) & (lane < block * span + span)
+        out = jnp.where(mask, lane_roll(face[block], block * span - part * span), out)
+    return out
+
+
+def expand_axial(chunk, part):
+    span = ET * ER
+    return jnp.stack([lane_roll(chunk, part * span - block * span) for block in range(4)], axis=0)
+
+
 def moment_kernel(adj_ref, left_ax_ref, right_ax_ref, up_ref, down_ref, outer_ref, inner_ref, scratch_ref):
     derivs, left_vals, right_vals, left_corr, right_corr = basis_tables()
     pick_outer = selector(128, 128, lambda k: k // ET * ET * ER + k % ET * ER + ER - 1, False)
     pick_inner = selector(128, 128, lambda k: k // ET * ET * ER + k % ET * ER, False)
     for chan in range(5):
         field = adj_ref[0, chan]
-        left_ax_ref[chan] = sweep(field, left_corr, lambda i: (i,))
-        right_ax_ref[chan] = sweep(field, right_corr, lambda i: (i,))
+        left_ax_ref[chan] = compact_axial(sweep(field, left_corr, lambda i: (i,)), 0)
+        right_ax_ref[chan] = compact_axial(sweep(field, right_corr, lambda i: (i,)), EA - 1)
         pick1 = lambda i: (slice(None), i)
         up_ref[chan] = compact_face(sweep(field, left_corr, pick1), 0)
         down_ref[chan] = compact_face(sweep(field, right_corr, pick1), ET - 1)
@@ -291,8 +306,8 @@
         down_az = expand_face(down_az_ref[chan], ET - 1)
         left0 = sweep(field, left_corr, lambda i: (i,))
         right0 = sweep(field, right_corr, lambda i: (i,))
-        next0 = lane_roll(jnp.where(flat_lane < ET * ER, up_ax_ref[chan], left0), -ET * ER)
-        prev0 = lane_roll(jnp.where(flat_lane >= (EA - 1) * ET * ER, down_ax_ref[chan], right0), ET * ER)
+        next0 = lane_roll(jnp.where(flat_lane < ET * ER, expand_axial(up_ax_ref[chan], 0), left0), -ET * ER)
+        prev0 = lane_roll(jnp.where(flat_lane >= (EA - 1) * ET * ER, expand_axial(down_ax_ref[chan], EA - 1), right0), ET * ER)
         jump_r = 0.5 * (next0 - right0)
         jump_l = 0.5 * (prev0 - left0)
         slabs = []
@@ -370,12 +385,10 @@
     rows16 = jax.ShapeDtypeStruct((5, 16, 128), jnp.float32)
     left_ax, right_ax, upper_face, lower_face, outer_moment, inner_moment = pl.pallas_call(
         moment_kernel,
-        out_shape=(face4, face4, chunk, chunk, rows16, rows16),
+        out_shape=(chunk, chunk, chunk, chunk, rows16, rows16),
         scratch_shapes=[pltpu.VMEM((2, 16, 128), jnp.float32)],
     )(adjoint)
     is_rotor = lax.axis_index("zone") == 0
-    up_ax = lax.ppermute(left_ax, "axial", [(i + 1, i) for i in range(n_axial - 1)])
-    down_ax = lax.ppermute(right_ax, "axial", [(i, i + 1) for i in range(n_axial - 1)])
     own_face = jnp.where(is_rotor, outer_moment, inner_moment)[:, :, : EA * ET]
     own_rows = own_face.reshape(5, 4, 4, EA, ET).transpose(0, 3, 1, 4, 2).reshape(5, AP, TP)
     shifts_local = intersection_shift.reshape(INTERSECTIONS, AP, TP)
@@ -398,8 +411,12 @@
         term = jnp.pad(coef[None] * own_rows, ((0, 0), (0, 0), (TP + rel, TP - rel)))
         contrib = term if contrib is None else contrib + term
     zone = lax.axis_index("zone")
+    axial = lax.axis_index("axial")
     azim = lax.axis_index("azim")
-    dest = jnp.arange(2 * n_azim, dtype=jnp.int32)
+    group = n_axial * n_azim
+    dest = jnp.arange(2 * group, dtype=jnp.int32)
+    dest_zone = dest // group
+    dest_axial = dest // n_azim % n_axial
     dest_azim = dest % n_azim
     gap = ((dest_azim - azim) % n_azim - turn) % n_azim
     gap = gap[:, None, None, None]
@@ -409,17 +426,31 @@
         jnp.where(gap == 0, contrib[None, :, :, TP : 2 * TP], contrib[None, :, :, 2 * TP :]),
     )
     iface_out = jnp.where(is_rotor, jnp.broadcast_to(own_rows[None], pieces.shape), pieces)
-    iface_out = jnp.pad(iface_out.reshape(2 * n_azim, 5, 2, 128), ((0, 0), (0, 0), (0, 2), (0, 0)))
-    same_zone = dest // n_azim == zone
-    to_prev = (same_zone & (dest_azim == (azim - 1) % n_azim))[:, None, None, None]
-    to_next = (same_zone & (dest_azim == (azim + 1) % n_azim))[:, None, None, None]
-    chunks = jnp.where(
-        to_prev, upper_face[None], jnp.where(to_next, lower_face[None], jnp.where(same_zone[:, None, None, None], 0.0, iface_out))
-    )
-    got = lax.all_to_all(chunks, ("zone", "azim"), 0, 0)
-    base = (1 - zone) * n_azim
-    up_az = lax.dynamic_index_in_dim(got, zone * n_azim + (azim + 1) % n_azim, 0, keepdims=False)
-    down_az = lax.dynamic_index_in_dim(got, zone * n_azim + (azim - 1) % n_azim, 0, keepdims=False)
+    iface_out = jnp.pad(iface_out.reshape(2 * group, 5, 2, 128), ((0, 0), (0, 0), (0, 2), (0, 0)))
+    same_zone = dest_zone == zone
+    same_ring = same_zone & (dest_axial == axial)
+    same_line = same_zone & (dest_azim == azim)
+    to_prev = (same_ring & (dest_azim == (azim - 1) % n_azim))[:, None, None, None]
+    to_next = (same_ring & (dest_azim == (azim + 1) % n_azim))[:, None, None, None]
+    to_below = (same_line & (dest_axial == axial - 1))[:, None, None, None]
+    to_above = (same_line & (dest_axial == axial + 1))[:, None, None, None]
+    is_iface = ((dest_zone != zone) & (dest_axial == axial))[:, None, None, None]
+    chunks = jnp.where(to_prev, upper_face[None], 0.0)
+    chunks = jnp.where(to_next, lower_face[None], chunks)
+    chunks = jnp.where(to_below, left_ax[None], chunks)
+    chunks = jnp.where(to_above, right_ax[None], chunks)
+    chunks = jnp.where(is_iface, iface_out, chunks)
+    got = lax.all_to_all(chunks, ("zone", "axial", "azim"), 0, 0)
+    ring = (zone * n_axial + axial) * n_azim
+    base = ((1 - zone) * n_axial + axial) * n_azim
+    up_az = lax.dynamic_index_in_dim(got, ring + (azim + 1) % n_azim, 0, keepdims=False)
+    down_az = lax.dynamic_index_in_dim(got, ring + (azim - 1) % n_azim, 0, keepdims=False)
+    above = jnp.minimum(axial + 1, n_axial - 1)
+    below = jnp.maximum(axial - 1, 0)
+    up_ax = lax.dynamic_index_in_dim(got, (zone * n_axial + above) * n_azim + azim, 0, keepdims=False)
+    down_ax = lax.dynamic_index_in_dim(got, (zone * n_axial + below) * n_azim + azim, 0, keepdims=False)
+    up_ax = jnp.where(axial + 1 < n_axial, up_ax, 0.0)
+    down_ax = jnp.where(axial > 0, down_ax, 0.0)
     direction = jnp.where(is_rotor, -1, 1)
     picked = [
         lax.dynamic_index_in_dim(

time: 37.2 us -> 41.1 us (1.10)
  waiting for transfers between devices: 2.17 us -> 12 us
  starting transfers between devices: 13.3 us -> 7.3 us
  local copies, waits for them, and re-layouts: 10.2 us -> 9.11 us
  other arithmetic: 3.76 us -> 4.58 us
    all_to_all x1, waiting for transfers between devices: 2.16 us -> 12 us  [local(): got = lax.all_to_all(chunks, ('zone', 'axial', 'azim'), 0, 0)]
    ppermute x2 -> x0, starting transfers between devices: 5.84 us -> none  [the longest x1 4.55 us: local(): lax.ppermute(right_ax, 'axial', [(i, i + 1) for i in range(n_axial - 1)])]
    squeeze x0 -> x1, other arithmetic: none -> 0.62 us  [local(): lax.dynamic_index_in_dim(got, base + (azim + direction * (turn + step)) %...]
    squeeze x1 -> x0, local copies, waits for them, and re-layouts: 0.6 us -> none  [local(): lax.dynamic_index_in_dim(got, base + (azim + direction * (turn + step)) %...]
    unnamed x18 -> x14, local copies, waits for them, and re-layouts: 2.53 us -> 2.04 us
  transfers between devices with their start and end apart: 3 -> 1, of which waited for: 1 -> 1; matrix products, arithmetic and copies ran while one was open for 13% -> 0% of each run, Pallas kernels for 0% -> 0%
where the time goes in v7:
time: 41.1 us; the launch traced here: 40.6 us
  waiting for transfers between devices  12 us (29%)
  local copies, waits for them, and re-layouts  9.11 us (22%)
  starting transfers between devices  7.3 us (18%)
  Pallas kernels  5.81 us (14%)
  other arithmetic  4.58 us (11%)
  between operations  1.8 us (4%)
    all_to_all x1, waiting for transfers between devices, local(): got = lax.all_to_all(chunks, ('zone', 'axial', 'azim'), 0, 0)  12 us
    all_to_all x1, starting transfers between devices, local(): got = lax.all_to_all(chunks, ('zone', 'axial', 'azim'), 0, 0)  7.3 us
    pallas_call x1, Pallas kernels, local(): pl.pallas_call(rate_kernel, out_shape=(field_shape, field_shape))  3.53 us
    mul x31, local copies, waits for them, and re-layouts, local(): coef[None] * own_rows  2.39 us
    pallas_call x1, Pallas kernels, local(): pl.pallas_call(moment_kernel, out_shape=(chunk, chunk, chunk, chunk, rows...  2.28 us
    unnamed x14, local copies, waits for them, and re-layouts  2.04 us
    pad x2, local copies, waits for them, and re-layouts, to_lanes(): return jnp.pad(face, ((0, 0), (0, 0), (0, 128 - EA * ET)))  1.24 us
    transpose x2, local copies, waits for them, and re-layouts, to_lanes(): rows_vals.reshape(5, EA, 4, ET, 4).transpose(0, 2, 4, 1, 3)  1.18 us
  transfers between devices with their start and end apart: 1, of which 1 were waited for; matrix products, arithmetic and copies ran while one was open for 0% of the time, Pallas kernels for 0%

profile of v7, /device:TPU:0, one launch (start us, length us, event | category | flops | bytes accessed | tf_op | source)
XLA Modules:
  0.0 40.6 jit_solution(9016237973768994009)
XLA Ops:
  1.4 0.6 %copy-done.4 = s32[4,256]{1,0:T(4,128)S(1)} copy-done((s32[4,256]{1,0:T(4,128)S(1)}, s32[4,256]{1,0:T(4,128)}, u32[]{:S(2)}) %copy-start.4) | copy-done | bytes 4120
  2.1 0.7 %copy-done.5 = s32[4,256]{1,0:T(4,128)S(1)} copy-done((s32[4,256]{1,0:T(4,128)S(1)}, s32[4,256]{1,0:T(4,128)}, u32[]{:S(2)}) %copy-start.5) | copy-done | bytes 4120
  2.7 0.4 select_reduce_fusion
  3.4 2.3 %shard_map.77 = (f32[5,4,128]{2,1,0:T(4,128)}, f32[5,4,128]{2,1,0:T(4,128)}, f32[5,4,128]{2,1,0:T(4,128)}, f32[5,4,128]{2,1,0:T(4,128)}, f32[5,16,128]{2,1,0:T(8,128)}, /*index=5*/f32[5,16,128]{2,1,0:T(8,128)}) custom-call(f32[1,5,4,4,4,128]{5,4,3,2,1,0:T(4,128)} %adj_ref.3), custom_call_target="tpu_custom_call" | custom-call | tf_op jit(solution)/shard_map/pallas_call | solution.py:386
  5.7 0.8 %slice_select_fusion = f32[5,16,16]{2,1,0:T(8,128)S(1)} fusion(f32[5,16,128]{2,1,0:T(8,128)} %get-tuple-element.9, f32[5,16,128]{2,1,0:T(8,128)} %get-tuple-element.8, pred[]{:T(512)S(6)} %eq.755), kind=kLoop, calls=%fused_computation.122 | loop fusion | flops 1280 | bytes 15361 | tf_op jit(solution)/shard_map/jit(_where)/select_n | solution.py:392
  6.7 0.6 %copy.13 = f32[5,4,4,4,4]{4,3,2,1,0:T(4,128)S(1)} copy(f32[5,4,4,4,4]{3,1,4,2,0:T(4,128)S(1)} %bitcast.20) | data formatting | bytes 10240 | tf_op jit(solution)/shard_map/transpose | solution.py:393
  7.3 0.2 broadcast_in_dim.348
  10.3 0.4 %pad_add_fusion = f32[5,16,48]{2,1,0:T(8,128)S(1)} fusion(f32[5,16,16]{2,1,0:T(8,128)S(1)} %get-tuple-element.55, f32[5,16,16]{2,1,0:T(8,128)S(1)} %get-tuple-element.56, f32[5,16,16]{2,1,0:T(8,128)S(1)} %get-tuple-element.57, f32[5,16,16]{2,1,0:T(8,128)S(1)} %get-tuple-element.58, f32[5,16,16]{2,1,0:T(8,128)S(1)} %get-tuple-element.59, ...), kind=kLoop, calls=%fused_computation.123 | loop fusion | flops 115200 | bytes 174080 | tf_op jit(solution)/shard_map/add | solution.py:412
  11.1 0.1 select_select_fusion.1
  11.3 0.5 %copy-done.1 = f32[5,4,128]{2,1,0:T(4,128)S(1)} copy-done((f32[5,4,128]{2,1,0:T(4,128)S(1)}, f32[5,4,128]{2,1,0:T(4,128)}, u32[]{:S(2)}) %copy-start.1) | copy-done | bytes 10264
  11.8 0.2 copy-done
  12.0 1.0 %select_select_fusion = f32[32,5,4,128]{3,2,1,0:T(4,128)} fusion(f32[32,5,2,128]{3,2,1,0:T(2,128)S(1)} %select_select_fusion.1, f32[5,4,128]{2,1,0:T(4,128)S(1)} %copy-done.2, f32[5,4,128]{2,1,0:T(4,128)S(1)} %copy-done.3, f32[5,4,128]{2,1,0:T(4,128)S(1)} %copy-done, f32[5,4,128]{2,1,0:T(4,128)S(1)} %copy-done.1, pred[32]{0:T(512)(128)(4,1)S(1)} %get-tuple-element.104, ...), kind=kLoop, calls=%fused_computation.2 | loop fusion | flops 409600 | bytes 532640 | tf_op jit(solution)/shard_map/jit(_where)/select_n | solution.py:442
  13.0 7.3 %all-to-all-start = ((f32[32,5,4,128]{3,2,1,0:T(4,128)}), f32[32,5,4,128]{3,2,1,0:T(4,128)S(1)}, u32[]{:S(2)}, u32[]{:S(2)}) async-start(f32[32,5,4,128]{3,2,1,0:T(4,128)} %select_select_fusion), calls=%async_computation | async-start | bytes 655360 | tf_op jit(solution)/shard_map/all_to_all | solution.py:443
  20.4 12.0 %all-to-all-done = f32[32,5,4,128]{3,2,1,0:T(4,128)S(1)} async-done(((f32[32,5,4,128]{3,2,1,0:T(4,128)}), f32[32,5,4,128]{3,2,1,0:T(4,128)S(1)}, u32[]{:S(2)}, u32[]{:S(2)}) %all-to-all-start) | async-done | bytes 327712 | tf_op jit(solution)/shard_map/all_to_all | solution.py:443
  32.4 0.6 %dynamic-slice_bitcast_fusion.2 = (f32[5,4,128]{2,1,0:T(4,128)S(1)}, f32[5,4,128]{2,1,0:T(4,128)S(1)}, f32[5,4,128]{2,1,0:T(4,128)S(1)}, f32[5,4,128]{2,1,0:T(4,...) fusion(f32[32,5,4,128]{3,2,1,0:T(4,128)S(1)} %all-to-all-done, s32[]{:T(128)S(6)} %select_n.1232, ...), kind=kLoop, calls=%fused_computation.157 | loop fusion | flops 5120 | bytes 143390 | tf_op jit(solution)/shard_map/jit(dynamic_index_in_dim)/squeeze | solution.py:456
  33.3 0.7 %fusion.2 = f32[5,16,16]{2,1,0:T(8,128)S(1)} fusion(f32[5,16,16]{2,1,0:T(8,128)S(1)} %reshape.832, f32[5,16,16]{2,1,0:T(8,128)S(1)} %reshape.831, f32[5,16,16]{2,1,0:T(8,128)S(1)} %reshape.830, f32[16,16]{1,0:T(8,128)S(1)} %mul.619, f32[16,16]{1,0:T(8,128)S(1)} %mul.616, f32[16,16]{1,0:T(8,128)S(1)} %mul.613, f32[16,16]{1,0:T(8,128)S(1)} %mul.610, ...), kind=kLoop, calls=%fused_computation.7 | loop fusion | flops 116480 | bytes 52225 | tf_op jit(solution)/shard_map/jit(_where)/select_n | solution.py:469
  34.1 0.6 %copy.16 = f32[5,4,4,4,4]{4,3,2,1,0:T(4,128)S(1)} copy(f32[5,4,4,4,4]{2,4,1,3,0:T(4,128)S(1)} %bitcast.21) | data formatting | bytes 10240 | tf_op jit(solution)/shard_map/transpose | solution.py:465
  34.7 0.1 reshape.834
  34.9 0.2 select_n.1238
  35.1 0.6 %copy.15 = f32[5,4,4,4,4]{4,3,2,1,0:T(4,128)S(1)} copy(f32[5,4,4,4,4]{2,4,1,3,0:T(4,128)S(1)} %bitcast.22) | data formatting | bytes 10240 | tf_op jit(solution)/shard_map/transpose | solution.py:465
  35.7 0.1 reshape.829
  35.9 0.6 %pad.168.inner_ref = f32[5,16,128]{2,1,0:T(8,128)} pad(f32[5,16,16]{2,1,0:T(8,128)S(1)} %reshape.834, f32[]{:T(128)} %constant.186.clone.1), padding=0_0x0_0x0_112 | pad | bytes 46084 | tf_op jit(solution)/shard_map/jit(_pad)/pad | solution.py:466
  36.5 0.6 %pad.167.outer_ref = f32[5,16,128]{2,1,0:T(8,128)} pad(f32[5,16,16]{2,1,0:T(8,128)S(1)} %reshape.829, f32[]{:T(128)} %constant.186.clone.1), padding=0_0x0_0x0_112 | pad | bytes 46084 | tf_op jit(solution)/shard_map/jit(_pad)/pad | solution.py:466
  37.1 3.5 %shard_map.78 = (f32[1,5,4,4,4,128]{5,4,3,2,1,0:T(4,128)}, f32[1,5,4,4,4,128]{5,4,3,2,1,0:T(4,128)}) custom-call(f32[1,5,4,4,4,128]{5,4,3,2,1,0:T(4,128)} %adj_ref.3, bf16[1,5,4,4,4,128]{5,4,3,2,1,0:T(4,128)(2,1)} %flow_ref.1, f32[5,4,128]{2,1,0:T(4,128)} %get-tuple-element.50.up_ax_ref, f32[5,4,128]{2,1,0:T(4,128)} %get-tuple-element.49.down_ax_ref, ...), custom_call_target="tpu_custom_call" | custom-call | tf_op jit(solution)/shard_map/pallas_call | solution.py:471
  (67 shorter events, 4.0 us)
Async XLA Ops:
  1.4 0.7 %copy-start.4 = (s32[4,256]{1,0:T(4,128)S(1)}, s32[4,256]{1,0:T(4,128)}, u32[]{:S(2)}) copy-start(s32[4,256]{1,0:T(4,128)} %param.8) | copy-start | bytes 12292
  2.0 0.7 %copy-start.5 = (s32[4,256]{1,0:T(4,128)S(1)}, s32[4,256]{1,0:T(4,128)}, u32[]{:S(2)}) copy-start(s32[4,256]{1,0:T(4,128)} %param.9) | copy-start | bytes 12292
  2.0 0.7 %copy-start.6 = (f32[128]{0:T(128)S(1)}, f32[128]{0:T(128)}, u32[]{:S(2)}) copy-start(f32[128]{0:T(128)} %param.10) | copy-start | bytes 1540
  11.1 0.7 %copy-start.1 = (f32[5,4,128]{2,1,0:T(4,128)S(1)}, f32[5,4,128]{2,1,0:T(4,128)}, u32[]{:S(2)}) copy-start(f32[5,4,128]{2,1,0:T(4,128)} %get-tuple-element.10) | copy-start | bytes 30724
  11.1 0.7 %copy-start.2 = (f32[5,4,128]{2,1,0:T(4,128)S(1)}, f32[5,4,128]{2,1,0:T(4,128)}, u32[]{:S(2)}) copy-start(f32[5,4,128]{2,1,0:T(4,128)} %get-tuple-element.13) | copy-start | bytes 30724
  11.1 0.7 %copy-start.3 = (f32[5,4,128]{2,1,0:T(4,128)S(1)}, f32[5,4,128]{2,1,0:T(4,128)}, u32[]{:S(2)}) copy-start(f32[5,4,128]{2,1,0:T(4,128)} %get-tuple-element.12) | copy-start | bytes 30724
  11.3 0.7 %copy-start = (f32[5,4,128]{2,1,0:T(4,128)S(1)}, f32[5,4,128]{2,1,0:T(4,128)}, u32[]{:S(2)}) copy-start(f32[5,4,128]{2,1,0:T(4,128)} %get-tuple-element.11) | copy-start | bytes 30724
  13.0 19.4 %all-to-all-start = ((f32[32,5,4,128]{3,2,1,0:T(4,128)}), f32[32,5,4,128]{3,2,1,0:T(4,128)S(1)}, u32[]{:S(2)}, u32[]{:S(2)}) async-start(f32[32,5,4,128]{3,2,1,0:T(4,128)} %select_select_fusion), calls=%async_computation | async-start | bytes 655360 | tf_op jit(solution)/shard_map/all_to_all | solution.py:443

commit v8 on v5

--- a/solution.py
+++ b/solution.py
@@ -387,12 +387,11 @@
     turn = (offset + TP // 2) // TP
     residue = offset - turn * TP
     offsets_k = residue + shifts_local
-    coefs = []
-    for rel in range(-TP, TP - 1):
-        coef = jnp.where(offsets_k[0] == rel, weights_local[0], 0.0)
-        for member in range(1, INTERSECTIONS):
-            coef = coef + jnp.where(offsets_k[member] == rel, weights_local[member], 0.0)
-        coefs.append((rel, coef))
+    rel_all = jnp.arange(-TP, TP - 1, dtype=jnp.int32)[:, None, None]
+    coef_all = jnp.where(offsets_k[0][None] == rel_all, weights_local[0][None], 0.0)
+    for member in range(1, INTERSECTIONS):
+        coef_all = coef_all + jnp.where(offsets_k[member][None] == rel_all, weights_local[member][None], 0.0)
+    coefs = [(rel, coef_all[rel + TP]) for rel in range(-TP, TP - 1)]
     contrib = None
     for rel, coef in coefs:
         term = jnp.pad(coef[None] * own_rows, ((0, 0), (0, 0), (TP + rel, TP - rel)))

time: 37.2 us -> 35.3 us (0.949)
  local copies, waits for them, and re-layouts: 10.2 us -> 8.5 us
    mul x31 -> x2, local copies, waits for them, and re-layouts: 2.39 us -> 0.03 us  [local(): coef[None] * own_rows]
where the time goes in v8:
time: 35.3 us; the launch traced here: 34.8 us
  starting transfers between devices  13.3 us (38%)
  local copies, waits for them, and re-layouts  8.5 us (24%)
  Pallas kernels  5.44 us (15%)
  other arithmetic  3.61 us (10%)
  waiting for transfers between devices  2.17 us (6%)
  between operations  1.72 us (5%)
    all_to_all x1, starting transfers between devices, local(): got = lax.all_to_all(chunks, ('zone', 'azim'), 0, 0)  7.49 us
    ppermute x1, starting transfers between devices, local(): lax.ppermute(right_ax, 'axial', [(i, i + 1) for i in range(n_axial - 1)])  4.55 us
    pallas_call x1, Pallas kernels, local(): pl.pallas_call(rate_kernel, out_shape=(field_shape, field_shape))  3.17 us
    unnamed x18, local copies, waits for them, and re-layouts  2.53 us
    pallas_call x1, Pallas kernels, local(): pl.pallas_call(moment_kernel, out_shape=(face4, face4, chunk, chunk, rows...  2.27 us
    all_to_all x1, waiting for transfers between devices, local(): got = lax.all_to_all(chunks, ('zone', 'azim'), 0, 0)  2.16 us
    ppermute x1, starting transfers between devices, local(): lax.ppermute(left_ax, 'axial', [(i + 1, i) for i in range(n_axial - 1)])  1.29 us
    pad x2, local copies, waits for them, and re-layouts, to_lanes(): return jnp.pad(face, ((0, 0), (0, 0), (0, 128 - EA * ET)))  1.23 us
  transfers between devices with their start and end apart: 3, of which 1 were waited for; matrix products, arithmetic and copies ran while one was open for 13% of the time, Pallas kernels for 0%

profile of v8, /device:TPU:0, one launch (start us, length us, event | category | flops | bytes accessed | tf_op | source)
XLA Modules:
  0.0 34.8 jit_solution(8217765739470845592)
XLA Ops:
  1.4 2.3 %shard_map.77 = (f32[5,4,4,128]{3,2,1,0:T(4,128)}, f32[5,4,4,128]{3,2,1,0:T(4,128)}, f32[5,4,128]{2,1,0:T(4,128)}, f32[5,4,128]{2,1,0:T(4,128)}, f32[5,16,128]{2,1,0:T(8,128)}, /*index=5*/f32[5,16,128]{2,1,0:T(8,128)}) custom-call(f32[1,5,4,4,4,128]{5,4,3,2,1,0:T(4,128)} %adj_ref.3), custom_call_target="tpu_custom_call" | custom-call | tf_op jit(solution)/shard_map/pallas_call | solution.py:371
  3.7 0.8 %slice_select_fusion = f32[5,16,16]{2,1,0:T(8,128)S(1)} fusion(f32[5,16,128]{2,1,0:T(8,128)} %get-tuple-element.13, f32[5,16,128]{2,1,0:T(8,128)} %get-tuple-element.12, pred[]{:T(512)S(6)} %eq.146), kind=kLoop, calls=%fused_computation.123 | loop fusion | flops 1280 | bytes 15361 | tf_op jit(solution)/shard_map/jit(_where)/select_n | solution.py:379
  4.6 0.6 %copy.12 = f32[5,4,4,4,4]{4,3,2,1,0:T(4,128)S(1)} copy(f32[5,4,4,4,4]{3,1,4,2,0:T(4,128)S(1)} %bitcast.78) | data formatting | bytes 10240 | tf_op jit(solution)/shard_map/transpose | solution.py:380
  5.2 0.2 broadcast_in_dim.168
  5.5 0.7 %copy-done.4 = s32[4,256]{1,0:T(4,128)S(1)} copy-done((s32[4,256]{1,0:T(4,128)S(1)}, s32[4,256]{1,0:T(4,128)}, u32[]{:S(2)}) %copy-start.4) | copy-done | bytes 4120
  6.2 0.7 %copy-done.5 = s32[4,256]{1,0:T(4,128)S(1)} copy-done((s32[4,256]{1,0:T(4,128)S(1)}, s32[4,256]{1,0:T(4,128)}, u32[]{:S(2)}) %copy-start.5) | copy-done | bytes 4120
  6.9 0.4 %select_reduce_fusion = f32[4,256]{1,0:T(4,128)S(1)} fusion(f32[128]{0:T(128)S(1)} %copy-done.6, s32[4,256]{1,0:T(4,128)S(1)} %copy-done.5), kind=kLoop, calls=%fused_computation | loop fusion | flops 392192 | bytes 8704 | tf_op jit(solution)/shard_map/reduce_sum | solution.py:383
  7.9 0.2 select_add_fusion
  8.3 0.4 %pad_add_fusion = f32[5,16,48]{2,1,0:T(8,128)S(1)} fusion(f32[5,16,16]{2,1,0:T(8,128)S(1)} %get-tuple-element.62, f32[5,16,16]{2,1,0:T(8,128)S(1)} %get-tuple-element.63, f32[5,16,16]{2,1,0:T(8,128)S(1)} %get-tuple-element.64, f32[5,16,16]{2,1,0:T(8,128)S(1)} %get-tuple-element.65, f32[5,16,16]{2,1,0:T(8,128)S(1)} %get-tuple-element.66, ...), kind=kLoop, calls=%fused_computation.124 | loop fusion | flops 115200 | bytes 174080 | tf_op jit(solution)/shard_map/add | solution.py:398
  9.3 0.6 %copy-done.2 = f32[5,4,128]{2,1,0:T(4,128)S(1)} copy-done((f32[5,4,128]{2,1,0:T(4,128)S(1)}, f32[5,4,128]{2,1,0:T(4,128)}, u32[]{:S(2)}) %copy-start.2) | copy-done | bytes 10264
  9.9 0.8 %select_select_fusion = f32[16,5,4,128]{3,2,1,0:T(4,128)} fusion(f32[16,5,2,128]{3,2,1,0:T(2,128)S(1)} %select_select_fusion.1, f32[5,4,128]{2,1,0:T(4,128)S(1)} %copy-done.3, f32[5,4,128]{2,1,0:T(4,128)S(1)} %copy-done.2, pred[16]{0:T(512)(128)(4,1)S(1)} %get-tuple-element.98, pred[16]{0:T(512)(128)(4,1)S(1)} %get-tuple-element.96, ...), kind=kLoop, calls=%fused_computation.3 | loop fusion | flops 122880 | bytes 266288 | tf_op jit(solution)/shard_map/jit(_where)/select_n | solution.py:415
  10.7 7.5 %all-to-all-start = ((f32[16,5,4,128]{3,2,1,0:T(4,128)}), f32[16,5,4,128]{3,2,1,0:T(4,128)S(1)}, u32[]{:S(2)}, u32[]{:S(2)}) async-start(f32[16,5,4,128]{3,2,1,0:T(4,128)} %select_select_fusion), calls=%async_computation | async-start | bytes 327680 | tf_op jit(solution)/shard_map/all_to_all | solution.py:418
  18.2 1.3 %collective-permute-start = (f32[5,4,4,128]{3,2,1,0:T(4,128)S(1)}, f32[5,4,4,128]{3,2,1,0:T(4,128)S(1)}, u32[]{:S(2)}, u32[]{:S(2)}) collective-permute-start(f32[5,4,4,128]{3,2,1,0:T(4,128)S(1)} %copy-done.8), channel_id=1, source_target_pairs={{8,0},{9,1},{10,2},{11,3},{12,4},{13,5},{14,6},{15,7},{24,16},{25,... | collective-permute-start | bytes 122888 | tf_op jit(solution)/shard_map/ppermute | solution.py:377
  19.5 4.5 %collective-permute-start.1 = (f32[5,4,4,128]{3,2,1,0:T(4,128)S(1)}, f32[5,4,4,128]{3,2,1,0:T(4,128)S(1)}, u32[]{:S(2)}, u32[]{:S(2)}) collective-permute-start(f32[5,4,4,128]{3,2,1,0:T(4,128)S(1)} %copy-done.7), channel_id=1, source_target_pairs={{0,8},{1,9},{2,10},{3,11},{4,12},{5,13},{6,14},{7,15},{16,24},{17,... | collective-permute-start | bytes 122888 | tf_op jit(solution)/shard_map/ppermute | solution.py:378
  24.1 2.2 %all-to-all-done = f32[16,5,4,128]{3,2,1,0:T(4,128)S(1)} async-done(((f32[16,5,4,128]{3,2,1,0:T(4,128)}), f32[16,5,4,128]{3,2,1,0:T(4,128)S(1)}, u32[]{:S(2)}, u32[]{:S(2)}) %all-to-all-start) | async-done | bytes 163872 | tf_op jit(solution)/shard_map/all_to_all | solution.py:418
  26.3 0.6 %dynamic-slice_bitcast_fusion.2 = (f32[5,4,128]{2,1,0:T(4,128)S(1)}, f32[5,4,128]{2,1,0:T(4,128)S(1)}, f32[5,4,128]{2,1,0:T(4,128)S(1)}, f32[5,4,128]{2,1,0:T(4,128)}, f32[5,4,128]{2,1,0:T(4,128)}) fusion(f32[16,5,4,128]{3,2,1,0:T(4,128)S(1)} %all-to-all-done, s32[]{:T(128)S(6)} %select_n.212, s32[]{:T(128)S(6)} %select_n.216, s32[]{:T(128)S(6)} %select_n.214, ...), kind=kLoop, calls=%fused_computation.158 | loop fusion | bytes 102420 | tf_op jit(solution)/shard_map/jit(dynamic_index_in_dim)/squeeze | solution.py:424
  27.2 0.7 %fusion.2 = f32[5,16,16]{2,1,0:T(8,128)S(1)} fusion(f32[5,16,16]{2,1,0:T(8,128)S(1)} %reshape.144, f32[5,16,16]{2,1,0:T(8,128)S(1)} %reshape.143, f32[5,16,16]{2,1,0:T(8,128)S(1)} %reshape.142, f32[16,16]{1,0:T(8,128)S(1)} %get-tuple-element.23, f32[16,16]{1,0:T(8,128)S(1)} %get-tuple-element.24, f32[16,16]{1,0:T(8,128)S(1)} %get-tuple-element.25, ...), kind=kLoop, calls=%fused_computation.8 | loop fusion | flops 116480 | bytes 52225 | tf_op jit(solution)/shard_map/jit(_where)/select_n | solution.py:437
  28.0 0.6 %copy.15 = f32[5,4,4,4,4]{4,3,2,1,0:T(4,128)S(1)} copy(f32[5,4,4,4,4]{2,4,1,3,0:T(4,128)S(1)} %bitcast.79) | data formatting | bytes 10240 | tf_op jit(solution)/shard_map/transpose | solution.py:433
  28.8 0.2 select_n.218
  29.0 0.6 %copy.14 = f32[5,4,4,4,4]{4,3,2,1,0:T(4,128)S(1)} copy(f32[5,4,4,4,4]{2,4,1,3,0:T(4,128)S(1)} %bitcast.80) | data formatting | bytes 10240 | tf_op jit(solution)/shard_map/transpose | solution.py:433
  29.7 0.6 %pad.168.inner_ref = f32[5,16,128]{2,1,0:T(8,128)} pad(f32[5,16,16]{2,1,0:T(8,128)S(1)} %reshape.146, f32[]{:T(128)} %constant.113.clone.1), padding=0_0x0_0x0_112 | pad | bytes 46084 | tf_op jit(solution)/shard_map/jit(_pad)/pad | solution.py:434
  30.4 0.6 %pad.167.outer_ref = f32[5,16,128]{2,1,0:T(8,128)} pad(f32[5,16,16]{2,1,0:T(8,128)S(1)} %reshape.141, f32[]{:T(128)} %constant.113.clone.1), padding=0_0x0_0x0_112 | pad | bytes 46084 | tf_op jit(solution)/shard_map/jit(_pad)/pad | solution.py:434
  31.0 0.6 %copy-done = f32[5,4,4,128]{3,2,1,0:T(4,128)} copy-done((f32[5,4,4,128]{3,2,1,0:T(4,128)}, f32[5,4,4,128]{3,2,1,0:T(4,128)S(1)}, u32[]{:S(2)}) %copy-start) | copy-done | bytes 40984
  31.6 3.2 %shard_map.78 = (f32[1,5,4,4,4,128]{5,4,3,2,1,0:T(4,128)}, f32[1,5,4,4,4,128]{5,4,3,2,1,0:T(4,128)}) custom-call(f32[1,5,4,4,4,128]{5,4,3,2,1,0:T(4,128)} %adj_ref.3, bf16[1,5,4,4,4,128]{5,4,3,2,1,0:T(4,128)(2,1)} %flow_ref.1, f32[5,4,4,128]{3,2,1,0:T(4,128)} %copy-done, f32[5,4,4,128]{3,2,1,0:T(4,128)} %copy-done.1, ...), custom_call_target="tpu_custom_call" | custom-call | tf_op jit(solution)/shard_map/pallas_call | solution.py:439
  (49 shorter events, 2.3 us)
Async XLA Ops:
  5.5 0.7 %copy-start.4 = (s32[4,256]{1,0:T(4,128)S(1)}, s32[4,256]{1,0:T(4,128)}, u32[]{:S(2)}) copy-start(s32[4,256]{1,0:T(4,128)} %param.8) | copy-start | bytes 12292
  6.2 0.7 %copy-start.5 = (s32[4,256]{1,0:T(4,128)S(1)}, s32[4,256]{1,0:T(4,128)}, u32[]{:S(2)}) copy-start(s32[4,256]{1,0:T(4,128)} %param.9) | copy-start | bytes 12292
  6.2 0.7 %copy-start.6 = (f32[128]{0:T(128)S(1)}, f32[128]{0:T(128)}, u32[]{:S(2)}) copy-start(f32[128]{0:T(128)} %param.10) | copy-start | bytes 1540
  9.2 0.7 %copy-start.2 = (f32[5,4,128]{2,1,0:T(4,128)S(1)}, f32[5,4,128]{2,1,0:T(4,128)}, u32[]{:S(2)}) copy-start(f32[5,4,128]{2,1,0:T(4,128)} %get-tuple-element.10) | copy-start | bytes 30724
  9.2 0.7 %copy-start.3 = (f32[5,4,128]{2,1,0:T(4,128)S(1)}, f32[5,4,128]{2,1,0:T(4,128)}, u32[]{:S(2)}) copy-start(f32[5,4,128]{2,1,0:T(4,128)} %get-tuple-element.11) | copy-start | bytes 30724
  10.7 7.5 %copy-start.8 = (f32[5,4,4,128]{3,2,1,0:T(4,128)S(1)}, f32[5,4,4,128]{3,2,1,0:T(4,128)}, u32[]{:S(2)}) copy-start(f32[5,4,4,128]{3,2,1,0:T(4,128)} %get-tuple-element.8) | copy-start | bytes 122884
  10.7 8.8 %copy-start.7 = (f32[5,4,4,128]{3,2,1,0:T(4,128)S(1)}, f32[5,4,4,128]{3,2,1,0:T(4,128)}, u32[]{:S(2)}) copy-start(f32[5,4,4,128]{3,2,1,0:T(4,128)} %get-tuple-element.9) | copy-start | bytes 122884
  10.7 15.6 %all-to-all-start = ((f32[16,5,4,128]{3,2,1,0:T(4,128)}), f32[16,5,4,128]{3,2,1,0:T(4,128)S(1)}, u32[]{:S(2)}, u32[]{:S(2)}) async-start(f32[16,5,4,128]{3,2,1,0:T(4,128)} %select_select_fusion), calls=%async_computation | async-start | bytes 327680 | tf_op jit(solution)/shard_map/all_to_all | solution.py:418
  18.2 12.8 %collective-permute-start = (f32[5,4,4,128]{3,2,1,0:T(4,128)S(1)}, f32[5,4,4,128]{3,2,1,0:T(4,128)S(1)}, u32[]{:S(2)}, u32[]{:S(2)}) collective-permute-start(f32[5,4,4,128]{3,2,1,0:T(4,128)S(1)} %copy-done.8), channel_id=1, source_target_pairs={{8,0},{9,1},{10,2},{11,3},{12,4},{13,5},{14,6},{15,7},{24,16},{25,... | collective-permute-start | bytes 122888 | tf_op jit(solution)/shard_map/ppermute | solution.py:377
  19.5 11.5 %collective-permute-start.1 = (f32[5,4,4,128]{3,2,1,0:T(4,128)S(1)}, f32[5,4,4,128]{3,2,1,0:T(4,128)S(1)}, u32[]{:S(2)}, u32[]{:S(2)}) collective-permute-start(f32[5,4,4,128]{3,2,1,0:T(4,128)S(1)} %copy-done.7), channel_id=1, source_target_pairs={{0,8},{1,9},{2,10},{3,11},{4,12},{5,13},{6,14},{7,15},{16,24},{17,... | collective-permute-start | bytes 122888 | tf_op jit(solution)/shard_map/ppermute | solution.py:378
  31.0 0.6 %copy-start = (f32[5,4,4,128]{3,2,1,0:T(4,128)}, f32[5,4,4,128]{3,2,1,0:T(4,128)S(1)}, u32[]{:S(2)}) copy-start(f32[5,4,4,128]{3,2,1,0:T(4,128)S(1)} %collective-permute-done.up_ax_ref) | copy-start | bytes 122884
  31.0 0.6 %copy-start.1 = (f32[5,4,4,128]{3,2,1,0:T(4,128)}, f32[5,4,4,128]{3,2,1,0:T(4,128)S(1)}, u32[]{:S(2)}) copy-start(f32[5,4,4,128]{3,2,1,0:T(4,128)S(1)} %collective-permute-done.1.down_ax_ref) | copy-start | bytes 122884

commit v9 on v8

--- a/solution.py
+++ b/solution.py
@@ -252,7 +252,7 @@
 
 
 def rate_kernel(
-    adj_ref, flow_ref, up_ax_ref, down_ax_ref, up_az_ref, down_az_ref, outer_ref, inner_ref,
+    adj_ref, flow_ref, up_ax_ref, down_ax_ref, up_az_ref, down_az_ref, sides_ref,
     rate_ref, next_ref,
 ):
     derivs, left_vals, right_vals, left_corr, right_corr = basis_tables()
@@ -262,31 +262,32 @@
     az_flat = flat_lane // ER % ET
     radial_lane = lane % ER
     brackets = [[None] * 5 for _ in range(3)]
-    spread = selector(128, 128, lambda k: k // (ET * ER) * ET + k // ER % ET, True)
+    col = lax.broadcasted_iota(jnp.int32, (16, 128), 1)
+    row = lax.broadcasted_iota(jnp.int32, (16, 128), 0)
+    sides = sides_ref[...]
+    spread = [
+        exact_dot(sides, jnp.where(row == col // ER % ET * 4 + azim, 1.0, 0.0)) for azim in range(4)
+    ]
+    group = lax.broadcasted_iota(jnp.int32, (1, 128), 1) // (ET * ER)
+
+    def side_face(side, chan):
+        blocks = []
+        for axial in range(4):
+            slabs = []
+            for azim in range(4):
+                base = (side * 5 + chan) * 16 + axial
+                value = spread[azim][base : base + 1]
+                for elem in range(1, EA):
+                    pos = base + elem * 4
+                    value = jnp.where(group == elem, spread[azim][pos : pos + 1], value)
+                slabs.append(jnp.broadcast_to(value, (4, 128)))
+            blocks.append(jnp.stack(slabs, axis=0))
+        return jnp.stack(blocks, axis=0)
+
     for chan in range(5):
         field = adj_ref[0, chan]
-        outer_lanes = exact_dot(outer_ref[chan], spread)
-        inner_lanes = exact_dot(inner_ref[chan], spread)
-        outer_face = jnp.stack(
-            [
-                jnp.stack(
-                    [jnp.broadcast_to(outer_lanes[axial * 4 + azim : axial * 4 + azim + 1], (4, 128)) for azim in range(4)],
-                    axis=0,
-                )
-                for axial in range(4)
-            ],
-            axis=0,
-        )
-        inner_face = jnp.stack(
-            [
-                jnp.stack(
-                    [jnp.broadcast_to(inner_lanes[axial * 4 + azim : axial * 4 + azim + 1], (4, 128)) for azim in range(4)],
-                    axis=0,
-                )
-                for axial in range(4)
-            ],
-            axis=0,
-        )
+        outer_face = side_face(0, chan)
+        inner_face = side_face(1, chan)
         up_az = expand_face(up_az_ref[chan], 0)
         down_az = expand_face(down_az_ref[chan], ET - 1)
         left0 = sweep(field, left_corr, lambda i: (i,))
@@ -429,16 +430,13 @@
     returned = picked[0] + picked[1] + picked[2]
     window = jnp.concatenate(picked, axis=2)
     incoming = shift_sum(window, coefs, TP)
-    def to_lanes(rows_vals):
-        face = rows_vals.reshape(5, EA, 4, ET, 4).transpose(0, 2, 4, 1, 3).reshape(5, 16, EA * ET)
-        return jnp.pad(face, ((0, 0), (0, 0), (0, 128 - EA * ET)))
-
-    outer = to_lanes(jnp.where(is_rotor, returned, 0.0))
-    inner = to_lanes(jnp.where(is_rotor, 0.0, incoming))
+    sides = jnp.concatenate(
+        [jnp.where(is_rotor, returned, 0.0), jnp.where(is_rotor, 0.0, incoming)], axis=0
+    ).reshape(10 * AP, TP)
     field_shape = jax.ShapeDtypeStruct(adjoint.shape, jnp.float32)
     adjoint_rate, next_adjoint = pl.pallas_call(
         rate_kernel, out_shape=(field_shape, field_shape)
-    )(adjoint, flow_prim, up_ax, down_ax, up_az, down_az, outer, inner)
+    )(adjoint, flow_prim, up_ax, down_ax, up_az, down_az, sides)
     return (adjoint_rate, next_adjoint)
 
 

time: 35.3 us -> 32.9 us (0.932)
  local copies, waits for them, and re-layouts: 8.5 us -> 5.46 us
  other arithmetic: 3.61 us -> 4.25 us
    pad x2 -> x0, local copies, waits for them, and re-layouts: 1.23 us -> none  [to_lanes(): return jnp.pad(face, ((0, 0), (0, 0), (0, 128 - EA * ET)))]
    transpose x2 -> x0, local copies, waits for them, and re-layouts: 1.18 us -> none  [to_lanes(): rows_vals.reshape(5, EA, 4, ET, 4).transpose(0, 2, 4, 1, 3)]
    concatenate x0 -> x1, other arithmetic: none -> 0.63 us  [local(): jnp.concatenate([jnp.where(is_rotor, returned, 0.0), jnp.where(is_rotor,...]
    reshape x3 -> x0, local copies, waits for them, and re-layouts: 0.41 us -> none  [to_lanes(): rows_vals.reshape(5, EA, 4, ET, 4).transpose(0, 2, 4, 1, 3)]
    select_n x1 -> x2, other arithmetic: 0.7 us -> 0.71 us  [the longest x1 0.7 us: local(): jnp.where(is_rotor, 0.0, incoming)]
  transfers between devices with their start and end apart: 3 -> 3, of which waited for: 1 -> 1; matrix products, arithmetic and copies ran while one was open for 13% -> 7% of each run, Pallas kernels for 0% -> 0%
where the time goes in v9:
time: 32.9 us; the launch traced here: 32.4 us
  starting transfers between devices  13.3 us (40%)
  Pallas kernels  5.54 us (17%)
  local copies, waits for them, and re-layouts  5.46 us (17%)
  other arithmetic  4.25 us (13%)
  waiting for transfers between devices  2.17 us (7%)
  between operations  1.69 us (5%)
    all_to_all x1, starting transfers between devices, local(): got = lax.all_to_all(chunks, ('zone', 'azim'), 0, 0)  7.49 us
    ppermute x1, starting transfers between devices, local(): lax.ppermute(right_ax, 'axial', [(i, i + 1) for i in range(n_axial - 1)])  4.55 us
    pallas_call x1, Pallas kernels, local(): pl.pallas_call(rate_kernel, out_shape=(field_shape, field_shape))  3.27 us
    unnamed x18, local copies, waits for them, and re-layouts  2.53 us
    pallas_call x1, Pallas kernels, local(): pl.pallas_call(moment_kernel, out_shape=(face4, face4, chunk, chunk, rows...  2.27 us
    all_to_all x1, waiting for transfers between devices, local(): got = lax.all_to_all(chunks, ('zone', 'azim'), 0, 0)  2.16 us
    ppermute x1, starting transfers between devices, local(): lax.ppermute(left_ax, 'axial', [(i + 1, i) for i in range(n_axial - 1)])  1.29 us
    select_n x1, other arithmetic, local(): own_face = jnp.where(is_rotor, outer_moment, inner_moment)[:, :, :EA * ET]  0.81 us
  transfers between devices with their start and end apart: 3, of which 1 were waited for; matrix products, arithmetic and copies ran while one was open for 7% of the time, Pallas kernels for 0%

profile of v9, /device:TPU:0, one launch (start us, length us, event | category | flops | bytes accessed | tf_op | source)
XLA Modules:
  0.0 32.4 jit_solution(1650326893872365877)
XLA Ops:
  1.4 2.3 %shard_map.77 = (f32[5,4,4,128]{3,2,1,0:T(4,128)}, f32[5,4,4,128]{3,2,1,0:T(4,128)}, f32[5,4,128]{2,1,0:T(4,128)}, f32[5,4,128]{2,1,0:T(4,128)}, f32[5,16,128]{2,1,0:T(8,128)}, /*index=5*/f32[5,16,128]{2,1,0:T(8,128)}) custom-call(f32[1,5,4,4,4,128]{5,4,3,2,1,0:T(4,128)} %adj_ref.3), custom_call_target="tpu_custom_call" | custom-call | tf_op jit(solution)/shard_map/pallas_call | solution.py:372
  3.7 0.8 %slice_select_fusion = f32[5,16,16]{2,1,0:T(8,128)S(1)} fusion(f32[5,16,128]{2,1,0:T(8,128)} %get-tuple-element.13, f32[5,16,128]{2,1,0:T(8,128)} %get-tuple-element.12, pred[]{:T(512)S(6)} %eq.146), kind=kLoop, calls=%fused_computation.124 | loop fusion | flops 1280 | bytes 15361 | tf_op jit(solution)/shard_map/jit(_where)/select_n | solution.py:380
  4.5 0.1 reshape.124
  4.6 0.6 %copy.11 = f32[5,4,4,4,4]{4,3,2,1,0:T(4,128)S(1)} copy(f32[5,4,4,4,4]{3,1,4,2,0:T(4,128)S(1)} %bitcast.77) | data formatting | bytes 10240 | tf_op jit(solution)/shard_map/transpose | solution.py:381
  5.2 0.2 broadcast_in_dim.166
  5.4 0.1 reshape.125
  5.5 0.7 %copy-done.4 = s32[4,256]{1,0:T(4,128)S(1)} copy-done((s32[4,256]{1,0:T(4,128)S(1)}, s32[4,256]{1,0:T(4,128)}, u32[]{:S(2)}) %copy-start.4) | copy-done | bytes 4120
  6.2 0.7 %copy-done.5 = s32[4,256]{1,0:T(4,128)S(1)} copy-done((s32[4,256]{1,0:T(4,128)S(1)}, s32[4,256]{1,0:T(4,128)}, u32[]{:S(2)}) %copy-start.5) | copy-done | bytes 4120
  6.9 0.4 %select_reduce_fusion = f32[4,256]{1,0:T(4,128)S(1)} fusion(f32[128]{0:T(128)S(1)} %copy-done.6, s32[4,256]{1,0:T(4,128)S(1)} %copy-done.5), kind=kLoop, calls=%fused_computation | loop fusion | flops 392192 | bytes 8704 | tf_op jit(solution)/shard_map/reduce_sum | solution.py:384
  7.9 0.2 select_add_fusion
  8.3 0.4 %pad_add_fusion = f32[5,16,48]{2,1,0:T(8,128)S(1)} fusion(f32[5,16,16]{2,1,0:T(8,128)S(1)} %get-tuple-element.62, f32[5,16,16]{2,1,0:T(8,128)S(1)} %get-tuple-element.63, f32[5,16,16]{2,1,0:T(8,128)S(1)} %get-tuple-element.64, f32[5,16,16]{2,1,0:T(8,128)S(1)} %get-tuple-element.65, f32[5,16,16]{2,1,0:T(8,128)S(1)} %get-tuple-element.66, ...), kind=kLoop, calls=%fused_computation.126 | loop fusion | flops 115200 | bytes 174080 | tf_op jit(solution)/shard_map/add | solution.py:399
  8.8 0.1 broadcast_in_dim.180
  9.2 0.1 select_select_fusion.1
  9.3 0.6 %copy-done.2 = f32[5,4,128]{2,1,0:T(4,128)S(1)} copy-done((f32[5,4,128]{2,1,0:T(4,128)S(1)}, f32[5,4,128]{2,1,0:T(4,128)}, u32[]{:S(2)}) %copy-start.2) | copy-done | bytes 10264
  9.9 0.8 %select_select_fusion = f32[16,5,4,128]{3,2,1,0:T(4,128)} fusion(f32[16,5,2,128]{3,2,1,0:T(2,128)S(1)} %select_select_fusion.1, f32[5,4,128]{2,1,0:T(4,128)S(1)} %copy-done.3, f32[5,4,128]{2,1,0:T(4,128)S(1)} %copy-done.2, pred[16]{0:T(512)(128)(4,1)S(1)} %get-tuple-element.94, pred[16]{0:T(512)(128)(4,1)S(1)} %get-tuple-element.92, ...), kind=kLoop, calls=%fused_computation.3 | loop fusion | flops 122880 | bytes 266288 | tf_op jit(solution)/shard_map/jit(_where)/select_n | solution.py:416
  10.7 7.5 %all-to-all-start = ((f32[16,5,4,128]{3,2,1,0:T(4,128)}), f32[16,5,4,128]{3,2,1,0:T(4,128)S(1)}, u32[]{:S(2)}, u32[]{:S(2)}) async-start(f32[16,5,4,128]{3,2,1,0:T(4,128)} %select_select_fusion), calls=%async_computation | async-start | bytes 327680 | tf_op jit(solution)/shard_map/all_to_all | solution.py:419
  18.2 1.3 %collective-permute-start = (f32[5,4,4,128]{3,2,1,0:T(4,128)S(1)}, f32[5,4,4,128]{3,2,1,0:T(4,128)S(1)}, u32[]{:S(2)}, u32[]{:S(2)}) collective-permute-start(f32[5,4,4,128]{3,2,1,0:T(4,128)S(1)} %copy-done.8), channel_id=1, source_target_pairs={{8,0},{9,1},{10,2},{11,3},{12,4},{13,5},{14,6},{15,7},{24,16},{25,... | collective-permute-start | bytes 122888 | tf_op jit(solution)/shard_map/ppermute | solution.py:378
  19.5 4.5 %collective-permute-start.1 = (f32[5,4,4,128]{3,2,1,0:T(4,128)S(1)}, f32[5,4,4,128]{3,2,1,0:T(4,128)S(1)}, u32[]{:S(2)}, u32[]{:S(2)}) collective-permute-start(f32[5,4,4,128]{3,2,1,0:T(4,128)S(1)} %copy-done.7), channel_id=1, source_target_pairs={{0,8},{1,9},{2,10},{3,11},{4,12},{5,13},{6,14},{7,15},{16,24},{17,... | collective-permute-start | bytes 122888 | tf_op jit(solution)/shard_map/ppermute | solution.py:379
  24.1 2.2 %all-to-all-done = f32[16,5,4,128]{3,2,1,0:T(4,128)S(1)} async-done(((f32[16,5,4,128]{3,2,1,0:T(4,128)}), f32[16,5,4,128]{3,2,1,0:T(4,128)S(1)}, u32[]{:S(2)}, u32[]{:S(2)}) %all-to-all-start) | async-done | bytes 163872 | tf_op jit(solution)/shard_map/all_to_all | solution.py:419
  26.3 0.6 %dynamic-slice_bitcast_fusion.2 = (f32[5,4,128]{2,1,0:T(4,128)S(1)}, f32[5,4,128]{2,1,0:T(4,128)S(1)}, f32[5,4,128]{2,1,0:T(4,128)S(1)}, f32[5,4,128]{2,1,0:T(4,128)}, f32[5,4,128]{2,1,0:T(4,128)}) fusion(f32[16,5,4,128]{3,2,1,0:T(4,128)S(1)} %all-to-all-done, s32[]{:T(128)S(6)} %select_n.206, s32[]{:T(128)S(6)} %select_n.210, s32[]{:T(128)S(6)} %select_n.208, ...), kind=kLoop, calls=%fused_computation.160 | loop fusion | bytes 102420 | tf_op jit(solution)/shard_map/jit(dynamic_index_in_dim)/squeeze | solution.py:425
  27.2 0.7 %fusion.2 = f32[5,16,16]{2,1,0:T(8,128)S(1)} fusion(f32[5,16,16]{2,1,0:T(8,128)S(1)} %reshape.128, f32[5,16,16]{2,1,0:T(8,128)S(1)} %reshape.127, f32[5,16,16]{2,1,0:T(8,128)S(1)} %reshape.126, f32[16,16]{1,0:T(8,128)S(1)} %get-tuple-element.23, f32[16,16]{1,0:T(8,128)S(1)} %get-tuple-element.24, f32[16,16]{1,0:T(8,128)S(1)} %get-tuple-element.25, ...), kind=kLoop, calls=%fused_computation.9 | loop fusion | flops 116480 | bytes 52225 | tf_op jit(solution)/shard_map/jit(_where)/select_n | solution.py:434
  27.9 0.6 %pad_maximum_fusion = f32[10,16,16]{2,1,0:T(8,128)} fusion(f32[5,16,16]{2,1,0:T(8,128)S(1)} %fusion.2, f32[5,16,16]{2,1,0:T(8,128)S(1)} %add_select_fusion), kind=kLoop, calls=%fused_computation.4 | loop fusion | flops 2560 | bytes 20480 | tf_op jit(solution)/shard_map/concatenate | solution.py:433
  28.6 0.6 %copy-done = f32[5,4,4,128]{3,2,1,0:T(4,128)} copy-done((f32[5,4,4,128]{3,2,1,0:T(4,128)}, f32[5,4,4,128]{3,2,1,0:T(4,128)S(1)}, u32[]{:S(2)}) %copy-start) | copy-done | bytes 40984
  29.2 3.3 %shard_map.78 = (f32[1,5,4,4,4,128]{5,4,3,2,1,0:T(4,128)}, f32[1,5,4,4,4,128]{5,4,3,2,1,0:T(4,128)}) custom-call(f32[1,5,4,4,4,128]{5,4,3,2,1,0:T(4,128)} %adj_ref.3, bf16[1,5,4,4,4,128]{5,4,3,2,1,0:T(4,128)(2,1)} %flow_ref.1, f32[5,4,4,128]{3,2,1,0:T(4,128)} %copy-done, f32[5,4,4,128]{3,2,1,0:T(4,128)} %copy-done.1, ...), custom_call_target="tpu_custom_call" | custom-call | tf_op jit(solution)/shard_map/pallas_call | solution.py:437
  (45 shorter events, 1.5 us)
Async XLA Ops:
  5.5 0.7 %copy-start.4 = (s32[4,256]{1,0:T(4,128)S(1)}, s32[4,256]{1,0:T(4,128)}, u32[]{:S(2)}) copy-start(s32[4,256]{1,0:T(4,128)} %param.8) | copy-start | bytes 12292
  6.2 0.7 %copy-start.5 = (s32[4,256]{1,0:T(4,128)S(1)}, s32[4,256]{1,0:T(4,128)}, u32[]{:S(2)}) copy-start(s32[4,256]{1,0:T(4,128)} %param.9) | copy-start | bytes 12292
  6.2 0.7 %copy-start.6 = (f32[128]{0:T(128)S(1)}, f32[128]{0:T(128)}, u32[]{:S(2)}) copy-start(f32[128]{0:T(128)} %param.10) | copy-start | bytes 1540
  9.2 0.7 %copy-start.2 = (f32[5,4,128]{2,1,0:T(4,128)S(1)}, f32[5,4,128]{2,1,0:T(4,128)}, u32[]{:S(2)}) copy-start(f32[5,4,128]{2,1,0:T(4,128)} %get-tuple-element.10) | copy-start | bytes 30724
  9.2 0.7 %copy-start.3 = (f32[5,4,128]{2,1,0:T(4,128)S(1)}, f32[5,4,128]{2,1,0:T(4,128)}, u32[]{:S(2)}) copy-start(f32[5,4,128]{2,1,0:T(4,128)} %get-tuple-element.11) | copy-start | bytes 30724
  10.7 7.5 %copy-start.8 = (f32[5,4,4,128]{3,2,1,0:T(4,128)S(1)}, f32[5,4,4,128]{3,2,1,0:T(4,128)}, u32[]{:S(2)}) copy-start(f32[5,4,4,128]{3,2,1,0:T(4,128)} %get-tuple-element.8) | copy-start | bytes 122884
  10.7 8.8 %copy-start.7 = (f32[5,4,4,128]{3,2,1,0:T(4,128)S(1)}, f32[5,4,4,128]{3,2,1,0:T(4,128)}, u32[]{:S(2)}) copy-start(f32[5,4,4,128]{3,2,1,0:T(4,128)} %get-tuple-element.9) | copy-start | bytes 122884
  10.7 15.6 %all-to-all-start = ((f32[16,5,4,128]{3,2,1,0:T(4,128)}), f32[16,5,4,128]{3,2,1,0:T(4,128)S(1)}, u32[]{:S(2)}, u32[]{:S(2)}) async-start(f32[16,5,4,128]{3,2,1,0:T(4,128)} %select_select_fusion), calls=%async_computation | async-start | bytes 327680 | tf_op jit(solution)/shard_map/all_to_all | solution.py:419
  18.2 10.4 %collective-permute-start = (f32[5,4,4,128]{3,2,1,0:T(4,128)S(1)}, f32[5,4,4,128]{3,2,1,0:T(4,128)S(1)}, u32[]{:S(2)}, u32[]{:S(2)}) collective-permute-start(f32[5,4,4,128]{3,2,1,0:T(4,128)S(1)} %copy-done.8), channel_id=1, source_target_pairs={{8,0},{9,1},{10,2},{11,3},{12,4},{13,5},{14,6},{15,7},{24,16},{25,... | collective-permute-start | bytes 122888 | tf_op jit(solution)/shard_map/ppermute | solution.py:378
  19.5 9.1 %collective-permute-start.1 = (f32[5,4,4,128]{3,2,1,0:T(4,128)S(1)}, f32[5,4,4,128]{3,2,1,0:T(4,128)S(1)}, u32[]{:S(2)}, u32[]{:S(2)}) collective-permute-start(f32[5,4,4,128]{3,2,1,0:T(4,128)S(1)} %copy-done.7), channel_id=1, source_target_pairs={{0,8},{1,9},{2,10},{3,11},{4,12},{5,13},{6,14},{7,15},{16,24},{17,... | collective-permute-start | bytes 122888 | tf_op jit(solution)/shard_map/ppermute | solution.py:379
  28.5 0.6 %copy-start = (f32[5,4,4,128]{3,2,1,0:T(4,128)}, f32[5,4,4,128]{3,2,1,0:T(4,128)S(1)}, u32[]{:S(2)}) copy-start(f32[5,4,4,128]{3,2,1,0:T(4,128)S(1)} %collective-permute-done.up_ax_ref) | copy-start | bytes 122884
  28.6 0.6 %copy-start.1 = (f32[5,4,4,128]{3,2,1,0:T(4,128)}, f32[5,4,4,128]{3,2,1,0:T(4,128)S(1)}, u32[]{:S(2)}) copy-start(f32[5,4,4,128]{3,2,1,0:T(4,128)S(1)} %collective-permute-done.1.down_ax_ref) | copy-start | bytes 122884

commit v10 on v9

--- a/solution.py
+++ b/solution.py
@@ -375,8 +375,16 @@
         scratch_shapes=[pltpu.VMEM((2, 16, 128), jnp.float32)],
     )(adjoint)
     is_rotor = lax.axis_index("zone") == 0
-    up_ax = lax.ppermute(left_ax, "axial", [(i + 1, i) for i in range(n_axial - 1)])
-    down_ax = lax.ppermute(right_ax, "axial", [(i, i + 1) for i in range(n_axial - 1)])
+    even = lax.axis_index("axial") % 2 == 0
+    first = [(i, i + 1) for i in range(0, n_axial - 1, 2)] + [(i, i - 1) for i in range(1, n_axial, 2)]
+    second = [(i, i + 1) for i in range(1, n_axial - 1, 2)] + [(i, i - 1) for i in range(2, n_axial, 2)]
+    got_first = lax.ppermute(jnp.where(even, right_ax, left_ax), "axial", first)
+    if second:
+        got_second = lax.ppermute(jnp.where(even, left_ax, right_ax), "axial", second)
+    else:
+        got_second = jnp.zeros_like(got_first)
+    up_ax = jnp.where(even, got_first, got_second)
+    down_ax = jnp.where(even, got_second, got_first)
     own_face = jnp.where(is_rotor, outer_moment, inner_moment)[:, :, : EA * ET]
     own_rows = own_face.reshape(5, 4, 4, EA, ET).transpose(0, 3, 1, 4, 2).reshape(5, AP, TP)
     shifts_local = intersection_shift.reshape(INTERSECTIONS, AP, TP)

time: 32.9 us -> 32.3 us (0.982)
  starting transfers between devices: 13.3 us -> 9.07 us
  waiting for transfers between devices: 2.17 us -> 5.87 us
  other arithmetic: 4.25 us -> 4.89 us
  local copies, waits for them, and re-layouts: 5.46 us -> 4.86 us
    ppermute x2 -> x1, starting transfers between devices: 5.84 us -> 1.58 us  [local(): got_first = lax.ppermute(jnp.where(even, right_ax, left_ax), 'axial', first)]
    ppermute x2 -> x1, waiting for transfers between devices: 0.01 us -> 2.48 us  [local(): got_first = lax.ppermute(jnp.where(even, right_ax, left_ax), 'axial', first)]
    all_to_all x1, waiting for transfers between devices: 2.16 us -> 3.38 us  [local(): got = lax.all_to_all(chunks, ('zone', 'azim'), 0, 0)]
    select_n x0 -> x2, other arithmetic: none -> 0.64 us  [the longest x1 0.64 us: local(): down_ax = jnp.where(even, got_second, got_first)]
    unnamed x18 -> x14, local copies, waits for them, and re-layouts: 2.53 us -> 1.92 us
  transfers between devices with their start and end apart: 3 -> 2, of which waited for: 1 -> 2; matrix products, arithmetic and copies ran while one was open for 7% -> 2% of each run, Pallas kernels for 0% -> 0%
where the time goes in v10:
time: 32.3 us; the launch traced here: 31.8 us
  starting transfers between devices  9.07 us (28%)
  waiting for transfers between devices  5.87 us (18%)
  Pallas kernels  5.54 us (17%)
  other arithmetic  4.89 us (15%)
  local copies, waits for them, and re-layouts  4.86 us (15%)
  between operations  1.59 us (5%)
    all_to_all x1, starting transfers between devices, local(): got = lax.all_to_all(chunks, ('zone', 'azim'), 0, 0)  7.49 us
    all_to_all x1, waiting for transfers between devices, local(): got = lax.all_to_all(chunks, ('zone', 'azim'), 0, 0)  3.38 us
    pallas_call x1, Pallas kernels, local(): pl.pallas_call(rate_kernel, out_shape=(field_shape, field_shape))  3.27 us
    ppermute x1, waiting for transfers between devices, local(): got_first = lax.ppermute(jnp.where(even, right_ax, left_ax), 'axial', first)  2.48 us
    pallas_call x1, Pallas kernels, local(): pl.pallas_call(moment_kernel, out_shape=(face4, face4, chunk, chunk, rows...  2.27 us
    unnamed x14, local copies, waits for them, and re-layouts  1.92 us
    ppermute x1, starting transfers between devices, local(): got_first = lax.ppermute(jnp.where(even, right_ax, left_ax), 'axial', first)  1.58 us
    select_n x1, other arithmetic, local(): own_face = jnp.where(is_rotor, outer_moment, inner_moment)[:, :, :EA * ET]  0.81 us
  transfers between devices with their start and end apart: 2, of which 2 were waited for; matrix products, arithmetic and copies ran while one was open for 2% of the time, Pallas kernels for 0%

profile of v10, /device:TPU:0, one launch (start us, length us, event | category | flops | bytes accessed | tf_op | source)
XLA Modules:
  0.0 31.8 jit_solution(16846467364632705601)
XLA Ops:
  1.4 2.3 %shard_map.77 = (f32[5,4,4,128]{3,2,1,0:T(4,128)}, f32[5,4,4,128]{3,2,1,0:T(4,128)}, f32[5,4,128]{2,1,0:T(4,128)}, f32[5,4,128]{2,1,0:T(4,128)}, f32[5,16,128]{2,1,0:T(8,128)}, /*index=5*/f32[5,16,128]{2,1,0:T(8,128)}) custom-call(f32[1,5,4,4,4,128]{5,4,3,2,1,0:T(4,128)} %adj_ref.3), custom_call_target="tpu_custom_call" | custom-call | tf_op jit(solution)/shard_map/pallas_call | solution.py:372
  3.7 0.8 %slice_select_fusion = f32[5,16,16]{2,1,0:T(8,128)S(1)} fusion(f32[5,16,128]{2,1,0:T(8,128)} %get-tuple-element.13, f32[5,16,128]{2,1,0:T(8,128)} %get-tuple-element.12, pred[]{:T(512)S(6)} %eq.151), kind=kLoop, calls=%fused_computation.124 | loop fusion | flops 1280 | bytes 15361 | tf_op jit(solution)/shard_map/jit(_where)/select_n | solution.py:388
  4.5 0.1 reshape.124
  4.6 0.6 %copy.11 = f32[5,4,4,4,4]{4,3,2,1,0:T(4,128)S(1)} copy(f32[5,4,4,4,4]{3,1,4,2,0:T(4,128)S(1)} %bitcast.80) | data formatting | bytes 10240 | tf_op jit(solution)/shard_map/transpose | solution.py:389
  5.2 0.2 broadcast_in_dim.170
  5.4 0.1 reshape.125
  5.5 0.7 %copy-done.4 = s32[4,256]{1,0:T(4,128)S(1)} copy-done((s32[4,256]{1,0:T(4,128)S(1)}, s32[4,256]{1,0:T(4,128)}, u32[]{:S(2)}) %copy-start.4) | copy-done | bytes 4120
  6.2 0.7 %copy-done.5 = s32[4,256]{1,0:T(4,128)S(1)} copy-done((s32[4,256]{1,0:T(4,128)S(1)}, s32[4,256]{1,0:T(4,128)}, u32[]{:S(2)}) %copy-start.5) | copy-done | bytes 4120
  6.9 0.4 %select_reduce_fusion = f32[4,256]{1,0:T(4,128)S(1)} fusion(f32[128]{0:T(128)S(1)} %copy-done.6, s32[4,256]{1,0:T(4,128)S(1)} %copy-done.5), kind=kLoop, calls=%fused_computation | loop fusion | flops 392192 | bytes 8704 | tf_op jit(solution)/shard_map/reduce_sum | solution.py:392
  7.9 0.2 select_add_fusion
  8.3 0.4 %pad_add_fusion = f32[5,16,48]{2,1,0:T(8,128)S(1)} fusion(f32[5,16,16]{2,1,0:T(8,128)S(1)} %get-tuple-element.62, f32[5,16,16]{2,1,0:T(8,128)S(1)} %get-tuple-element.63, f32[5,16,16]{2,1,0:T(8,128)S(1)} %get-tuple-element.64, f32[5,16,16]{2,1,0:T(8,128)S(1)} %get-tuple-element.65, f32[5,16,16]{2,1,0:T(8,128)S(1)} %get-tuple-element.66, ...), kind=kLoop, calls=%fused_computation.126 | loop fusion | flops 115200 | bytes 174080 | tf_op jit(solution)/shard_map/add | solution.py:407
  8.8 0.1 broadcast_in_dim.184
  9.2 0.1 select_select_fusion.1
  9.3 0.6 %copy-done.2 = f32[5,4,128]{2,1,0:T(4,128)S(1)} copy-done((f32[5,4,128]{2,1,0:T(4,128)S(1)}, f32[5,4,128]{2,1,0:T(4,128)}, u32[]{:S(2)}) %copy-start.2) | copy-done | bytes 10264
  9.9 0.8 %select_select_fusion = f32[16,5,4,128]{3,2,1,0:T(4,128)} fusion(f32[16,5,2,128]{3,2,1,0:T(2,128)S(1)} %select_select_fusion.1, f32[5,4,128]{2,1,0:T(4,128)S(1)} %copy-done.3, f32[5,4,128]{2,1,0:T(4,128)S(1)} %copy-done.2, pred[16]{0:T(512)(128)(4,1)S(1)} %get-tuple-element.96, pred[16]{0:T(512)(128)(4,1)S(1)} %get-tuple-element.94, ...), kind=kLoop, calls=%fused_computation.3 | loop fusion | flops 122880 | bytes 266288 | tf_op jit(solution)/shard_map/jit(_where)/select_n | solution.py:424
  10.7 7.5 %all-to-all-start = ((f32[16,5,4,128]{3,2,1,0:T(4,128)}), f32[16,5,4,128]{3,2,1,0:T(4,128)S(1)}, u32[]{:S(2)}, u32[]{:S(2)}) async-start(f32[16,5,4,128]{3,2,1,0:T(4,128)} %select_select_fusion), calls=%async_computation | async-start | bytes 327680 | tf_op jit(solution)/shard_map/all_to_all | solution.py:427
  18.2 1.6 %collective-permute-start = (f32[5,4,4,128]{3,2,1,0:T(4,128)S(1)}, f32[5,4,4,128]{3,2,1,0:T(4,128)S(1)}, u32[]{:S(2)}, u32[]{:S(2)}) collective-permute-start(f32[5,4,4,128]{3,2,1,0:T(4,128)S(1)} %bitcast.84), channel_id=1, source_target_pairs={{0,8},{8,0},{1,9},{9,1},{2,10},{10,2},{3,11},{11,3},{4,12},{12,4},... | collective-permute-start | bytes 122888 | tf_op jit(solution)/shard_map/ppermute | solution.py:381
  19.8 2.5 %collective-permute-done = f32[5,4,4,128]{3,2,1,0:T(4,128)S(1)} collective-permute-done((f32[5,4,4,128]{3,2,1,0:T(4,128)S(1)}, f32[5,4,4,128]{3,2,1,0:T(4,128)S(1)}, u32[]{:S(2)}, u32[]{:S(2)}) %collective-permute-start) | collective-permute-done | bytes 40992 | tf_op jit(solution)/shard_map/ppermute | solution.py:381
  22.3 0.6 %broadcast_select_fusion = (f32[5,4,4,128]{3,2,1,0:T(4,128)}, f32[5,4,4,128]{3,2,1,0:T(4,128)}) fusion(f32[5,4,4,128]{3,2,1,0:T(4,128)S(1)} %collective-permute-done, pred[]{:T(512)S(6)} %eq.144), kind=kLoop, calls=%fused_computation.158 | loop fusion | flops 20480 | bytes 122881 | tf_op jit(solution)/shard_map/jit(_where)/select_n | solution.py:387
  22.9 3.4 %all-to-all-done = f32[16,5,4,128]{3,2,1,0:T(4,128)S(1)} async-done(((f32[16,5,4,128]{3,2,1,0:T(4,128)}), f32[16,5,4,128]{3,2,1,0:T(4,128)S(1)}, u32[]{:S(2)}, u32[]{:S(2)}) %all-to-all-start) | async-done | bytes 163872 | tf_op jit(solution)/shard_map/all_to_all | solution.py:427
  26.3 0.6 %dynamic-slice_bitcast_fusion.2 = (f32[5,4,128]{2,1,0:T(4,128)S(1)}, f32[5,4,128]{2,1,0:T(4,128)S(1)}, f32[5,4,128]{2,1,0:T(4,128)S(1)}, f32[5,4,128]{2,1,0:T(4,128)}, f32[5,4,128]{2,1,0:T(4,128)}) fusion(f32[16,5,4,128]{3,2,1,0:T(4,128)S(1)} %all-to-all-done, s32[]{:T(128)S(6)} %select_n.231, s32[]{:T(128)S(6)} %select_n.235, s32[]{:T(128)S(6)} %select_n.233, ...), kind=kLoop, calls=%fused_computation.163 | loop fusion | bytes 102420 | tf_op jit(solution)/shard_map/jit(dynamic_index_in_dim)/squeeze | solution.py:433
  27.2 0.7 %fusion.2 = f32[5,16,16]{2,1,0:T(8,128)S(1)} fusion(f32[5,16,16]{2,1,0:T(8,128)S(1)} %reshape.128, f32[5,16,16]{2,1,0:T(8,128)S(1)} %reshape.127, f32[5,16,16]{2,1,0:T(8,128)S(1)} %reshape.126, f32[16,16]{1,0:T(8,128)S(1)} %get-tuple-element.23, f32[16,16]{1,0:T(8,128)S(1)} %get-tuple-element.24, f32[16,16]{1,0:T(8,128)S(1)} %get-tuple-element.25, ...), kind=kLoop, calls=%fused_computation.9 | loop fusion | flops 116480 | bytes 52225 | tf_op jit(solution)/shard_map/jit(_where)/select_n | solution.py:442
  27.9 0.6 %pad_maximum_fusion = f32[10,16,16]{2,1,0:T(8,128)} fusion(f32[5,16,16]{2,1,0:T(8,128)S(1)} %fusion.2, f32[5,16,16]{2,1,0:T(8,128)S(1)} %add_select_fusion), kind=kLoop, calls=%fused_computation.4 | loop fusion | flops 2560 | bytes 20480 | tf_op jit(solution)/shard_map/concatenate | solution.py:441
  28.5 3.3 %shard_map.78 = (f32[1,5,4,4,4,128]{5,4,3,2,1,0:T(4,128)}, f32[1,5,4,4,4,128]{5,4,3,2,1,0:T(4,128)}) custom-call(f32[1,5,4,4,4,128]{5,4,3,2,1,0:T(4,128)} %adj_ref.3, bf16[1,5,4,4,4,128]{5,4,3,2,1,0:T(4,128)(2,1)} %flow_ref.1, f32[5,4,4,128]{3,2,1,0:T(4,128)} %get-tuple-element.93.up_ax_ref, f32[5,4,4,128]{3,2,1,0:T(4,128)} %get-tuple-element.92.down_ax_ref, ...), custom_call_target="tpu_custom_call" | custom-call | tf_op jit(solution)/shard_map/pallas_call | solution.py:445
  (41 shorter events, 1.4 us)
Async XLA Ops:
  5.5 0.7 %copy-start.4 = (s32[4,256]{1,0:T(4,128)S(1)}, s32[4,256]{1,0:T(4,128)}, u32[]{:S(2)}) copy-start(s32[4,256]{1,0:T(4,128)} %param.8) | copy-start | bytes 12292
  6.2 0.7 %copy-start.5 = (s32[4,256]{1,0:T(4,128)S(1)}, s32[4,256]{1,0:T(4,128)}, u32[]{:S(2)}) copy-start(s32[4,256]{1,0:T(4,128)} %param.9) | copy-start | bytes 12292
  6.2 0.7 %copy-start.6 = (f32[128]{0:T(128)S(1)}, f32[128]{0:T(128)}, u32[]{:S(2)}) copy-start(f32[128]{0:T(128)} %param.10) | copy-start | bytes 1540
  9.2 0.7 %copy-start.2 = (f32[5,4,128]{2,1,0:T(4,128)S(1)}, f32[5,4,128]{2,1,0:T(4,128)}, u32[]{:S(2)}) copy-start(f32[5,4,128]{2,1,0:T(4,128)} %get-tuple-element.10) | copy-start | bytes 30724
  9.2 0.7 %copy-start.3 = (f32[5,4,128]{2,1,0:T(4,128)S(1)}, f32[5,4,128]{2,1,0:T(4,128)}, u32[]{:S(2)}) copy-start(f32[5,4,128]{2,1,0:T(4,128)} %get-tuple-element.11) | copy-start | bytes 30724
  10.7 7.5 %copy-start = (f32[5,4,4,128]{3,2,1,0:T(4,128)S(1)}, f32[5,4,4,128]{3,2,1,0:T(4,128)}, u32[]{:S(2)}) copy-start(f32[5,4,4,128]{3,2,1,0:T(4,128)} %get-tuple-element.9) | copy-start | bytes 122884
  10.7 7.5 %copy-start.1 = (f32[5,4,4,128]{3,2,1,0:T(4,128)S(1)}, f32[5,4,4,128]{3,2,1,0:T(4,128)}, u32[]{:S(2)}) copy-start(f32[5,4,4,128]{3,2,1,0:T(4,128)} %get-tuple-element.8) | copy-start | bytes 122884
  10.7 15.6 %all-to-all-start = ((f32[16,5,4,128]{3,2,1,0:T(4,128)}), f32[16,5,4,128]{3,2,1,0:T(4,128)S(1)}, u32[]{:S(2)}, u32[]{:S(2)}) async-start(f32[16,5,4,128]{3,2,1,0:T(4,128)} %select_select_fusion), calls=%async_computation | async-start | bytes 327680 | tf_op jit(solution)/shard_map/all_to_all | solution.py:427
  18.2 4.1 %collective-permute-start = (f32[5,4,4,128]{3,2,1,0:T(4,128)S(1)}, f32[5,4,4,128]{3,2,1,0:T(4,128)S(1)}, u32[]{:S(2)}, u32[]{:S(2)}) collective-permute-start(f32[5,4,4,128]{3,2,1,0:T(4,128)S(1)} %bitcast.84), channel_id=1, source_target_pairs={{0,8},{8,0},{1,9},{9,1},{2,10},{10,2},{3,11},{11,3},{4,12},{12,4},... | collective-permute-start | bytes 122888 | tf_op jit(solution)/shard_map/ppermute | solution.py:381

commit v11 on v10

--- a/solution.py
+++ b/solution.py
@@ -228,10 +228,12 @@
     return jnp.dot(left, right, precision=lax.Precision.HIGHEST, preferred_element_type=jnp.float32)
 
 
-def moment_kernel(adj_ref, left_ax_ref, right_ax_ref, up_ref, down_ref, outer_ref, inner_ref, scratch_ref):
+def moment_kernel(adj_ref, left_ax_ref, right_ax_ref, up_ref, down_ref, own_ref, scratch_ref):
     derivs, left_vals, right_vals, left_corr, right_corr = basis_tables()
     pick_outer = selector(128, 128, lambda k: k // ET * ET * ER + k % ET * ER + ER - 1, False)
     pick_inner = selector(128, 128, lambda k: k // ET * ET * ER + k % ET * ER, False)
+    rotor = lax.axis_index("zone") == 0
+    pick = jnp.where(rotor, pick_outer, pick_inner)
     for chan in range(5):
         field = adj_ref[0, chan]
         left_ax_ref[chan] = sweep(field, left_corr, lambda i: (i,))
@@ -247,8 +249,8 @@
                 row = axial * 4 + azim
                 scratch_ref[0, row : row + 1] = outer[axial, azim]
                 scratch_ref[1, row : row + 1] = inner[axial, azim]
-        outer_ref[chan] = exact_dot(scratch_ref[0], pick_outer)
-        inner_ref[chan] = exact_dot(scratch_ref[1], pick_inner)
+        rows = jnp.where(rotor, scratch_ref[0], scratch_ref[1])
+        own_ref[chan] = exact_dot(rows, pick)[:, : EA * ET]
 
 
 def rate_kernel(
@@ -369,9 +371,9 @@
     face4 = jax.ShapeDtypeStruct((5, 4, 4, 128), jnp.float32)
     chunk = jax.ShapeDtypeStruct((5, 4, 128), jnp.float32)
     rows16 = jax.ShapeDtypeStruct((5, 16, 128), jnp.float32)
-    left_ax, right_ax, upper_face, lower_face, outer_moment, inner_moment = pl.pallas_call(
+    left_ax, right_ax, upper_face, lower_face, own_face = pl.pallas_call(
         moment_kernel,
-        out_shape=(face4, face4, chunk, chunk, rows16, rows16),
+        out_shape=(face4, face4, chunk, chunk, jax.ShapeDtypeStruct((5, 16, EA * ET), jnp.float32)),
         scratch_shapes=[pltpu.VMEM((2, 16, 128), jnp.float32)],
     )(adjoint)
     is_rotor = lax.axis_index("zone") == 0
@@ -385,7 +387,6 @@
         got_second = jnp.zeros_like(got_first)
     up_ax = jnp.where(even, got_first, got_second)
     down_ax = jnp.where(even, got_second, got_first)
-    own_face = jnp.where(is_rotor, outer_moment, inner_moment)[:, :, : EA * ET]
     own_rows = own_face.reshape(5, 4, 4, EA, ET).transpose(0, 3, 1, 4, 2).reshape(5, AP, TP)
     shifts_local = intersection_shift.reshape(INTERSECTIONS, AP, TP)
     table_match = weight_index[:, :, None] == jnp.arange(NW, dtype=jnp.int32)[None, None, :]

time: 32.3 us -> 32.1 us (level)
  other arithmetic: 4.89 us -> 4.09 us
  local copies, waits for them, and re-layouts: 4.86 us -> 5.63 us
    select_n x1 -> x0, other arithmetic: 0.81 us -> none  [local(): own_face = jnp.where(is_rotor, outer_moment, inner_moment)[:, :, :EA * ET]]
    reshape x2, local copies, waits for them, and re-layouts: 0.26 us -> 1.03 us  [local(): own_face.reshape(5, 4, 4, EA, ET).transpose(0, 3, 1, 4, 2)]
where the time goes in v11:
time: 32.1 us; the launch traced here: 31.6 us
  starting transfers between devices  9.07 us (28%)
  waiting for transfers between devices  5.87 us (18%)
  local copies, waits for them, and re-layouts  5.63 us (18%)
  Pallas kernels  5.37 us (17%)
  other arithmetic  4.09 us (13%)
  between operations  1.59 us (5%)
    all_to_all x1, starting transfers between devices, local(): got = lax.all_to_all(chunks, ('zone', 'azim'), 0, 0)  7.49 us
    all_to_all x1, waiting for transfers between devices, local(): got = lax.all_to_all(chunks, ('zone', 'azim'), 0, 0)  3.38 us
    pallas_call x1, Pallas kernels, local(): pl.pallas_call(rate_kernel, out_shape=(field_shape, field_shape))  3.27 us
    ppermute x1, waiting for transfers between devices, local(): got_first = lax.ppermute(jnp.where(even, right_ax, left_ax), 'axial', first)  2.48 us
    pallas_call x1, Pallas kernels, local(): pl.pallas_call(moment_kernel, out_shape=(face4, face4, chunk, chunk, jax....  2.11 us
    unnamed x14, local copies, waits for them, and re-layouts  1.92 us
    ppermute x1, starting transfers between devices, local(): got_first = lax.ppermute(jnp.where(even, right_ax, left_ax), 'axial', first)  1.58 us
    reshape x2, local copies, waits for them, and re-layouts, local(): own_face.reshape(5, 4, 4, EA, ET).transpose(0, 3, 1, 4, 2)  1.03 us
  transfers between devices with their start and end apart: 2, of which 2 were waited for; matrix products, arithmetic and copies ran while one was open for 2% of the time, Pallas kernels for 0%

profile of v11, /device:TPU:0, one launch (start us, length us, event | category | flops | bytes accessed | tf_op | source)
XLA Modules:
  0.0 31.6 jit_solution(14121600760849509307)
XLA Ops:
  1.4 2.1 %shard_map.77 = (f32[5,4,4,128]{3,2,1,0:T(4,128)}, f32[5,4,4,128]{3,2,1,0:T(4,128)}, f32[5,4,128]{2,1,0:T(4,128)}, f32[5,4,128]{2,1,0:T(4,128)}, f32[5,16,16]{2,1,0:T(8,128)}) custom-call(f32[1,5,4,4,4,128]{5,4,3,2,1,0:T(4,128)} %adj_ref.3), custom_call_target="tpu_custom_call" | custom-call | tf_op jit(solution)/shard_map/pallas_call | solution.py:374
  3.5 0.9 %reshape.124 = f32[5,4,4,4,4]{4,3,2,1,0:T(4,128)S(1)} reshape(f32[5,16,16]{2,1,0:T(8,128)} %get-tuple-element.11) | data formatting | bytes 10240 | tf_op jit(solution)/shard_map/reshape | solution.py:390
  4.4 0.6 %copy.11 = f32[5,4,4,4,4]{4,3,2,1,0:T(4,128)S(1)} copy(f32[5,4,4,4,4]{3,1,4,2,0:T(4,128)S(1)} %bitcast.80) | data formatting | bytes 10240 | tf_op jit(solution)/shard_map/transpose | solution.py:390
  5.0 0.2 broadcast_in_dim.170
  5.2 0.1 reshape.125
  5.3 0.7 %copy-done.4 = s32[4,256]{1,0:T(4,128)S(1)} copy-done((s32[4,256]{1,0:T(4,128)S(1)}, s32[4,256]{1,0:T(4,128)}, u32[]{:S(2)}) %copy-start.4) | copy-done | bytes 4120
  6.0 0.7 %copy-done.5 = s32[4,256]{1,0:T(4,128)S(1)} copy-done((s32[4,256]{1,0:T(4,128)S(1)}, s32[4,256]{1,0:T(4,128)}, u32[]{:S(2)}) %copy-start.5) | copy-done | bytes 4120
  6.7 0.4 %select_reduce_fusion = f32[4,256]{1,0:T(4,128)S(1)} fusion(f32[128]{0:T(128)S(1)} %copy-done.6, s32[4,256]{1,0:T(4,128)S(1)} %copy-done.5), kind=kLoop, calls=%fused_computation | loop fusion | flops 392192 | bytes 8704 | tf_op jit(solution)/shard_map/reduce_sum | solution.py:393
  7.7 0.2 select_add_fusion
  8.0 0.1 broadcast_multiply_fusion.30
  8.1 0.4 %pad_add_fusion = f32[5,16,48]{2,1,0:T(8,128)S(1)} fusion(f32[5,16,16]{2,1,0:T(8,128)S(1)} %get-tuple-element.60, f32[5,16,16]{2,1,0:T(8,128)S(1)} %get-tuple-element.61, f32[5,16,16]{2,1,0:T(8,128)S(1)} %get-tuple-element.62, f32[5,16,16]{2,1,0:T(8,128)S(1)} %get-tuple-element.63, f32[5,16,16]{2,1,0:T(8,128)S(1)} %get-tuple-element.64, ...), kind=kLoop, calls=%fused_computation.125 | loop fusion | flops 115200 | bytes 174080 | tf_op jit(solution)/shard_map/add | solution.py:408
  8.6 0.1 broadcast_in_dim.184
  9.0 0.1 select_select_fusion.1
  9.1 0.6 %copy-done.2 = f32[5,4,128]{2,1,0:T(4,128)S(1)} copy-done((f32[5,4,128]{2,1,0:T(4,128)S(1)}, f32[5,4,128]{2,1,0:T(4,128)}, u32[]{:S(2)}) %copy-start.2) | copy-done | bytes 10264
  9.7 0.8 %select_select_fusion = f32[16,5,4,128]{3,2,1,0:T(4,128)} fusion(f32[16,5,2,128]{3,2,1,0:T(2,128)S(1)} %select_select_fusion.1, f32[5,4,128]{2,1,0:T(4,128)S(1)} %copy-done.3, f32[5,4,128]{2,1,0:T(4,128)S(1)} %copy-done.2, pred[16]{0:T(512)(128)(4,1)S(1)} %get-tuple-element.94, pred[16]{0:T(512)(128)(4,1)S(1)} %get-tuple-element.92, ...), kind=kLoop, calls=%fused_computation.3 | loop fusion | flops 122880 | bytes 266288 | tf_op jit(solution)/shard_map/jit(_where)/select_n | solution.py:425
  10.5 7.5 %all-to-all-start = ((f32[16,5,4,128]{3,2,1,0:T(4,128)}), f32[16,5,4,128]{3,2,1,0:T(4,128)S(1)}, u32[]{:S(2)}, u32[]{:S(2)}) async-start(f32[16,5,4,128]{3,2,1,0:T(4,128)} %select_select_fusion), calls=%async_computation | async-start | bytes 327680 | tf_op jit(solution)/shard_map/all_to_all | solution.py:428
  18.0 1.6 %collective-permute-start = (f32[5,4,4,128]{3,2,1,0:T(4,128)S(1)}, f32[5,4,4,128]{3,2,1,0:T(4,128)S(1)}, u32[]{:S(2)}, u32[]{:S(2)}) collective-permute-start(f32[5,4,4,128]{3,2,1,0:T(4,128)S(1)} %bitcast.84), channel_id=1, source_target_pairs={{0,8},{8,0},{1,9},{9,1},{2,10},{10,2},{3,11},{11,3},{4,12},{12,4},... | collective-permute-start | bytes 122888 | tf_op jit(solution)/shard_map/ppermute | solution.py:383
  19.6 2.5 %collective-permute-done = f32[5,4,4,128]{3,2,1,0:T(4,128)S(1)} collective-permute-done((f32[5,4,4,128]{3,2,1,0:T(4,128)S(1)}, f32[5,4,4,128]{3,2,1,0:T(4,128)S(1)}, u32[]{:S(2)}, u32[]{:S(2)}) %collective-permute-start) | collective-permute-done | bytes 40992 | tf_op jit(solution)/shard_map/ppermute | solution.py:383
  22.1 0.6 %broadcast_select_fusion = (f32[5,4,4,128]{3,2,1,0:T(4,128)}, f32[5,4,4,128]{3,2,1,0:T(4,128)}) fusion(f32[5,4,4,128]{3,2,1,0:T(4,128)S(1)} %collective-permute-done, pred[]{:T(512)S(6)} %eq.144), kind=kLoop, calls=%fused_computation.157 | loop fusion | flops 20480 | bytes 122881 | tf_op jit(solution)/shard_map/jit(_where)/select_n | solution.py:389
  22.7 3.4 %all-to-all-done = f32[16,5,4,128]{3,2,1,0:T(4,128)S(1)} async-done(((f32[16,5,4,128]{3,2,1,0:T(4,128)}), f32[16,5,4,128]{3,2,1,0:T(4,128)S(1)}, u32[]{:S(2)}, u32[]{:S(2)}) %all-to-all-start) | async-done | bytes 163872 | tf_op jit(solution)/shard_map/all_to_all | solution.py:428
  26.1 0.6 %dynamic-slice_bitcast_fusion.2 = (f32[5,4,128]{2,1,0:T(4,128)S(1)}, f32[5,4,128]{2,1,0:T(4,128)S(1)}, f32[5,4,128]{2,1,0:T(4,128)S(1)}, f32[5,4,128]{2,1,0:T(4,128)}, f32[5,4,128]{2,1,0:T(4,128)}) fusion(f32[16,5,4,128]{3,2,1,0:T(4,128)S(1)} %all-to-all-done, s32[]{:T(128)S(6)} %select_n.221, s32[]{:T(128)S(6)} %select_n.225, s32[]{:T(128)S(6)} %select_n.223, ...), kind=kLoop, calls=%fused_computation.162 | loop fusion | bytes 102420 | tf_op jit(solution)/shard_map/jit(dynamic_index_in_dim)/squeeze | solution.py:434
  27.0 0.7 %fusion.2 = f32[5,16,16]{2,1,0:T(8,128)S(1)} fusion(f32[5,16,16]{2,1,0:T(8,128)S(1)} %reshape.128, f32[5,16,16]{2,1,0:T(8,128)S(1)} %reshape.127, f32[5,16,16]{2,1,0:T(8,128)S(1)} %reshape.126, f32[16,16]{1,0:T(8,128)S(1)} %get-tuple-element.21, f32[16,16]{1,0:T(8,128)S(1)} %get-tuple-element.22, f32[16,16]{1,0:T(8,128)S(1)} %get-tuple-element.23, ...), kind=kLoop, calls=%fused_computation.9 | loop fusion | flops 116480 | bytes 52225 | tf_op jit(solution)/shard_map/jit(_where)/select_n | solution.py:443
  27.7 0.6 %pad_maximum_fusion = f32[10,16,16]{2,1,0:T(8,128)} fusion(f32[5,16,16]{2,1,0:T(8,128)S(1)} %fusion.2, f32[5,16,16]{2,1,0:T(8,128)S(1)} %add_select_fusion), kind=kLoop, calls=%fused_computation.4 | loop fusion | flops 2560 | bytes 20480 | tf_op jit(solution)/shard_map/concatenate | solution.py:442
  28.4 3.3 %shard_map.78 = (f32[1,5,4,4,4,128]{5,4,3,2,1,0:T(4,128)}, f32[1,5,4,4,4,128]{5,4,3,2,1,0:T(4,128)}) custom-call(f32[1,5,4,4,4,128]{5,4,3,2,1,0:T(4,128)} %adj_ref.3, bf16[1,5,4,4,4,128]{5,4,3,2,1,0:T(4,128)(2,1)} %flow_ref.1, f32[5,4,4,128]{3,2,1,0:T(4,128)} %get-tuple-element.91.up_ax_ref, f32[5,4,4,128]{3,2,1,0:T(4,128)} %get-tuple-element.90.down_ax_ref, ...), custom_call_target="tpu_custom_call" | custom-call | tf_op jit(solution)/shard_map/pallas_call | solution.py:446
  (40 shorter events, 1.4 us)
Async XLA Ops:
  5.3 0.7 %copy-start.4 = (s32[4,256]{1,0:T(4,128)S(1)}, s32[4,256]{1,0:T(4,128)}, u32[]{:S(2)}) copy-start(s32[4,256]{1,0:T(4,128)} %param.8) | copy-start | bytes 12292
  6.0 0.7 %copy-start.5 = (s32[4,256]{1,0:T(4,128)S(1)}, s32[4,256]{1,0:T(4,128)}, u32[]{:S(2)}) copy-start(s32[4,256]{1,0:T(4,128)} %param.9) | copy-start | bytes 12292
  6.0 0.7 %copy-start.6 = (f32[128]{0:T(128)S(1)}, f32[128]{0:T(128)}, u32[]{:S(2)}) copy-start(f32[128]{0:T(128)} %param.10) | copy-start | bytes 1540
  9.0 0.7 %copy-start.2 = (f32[5,4,128]{2,1,0:T(4,128)S(1)}, f32[5,4,128]{2,1,0:T(4,128)}, u32[]{:S(2)}) copy-start(f32[5,4,128]{2,1,0:T(4,128)} %get-tuple-element.9) | copy-start | bytes 30724
  9.0 0.7 %copy-start.3 = (f32[5,4,128]{2,1,0:T(4,128)S(1)}, f32[5,4,128]{2,1,0:T(4,128)}, u32[]{:S(2)}) copy-start(f32[5,4,128]{2,1,0:T(4,128)} %get-tuple-element.10) | copy-start | bytes 30724
  10.5 7.5 %copy-start = (f32[5,4,4,128]{3,2,1,0:T(4,128)S(1)}, f32[5,4,4,128]{3,2,1,0:T(4,128)}, u32[]{:S(2)}) copy-start(f32[5,4,4,128]{3,2,1,0:T(4,128)} %get-tuple-element.8) | copy-start | bytes 122884
  10.5 7.5 %copy-start.1 = (f32[5,4,4,128]{3,2,1,0:T(4,128)S(1)}, f32[5,4,4,128]{3,2,1,0:T(4,128)}, u32[]{:S(2)}) copy-start(f32[5,4,4,128]{3,2,1,0:T(4,128)} %get-tuple-element.7) | copy-start | bytes 122884
  10.5 15.6 %all-to-all-start = ((f32[16,5,4,128]{3,2,1,0:T(4,128)}), f32[16,5,4,128]{3,2,1,0:T(4,128)S(1)}, u32[]{:S(2)}, u32[]{:S(2)}) async-start(f32[16,5,4,128]{3,2,1,0:T(4,128)} %select_select_fusion), calls=%async_computation | async-start | bytes 327680 | tf_op jit(solution)/shard_map/all_to_all | solution.py:428
  18.0 4.1 %collective-permute-start = (f32[5,4,4,128]{3,2,1,0:T(4,128)S(1)}, f32[5,4,4,128]{3,2,1,0:T(4,128)S(1)}, u32[]{:S(2)}, u32[]{:S(2)}) collective-permute-start(f32[5,4,4,128]{3,2,1,0:T(4,128)S(1)} %bitcast.84), channel_id=1, source_target_pairs={{0,8},{8,0},{1,9},{9,1},{2,10},{10,2},{3,11},{11,3},{4,12},{12,4},... | collective-permute-start | bytes 122888 | tf_op jit(solution)/shard_map/ppermute | solution.py:383

commit v12 on v11

--- a/solution.py
+++ b/solution.py
@@ -1,3 +1,4 @@
+import functools
 import math
 
 import jax
@@ -253,8 +254,12 @@
         own_ref[chan] = exact_dot(rows, pick)[:, : EA * ET]
 
 
+def rate_kernel_single(body, adj_ref, flow_ref, first_ref, *rest):
+    return body(adj_ref, flow_ref, first_ref, None, *rest)
+
+
 def rate_kernel(
-    adj_ref, flow_ref, up_ax_ref, down_ax_ref, up_az_ref, down_az_ref, sides_ref,
+    adj_ref, flow_ref, first_ref, second_ref, up_az_ref, down_az_ref, sides_ref,
     rate_ref, next_ref,
 ):
     derivs, left_vals, right_vals, left_corr, right_corr = basis_tables()
@@ -267,6 +272,8 @@
     col = lax.broadcasted_iota(jnp.int32, (16, 128), 1)
     row = lax.broadcasted_iota(jnp.int32, (16, 128), 0)
     sides = sides_ref[...]
+    even = lax.axis_index("axial") % 2 == 0
+    rotor = lax.axis_index("zone") == 0
     spread = [
         exact_dot(sides, jnp.where(row == col // ER % ET * 4 + azim, 1.0, 0.0)) for azim in range(4)
     ]
@@ -277,7 +284,7 @@
         for axial in range(4):
             slabs = []
             for azim in range(4):
-                base = (side * 5 + chan) * 16 + axial
+                base = chan * 16 + axial
                 value = spread[azim][base : base + 1]
                 for elem in range(1, EA):
                     pos = base + elem * 4
@@ -288,14 +295,19 @@
 
     for chan in range(5):
         field = adj_ref[0, chan]
-        outer_face = side_face(0, chan)
-        inner_face = side_face(1, chan)
+        own_face = side_face(0, chan)
+        outer_face = jnp.where(rotor, own_face, 0.0)
+        inner_face = jnp.where(rotor, 0.0, own_face)
+        first = first_ref[chan]
+        second = first * 0.0 if second_ref is None else second_ref[chan]
+        up_ax = jnp.where(even, first, second)
+        down_ax = jnp.where(even, second, first)
         up_az = expand_face(up_az_ref[chan], 0)
         down_az = expand_face(down_az_ref[chan], ET - 1)
         left0 = sweep(field, left_corr, lambda i: (i,))
         right0 = sweep(field, right_corr, lambda i: (i,))
-        next0 = lane_roll(jnp.where(flat_lane < ET * ER, up_ax_ref[chan], left0), -ET * ER)
-        prev0 = lane_roll(jnp.where(flat_lane >= (EA - 1) * ET * ER, down_ax_ref[chan], right0), ET * ER)
+        next0 = lane_roll(jnp.where(flat_lane < ET * ER, up_ax, left0), -ET * ER)
+        prev0 = lane_roll(jnp.where(flat_lane >= (EA - 1) * ET * ER, down_ax, right0), ET * ER)
         jump_r = 0.5 * (next0 - right0)
         jump_l = 0.5 * (prev0 - left0)
         slabs = []
@@ -384,9 +396,7 @@
     if second:
         got_second = lax.ppermute(jnp.where(even, left_ax, right_ax), "axial", second)
     else:
-        got_second = jnp.zeros_like(got_first)
-    up_ax = jnp.where(even, got_first, got_second)
-    down_ax = jnp.where(even, got_second, got_first)
+        got_second = None
     own_rows = own_face.reshape(5, 4, 4, EA, ET).transpose(0, 3, 1, 4, 2).reshape(5, AP, TP)
     shifts_local = intersection_shift.reshape(INTERSECTIONS, AP, TP)
     table_match = weight_index[:, :, None] == jnp.arange(NW, dtype=jnp.int32)[None, None, :]
@@ -439,13 +449,16 @@
     returned = picked[0] + picked[1] + picked[2]
     window = jnp.concatenate(picked, axis=2)
     incoming = shift_sum(window, coefs, TP)
-    sides = jnp.concatenate(
-        [jnp.where(is_rotor, returned, 0.0), jnp.where(is_rotor, 0.0, incoming)], axis=0
-    ).reshape(10 * AP, TP)
+    sides = jnp.where(is_rotor, returned, incoming).reshape(5 * AP, TP)
     field_shape = jax.ShapeDtypeStruct(adjoint.shape, jnp.float32)
+    operands = (adjoint, flow_prim, got_first, got_second, up_az, down_az, sides)
+    kernel = rate_kernel
+    if got_second is None:
+        operands = (adjoint, flow_prim, got_first, up_az, down_az, sides)
+        kernel = functools.partial(rate_kernel_single, rate_kernel)
     adjoint_rate, next_adjoint = pl.pallas_call(
-        rate_kernel, out_shape=(field_shape, field_shape)
-    )(adjoint, flow_prim, up_ax, down_ax, up_az, down_az, sides)
+        kernel, out_shape=(field_shape, field_shape)
+    )(*operands)
     return (adjoint_rate, next_adjoint)
 
 

time: 32.1 us -> 32.6 us (1.016)
  other arithmetic: 4.09 us -> 3.46 us
  waiting for transfers between devices: 5.87 us -> 6.5 us
  local copies, waits for them, and re-layouts: 5.63 us -> 6.25 us
    all_to_all x1, waiting for transfers between devices: 3.38 us -> 6.5 us  [local(): got = lax.all_to_all(chunks, ('zone', 'azim'), 0, 0)]
    ppermute x1, waiting for transfers between devices: 2.48 us -> 0.01 us  [local(): got_first = lax.ppermute(jnp.where(even, right_ax, left_ax), 'axial', first)]
    concatenate x1 -> x0, other arithmetic: 0.63 us -> none  [local(): jnp.concatenate([jnp.where(is_rotor, returned, 0.0), jnp.where(is_rotor,...]
    unnamed x14 -> x16, local copies, waits for them, and re-layouts: 1.92 us -> 2.54 us
    select_n x3 -> x1, other arithmetic: 1.35 us -> 1.35 us  [local(): sides = jnp.where(is_rotor, returned, incoming).reshape(5 * AP, TP)]
  transfers between devices with their start and end apart: 2 -> 2, of which waited for: 2 -> 1; matrix products, arithmetic and copies ran while one was open for 2% -> 7% of each run, Pallas kernels for 0% -> 0%
where the time goes in v12:
time: 32.6 us; the launch traced here: 32.1 us
  starting transfers between devices  9.07 us (28%)
  waiting for transfers between devices  6.5 us (20%)
  local copies, waits for them, and re-layouts  6.25 us (19%)
  Pallas kernels  5.29 us (16%)
  other arithmetic  3.46 us (11%)
  between operations  1.58 us (5%)
    all_to_all x1, starting transfers between devices, local(): got = lax.all_to_all(chunks, ('zone', 'azim'), 0, 0)  7.49 us
    all_to_all x1, waiting for transfers between devices, local(): got = lax.all_to_all(chunks, ('zone', 'azim'), 0, 0)  6.5 us
    pallas_call x1, Pallas kernels, local(): pl.pallas_call(kernel, out_shape=(field_shape, field_shape))(*operands)  3.18 us
    unnamed x16, local copies, waits for them, and re-layouts  2.54 us
    pallas_call x1, Pallas kernels, local(): pl.pallas_call(moment_kernel, out_shape=(face4, face4, chunk, chunk, jax....  2.11 us
    ppermute x1, starting transfers between devices, local(): got_first = lax.ppermute(jnp.where(even, right_ax, left_ax), 'axial', first)  1.58 us
    select_n x1, other arithmetic, local(): sides = jnp.where(is_rotor, returned, incoming).reshape(5 * AP, TP)  1.35 us
    reshape x2, local copies, waits for them, and re-layouts, local(): own_face.reshape(5, 4, 4, EA, ET).transpose(0, 3, 1, 4, 2)  1.03 us
  transfers between devices with their start and end apart: 2, of which 1 were waited for; matrix products, arithmetic and copies ran while one was open for 7% of the time, Pallas kernels for 0%

profile of v12, /device:TPU:0, one launch (start us, length us, event | category | flops | bytes accessed | tf_op | source)
XLA Modules:
  0.0 32.1 jit_solution(13098846978661013479)
XLA Ops:
  1.4 2.1 %shard_map.77 = (f32[5,4,4,128]{3,2,1,0:T(4,128)}, f32[5,4,4,128]{3,2,1,0:T(4,128)}, f32[5,4,128]{2,1,0:T(4,128)}, f32[5,4,128]{2,1,0:T(4,128)}, f32[5,16,16]{2,1,0:T(8,128)}) custom-call(f32[1,5,4,4,4,128]{5,4,3,2,1,0:T(4,128)} %adj_ref.3), custom_call_target="tpu_custom_call" | custom-call | tf_op jit(solution)/shard_map/pallas_call | solution.py:386
  3.5 0.9 %reshape.124 = f32[5,4,4,4,4]{4,3,2,1,0:T(4,128)S(1)} reshape(f32[5,16,16]{2,1,0:T(8,128)} %get-tuple-element.11) | data formatting | bytes 10240 | tf_op jit(solution)/shard_map/reshape | solution.py:400
  4.4 0.6 %copy.11 = f32[5,4,4,4,4]{4,3,2,1,0:T(4,128)S(1)} copy(f32[5,4,4,4,4]{3,1,4,2,0:T(4,128)S(1)} %bitcast.80) | data formatting | bytes 10240 | tf_op jit(solution)/shard_map/transpose | solution.py:400
  5.0 0.2 broadcast_in_dim.160
  5.2 0.1 reshape.125
  5.3 0.7 %copy-done.5 = s32[4,256]{1,0:T(4,128)S(1)} copy-done((s32[4,256]{1,0:T(4,128)S(1)}, s32[4,256]{1,0:T(4,128)}, u32[]{:S(2)}) %copy-start.5) | copy-done | bytes 4120
  6.0 0.7 %copy-done.6 = s32[4,256]{1,0:T(4,128)S(1)} copy-done((s32[4,256]{1,0:T(4,128)S(1)}, s32[4,256]{1,0:T(4,128)}, u32[]{:S(2)}) %copy-start.6) | copy-done | bytes 4120
  6.7 0.4 %select_reduce_fusion = f32[4,256]{1,0:T(4,128)S(1)} fusion(f32[128]{0:T(128)S(1)} %copy-done.7, s32[4,256]{1,0:T(4,128)S(1)} %copy-done.6), kind=kLoop, calls=%fused_computation | loop fusion | flops 392192 | bytes 8704 | tf_op jit(solution)/shard_map/reduce_sum | solution.py:403
  7.7 0.2 select_add_fusion
  8.0 0.1 broadcast_multiply_fusion.30
  8.1 0.4 %pad_add_fusion = f32[5,16,48]{2,1,0:T(8,128)S(1)} fusion(f32[5,16,16]{2,1,0:T(8,128)S(1)} %get-tuple-element.60, f32[5,16,16]{2,1,0:T(8,128)S(1)} %get-tuple-element.61, f32[5,16,16]{2,1,0:T(8,128)S(1)} %get-tuple-element.62, f32[5,16,16]{2,1,0:T(8,128)S(1)} %get-tuple-element.63, f32[5,16,16]{2,1,0:T(8,128)S(1)} %get-tuple-element.64, ...), kind=kLoop, calls=%fused_computation.123 | loop fusion | flops 115200 | bytes 174080 | tf_op jit(solution)/shard_map/add | solution.py:418
  8.6 0.1 broadcast_in_dim.174
  8.7 0.1 broadcast_in_dim.179
  8.8 0.1 broadcast_in_dim.177
  9.0 0.1 select_select_fusion.1
  9.1 0.6 %copy-done.3 = f32[5,4,128]{2,1,0:T(4,128)S(1)} copy-done((f32[5,4,128]{2,1,0:T(4,128)S(1)}, f32[5,4,128]{2,1,0:T(4,128)}, u32[]{:S(2)}) %copy-start.3) | copy-done | bytes 10264
  9.7 0.8 %select_select_fusion = f32[16,5,4,128]{3,2,1,0:T(4,128)} fusion(f32[16,5,2,128]{3,2,1,0:T(2,128)S(1)} %select_select_fusion.1, f32[5,4,128]{2,1,0:T(4,128)S(1)} %copy-done.4, f32[5,4,128]{2,1,0:T(4,128)S(1)} %copy-done.3, pred[16]{0:T(512)(128)(4,1)S(1)} %get-tuple-element.92, pred[16]{0:T(512)(128)(4,1)S(1)} %get-tuple-element.90, ...), kind=kLoop, calls=%fused_computation.3 | loop fusion | flops 122880 | bytes 266288 | tf_op jit(solution)/shard_map/jit(_where)/select_n | solution.py:435
  10.5 7.5 %all-to-all-start = ((f32[16,5,4,128]{3,2,1,0:T(4,128)}), f32[16,5,4,128]{3,2,1,0:T(4,128)S(1)}, u32[]{:S(2)}, u32[]{:S(2)}) async-start(f32[16,5,4,128]{3,2,1,0:T(4,128)} %select_select_fusion), calls=%async_computation | async-start | bytes 327680 | tf_op jit(solution)/shard_map/all_to_all | solution.py:438
  18.0 1.6 %collective-permute-start = (f32[5,4,4,128]{3,2,1,0:T(4,128)S(1)}, f32[5,4,4,128]{3,2,1,0:T(4,128)S(1)}, u32[]{:S(2)}, u32[]{:S(2)}) collective-permute-start(f32[5,4,4,128]{3,2,1,0:T(4,128)S(1)} %bitcast.84), channel_id=1, source_target_pairs={{0,8},{8,0},{1,9},{9,1},{2,10},{10,2},{3,11},{11,3},{4,12},{12,4},... | collective-permute-start | bytes 122888 | tf_op jit(solution)/shard_map/ppermute | solution.py:395
  19.6 6.5 %all-to-all-done = f32[16,5,4,128]{3,2,1,0:T(4,128)S(1)} async-done(((f32[16,5,4,128]{3,2,1,0:T(4,128)}), f32[16,5,4,128]{3,2,1,0:T(4,128)S(1)}, u32[]{:S(2)}, u32[]{:S(2)}) %all-to-all-start) | async-done | bytes 163872 | tf_op jit(solution)/shard_map/all_to_all | solution.py:438
  26.1 0.6 %dynamic-slice_bitcast_fusion.2 = (f32[5,4,128]{2,1,0:T(4,128)S(1)}, f32[5,4,128]{2,1,0:T(4,128)S(1)}, f32[5,4,128]{2,1,0:T(4,128)S(1)}, f32[5,4,128]{2,1,0:T(4,128)}, f32[5,4,128]{2,1,0:T(4,128)}) fusion(f32[16,5,4,128]{3,2,1,0:T(4,128)S(1)} %all-to-all-done, s32[]{:T(128)S(6)} %select_n.205, s32[]{:T(128)S(6)} %select_n.209, s32[]{:T(128)S(6)} %select_n.207, ...), kind=kLoop, calls=%fused_computation.158 | loop fusion | bytes 102420 | tf_op jit(solution)/shard_map/jit(dynamic_index_in_dim)/squeeze | solution.py:444
  27.0 1.4 %fusion.2 = f32[5,16,16]{2,1,0:T(8,128)} fusion(f32[5,16,16]{2,1,0:T(8,128)S(1)} %reshape.128, f32[5,16,16]{2,1,0:T(8,128)S(1)} %reshape.127, f32[5,16,16]{2,1,0:T(8,128)S(1)} %reshape.126, f32[16,16]{1,0:T(8,128)S(1)} %get-tuple-element.21, f32[16,16]{1,0:T(8,128)S(1)} %get-tuple-element.22, f32[16,16]{1,0:T(8,128)S(1)} %get-tuple-element.23, ...), kind=kLoop, calls=%fused_computation.8 | loop fusion | flops 119040 | bytes 52225 | tf_op jit(solution)/shard_map/jit(_where)/select_n | solution.py:452
  28.4 0.6 %copy-done.2 = f32[5,4,4,128]{3,2,1,0:T(4,128)} copy-done((f32[5,4,4,128]{3,2,1,0:T(4,128)}, f32[5,4,4,128]{3,2,1,0:T(4,128)S(1)}, u32[]{:S(2)}) %copy-start.2) | copy-done | bytes 40984
  29.0 3.2 %shard_map.78 = (f32[1,5,4,4,4,128]{5,4,3,2,1,0:T(4,128)}, f32[1,5,4,4,4,128]{5,4,3,2,1,0:T(4,128)}) custom-call(f32[1,5,4,4,4,128]{5,4,3,2,1,0:T(4,128)} %adj_ref.3, bf16[1,5,4,4,4,128]{5,4,3,2,1,0:T(4,128)(2,1)} %flow_ref.1, f32[5,4,4,128]{3,2,1,0:T(4,128)} %copy-done.2, f32[5,4,128]{2,1,0:T(4,128)} %get-tuple-element.55.rest_0_, ...), custom_call_target="tpu_custom_call" | custom-call | tf_op jit(solution)/shard_map/pallas_call | solution.py:459
  (39 shorter events, 1.2 us)
Async XLA Ops:
  5.3 0.7 %copy-start.5 = (s32[4,256]{1,0:T(4,128)S(1)}, s32[4,256]{1,0:T(4,128)}, u32[]{:S(2)}) copy-start(s32[4,256]{1,0:T(4,128)} %param.8) | copy-start | bytes 12292
  6.0 0.7 %copy-start.6 = (s32[4,256]{1,0:T(4,128)S(1)}, s32[4,256]{1,0:T(4,128)}, u32[]{:S(2)}) copy-start(s32[4,256]{1,0:T(4,128)} %param.9) | copy-start | bytes 12292
  6.0 0.7 %copy-start.7 = (f32[128]{0:T(128)S(1)}, f32[128]{0:T(128)}, u32[]{:S(2)}) copy-start(f32[128]{0:T(128)} %param.10) | copy-start | bytes 1540
  9.0 0.7 %copy-start.3 = (f32[5,4,128]{2,1,0:T(4,128)S(1)}, f32[5,4,128]{2,1,0:T(4,128)}, u32[]{:S(2)}) copy-start(f32[5,4,128]{2,1,0:T(4,128)} %get-tuple-element.9) | copy-start | bytes 30724
  9.0 0.7 %copy-start.4 = (f32[5,4,128]{2,1,0:T(4,128)S(1)}, f32[5,4,128]{2,1,0:T(4,128)}, u32[]{:S(2)}) copy-start(f32[5,4,128]{2,1,0:T(4,128)} %get-tuple-element.10) | copy-start | bytes 30724
  10.5 7.5 %copy-start = (f32[5,4,4,128]{3,2,1,0:T(4,128)S(1)}, f32[5,4,4,128]{3,2,1,0:T(4,128)}, u32[]{:S(2)}) copy-start(f32[5,4,4,128]{3,2,1,0:T(4,128)} %get-tuple-element.8) | copy-start | bytes 122884
  10.5 7.5 %copy-start.1 = (f32[5,4,4,128]{3,2,1,0:T(4,128)S(1)}, f32[5,4,4,128]{3,2,1,0:T(4,128)}, u32[]{:S(2)}) copy-start(f32[5,4,4,128]{3,2,1,0:T(4,128)} %get-tuple-element.7) | copy-start | bytes 122884
  10.5 15.6 %all-to-all-start = ((f32[16,5,4,128]{3,2,1,0:T(4,128)}), f32[16,5,4,128]{3,2,1,0:T(4,128)S(1)}, u32[]{:S(2)}, u32[]{:S(2)}) async-start(f32[16,5,4,128]{3,2,1,0:T(4,128)} %select_select_fusion), calls=%async_computation | async-start | bytes 327680 | tf_op jit(solution)/shard_map/all_to_all | solution.py:438
  18.0 10.3 %collective-permute-start = (f32[5,4,4,128]{3,2,1,0:T(4,128)S(1)}, f32[5,4,4,128]{3,2,1,0:T(4,128)S(1)}, u32[]{:S(2)}, u32[]{:S(2)}) collective-permute-start(f32[5,4,4,128]{3,2,1,0:T(4,128)S(1)} %bitcast.84), channel_id=1, source_target_pairs={{0,8},{8,0},{1,9},{9,1},{2,10},{10,2},{3,11},{11,3},{4,12},{12,4},... | collective-permute-start | bytes 122888 | tf_op jit(solution)/shard_map/ppermute | solution.py:395
  28.4 0.6 %copy-start.2 = (f32[5,4,4,128]{3,2,1,0:T(4,128)}, f32[5,4,4,128]{3,2,1,0:T(4,128)S(1)}, u32[]{:S(2)}) copy-start(f32[5,4,4,128]{3,2,1,0:T(4,128)S(1)} %collective-permute-done.first_ref) | copy-start | bytes 122884

commit v13 on v12

--- a/solution.py
+++ b/solution.py
@@ -254,32 +254,103 @@
         own_ref[chan] = exact_dot(rows, pick)[:, : EA * ET]
 
 
-def rate_kernel_single(body, adj_ref, flow_ref, first_ref, *rest):
-    return body(adj_ref, flow_ref, first_ref, None, *rest)
-
-
-def rate_kernel(
-    adj_ref, flow_ref, first_ref, second_ref, up_az_ref, down_az_ref, sides_ref,
-    rate_ref, next_ref,
-):
+def flow_terms(flow_ref):
+    prim = [flow_ref[0, chan].astype(jnp.float32) for chan in range(5)]
+    density = prim[0]
+    speed_sq = prim[1] * prim[1] + prim[2] * prim[2] + prim[3] * prim[3]
+    energy = prim[4] / (GAMMA - 1.0) + 0.5 * density * speed_sq
+    momentum = [density * prim[1 + k] for k in range(3)]
+    velocity = [momentum[k] / density for k in range(3)]
+    kinetic = momentum[0] * velocity[0] + momentum[1] * velocity[1] + momentum[2] * velocity[2]
+    pressure = (GAMMA - 1.0) * (energy - 0.5 * kinetic)
+    enthalpy = (energy + pressure) / density
+    vel_sq = velocity[0] * velocity[0] + velocity[1] * velocity[1] + velocity[2] * velocity[2]
+    return velocity, enthalpy, vel_sq
+
+
+def flux_transpose(grad, cot, direction, velocity, enthalpy, vel_sq):
+    normal = velocity[direction]
+    dotted = cot[1] * velocity[0] + cot[2] * velocity[1] + cot[3] * velocity[2] + cot[4] * enthalpy
+    weight = cot[1 + direction] + cot[4] * normal
+    terms = [
+        0.5 * (GAMMA - 1.0) * vel_sq * weight - dotted * normal,
+        None,
+        None,
+        None,
+        (GAMMA - 1.0) * weight + cot[4] * normal,
+    ]
+    for k in range(3):
+        term = cot[1 + k] * normal - (GAMMA - 1.0) * weight * velocity[k]
+        if k == direction:
+            term = term + (cot[0] + dotted)
+        terms[1 + k] = term
+    return [terms[c] if grad[c] is None else grad[c] + terms[c] for c in range(5)]
+
+
+def early_kernel(adj_ref, flow_ref, first_ref, *rest):
+    if len(rest) == 2:
+        second_ref, grad_ref = rest
+    else:
+        second_ref, grad_ref = None, rest[0]
+    derivs, left_vals, right_vals, left_corr, right_corr = basis_tables()
+    shape = (4, 4, 4, 128)
+    lane = lax.broadcasted_iota(jnp.int32, shape, 3)
+    flat_lane = lax.broadcasted_iota(jnp.int32, (4, 4, 128), 2)
+    radial_lane = lane % ER
+    even = lax.axis_index("axial") % 2 == 0
+    brackets = [[None] * 5 for _ in range(3)]
+    for chan in range(5):
+        field = adj_ref[0, chan]
+        first = first_ref[chan]
+        second = first * 0.0 if second_ref is None else second_ref[chan]
+        up_ax = jnp.where(even, first, second)
+        down_ax = jnp.where(even, second, first)
+        left0 = sweep(field, left_corr, lambda i: (i,))
+        right0 = sweep(field, right_corr, lambda i: (i,))
+        next0 = lane_roll(jnp.where(flat_lane < ET * ER, up_ax, left0), -ET * ER)
+        prev0 = lane_roll(jnp.where(flat_lane >= (EA - 1) * ET * ER, down_ax, right0), ET * ER)
+        jump_r = 0.5 * (next0 - right0)
+        jump_l = 0.5 * (prev0 - left0)
+        slabs = []
+        for target in range(4):
+            slab = sweep(field, [derivs[i][target] for i in range(4)], lambda i: (i,))
+            slabs.append(slab + jump_r * float(right_vals[target]) + jump_l * float(left_vals[target]))
+        brackets[0][chan] = jnp.stack(slabs, axis=0)
+        points = [jnp.broadcast_to(field[:, :, i : i + 1, :], shape) for i in range(4)]
+        left2 = sweep(points, left_corr, lambda i: i)
+        right2 = sweep(points, right_corr, lambda i: i)
+        next2 = jnp.where(radial_lane == ER - 1, 0.0, lane_roll(left2, -1))
+        prev2 = jnp.where(radial_lane == 0, 0.0, lane_roll(right2, 1))
+        bracket = 0.5 * (next2 - right2) * column(right_vals, shape)
+        bracket = bracket + 0.5 * (prev2 - left2) * column(left_vals, shape)
+        for source in range(4):
+            bracket = bracket + points[source] * column(derivs[source], shape)
+        brackets[2][chan] = bracket
+    velocity, enthalpy, vel_sq = flow_terms(flow_ref)
+    grad = [None] * 5
+    for direction in (0, 2):
+        grad = flux_transpose(grad, brackets[direction], direction, velocity, enthalpy, vel_sq)
+    for chan in range(5):
+        grad_ref[0, chan] = grad[chan]
+
+
+def late_kernel(adj_ref, flow_ref, grad_ref, up_az_ref, down_az_ref, sides_ref, rate_ref, next_ref):
     derivs, left_vals, right_vals, left_corr, right_corr = basis_tables()
     shape = (4, 4, 4, 128)
     lane = lax.broadcasted_iota(jnp.int32, shape, 3)
     flat_lane = lax.broadcasted_iota(jnp.int32, (4, 4, 128), 2)
     az_flat = flat_lane // ER % ET
     radial_lane = lane % ER
-    brackets = [[None] * 5 for _ in range(3)]
     col = lax.broadcasted_iota(jnp.int32, (16, 128), 1)
     row = lax.broadcasted_iota(jnp.int32, (16, 128), 0)
     sides = sides_ref[...]
-    even = lax.axis_index("axial") % 2 == 0
     rotor = lax.axis_index("zone") == 0
     spread = [
         exact_dot(sides, jnp.where(row == col // ER % ET * 4 + azim, 1.0, 0.0)) for azim in range(4)
     ]
     group = lax.broadcasted_iota(jnp.int32, (1, 128), 1) // (ET * ER)
 
-    def side_face(side, chan):
+    def side_face(chan):
         blocks = []
         for axial in range(4):
             slabs = []
@@ -293,84 +364,34 @@
             blocks.append(jnp.stack(slabs, axis=0))
         return jnp.stack(blocks, axis=0)
 
+    azim_b = [None] * 5
+    radial_b = [None] * 5
     for chan in range(5):
         field = adj_ref[0, chan]
-        own_face = side_face(0, chan)
-        outer_face = jnp.where(rotor, own_face, 0.0)
-        inner_face = jnp.where(rotor, 0.0, own_face)
-        first = first_ref[chan]
-        second = first * 0.0 if second_ref is None else second_ref[chan]
-        up_ax = jnp.where(even, first, second)
-        down_ax = jnp.where(even, second, first)
+        own_face = side_face(chan)
+        outer_face = jnp.where(rotor & (radial_lane == ER - 1), own_face, 0.0)
+        inner_face = jnp.where(rotor | (radial_lane != 0), 0.0, own_face)
+        radial_b[chan] = 0.5 * outer_face * column(right_vals, shape) + 0.5 * inner_face * column(
+            left_vals, shape
+        )
         up_az = expand_face(up_az_ref[chan], 0)
         down_az = expand_face(down_az_ref[chan], ET - 1)
-        left0 = sweep(field, left_corr, lambda i: (i,))
-        right0 = sweep(field, right_corr, lambda i: (i,))
-        next0 = lane_roll(jnp.where(flat_lane < ET * ER, up_ax, left0), -ET * ER)
-        prev0 = lane_roll(jnp.where(flat_lane >= (EA - 1) * ET * ER, down_ax, right0), ET * ER)
-        jump_r = 0.5 * (next0 - right0)
-        jump_l = 0.5 * (prev0 - left0)
-        slabs = []
-        for target in range(4):
-            slab = sweep(field, [derivs[i][target] for i in range(4)], lambda i: (i,))
-            slabs.append(slab + jump_r * float(right_vals[target]) + jump_l * float(left_vals[target]))
-        brackets[0][chan] = jnp.stack(slabs, axis=0)
         pick1 = lambda i: (slice(None), i)
         left1 = sweep(field, left_corr, pick1)
         right1 = sweep(field, right_corr, pick1)
-        next1 = lane_roll(
-            jnp.where(az_flat == 0, lane_roll(up_az, ET * ER), left1), -ER
-        )
-        prev1 = lane_roll(
-            jnp.where(az_flat == ET - 1, lane_roll(down_az, -ET * ER), right1), ER
-        )
+        next1 = lane_roll(jnp.where(az_flat == 0, lane_roll(up_az, ET * ER), left1), -ER)
+        prev1 = lane_roll(jnp.where(az_flat == ET - 1, lane_roll(down_az, -ET * ER), right1), ER)
         jump_r = 0.5 * (next1 - right1)
         jump_l = 0.5 * (prev1 - left1)
         slabs = []
         for target in range(4):
             slab = sweep(field, [derivs[i][target] for i in range(4)], pick1)
             slabs.append(slab + jump_r * float(right_vals[target]) + jump_l * float(left_vals[target]))
-        brackets[1][chan] = jnp.stack(slabs, axis=1)
-        points = [jnp.broadcast_to(field[:, :, i : i + 1, :], shape) for i in range(4)]
-        left2 = sweep(points, left_corr, lambda i: i)
-        right2 = sweep(points, right_corr, lambda i: i)
-        next2 = jnp.where(radial_lane == ER - 1, outer_face, lane_roll(left2, -1))
-        prev2 = jnp.where(radial_lane == 0, inner_face, lane_roll(right2, 1))
-        bracket = 0.5 * (next2 - right2) * column(right_vals, shape)
-        bracket = bracket + 0.5 * (prev2 - left2) * column(left_vals, shape)
-        for source in range(4):
-            bracket = bracket + points[source] * column(derivs[source], shape)
-        brackets[2][chan] = bracket
-    prim = [flow_ref[0, chan].astype(jnp.float32) for chan in range(5)]
-    density = prim[0]
-    speed_sq = prim[1] * prim[1] + prim[2] * prim[2] + prim[3] * prim[3]
-    energy = prim[4] / (GAMMA - 1.0) + 0.5 * density * speed_sq
-    momentum = [density * prim[1 + k] for k in range(3)]
-    velocity = [momentum[k] / density for k in range(3)]
-    kinetic = momentum[0] * velocity[0] + momentum[1] * velocity[1] + momentum[2] * velocity[2]
-    pressure = (GAMMA - 1.0) * (energy - 0.5 * kinetic)
-    enthalpy = (energy + pressure) / density
-    vel_sq = velocity[0] * velocity[0] + velocity[1] * velocity[1] + velocity[2] * velocity[2]
-    grad = [None] * 5
-    for direction in range(3):
-        cot = brackets[direction]
-        normal = velocity[direction]
-        dotted = cot[1] * velocity[0] + cot[2] * velocity[1] + cot[3] * velocity[2] + cot[4] * enthalpy
-        weight = cot[1 + direction] + cot[4] * normal
-        terms = [
-            0.5 * (GAMMA - 1.0) * vel_sq * weight - dotted * normal,
-            None,
-            None,
-            None,
-            (GAMMA - 1.0) * weight + cot[4] * normal,
-        ]
-        for k in range(3):
-            term = cot[1 + k] * normal - (GAMMA - 1.0) * weight * velocity[k]
-            if k == direction:
-                term = term + (cot[0] + dotted)
-            terms[1 + k] = term
-        for chan in range(5):
-            grad[chan] = terms[chan] if grad[chan] is None else grad[chan] + terms[chan]
+        azim_b[chan] = jnp.stack(slabs, axis=1)
+    velocity, enthalpy, vel_sq = flow_terms(flow_ref)
+    grad = [grad_ref[0, chan] for chan in range(5)]
+    grad = flux_transpose(grad, azim_b, 1, velocity, enthalpy, vel_sq)
+    grad = flux_transpose(grad, radial_b, 2, velocity, enthalpy, vel_sq)
     for chan in range(5):
         rate = -METRIC * grad[chan]
         rate_ref[0, chan] = rate
@@ -451,14 +472,11 @@
     incoming = shift_sum(window, coefs, TP)
     sides = jnp.where(is_rotor, returned, incoming).reshape(5 * AP, TP)
     field_shape = jax.ShapeDtypeStruct(adjoint.shape, jnp.float32)
-    operands = (adjoint, flow_prim, got_first, got_second, up_az, down_az, sides)
-    kernel = rate_kernel
-    if got_second is None:
-        operands = (adjoint, flow_prim, got_first, up_az, down_az, sides)
-        kernel = functools.partial(rate_kernel_single, rate_kernel)
-    adjoint_rate, next_adjoint = pl.pallas_call(
-        kernel, out_shape=(field_shape, field_shape)
-    )(*operands)
+    early_in = (adjoint, flow_prim, got_first) + (() if got_second is None else (got_second,))
+    partial = pl.pallas_call(early_kernel, out_shape=field_shape)(*early_in)
+    adjoint_rate, next_adjoint = pl.pallas_call(late_kernel, out_shape=(field_shape, field_shape))(
+        adjoint, flow_prim, partial, up_az, down_az, sides
+    )
     return (adjoint_rate, next_adjoint)
 
 

time: 32.6 us -> 31.4 us (0.963)
  waiting for transfers between devices: 6.5 us -> 3.49 us
  Pallas kernels: 5.29 us -> 7.05 us
    all_to_all x1, waiting for transfers between devices: 6.5 us -> 1.01 us  [local(): got = lax.all_to_all(chunks, ('zone', 'azim'), 0, 0)]
    ppermute x1, waiting for transfers between devices: 0.01 us -> 2.48 us  [local(): got_first = lax.ppermute(jnp.where(even, right_ax, left_ax), 'axial', first)]
    pallas_call x1 -> x2, Pallas kernels: 3.18 us -> 4.95 us  [the longest x1 2.55 us: local(): pl.pallas_call(late_kernel, out_shape=(field_shape, field_shape))]
  transfers between devices with their start and end apart: 2 -> 2, of which waited for: 1 -> 2; matrix products, arithmetic and copies ran while one was open for 7% -> 0% of each run, Pallas kernels for 0% -> 8%
where the time goes in v13:
time: 31.4 us; the launch traced here: 30.9 us
  starting transfers between devices  9.07 us (29%)
  Pallas kernels  7.05 us (22%)
  local copies, waits for them, and re-layouts  6.26 us (20%)
  waiting for transfers between devices  3.49 us (11%)
  other arithmetic  3.46 us (11%)
  between operations  1.58 us (5%)
    all_to_all x1, starting transfers between devices, local(): got = lax.all_to_all(chunks, ('zone', 'azim'), 0, 0)  7.49 us
    pallas_call x1, Pallas kernels, local(): pl.pallas_call(late_kernel, out_shape=(field_shape, field_shape))  2.55 us
    unnamed x16, local copies, waits for them, and re-layouts  2.54 us
    ppermute x1, waiting for transfers between devices, local(): got_first = lax.ppermute(jnp.where(even, right_ax, left_ax), 'axial', first)  2.48 us
    pallas_call x1, Pallas kernels, local(): partial = pl.pallas_call(early_kernel, out_shape=field_shape)(*early_in)  2.39 us
    pallas_call x1, Pallas kernels, local(): pl.pallas_call(moment_kernel, out_shape=(face4, face4, chunk, chunk, jax....  2.11 us
    ppermute x1, starting transfers between devices, local(): got_first = lax.ppermute(jnp.where(even, right_ax, left_ax), 'axial', first)  1.58 us
    select_n x1, other arithmetic, local(): sides = jnp.where(is_rotor, returned, incoming).reshape(5 * AP, TP)  1.35 us
  transfers between devices with their start and end apart: 2, of which 2 were waited for; matrix products, arithmetic and copies ran while one was open for 0% of the time, Pallas kernels for 8%

profile of v13, /device:TPU:0, one launch (start us, length us, event | category | flops | bytes accessed | tf_op | source)
XLA Modules:
  0.0 30.9 jit_solution(6406774876782642884)
XLA Ops:
  1.4 2.1 %shard_map.77 = (f32[5,4,4,128]{3,2,1,0:T(4,128)}, f32[5,4,4,128]{3,2,1,0:T(4,128)}, f32[5,4,128]{2,1,0:T(4,128)}, f32[5,4,128]{2,1,0:T(4,128)}, f32[5,16,16]{2,1,0:T(8,128)}) custom-call(f32[1,5,4,4,4,128]{5,4,3,2,1,0:T(4,128)} %adj_ref.5), custom_call_target="tpu_custom_call" | custom-call | tf_op jit(solution)/shard_map/pallas_call | solution.py:407
  3.5 0.9 %reshape.124 = f32[5,4,4,4,4]{4,3,2,1,0:T(4,128)S(1)} reshape(f32[5,16,16]{2,1,0:T(8,128)} %get-tuple-element.11) | data formatting | bytes 10240 | tf_op jit(solution)/shard_map/reshape | solution.py:421
  4.4 0.6 %copy.11 = f32[5,4,4,4,4]{4,3,2,1,0:T(4,128)S(1)} copy(f32[5,4,4,4,4]{3,1,4,2,0:T(4,128)S(1)} %bitcast.80) | data formatting | bytes 10240 | tf_op jit(solution)/shard_map/transpose | solution.py:421
  5.0 0.2 broadcast_in_dim.160
  5.2 0.1 reshape.125
  5.3 0.7 %copy-done.5 = s32[4,256]{1,0:T(4,128)S(1)} copy-done((s32[4,256]{1,0:T(4,128)S(1)}, s32[4,256]{1,0:T(4,128)}, u32[]{:S(2)}) %copy-start.5) | copy-done | bytes 4120
  6.0 0.7 %copy-done.6 = s32[4,256]{1,0:T(4,128)S(1)} copy-done((s32[4,256]{1,0:T(4,128)S(1)}, s32[4,256]{1,0:T(4,128)}, u32[]{:S(2)}) %copy-start.6) | copy-done | bytes 4120
  6.7 0.4 %select_reduce_fusion = f32[4,256]{1,0:T(4,128)S(1)} fusion(f32[128]{0:T(128)S(1)} %copy-done.7, s32[4,256]{1,0:T(4,128)S(1)} %copy-done.6), kind=kLoop, calls=%fused_computation | loop fusion | flops 392192 | bytes 8704 | tf_op jit(solution)/shard_map/reduce_sum | solution.py:424
  7.7 0.2 select_add_fusion
  8.0 0.1 broadcast_multiply_fusion.30
  8.1 0.4 %pad_add_fusion = f32[5,16,48]{2,1,0:T(8,128)S(1)} fusion(f32[5,16,16]{2,1,0:T(8,128)S(1)} %get-tuple-element.60, f32[5,16,16]{2,1,0:T(8,128)S(1)} %get-tuple-element.61, f32[5,16,16]{2,1,0:T(8,128)S(1)} %get-tuple-element.62, f32[5,16,16]{2,1,0:T(8,128)S(1)} %get-tuple-element.63, f32[5,16,16]{2,1,0:T(8,128)S(1)} %get-tuple-element.64, ...), kind=kLoop, calls=%fused_computation.123 | loop fusion | flops 115200 | bytes 174080 | tf_op jit(solution)/shard_map/add | solution.py:439
  8.6 0.1 broadcast_in_dim.174
  9.0 0.1 select_select_fusion.1
  9.1 0.6 %copy-done.3 = f32[5,4,128]{2,1,0:T(4,128)S(1)} copy-done((f32[5,4,128]{2,1,0:T(4,128)S(1)}, f32[5,4,128]{2,1,0:T(4,128)}, u32[]{:S(2)}) %copy-start.3) | copy-done | bytes 10264
  9.7 0.8 %select_select_fusion = f32[16,5,4,128]{3,2,1,0:T(4,128)} fusion(f32[16,5,2,128]{3,2,1,0:T(2,128)S(1)} %select_select_fusion.1, f32[5,4,128]{2,1,0:T(4,128)S(1)} %copy-done.4, f32[5,4,128]{2,1,0:T(4,128)S(1)} %copy-done.3, pred[16]{0:T(512)(128)(4,1)S(1)} %get-tuple-element.92, pred[16]{0:T(512)(128)(4,1)S(1)} %get-tuple-element.90, ...), kind=kLoop, calls=%fused_computation.3 | loop fusion | flops 122880 | bytes 266288 | tf_op jit(solution)/shard_map/jit(_where)/select_n | solution.py:456
  10.5 7.5 %all-to-all-start = ((f32[16,5,4,128]{3,2,1,0:T(4,128)}), f32[16,5,4,128]{3,2,1,0:T(4,128)S(1)}, u32[]{:S(2)}, u32[]{:S(2)}) async-start(f32[16,5,4,128]{3,2,1,0:T(4,128)} %select_select_fusion), calls=%async_computation | async-start | bytes 327680 | tf_op jit(solution)/shard_map/all_to_all | solution.py:459
  18.0 1.6 %collective-permute-start = (f32[5,4,4,128]{3,2,1,0:T(4,128)S(1)}, f32[5,4,4,128]{3,2,1,0:T(4,128)S(1)}, u32[]{:S(2)}, u32[]{:S(2)}) collective-permute-start(f32[5,4,4,128]{3,2,1,0:T(4,128)S(1)} %bitcast.84), channel_id=1, source_target_pairs={{0,8},{8,0},{1,9},{9,1},{2,10},{10,2},{3,11},{11,3},{4,12},{12,4},... | collective-permute-start | bytes 122888 | tf_op jit(solution)/shard_map/ppermute | solution.py:416
  19.6 2.5 %collective-permute-done.first_ref = f32[5,4,4,128]{3,2,1,0:T(4,128)S(1)} collective-permute-done((f32[5,4,4,128]{3,2,1,0:T(4,128)S(1)}, f32[5,4,4,128]{3,2,1,0:T(4,128)S(1)}, u32[]{:S(2)}, u32[]{:S(2)}) %collective-permute-start) | collective-permute-done | bytes 40992 | tf_op jit(solution)/shard_map/ppermute | solution.py:416
  22.1 0.6 %copy-done = f32[5,4,4,128]{3,2,1,0:T(4,128)} copy-done((f32[5,4,4,128]{3,2,1,0:T(4,128)}, f32[5,4,4,128]{3,2,1,0:T(4,128)S(1)}, u32[]{:S(2)}) %copy-start) | copy-done | bytes 40984
  22.7 2.4 %shard_map.78.grad_ref = f32[1,5,4,4,4,128]{5,4,3,2,1,0:T(4,128)} custom-call(f32[1,5,4,4,4,128]{5,4,3,2,1,0:T(4,128)} %adj_ref.5, bf16[1,5,4,4,4,128]{5,4,3,2,1,0:T(4,128)(2,1)} %flow_ref.3, f32[5,4,4,128]{3,2,1,0:T(4,128)} %copy-done), custom_call_target="tpu_custom_call" | custom-call | tf_op jit(solution)/shard_map/pallas_call | solution.py:476
  25.1 1.0 %all-to-all-done = f32[16,5,4,128]{3,2,1,0:T(4,128)S(1)} async-done(((f32[16,5,4,128]{3,2,1,0:T(4,128)}), f32[16,5,4,128]{3,2,1,0:T(4,128)S(1)}, u32[]{:S(2)}, u32[]{:S(2)}) %all-to-all-start) | async-done | bytes 163872 | tf_op jit(solution)/shard_map/all_to_all | solution.py:459
  26.1 0.6 %dynamic-slice_bitcast_fusion.2 = (f32[5,4,128]{2,1,0:T(4,128)S(1)}, f32[5,4,128]{2,1,0:T(4,128)S(1)}, f32[5,4,128]{2,1,0:T(4,128)S(1)}, f32[5,4,128]{2,1,0:T(4,128)}, f32[5,4,128]{2,1,0:T(4,128)}) fusion(f32[16,5,4,128]{3,2,1,0:T(4,128)S(1)} %all-to-all-done, s32[]{:T(128)S(6)} %select_n.205, s32[]{:T(128)S(6)} %select_n.209, s32[]{:T(128)S(6)} %select_n.207, ...), kind=kLoop, calls=%fused_computation.158 | loop fusion | bytes 102420 | tf_op jit(solution)/shard_map/jit(dynamic_index_in_dim)/squeeze | solution.py:465
  27.0 1.4 %fusion.2 = f32[5,16,16]{2,1,0:T(8,128)} fusion(f32[5,16,16]{2,1,0:T(8,128)S(1)} %reshape.128, f32[5,16,16]{2,1,0:T(8,128)S(1)} %reshape.127, f32[5,16,16]{2,1,0:T(8,128)S(1)} %reshape.126, f32[16,16]{1,0:T(8,128)S(1)} %get-tuple-element.21, f32[16,16]{1,0:T(8,128)S(1)} %get-tuple-element.22, f32[16,16]{1,0:T(8,128)S(1)} %get-tuple-element.23, ...), kind=kLoop, calls=%fused_computation.8 | loop fusion | flops 119040 | bytes 52225 | tf_op jit(solution)/shard_map/jit(_where)/select_n | solution.py:473
  28.4 2.6 %shard_map.79 = (f32[1,5,4,4,4,128]{5,4,3,2,1,0:T(4,128)}, f32[1,5,4,4,4,128]{5,4,3,2,1,0:T(4,128)}) custom-call(f32[1,5,4,4,4,128]{5,4,3,2,1,0:T(4,128)} %adj_ref.5, bf16[1,5,4,4,4,128]{5,4,3,2,1,0:T(4,128)(2,1)} %flow_ref.3, f32[1,5,4,4,4,128]{5,4,3,2,1,0:T(4,128)} %shard_map.78.grad_ref, f32[5,4,128]{2,1,0:T(4,128)} %get-tuple-element.55.up_az_ref, ...), custom_call_target="tpu_custom_call" | custom-call | tf_op jit(solution)/shard_map/pallas_call | solution.py:477
  (40 shorter events, 1.3 us)
Async XLA Ops:
  5.3 0.7 %copy-start.5 = (s32[4,256]{1,0:T(4,128)S(1)}, s32[4,256]{1,0:T(4,128)}, u32[]{:S(2)}) copy-start(s32[4,256]{1,0:T(4,128)} %param.8) | copy-start | bytes 12292
  6.0 0.7 %copy-start.6 = (s32[4,256]{1,0:T(4,128)S(1)}, s32[4,256]{1,0:T(4,128)}, u32[]{:S(2)}) copy-start(s32[4,256]{1,0:T(4,128)} %param.9) | copy-start | bytes 12292
  6.0 0.7 %copy-start.7 = (f32[128]{0:T(128)S(1)}, f32[128]{0:T(128)}, u32[]{:S(2)}) copy-start(f32[128]{0:T(128)} %param.10) | copy-start | bytes 1540
  9.0 0.7 %copy-start.3 = (f32[5,4,128]{2,1,0:T(4,128)S(1)}, f32[5,4,128]{2,1,0:T(4,128)}, u32[]{:S(2)}) copy-start(f32[5,4,128]{2,1,0:T(4,128)} %get-tuple-element.9) | copy-start | bytes 30724
  9.0 0.7 %copy-start.4 = (f32[5,4,128]{2,1,0:T(4,128)S(1)}, f32[5,4,128]{2,1,0:T(4,128)}, u32[]{:S(2)}) copy-start(f32[5,4,128]{2,1,0:T(4,128)} %get-tuple-element.10) | copy-start | bytes 30724
  10.5 7.5 %copy-start.1 = (f32[5,4,4,128]{3,2,1,0:T(4,128)S(1)}, f32[5,4,4,128]{3,2,1,0:T(4,128)}, u32[]{:S(2)}) copy-start(f32[5,4,4,128]{3,2,1,0:T(4,128)} %get-tuple-element.8) | copy-start | bytes 122884
  10.5 7.5 %copy-start.2 = (f32[5,4,4,128]{3,2,1,0:T(4,128)S(1)}, f32[5,4,4,128]{3,2,1,0:T(4,128)}, u32[]{:S(2)}) copy-start(f32[5,4,4,128]{3,2,1,0:T(4,128)} %get-tuple-element.7) | copy-start | bytes 122884
  10.5 15.6 %all-to-all-start = ((f32[16,5,4,128]{3,2,1,0:T(4,128)}), f32[16,5,4,128]{3,2,1,0:T(4,128)S(1)}, u32[]{:S(2)}, u32[]{:S(2)}) async-start(f32[16,5,4,128]{3,2,1,0:T(4,128)} %select_select_fusion), calls=%async_computation | async-start | bytes 327680 | tf_op jit(solution)/shard_map/all_to_all | solution.py:459
  18.0 4.1 %collective-permute-start = (f32[5,4,4,128]{3,2,1,0:T(4,128)S(1)}, f32[5,4,4,128]{3,2,1,0:T(4,128)S(1)}, u32[]{:S(2)}, u32[]{:S(2)}) collective-permute-start(f32[5,4,4,128]{3,2,1,0:T(4,128)S(1)} %bitcast.84), channel_id=1, source_target_pairs={{0,8},{8,0},{1,9},{9,1},{2,10},{10,2},{3,11},{11,3},{4,12},{12,4},... | collective-permute-start | bytes 122888 | tf_op jit(solution)/shard_map/ppermute | solution.py:416
  22.1 0.6 %copy-start = (f32[5,4,4,128]{3,2,1,0:T(4,128)}, f32[5,4,4,128]{3,2,1,0:T(4,128)S(1)}, u32[]{:S(2)}) copy-start(f32[5,4,4,128]{3,2,1,0:T(4,128)S(1)} %collective-permute-done.first_ref) | copy-start | bytes 122884

commit v14 on v13

--- a/solution.py
+++ b/solution.py
@@ -334,7 +334,7 @@
         grad_ref[0, chan] = grad[chan]
 
 
-def late_kernel(adj_ref, flow_ref, grad_ref, up_az_ref, down_az_ref, sides_ref, rate_ref, next_ref):
+def late_kernel(adj_ref, flow_ref, grad_ref, up_az_ref, down_az_ref, returned_ref, incoming_ref, rate_ref, next_ref):
     derivs, left_vals, right_vals, left_corr, right_corr = basis_tables()
     shape = (4, 4, 4, 128)
     lane = lax.broadcasted_iota(jnp.int32, shape, 3)
@@ -343,8 +343,8 @@
     radial_lane = lane % ER
     col = lax.broadcasted_iota(jnp.int32, (16, 128), 1)
     row = lax.broadcasted_iota(jnp.int32, (16, 128), 0)
-    sides = sides_ref[...]
     rotor = lax.axis_index("zone") == 0
+    sides = jnp.where(rotor, returned_ref[...], incoming_ref[...])
     spread = [
         exact_dot(sides, jnp.where(row == col // ER % ET * 4 + azim, 1.0, 0.0)) for azim in range(4)
     ]
@@ -470,12 +470,11 @@
     returned = picked[0] + picked[1] + picked[2]
     window = jnp.concatenate(picked, axis=2)
     incoming = shift_sum(window, coefs, TP)
-    sides = jnp.where(is_rotor, returned, incoming).reshape(5 * AP, TP)
     field_shape = jax.ShapeDtypeStruct(adjoint.shape, jnp.float32)
     early_in = (adjoint, flow_prim, got_first) + (() if got_second is None else (got_second,))
     partial = pl.pallas_call(early_kernel, out_shape=field_shape)(*early_in)
     adjoint_rate, next_adjoint = pl.pallas_call(late_kernel, out_shape=(field_shape, field_shape))(
-        adjoint, flow_prim, partial, up_az, down_az, sides
+        adjoint, flow_prim, partial, up_az, down_az, returned.reshape(5 * AP, TP), incoming.reshape(5 * AP, TP)
     )
     return (adjoint_rate, next_adjoint)
 

time: 31.4 us -> 32.1 us (1.022)
  local copies, waits for them, and re-layouts: 6.26 us -> 6.94 us
    add x0 -> x1, other arithmetic: none -> 1.35 us  [shift_sum(): total = term if total is None else total + term]
    select_n x1 -> x0, other arithmetic: 1.35 us -> none  [local(): sides = jnp.where(is_rotor, returned, incoming).reshape(5 * AP, TP)]
    add x0 -> x1, local copies, waits for them, and re-layouts: none -> 0.7 us  [local(): returned = picked[0] + picked[1] + picked[2]]
where the time goes in v14:
time: 32.1 us; the launch traced here: 31.6 us
  starting transfers between devices  9.07 us (28%)
  Pallas kernels  7.08 us (22%)
  local copies, waits for them, and re-layouts  6.94 us (22%)
  waiting for transfers between devices  3.49 us (11%)
  other arithmetic  3.47 us (11%)
  between operations  1.57 us (5%)
    all_to_all x1, starting transfers between devices, local(): got = lax.all_to_all(chunks, ('zone', 'azim'), 0, 0)  7.49 us
    pallas_call x1, Pallas kernels, local(): pl.pallas_call(late_kernel, out_shape=(field_shape, field_shape))  2.58 us
    unnamed x16, local copies, waits for them, and re-layouts  2.54 us
    ppermute x1, waiting for transfers between devices, local(): got_first = lax.ppermute(jnp.where(even, right_ax, left_ax), 'axial', first)  2.48 us
    pallas_call x1, Pallas kernels, local(): partial = pl.pallas_call(early_kernel, out_shape=field_shape)(*early_in)  2.39 us
    pallas_call x1, Pallas kernels, local(): pl.pallas_call(moment_kernel, out_shape=(face4, face4, chunk, chunk, jax....  2.11 us
    ppermute x1, starting transfers between devices, local(): got_first = lax.ppermute(jnp.where(even, right_ax, left_ax), 'axial', first)  1.58 us
    add x1, other arithmetic, shift_sum(): total = term if total is None else total + term  1.35 us
  transfers between devices with their start and end apart: 2, of which 2 were waited for; matrix products, arithmetic and copies ran while one was open for 0% of the time, Pallas kernels for 8%

profile of v14, /device:TPU:0, one launch (start us, length us, event | category | flops | bytes accessed | tf_op | source)
XLA Modules:
  0.0 31.6 jit_solution(6778926573223770481)
XLA Ops:
  1.4 2.1 %shard_map.77 = (f32[5,4,4,128]{3,2,1,0:T(4,128)}, f32[5,4,4,128]{3,2,1,0:T(4,128)}, f32[5,4,128]{2,1,0:T(4,128)}, f32[5,4,128]{2,1,0:T(4,128)}, f32[5,16,16]{2,1,0:T(8,128)}) custom-call(f32[1,5,4,4,4,128]{5,4,3,2,1,0:T(4,128)} %adj_ref.5), custom_call_target="tpu_custom_call" | custom-call | tf_op jit(solution)/shard_map/pallas_call | solution.py:407
  3.5 0.9 %reshape.130 = f32[5,4,4,4,4]{4,3,2,1,0:T(4,128)S(1)} reshape(f32[5,16,16]{2,1,0:T(8,128)} %get-tuple-element.11) | data formatting | bytes 10240 | tf_op jit(solution)/shard_map/reshape | solution.py:421
  4.4 0.6 %copy.11 = f32[5,4,4,4,4]{4,3,2,1,0:T(4,128)S(1)} copy(f32[5,4,4,4,4]{3,1,4,2,0:T(4,128)S(1)} %bitcast.80) | data formatting | bytes 10240 | tf_op jit(solution)/shard_map/transpose | solution.py:421
  5.0 0.2 broadcast_in_dim.160
  5.2 0.1 reshape.131
  5.3 0.7 %copy-done.5 = s32[4,256]{1,0:T(4,128)S(1)} copy-done((s32[4,256]{1,0:T(4,128)S(1)}, s32[4,256]{1,0:T(4,128)}, u32[]{:S(2)}) %copy-start.5) | copy-done | bytes 4120
  6.0 0.7 %copy-done.6 = s32[4,256]{1,0:T(4,128)S(1)} copy-done((s32[4,256]{1,0:T(4,128)S(1)}, s32[4,256]{1,0:T(4,128)}, u32[]{:S(2)}) %copy-start.6) | copy-done | bytes 4120
  6.7 0.4 %select_reduce_fusion = f32[4,256]{1,0:T(4,128)S(1)} fusion(f32[128]{0:T(128)S(1)} %copy-done.7, s32[4,256]{1,0:T(4,128)S(1)} %copy-done.6), kind=kLoop, calls=%fused_computation | loop fusion | flops 392192 | bytes 8704 | tf_op jit(solution)/shard_map/reduce_sum | solution.py:424
  7.7 0.2 select_add_fusion
  8.1 0.4 %pad_add_fusion = f32[5,16,48]{2,1,0:T(8,128)S(1)} fusion(f32[5,16,16]{2,1,0:T(8,128)S(1)} %get-tuple-element.60, f32[5,16,16]{2,1,0:T(8,128)S(1)} %get-tuple-element.61, f32[5,16,16]{2,1,0:T(8,128)S(1)} %get-tuple-element.62, f32[5,16,16]{2,1,0:T(8,128)S(1)} %get-tuple-element.63, f32[5,16,16]{2,1,0:T(8,128)S(1)} %get-tuple-element.64, ...), kind=kLoop, calls=%fused_computation.122 | loop fusion | flops 115200 | bytes 174080 | tf_op jit(solution)/shard_map/add | solution.py:439
  8.6 0.1 broadcast_in_dim.174
  9.0 0.1 select_select_fusion.1
  9.1 0.6 %copy-done.3 = f32[5,4,128]{2,1,0:T(4,128)S(1)} copy-done((f32[5,4,128]{2,1,0:T(4,128)S(1)}, f32[5,4,128]{2,1,0:T(4,128)}, u32[]{:S(2)}) %copy-start.3) | copy-done | bytes 10264
  9.7 0.8 %select_select_fusion = f32[16,5,4,128]{3,2,1,0:T(4,128)} fusion(f32[16,5,2,128]{3,2,1,0:T(2,128)S(1)} %select_select_fusion.1, f32[5,4,128]{2,1,0:T(4,128)S(1)} %copy-done.4, f32[5,4,128]{2,1,0:T(4,128)S(1)} %copy-done.3, pred[16]{0:T(512)(128)(4,1)S(1)} %get-tuple-element.96, pred[16]{0:T(512)(128)(4,1)S(1)} %get-tuple-element.94, ...), kind=kLoop, calls=%fused_computation.3 | loop fusion | flops 122880 | bytes 266288 | tf_op jit(solution)/shard_map/jit(_where)/select_n | solution.py:456
  10.5 7.5 %all-to-all-start = ((f32[16,5,4,128]{3,2,1,0:T(4,128)}), f32[16,5,4,128]{3,2,1,0:T(4,128)S(1)}, u32[]{:S(2)}, u32[]{:S(2)}) async-start(f32[16,5,4,128]{3,2,1,0:T(4,128)} %select_select_fusion), calls=%async_computation | async-start | bytes 327680 | tf_op jit(solution)/shard_map/all_to_all | solution.py:459
  18.0 1.6 %collective-permute-start = (f32[5,4,4,128]{3,2,1,0:T(4,128)S(1)}, f32[5,4,4,128]{3,2,1,0:T(4,128)S(1)}, u32[]{:S(2)}, u32[]{:S(2)}) collective-permute-start(f32[5,4,4,128]{3,2,1,0:T(4,128)S(1)} %bitcast.84), channel_id=1, source_target_pairs={{0,8},{8,0},{1,9},{9,1},{2,10},{10,2},{3,11},{11,3},{4,12},{12,4},... | collective-permute-start | bytes 122888 | tf_op jit(solution)/shard_map/ppermute | solution.py:416
  19.6 2.5 %collective-permute-done.first_ref = f32[5,4,4,128]{3,2,1,0:T(4,128)S(1)} collective-permute-done((f32[5,4,4,128]{3,2,1,0:T(4,128)S(1)}, f32[5,4,4,128]{3,2,1,0:T(4,128)S(1)}, u32[]{:S(2)}, u32[]{:S(2)}) %collective-permute-start) | collective-permute-done | bytes 40992 | tf_op jit(solution)/shard_map/ppermute | solution.py:416
  22.1 0.6 %copy-done = f32[5,4,4,128]{3,2,1,0:T(4,128)} copy-done((f32[5,4,4,128]{3,2,1,0:T(4,128)}, f32[5,4,4,128]{3,2,1,0:T(4,128)S(1)}, u32[]{:S(2)}) %copy-start) | copy-done | bytes 40984
  22.7 2.4 %shard_map.78.grad_ref = f32[1,5,4,4,4,128]{5,4,3,2,1,0:T(4,128)} custom-call(f32[1,5,4,4,4,128]{5,4,3,2,1,0:T(4,128)} %adj_ref.5, bf16[1,5,4,4,4,128]{5,4,3,2,1,0:T(4,128)(2,1)} %flow_ref.3, f32[5,4,4,128]{3,2,1,0:T(4,128)} %copy-done), custom_call_target="tpu_custom_call" | custom-call | tf_op jit(solution)/shard_map/pallas_call | solution.py:475
  25.1 1.0 %all-to-all-done = f32[16,5,4,128]{3,2,1,0:T(4,128)S(1)} async-done(((f32[16,5,4,128]{3,2,1,0:T(4,128)}), f32[16,5,4,128]{3,2,1,0:T(4,128)S(1)}, u32[]{:S(2)}, u32[]{:S(2)}) %all-to-all-start) | async-done | bytes 163872 | tf_op jit(solution)/shard_map/all_to_all | solution.py:459
  26.1 0.6 %dynamic-slice_bitcast_fusion.2 = (f32[5,4,128]{2,1,0:T(4,128)S(1)}, f32[5,4,128]{2,1,0:T(4,128)S(1)}, f32[5,4,128]{2,1,0:T(4,128)S(1)}, f32[5,4,128]{2,1,0:T(4,128)}, f32[5,4,128]{2,1,0:T(4,128)}) fusion(f32[16,5,4,128]{3,2,1,0:T(4,128)S(1)} %all-to-all-done, s32[]{:T(128)S(6)} %select_n.196, s32[]{:T(128)S(6)} %select_n.200, s32[]{:T(128)S(6)} %select_n.198, ...), kind=kLoop, calls=%fused_computation.157 | loop fusion | bytes 102420 | tf_op jit(solution)/shard_map/jit(dynamic_index_in_dim)/squeeze | solution.py:465
  26.8 0.7 %add.481.returned_ref = f32[80,16]{1,0:T(8,128)} reshape(f32[5,2,128]{2,1,0:T(2,128)S(1)} %get-tuple-element.91) | data formatting | bytes 10240 | tf_op jit(solution)/shard_map/add | solution.py:470
  27.7 1.4 %fusion.1 = f32[5,16,16]{2,1,0:T(8,128)} fusion(f32[5,16,16]{2,1,0:T(8,128)S(1)} %reshape.134, f32[5,16,16]{2,1,0:T(8,128)S(1)} %reshape.133, f32[5,16,16]{2,1,0:T(8,128)S(1)} %reshape.132, f32[16,16]{1,0:T(8,128)S(1)} %get-tuple-element.21, f32[16,16]{1,0:T(8,128)S(1)} %get-tuple-element.22, f32[16,16]{1,0:T(8,128)S(1)} %get-tuple-element.23, ...), kind=kLoop, calls=%fused_computation.7 | loop fusion | flops 115200 | bytes 52224 | tf_op jit(solution)/shard_map/add | solution.py:169
  29.0 2.6 %shard_map.79 = (f32[1,5,4,4,4,128]{5,4,3,2,1,0:T(4,128)}, f32[1,5,4,4,4,128]{5,4,3,2,1,0:T(4,128)}) custom-call(f32[1,5,4,4,4,128]{5,4,3,2,1,0:T(4,128)} %adj_ref.5, bf16[1,5,4,4,4,128]{5,4,3,2,1,0:T(4,128)(2,1)} %flow_ref.3, f32[1,5,4,4,4,128]{5,4,3,2,1,0:T(4,128)} %shard_map.78.grad_ref, f32[5,4,128]{2,1,0:T(4,128)} %get-tuple-element.55.up_az_ref, ...), custom_call_target="tpu_custom_call" | custom-call | tf_op jit(solution)/shard_map/pallas_call | solution.py:476
  (39 shorter events, 1.4 us)
Async XLA Ops:
  5.3 0.7 %copy-start.5 = (s32[4,256]{1,0:T(4,128)S(1)}, s32[4,256]{1,0:T(4,128)}, u32[]{:S(2)}) copy-start(s32[4,256]{1,0:T(4,128)} %param.8) | copy-start | bytes 12292
  6.0 0.7 %copy-start.6 = (s32[4,256]{1,0:T(4,128)S(1)}, s32[4,256]{1,0:T(4,128)}, u32[]{:S(2)}) copy-start(s32[4,256]{1,0:T(4,128)} %param.9) | copy-start | bytes 12292
  6.0 0.7 %copy-start.7 = (f32[128]{0:T(128)S(1)}, f32[128]{0:T(128)}, u32[]{:S(2)}) copy-start(f32[128]{0:T(128)} %param.10) | copy-start | bytes 1540
  9.0 0.7 %copy-start.3 = (f32[5,4,128]{2,1,0:T(4,128)S(1)}, f32[5,4,128]{2,1,0:T(4,128)}, u32[]{:S(2)}) copy-start(f32[5,4,128]{2,1,0:T(4,128)} %get-tuple-element.9) | copy-start | bytes 30724
  9.0 0.7 %copy-start.4 = (f32[5,4,128]{2,1,0:T(4,128)S(1)}, f32[5,4,128]{2,1,0:T(4,128)}, u32[]{:S(2)}) copy-start(f32[5,4,128]{2,1,0:T(4,128)} %get-tuple-element.10) | copy-start | bytes 30724
  10.5 7.5 %copy-start.1 = (f32[5,4,4,128]{3,2,1,0:T(4,128)S(1)}, f32[5,4,4,128]{3,2,1,0:T(4,128)}, u32[]{:S(2)}) copy-start(f32[5,4,4,128]{3,2,1,0:T(4,128)} %get-tuple-element.8) | copy-start | bytes 122884
  10.5 7.5 %copy-start.2 = (f32[5,4,4,128]{3,2,1,0:T(4,128)S(1)}, f32[5,4,4,128]{3,2,1,0:T(4,128)}, u32[]{:S(2)}) copy-start(f32[5,4,4,128]{3,2,1,0:T(4,128)} %get-tuple-element.7) | copy-start | bytes 122884
  10.5 15.6 %all-to-all-start = ((f32[16,5,4,128]{3,2,1,0:T(4,128)}), f32[16,5,4,128]{3,2,1,0:T(4,128)S(1)}, u32[]{:S(2)}, u32[]{:S(2)}) async-start(f32[16,5,4,128]{3,2,1,0:T(4,128)} %select_select_fusion), calls=%async_computation | async-start | bytes 327680 | tf_op jit(solution)/shard_map/all_to_all | solution.py:459
  18.0 4.1 %collective-permute-start = (f32[5,4,4,128]{3,2,1,0:T(4,128)S(1)}, f32[5,4,4,128]{3,2,1,0:T(4,128)S(1)}, u32[]{:S(2)}, u32[]{:S(2)}) collective-permute-start(f32[5,4,4,128]{3,2,1,0:T(4,128)S(1)} %bitcast.84), channel_id=1, source_target_pairs={{0,8},{8,0},{1,9},{9,1},{2,10},{10,2},{3,11},{11,3},{4,12},{12,4},... | collective-permute-start | bytes 122888 | tf_op jit(solution)/shard_map/ppermute | solution.py:416
  22.1 0.6 %copy-start = (f32[5,4,4,128]{3,2,1,0:T(4,128)}, f32[5,4,4,128]{3,2,1,0:T(4,128)S(1)}, u32[]{:S(2)}) copy-start(f32[5,4,4,128]{3,2,1,0:T(4,128)S(1)} %collective-permute-done.first_ref) | copy-start | bytes 122884

commit v15 on v13

--- a/solution.py
+++ b/solution.py
@@ -229,7 +229,18 @@
     return jnp.dot(left, right, precision=lax.Precision.HIGHEST, preferred_element_type=jnp.float32)
 
 
-def moment_kernel(adj_ref, left_ax_ref, right_ax_ref, up_ref, down_ref, own_ref, scratch_ref):
+def moment_kernel(
+    adj_ref, shift_ref, index_ref, table_ref, offset_ref,
+    left_ax_ref, right_ax_ref, up_ref, down_ref, own_ref, weight_ref, place_ref, scratch_ref,
+):
+    index = index_ref[...]
+    weight = jnp.zeros(index.shape, jnp.float32)
+    for entry in range(table_ref.shape[0]):
+        weight = jnp.where(index == entry, table_ref[entry], weight)
+    weight_ref[...] = weight
+    offset = offset_ref[0]
+    turn = (offset + TP // 2) // TP
+    place_ref[...] = shift_ref[...] + (offset - turn * TP)
     derivs, left_vals, right_vals, left_corr, right_corr = basis_tables()
     pick_outer = selector(128, 128, lambda k: k // ET * ET * ER + k % ET * ER + ER - 1, False)
     pick_inner = selector(128, 128, lambda k: k // ET * ET * ER + k % ET * ER, False)
@@ -404,11 +415,15 @@
     face4 = jax.ShapeDtypeStruct((5, 4, 4, 128), jnp.float32)
     chunk = jax.ShapeDtypeStruct((5, 4, 128), jnp.float32)
     rows16 = jax.ShapeDtypeStruct((5, 16, 128), jnp.float32)
-    left_ax, right_ax, upper_face, lower_face, own_face = pl.pallas_call(
+    left_ax, right_ax, upper_face, lower_face, own_face, weights_flat, places = pl.pallas_call(
         moment_kernel,
-        out_shape=(face4, face4, chunk, chunk, jax.ShapeDtypeStruct((5, 16, EA * ET), jnp.float32)),
+        out_shape=(face4, face4, chunk, chunk, jax.ShapeDtypeStruct((5, 16, EA * ET), jnp.float32),
+            jax.ShapeDtypeStruct(weight_index.shape, jnp.float32),
+            jax.ShapeDtypeStruct(intersection_shift.shape, jnp.int32),
+        ),
+        in_specs=[pl.BlockSpec(memory_space=pltpu.VMEM)] * 3 + [pl.BlockSpec(memory_space=pltpu.SMEM)] * 2,
         scratch_shapes=[pltpu.VMEM((2, 16, 128), jnp.float32)],
-    )(adjoint)
+    )(adjoint, intersection_shift, weight_index, mortar_weights, sector_offset)
     is_rotor = lax.axis_index("zone") == 0
     even = lax.axis_index("axial") % 2 == 0
     first = [(i, i + 1) for i in range(0, n_axial - 1, 2)] + [(i, i - 1) for i in range(1, n_axial, 2)]
@@ -419,15 +434,10 @@
     else:
         got_second = None
     own_rows = own_face.reshape(5, 4, 4, EA, ET).transpose(0, 3, 1, 4, 2).reshape(5, AP, TP)
-    shifts_local = intersection_shift.reshape(INTERSECTIONS, AP, TP)
-    table_match = weight_index[:, :, None] == jnp.arange(NW, dtype=jnp.int32)[None, None, :]
-    weights_local = jnp.sum(
-        jnp.where(table_match, mortar_weights[None, None, :], 0.0), axis=2
-    ).reshape(INTERSECTIONS, AP, TP)
+    weights_local = weights_flat.reshape(INTERSECTIONS, AP, TP)
     offset = sector_offset[0]
     turn = (offset + TP // 2) // TP
-    residue = offset - turn * TP
-    offsets_k = residue + shifts_local
+    offsets_k = places.reshape(INTERSECTIONS, AP, TP)
     rel_all = jnp.arange(-TP, TP - 1, dtype=jnp.int32)[:, None, None]
     coef_all = jnp.where(offsets_k[0][None] == rel_all, weights_local[0][None], 0.0)
     for member in range(1, INTERSECTIONS):

time: 31.4 us -> 30.9 us (0.984)
  other arithmetic: 3.46 us -> 3.08 us
    reduce_sum x1 -> x0, other arithmetic: 0.38 us -> none  [local(): jnp.sum(jnp.where(table_match, mortar_weights[None, None, :], 0.0), axis=2)]
    unnamed x16 -> x14, local copies, waits for them, and re-layouts: 2.54 us -> 2.4 us
where the time goes in v15:
time: 30.9 us; the launch traced here: 30.4 us
  starting transfers between devices  9.07 us (29%)
  Pallas kernels  7.09 us (23%)
  local copies, waits for them, and re-layouts  6.12 us (20%)
  waiting for transfers between devices  3.49 us (11%)
  other arithmetic  3.08 us (10%)
  between operations  1.56 us (5%)
    all_to_all x1, starting transfers between devices, local(): got = lax.all_to_all(chunks, ('zone', 'azim'), 0, 0)  7.49 us
    pallas_call x1, Pallas kernels, local(): pl.pallas_call(late_kernel, out_shape=(field_shape, field_shape))  2.55 us
    ppermute x1, waiting for transfers between devices, local(): got_first = lax.ppermute(jnp.where(even, right_ax, left_ax), 'axial', first)  2.48 us
    unnamed x14, local copies, waits for them, and re-layouts  2.4 us
    pallas_call x1, Pallas kernels, local(): partial = pl.pallas_call(early_kernel, out_shape=field_shape)(*early_in)  2.39 us
    pallas_call x1, Pallas kernels, local(): pl.pallas_call(moment_kernel, out_shape=(face4, face4, chunk, chunk, jax....  2.14 us
    ppermute x1, starting transfers between devices, local(): got_first = lax.ppermute(jnp.where(even, right_ax, left_ax), 'axial', first)  1.58 us
    select_n x1, other arithmetic, local(): sides = jnp.where(is_rotor, returned, incoming).reshape(5 * AP, TP)  1.35 us
  transfers between devices with their start and end apart: 2, of which 2 were waited for; matrix products, arithmetic and copies ran while one was open for 0% of the time, Pallas kernels for 8%

profile of v15, /device:TPU:0, one launch (start us, length us, event | category | flops | bytes accessed | tf_op | source)
XLA Modules:
  0.0 30.4 jit_solution(5769419999687827570)
XLA Ops:
  1.4 2.1 %shard_map.77 = (f32[5,4,4,128]{3,2,1,0:T(4,128)}, f32[5,4,4,128]{3,2,1,0:T(4,128)}, f32[5,4,128]{2,1,0:T(4,128)}, f32[5,4,128]{2,1,0:T(4,128)}, f32[5,16,16]{2,...) custom-call(f32[1,5,4,4,4,128]{5,4,3,2,1,0:T(4,128)} %adj_ref.5, s32[4,256]{1,0:T(4,128)} %shift_ref.1, ...), custom_call_target="tpu_custom_call" | custom-call | tf_op jit(solution)/shard_map/pallas_call | solution.py:418
  3.5 0.9 %reshape.122 = f32[5,4,4,4,4]{4,3,2,1,0:T(4,128)S(1)} reshape(f32[5,16,16]{2,1,0:T(8,128)} %get-tuple-element.13) | data formatting | bytes 10240 | tf_op jit(solution)/shard_map/reshape | solution.py:436
  4.4 0.6 %copy.9 = f32[5,4,4,4,4]{4,3,2,1,0:T(4,128)S(1)} copy(f32[5,4,4,4,4]{3,1,4,2,0:T(4,128)S(1)} %bitcast.78) | data formatting | bytes 10240 | tf_op jit(solution)/shard_map/transpose | solution.py:436
  5.0 0.2 broadcast_in_dim.145
  5.2 0.1 reshape.123
  5.4 0.5 %copy-done.6 = s32[4,256]{1,0:T(4,128)S(1)} copy-done((s32[4,256]{1,0:T(4,128)S(1)}, s32[4,256]{1,0:T(4,128)}, u32[]{:S(2)}) %copy-start.6) | copy-done | bytes 4120
  5.9 0.7 %copy-done.5 = f32[4,256]{1,0:T(4,128)S(1)} copy-done((f32[4,256]{1,0:T(4,128)S(1)}, f32[4,256]{1,0:T(4,128)}, u32[]{:S(2)}) %copy-start.5) | copy-done | bytes 4120
  7.2 0.2 select_add_fusion
  7.5 0.1 broadcast_multiply_fusion.30
  7.6 0.4 %pad_add_fusion = f32[5,16,48]{2,1,0:T(8,128)S(1)} fusion(f32[5,16,16]{2,1,0:T(8,128)S(1)} %get-tuple-element.64, f32[5,16,16]{2,1,0:T(8,128)S(1)} %get-tuple-element.65, f32[5,16,16]{2,1,0:T(8,128)S(1)} %get-tuple-element.66, f32[5,16,16]{2,1,0:T(8,128)S(1)} %get-tuple-element.67, f32[5,16,16]{2,1,0:T(8,128)S(1)} %get-tuple-element.68, ...), kind=kLoop, calls=%fused_computation.121 | loop fusion | flops 115200 | bytes 174080 | tf_op jit(solution)/shard_map/add | solution.py:449
  8.1 0.1 broadcast_in_dim.157
  8.3 0.1 broadcast_in_dim.160
  8.5 0.1 select_select_fusion.1
  8.6 0.6 %copy-done.3 = f32[5,4,128]{2,1,0:T(4,128)S(1)} copy-done((f32[5,4,128]{2,1,0:T(4,128)S(1)}, f32[5,4,128]{2,1,0:T(4,128)}, u32[]{:S(2)}) %copy-start.3) | copy-done | bytes 10264
  9.2 0.8 %select_select_fusion = f32[16,5,4,128]{3,2,1,0:T(4,128)} fusion(f32[16,5,2,128]{3,2,1,0:T(2,128)S(1)} %select_select_fusion.1, f32[5,4,128]{2,1,0:T(4,128)S(1)} %copy-done.4, f32[5,4,128]{2,1,0:T(4,128)S(1)} %copy-done.3, pred[16]{0:T(512)(128)(4,1)S(1)} %get-tuple-element.96, pred[16]{0:T(512)(128)(4,1)S(1)} %get-tuple-element.94, ...), kind=kLoop, calls=%fused_computation.1 | loop fusion | flops 122880 | bytes 266288 | tf_op jit(solution)/shard_map/jit(_where)/select_n | solution.py:466
  10.0 7.5 %all-to-all-start = ((f32[16,5,4,128]{3,2,1,0:T(4,128)}), f32[16,5,4,128]{3,2,1,0:T(4,128)S(1)}, u32[]{:S(2)}, u32[]{:S(2)}) async-start(f32[16,5,4,128]{3,2,1,0:T(4,128)} %select_select_fusion), calls=%async_computation | async-start | bytes 327680 | tf_op jit(solution)/shard_map/all_to_all | solution.py:469
  17.5 1.6 %collective-permute-start = (f32[5,4,4,128]{3,2,1,0:T(4,128)S(1)}, f32[5,4,4,128]{3,2,1,0:T(4,128)S(1)}, u32[]{:S(2)}, u32[]{:S(2)}) collective-permute-start(f32[5,4,4,128]{3,2,1,0:T(4,128)S(1)} %bitcast.82), channel_id=1, source_target_pairs={{0,8},{8,0},{1,9},{9,1},{2,10},{10,2},{3,11},{11,3},{4,12},{12,4},... | collective-permute-start | bytes 122888 | tf_op jit(solution)/shard_map/ppermute | solution.py:431
  19.1 2.5 %collective-permute-done.first_ref = f32[5,4,4,128]{3,2,1,0:T(4,128)S(1)} collective-permute-done((f32[5,4,4,128]{3,2,1,0:T(4,128)S(1)}, f32[5,4,4,128]{3,2,1,0:T(4,128)S(1)}, u32[]{:S(2)}, u32[]{:S(2)}) %collective-permute-start) | collective-permute-done | bytes 40992 | tf_op jit(solution)/shard_map/ppermute | solution.py:431
  21.6 0.6 %copy-done = f32[5,4,4,128]{3,2,1,0:T(4,128)} copy-done((f32[5,4,4,128]{3,2,1,0:T(4,128)}, f32[5,4,4,128]{3,2,1,0:T(4,128)S(1)}, u32[]{:S(2)}) %copy-start) | copy-done | bytes 40984
  22.2 2.4 %shard_map.78.grad_ref = f32[1,5,4,4,4,128]{5,4,3,2,1,0:T(4,128)} custom-call(f32[1,5,4,4,4,128]{5,4,3,2,1,0:T(4,128)} %adj_ref.5, bf16[1,5,4,4,4,128]{5,4,3,2,1,0:T(4,128)(2,1)} %flow_ref.3, f32[5,4,4,128]{3,2,1,0:T(4,128)} %copy-done), custom_call_target="tpu_custom_call" | custom-call | tf_op jit(solution)/shard_map/pallas_call | solution.py:486
  24.6 1.0 %all-to-all-done = f32[16,5,4,128]{3,2,1,0:T(4,128)S(1)} async-done(((f32[16,5,4,128]{3,2,1,0:T(4,128)}), f32[16,5,4,128]{3,2,1,0:T(4,128)S(1)}, u32[]{:S(2)}, u32[]{:S(2)}) %all-to-all-start) | async-done | bytes 163872 | tf_op jit(solution)/shard_map/all_to_all | solution.py:469
  25.6 0.6 %dynamic-slice_bitcast_fusion.2 = (f32[5,4,128]{2,1,0:T(4,128)S(1)}, f32[5,4,128]{2,1,0:T(4,128)S(1)}, f32[5,4,128]{2,1,0:T(4,128)S(1)}, f32[5,4,128]{2,1,0:T(4,128)}, f32[5,4,128]{2,1,0:T(4,128)}) fusion(f32[16,5,4,128]{3,2,1,0:T(4,128)S(1)} %all-to-all-done, s32[]{:T(128)S(6)} %select_n.200, s32[]{:T(128)S(6)} %select_n.204, s32[]{:T(128)S(6)} %select_n.202, ...), kind=kLoop, calls=%fused_computation.156 | loop fusion | bytes 102420 | tf_op jit(solution)/shard_map/jit(dynamic_index_in_dim)/squeeze | solution.py:475
  26.5 1.4 %fusion.2 = f32[5,16,16]{2,1,0:T(8,128)} fusion(f32[5,16,16]{2,1,0:T(8,128)S(1)} %reshape.126, f32[5,16,16]{2,1,0:T(8,128)S(1)} %reshape.125, f32[5,16,16]{2,1,0:T(8,128)S(1)} %reshape.124, f32[16,16]{1,0:T(8,128)S(1)} %get-tuple-element.25, f32[16,16]{1,0:T(8,128)S(1)} %get-tuple-element.26, f32[16,16]{1,0:T(8,128)S(1)} %get-tuple-element.27, ...), kind=kLoop, calls=%fused_computation.6 | loop fusion | flops 119040 | bytes 52225 | tf_op jit(solution)/shard_map/jit(_where)/select_n | solution.py:483
  27.9 2.6 %shard_map.79 = (f32[1,5,4,4,4,128]{5,4,3,2,1,0:T(4,128)}, f32[1,5,4,4,4,128]{5,4,3,2,1,0:T(4,128)}) custom-call(f32[1,5,4,4,4,128]{5,4,3,2,1,0:T(4,128)} %adj_ref.5, bf16[1,5,4,4,4,128]{5,4,3,2,1,0:T(4,128)(2,1)} %flow_ref.3, f32[1,5,4,4,4,128]{5,4,3,2,1,0:T(4,128)} %shard_map.78.grad_ref, f32[5,4,128]{2,1,0:T(4,128)} %get-tuple-element.59.up_az_ref, ...), custom_call_target="tpu_custom_call" | custom-call | tf_op jit(solution)/shard_map/pallas_call | solution.py:487
  (36 shorter events, 1.2 us)
Async XLA Ops:
  5.2 0.7 %copy-start.6 = (s32[4,256]{1,0:T(4,128)S(1)}, s32[4,256]{1,0:T(4,128)}, u32[]{:S(2)}) copy-start(s32[4,256]{1,0:T(4,128)} %get-tuple-element.14) | copy-start | bytes 12292
  5.9 0.7 %copy-start.5 = (f32[4,256]{1,0:T(4,128)S(1)}, f32[4,256]{1,0:T(4,128)}, u32[]{:S(2)}) copy-start(f32[4,256]{1,0:T(4,128)} %get-tuple-element.15) | copy-start | bytes 12292
  8.5 0.7 %copy-start.3 = (f32[5,4,128]{2,1,0:T(4,128)S(1)}, f32[5,4,128]{2,1,0:T(4,128)}, u32[]{:S(2)}) copy-start(f32[5,4,128]{2,1,0:T(4,128)} %get-tuple-element.11) | copy-start | bytes 30724
  8.5 0.7 %copy-start.4 = (f32[5,4,128]{2,1,0:T(4,128)S(1)}, f32[5,4,128]{2,1,0:T(4,128)}, u32[]{:S(2)}) copy-start(f32[5,4,128]{2,1,0:T(4,128)} %get-tuple-element.12) | copy-start | bytes 30724
  10.0 7.5 %copy-start.1 = (f32[5,4,4,128]{3,2,1,0:T(4,128)S(1)}, f32[5,4,4,128]{3,2,1,0:T(4,128)}, u32[]{:S(2)}) copy-start(f32[5,4,4,128]{3,2,1,0:T(4,128)} %get-tuple-element.10) | copy-start | bytes 122884
  10.0 7.5 %copy-start.2 = (f32[5,4,4,128]{3,2,1,0:T(4,128)S(1)}, f32[5,4,4,128]{3,2,1,0:T(4,128)}, u32[]{:S(2)}) copy-start(f32[5,4,4,128]{3,2,1,0:T(4,128)} %get-tuple-element.9) | copy-start | bytes 122884
  10.0 15.6 %all-to-all-start = ((f32[16,5,4,128]{3,2,1,0:T(4,128)}), f32[16,5,4,128]{3,2,1,0:T(4,128)S(1)}, u32[]{:S(2)}, u32[]{:S(2)}) async-start(f32[16,5,4,128]{3,2,1,0:T(4,128)} %select_select_fusion), calls=%async_computation | async-start | bytes 327680 | tf_op jit(solution)/shard_map/all_to_all | solution.py:469
  17.5 4.1 %collective-permute-start = (f32[5,4,4,128]{3,2,1,0:T(4,128)S(1)}, f32[5,4,4,128]{3,2,1,0:T(4,128)S(1)}, u32[]{:S(2)}, u32[]{:S(2)}) collective-permute-start(f32[5,4,4,128]{3,2,1,0:T(4,128)S(1)} %bitcast.82), channel_id=1, source_target_pairs={{0,8},{8,0},{1,9},{9,1},{2,10},{10,2},{3,11},{11,3},{4,12},{12,4},... | collective-permute-start | bytes 122888 | tf_op jit(solution)/shard_map/ppermute | solution.py:431
  21.6 0.6 %copy-start = (f32[5,4,4,128]{3,2,1,0:T(4,128)}, f32[5,4,4,128]{3,2,1,0:T(4,128)S(1)}, u32[]{:S(2)}) copy-start(f32[5,4,4,128]{3,2,1,0:T(4,128)S(1)} %collective-permute-done.first_ref) | copy-start | bytes 122884

commit v16 on v15

--- a/solution.py
+++ b/solution.py
@@ -345,7 +345,7 @@
         grad_ref[0, chan] = grad[chan]
 
 
-def late_kernel(adj_ref, flow_ref, grad_ref, up_az_ref, down_az_ref, sides_ref, rate_ref, next_ref):
+def late_kernel(adj_ref, flow_ref, grad_ref, up_az_ref, down_az_ref, window_ref, coef_ref, rate_ref, next_ref):
     derivs, left_vals, right_vals, left_corr, right_corr = basis_tables()
     shape = (4, 4, 4, 128)
     lane = lax.broadcasted_iota(jnp.int32, shape, 3)
@@ -354,8 +354,18 @@
     radial_lane = lane % ER
     col = lax.broadcasted_iota(jnp.int32, (16, 128), 1)
     row = lax.broadcasted_iota(jnp.int32, (16, 128), 0)
-    sides = sides_ref[...]
     rotor = lax.axis_index("zone") == 0
+    window = window_ref[...]
+    own = []
+    for chan in range(5):
+        rows = window[chan * AP : (chan + 1) * AP]
+        returned = rows[:, :TP] + rows[:, TP : 2 * TP] + rows[:, 2 * TP :]
+        incoming = None
+        for rel in range(-TP, TP - 1):
+            term = coef_ref[rel + TP] * rows[:, TP + rel : 2 * TP + rel]
+            incoming = term if incoming is None else incoming + term
+        own.append(jnp.where(rotor, returned, incoming))
+    sides = jnp.concatenate(own, axis=0)
     spread = [
         exact_dot(sides, jnp.where(row == col // ER % ET * 4 + azim, 1.0, 0.0)) for azim in range(4)
     ]
@@ -477,15 +487,12 @@
         )[:, :2].reshape(5, AP, TP)
         for step in (-1, 0, 1)
     ]
-    returned = picked[0] + picked[1] + picked[2]
-    window = jnp.concatenate(picked, axis=2)
-    incoming = shift_sum(window, coefs, TP)
-    sides = jnp.where(is_rotor, returned, incoming).reshape(5 * AP, TP)
+    window = jnp.concatenate(picked, axis=2).reshape(5 * AP, 3 * TP)
     field_shape = jax.ShapeDtypeStruct(adjoint.shape, jnp.float32)
     early_in = (adjoint, flow_prim, got_first) + (() if got_second is None else (got_second,))
     partial = pl.pallas_call(early_kernel, out_shape=field_shape)(*early_in)
     adjoint_rate, next_adjoint = pl.pallas_call(late_kernel, out_shape=(field_shape, field_shape))(
-        adjoint, flow_prim, partial, up_az, down_az, sides
+        adjoint, flow_prim, partial, up_az, down_az, window, coef_all
     )
     return (adjoint_rate, next_adjoint)
 

time: 30.9 us -> 31.5 us (1.019)
  Pallas kernels: 7.09 us -> 7.76 us
  other arithmetic: 3.08 us -> 2.43 us
  local copies, waits for them, and re-layouts: 6.12 us -> 6.73 us
    select_n x1 -> x0, other arithmetic: 1.35 us -> none  [local(): sides = jnp.where(is_rotor, returned, incoming).reshape(5 * AP, TP)]
    concatenate x0 -> x1, other arithmetic: none -> 0.71 us  [local(): window = jnp.concatenate(picked, axis=2).reshape(5 * AP, 3 * TP)]
    pallas_call x1, Pallas kernels: 2.55 us -> 3.22 us  [local(): pl.pallas_call(late_kernel, out_shape=(field_shape, field_shape))]
    unnamed x14 -> x16, local copies, waits for them, and re-layouts: 2.4 us -> 3.03 us
where the time goes in v16:
time: 31.5 us; the launch traced here: 31 us
  starting transfers between devices  9.07 us (29%)
  Pallas kernels  7.76 us (25%)
  local copies, waits for them, and re-layouts  6.73 us (21%)
  waiting for transfers between devices  3.48 us (11%)
  other arithmetic  2.43 us (8%)
  between operations  1.56 us (5%)
    all_to_all x1, starting transfers between devices, local(): got = lax.all_to_all(chunks, ('zone', 'azim'), 0, 0)  7.49 us
    pallas_call x1, Pallas kernels, local(): pl.pallas_call(late_kernel, out_shape=(field_shape, field_shape))  3.22 us
    unnamed x16, local copies, waits for them, and re-layouts  3.03 us
    ppermute x1, waiting for transfers between devices, local(): got_first = lax.ppermute(jnp.where(even, right_ax, left_ax), 'axial', first)  2.48 us
    pallas_call x1, Pallas kernels, local(): partial = pl.pallas_call(early_kernel, out_shape=field_shape)(*early_in)  2.4 us
    pallas_call x1, Pallas kernels, local(): pl.pallas_call(moment_kernel, out_shape=(face4, face4, chunk, chunk, jax....  2.14 us
    ppermute x1, starting transfers between devices, local(): got_first = lax.ppermute(jnp.where(even, right_ax, left_ax), 'axial', first)  1.58 us
    reshape x2, local copies, waits for them, and re-layouts, local(): own_face.reshape(5, 4, 4, EA, ET).transpose(0, 3, 1, 4, 2)  1.03 us
  transfers between devices with their start and end apart: 2, of which 2 were waited for; matrix products, arithmetic and copies ran while one was open for 0% of the time, Pallas kernels for 8%

profile of v16, /device:TPU:0, one launch (start us, length us, event | category | flops | bytes accessed | tf_op | source)
XLA Modules:
  0.0 31.0 jit_solution(13344224050410574978)
XLA Ops:
  1.4 2.1 %shard_map.77 = (f32[5,4,4,128]{3,2,1,0:T(4,128)}, f32[5,4,4,128]{3,2,1,0:T(4,128)}, f32[5,4,128]{2,1,0:T(4,128)}, f32[5,4,128]{2,1,0:T(4,128)}, f32[5,16,16]{2,...) custom-call(f32[1,5,4,4,4,128]{5,4,3,2,1,0:T(4,128)} %adj_ref.5, s32[4,256]{1,0:T(4,128)} %shift_ref.1, ...), custom_call_target="tpu_custom_call" | custom-call | tf_op jit(solution)/shard_map/pallas_call | solution.py:428
  3.5 0.9 %reshape.120 = f32[5,4,4,4,4]{4,3,2,1,0:T(4,128)S(1)} reshape(f32[5,16,16]{2,1,0:T(8,128)} %get-tuple-element.13) | data formatting | bytes 10240 | tf_op jit(solution)/shard_map/reshape | solution.py:446
  4.4 0.6 %copy.8 = f32[5,4,4,4,4]{4,3,2,1,0:T(4,128)S(1)} copy(f32[5,4,4,4,4]{3,1,4,2,0:T(4,128)S(1)} %bitcast.77) | data formatting | bytes 10240 | tf_op jit(solution)/shard_map/transpose | solution.py:446
  5.0 0.2 broadcast_in_dim.145
  5.2 0.1 reshape.121
  5.4 0.5 %copy-done.7 = s32[4,256]{1,0:T(4,128)S(1)} copy-done((s32[4,256]{1,0:T(4,128)S(1)}, s32[4,256]{1,0:T(4,128)}, u32[]{:S(2)}) %copy-start.7) | copy-done | bytes 4120
  5.9 0.7 %copy-done.6 = f32[4,256]{1,0:T(4,128)S(1)} copy-done((f32[4,256]{1,0:T(4,128)S(1)}, f32[4,256]{1,0:T(4,128)}, u32[]{:S(2)}) %copy-start.6) | copy-done | bytes 4120
  7.2 0.2 select_add_fusion.coef_ref
  7.5 0.6 %copy-done = f32[31,16,16]{2,1,0:T(8,128)} copy-done((f32[31,16,16]{2,1,0:T(8,128)}, f32[31,16,16]{2,1,0:T(8,128)S(1)}, u32[]{:S(2)}) %copy-start) | copy-done | bytes 31768
  8.2 0.1 broadcast_multiply_fusion.30
  8.3 0.4 %pad_add_fusion = f32[5,16,48]{2,1,0:T(8,128)S(1)} fusion(f32[5,16,16]{2,1,0:T(8,128)S(1)} %get-tuple-element.64, f32[5,16,16]{2,1,0:T(8,128)S(1)} %get-tuple-element.65, f32[5,16,16]{2,1,0:T(8,128)S(1)} %get-tuple-element.66, f32[5,16,16]{2,1,0:T(8,128)S(1)} %get-tuple-element.67, f32[5,16,16]{2,1,0:T(8,128)S(1)} %get-tuple-element.68, ...), kind=kLoop, calls=%fused_computation.4 | loop fusion | flops 115200 | bytes 174080 | tf_op jit(solution)/shard_map/add | solution.py:459
  8.8 0.1 broadcast_in_dim.157
  9.1 0.1 select_select_fusion.1
  9.2 0.6 %copy-done.4 = f32[5,4,128]{2,1,0:T(4,128)S(1)} copy-done((f32[5,4,128]{2,1,0:T(4,128)S(1)}, f32[5,4,128]{2,1,0:T(4,128)}, u32[]{:S(2)}) %copy-start.4) | copy-done | bytes 10264
  9.8 0.8 %select_select_fusion = f32[16,5,4,128]{3,2,1,0:T(4,128)} fusion(f32[16,5,2,128]{3,2,1,0:T(2,128)S(1)} %select_select_fusion.1, f32[5,4,128]{2,1,0:T(4,128)S(1)} %copy-done.5, f32[5,4,128]{2,1,0:T(4,128)S(1)} %copy-done.4, pred[16]{0:T(512)(128)(4,1)S(1)} %get-tuple-element.96, pred[16]{0:T(512)(128)(4,1)S(1)} %get-tuple-element.94, ...), kind=kLoop, calls=%fused_computation.1 | loop fusion | flops 122880 | bytes 266288 | tf_op jit(solution)/shard_map/jit(_where)/select_n | solution.py:476
  10.6 7.5 %all-to-all-start = ((f32[16,5,4,128]{3,2,1,0:T(4,128)}), f32[16,5,4,128]{3,2,1,0:T(4,128)S(1)}, u32[]{:S(2)}, u32[]{:S(2)}) async-start(f32[16,5,4,128]{3,2,1,0:T(4,128)} %select_select_fusion), calls=%async_computation | async-start | bytes 327680 | tf_op jit(solution)/shard_map/all_to_all | solution.py:479
  18.1 1.6 %collective-permute-start = (f32[5,4,4,128]{3,2,1,0:T(4,128)S(1)}, f32[5,4,4,128]{3,2,1,0:T(4,128)S(1)}, u32[]{:S(2)}, u32[]{:S(2)}) collective-permute-start(f32[5,4,4,128]{3,2,1,0:T(4,128)S(1)} %bitcast.80), channel_id=1, source_target_pairs={{0,8},{8,0},{1,9},{9,1},{2,10},{10,2},{3,11},{11,3},{4,12},{12,4},... | collective-permute-start | bytes 122888 | tf_op jit(solution)/shard_map/ppermute | solution.py:441
  19.7 2.5 %collective-permute-done.first_ref = f32[5,4,4,128]{3,2,1,0:T(4,128)S(1)} collective-permute-done((f32[5,4,4,128]{3,2,1,0:T(4,128)S(1)}, f32[5,4,4,128]{3,2,1,0:T(4,128)S(1)}, u32[]{:S(2)}, u32[]{:S(2)}) %collective-permute-start) | collective-permute-done | bytes 40992 | tf_op jit(solution)/shard_map/ppermute | solution.py:441
  22.2 0.6 %copy-done.1 = f32[5,4,4,128]{3,2,1,0:T(4,128)} copy-done((f32[5,4,4,128]{3,2,1,0:T(4,128)}, f32[5,4,4,128]{3,2,1,0:T(4,128)S(1)}, u32[]{:S(2)}) %copy-start.1) | copy-done | bytes 40984
  22.8 2.4 %shard_map.78.grad_ref = f32[1,5,4,4,4,128]{5,4,3,2,1,0:T(4,128)} custom-call(f32[1,5,4,4,4,128]{5,4,3,2,1,0:T(4,128)} %adj_ref.5, bf16[1,5,4,4,4,128]{5,4,3,2,1,0:T(4,128)(2,1)} %flow_ref.3, f32[5,4,4,128]{3,2,1,0:T(4,128)} %copy-done.1), custom_call_target="tpu_custom_call" | custom-call | tf_op jit(solution)/shard_map/pallas_call | solution.py:493
  25.2 1.0 %all-to-all-done = f32[16,5,4,128]{3,2,1,0:T(4,128)S(1)} async-done(((f32[16,5,4,128]{3,2,1,0:T(4,128)}), f32[16,5,4,128]{3,2,1,0:T(4,128)S(1)}, u32[]{:S(2)}, u32[]{:S(2)}) %all-to-all-start) | async-done | bytes 163872 | tf_op jit(solution)/shard_map/all_to_all | solution.py:479
  26.2 0.6 %dynamic-slice_bitcast_fusion.2 = (f32[5,4,128]{2,1,0:T(4,128)S(1)}, f32[5,4,128]{2,1,0:T(4,128)S(1)}, f32[5,4,128]{2,1,0:T(4,128)S(1)}, f32[5,4,128]{2,1,0:T(4,128)}, f32[5,4,128]{2,1,0:T(4,128)}) fusion(f32[16,5,4,128]{3,2,1,0:T(4,128)S(1)} %all-to-all-done, s32[]{:T(128)S(6)} %select_n.191, s32[]{:T(128)S(6)} %select_n.195, s32[]{:T(128)S(6)} %select_n.193, ...), kind=kLoop, calls=%fused_computation.39 | loop fusion | bytes 102420 | tf_op jit(solution)/shard_map/jit(dynamic_index_in_dim)/squeeze | solution.py:485
  27.1 0.7 %pad_maximum_fusion.window_ref = f32[80,48]{1,0:T(8,128)} fusion(f32[80,16]{1,0:T(8,128)S(1)} %concatenate.12, f32[80,16]{1,0:T(8,128)S(1)} %concatenate.11, f32[80,16]{1,0:T(8,128)S(1)} %concatenate.10), kind=kLoop, calls=%fused_computation.3 | loop fusion | flops 7680 | bytes 30720 | tf_op jit(solution)/shard_map/concatenate | solution.py:490
  27.8 3.2 %shard_map.79 = (f32[1,5,4,4,4,128]{5,4,3,2,1,0:T(4,128)}, f32[1,5,4,4,4,128]{5,4,3,2,1,0:T(4,128)}) custom-call(f32[1,5,4,4,4,128]{5,4,3,2,1,0:T(4,128)} %adj_ref.5, bf16[1,5,4,4,4,128]{5,4,3,2,1,0:T(4,128)(2,1)} %flow_ref.3, f32[1,5,4,4,4,128]{5,4,3,2,1,0:T(4,128)} %shard_map.78.grad_ref, f32[5,4,128]{2,1,0:T(4,128)} %get-tuple-element.59.up_az_ref, ...), custom_call_target="tpu_custom_call" | custom-call | tf_op jit(solution)/shard_map/pallas_call | solution.py:494
  (38 shorter events, 1.3 us)
Async XLA Ops:
  5.2 0.7 %copy-start.7 = (s32[4,256]{1,0:T(4,128)S(1)}, s32[4,256]{1,0:T(4,128)}, u32[]{:S(2)}) copy-start(s32[4,256]{1,0:T(4,128)} %get-tuple-element.14) | copy-start | bytes 12292
  5.9 0.7 %copy-start.6 = (f32[4,256]{1,0:T(4,128)S(1)}, f32[4,256]{1,0:T(4,128)}, u32[]{:S(2)}) copy-start(f32[4,256]{1,0:T(4,128)} %get-tuple-element.15) | copy-start | bytes 12292
  7.4 0.7 %copy-start = (f32[31,16,16]{2,1,0:T(8,128)}, f32[31,16,16]{2,1,0:T(8,128)S(1)}, u32[]{:S(2)}) copy-start(f32[31,16,16]{2,1,0:T(8,128)S(1)} %select_add_fusion.coef_ref) | copy-start | bytes 95236
  9.1 0.7 %copy-start.4 = (f32[5,4,128]{2,1,0:T(4,128)S(1)}, f32[5,4,128]{2,1,0:T(4,128)}, u32[]{:S(2)}) copy-start(f32[5,4,128]{2,1,0:T(4,128)} %get-tuple-element.11) | copy-start | bytes 30724
  9.1 0.7 %copy-start.5 = (f32[5,4,128]{2,1,0:T(4,128)S(1)}, f32[5,4,128]{2,1,0:T(4,128)}, u32[]{:S(2)}) copy-start(f32[5,4,128]{2,1,0:T(4,128)} %get-tuple-element.12) | copy-start | bytes 30724
  10.6 7.5 %copy-start.2 = (f32[5,4,4,128]{3,2,1,0:T(4,128)S(1)}, f32[5,4,4,128]{3,2,1,0:T(4,128)}, u32[]{:S(2)}) copy-start(f32[5,4,4,128]{3,2,1,0:T(4,128)} %get-tuple-element.10) | copy-start | bytes 122884
  10.6 7.5 %copy-start.3 = (f32[5,4,4,128]{3,2,1,0:T(4,128)S(1)}, f32[5,4,4,128]{3,2,1,0:T(4,128)}, u32[]{:S(2)}) copy-start(f32[5,4,4,128]{3,2,1,0:T(4,128)} %get-tuple-element.9) | copy-start | bytes 122884
  10.6 15.6 %all-to-all-start = ((f32[16,5,4,128]{3,2,1,0:T(4,128)}), f32[16,5,4,128]{3,2,1,0:T(4,128)S(1)}, u32[]{:S(2)}, u32[]{:S(2)}) async-start(f32[16,5,4,128]{3,2,1,0:T(4,128)} %select_select_fusion), calls=%async_computation | async-start | bytes 327680 | tf_op jit(solution)/shard_map/all_to_all | solution.py:479
  18.1 4.1 %collective-permute-start = (f32[5,4,4,128]{3,2,1,0:T(4,128)S(1)}, f32[5,4,4,128]{3,2,1,0:T(4,128)S(1)}, u32[]{:S(2)}, u32[]{:S(2)}) collective-permute-start(f32[5,4,4,128]{3,2,1,0:T(4,128)S(1)} %bitcast.80), channel_id=1, source_target_pairs={{0,8},{8,0},{1,9},{9,1},{2,10},{10,2},{3,11},{11,3},{4,12},{12,4},... | collective-permute-start | bytes 122888 | tf_op jit(solution)/shard_map/ppermute | solution.py:441
  22.2 0.6 %copy-start.1 = (f32[5,4,4,128]{3,2,1,0:T(4,128)}, f32[5,4,4,128]{3,2,1,0:T(4,128)S(1)}, u32[]{:S(2)}) copy-start(f32[5,4,4,128]{3,2,1,0:T(4,128)S(1)} %collective-permute-done.first_ref) | copy-start | bytes 122884

commit v17 on v15

--- a/solution.py
+++ b/solution.py
@@ -271,10 +271,11 @@
     speed_sq = prim[1] * prim[1] + prim[2] * prim[2] + prim[3] * prim[3]
     energy = prim[4] / (GAMMA - 1.0) + 0.5 * density * speed_sq
     momentum = [density * prim[1 + k] for k in range(3)]
-    velocity = [momentum[k] / density for k in range(3)]
+    inverse = 1.0 / density
+    velocity = [momentum[k] * inverse for k in range(3)]
     kinetic = momentum[0] * velocity[0] + momentum[1] * velocity[1] + momentum[2] * velocity[2]
     pressure = (GAMMA - 1.0) * (energy - 0.5 * kinetic)
-    enthalpy = (energy + pressure) / density
+    enthalpy = (energy + pressure) * inverse
     vel_sq = velocity[0] * velocity[0] + velocity[1] * velocity[1] + velocity[2] * velocity[2]
     return velocity, enthalpy, vel_sq
 

time: 30.9 us -> 30.9 us (level)
  no operation moved by 1% of the time
where the time goes in v17:
time: 30.9 us; the launch traced here: 30.4 us
  starting transfers between devices  9.07 us (29%)
  Pallas kernels  7.09 us (23%)
  local copies, waits for them, and re-layouts  6.12 us (20%)
  waiting for transfers between devices  3.49 us (11%)
  other arithmetic  3.08 us (10%)
  between operations  1.56 us (5%)
    all_to_all x1, starting transfers between devices, local(): got = lax.all_to_all(chunks, ('zone', 'azim'), 0, 0)  7.49 us
    pallas_call x1, Pallas kernels, local(): pl.pallas_call(late_kernel, out_shape=(field_shape, field_shape))  2.55 us
    ppermute x1, waiting for transfers between devices, local(): got_first = lax.ppermute(jnp.where(even, right_ax, left_ax), 'axial', first)  2.48 us
    unnamed x14, local copies, waits for them, and re-layouts  2.4 us
    pallas_call x1, Pallas kernels, local(): partial = pl.pallas_call(early_kernel, out_shape=field_shape)(*early_in)  2.39 us
    pallas_call x1, Pallas kernels, local(): pl.pallas_call(moment_kernel, out_shape=(face4, face4, chunk, chunk, jax....  2.14 us
    ppermute x1, starting transfers between devices, local(): got_first = lax.ppermute(jnp.where(even, right_ax, left_ax), 'axial', first)  1.58 us
    select_n x1, other arithmetic, local(): sides = jnp.where(is_rotor, returned, incoming).reshape(5 * AP, TP)  1.35 us
  transfers between devices with their start and end apart: 2, of which 2 were waited for; matrix products, arithmetic and copies ran while one was open for 0% of the time, Pallas kernels for 8%

profile of v17, /device:TPU:0, one launch (start us, length us, event | category | flops | bytes accessed | tf_op | source)
XLA Modules:
  0.0 30.4 jit_solution(5769419999687827570)
XLA Ops:
  1.4 2.1 %shard_map.77 = (f32[5,4,4,128]{3,2,1,0:T(4,128)}, f32[5,4,4,128]{3,2,1,0:T(4,128)}, f32[5,4,128]{2,1,0:T(4,128)}, f32[5,4,128]{2,1,0:T(4,128)}, f32[5,16,16]{2,...) custom-call(f32[1,5,4,4,4,128]{5,4,3,2,1,0:T(4,128)} %adj_ref.5, s32[4,256]{1,0:T(4,128)} %shift_ref.1, ...), custom_call_target="tpu_custom_call" | custom-call | tf_op jit(solution)/shard_map/pallas_call | solution.py:419
  3.5 0.9 %reshape.122 = f32[5,4,4,4,4]{4,3,2,1,0:T(4,128)S(1)} reshape(f32[5,16,16]{2,1,0:T(8,128)} %get-tuple-element.13) | data formatting | bytes 10240 | tf_op jit(solution)/shard_map/reshape | solution.py:437
  4.4 0.6 %copy.9 = f32[5,4,4,4,4]{4,3,2,1,0:T(4,128)S(1)} copy(f32[5,4,4,4,4]{3,1,4,2,0:T(4,128)S(1)} %bitcast.78) | data formatting | bytes 10240 | tf_op jit(solution)/shard_map/transpose | solution.py:437
  5.0 0.2 broadcast_in_dim.145
  5.2 0.1 reshape.123
  5.4 0.5 %copy-done.6 = s32[4,256]{1,0:T(4,128)S(1)} copy-done((s32[4,256]{1,0:T(4,128)S(1)}, s32[4,256]{1,0:T(4,128)}, u32[]{:S(2)}) %copy-start.6) | copy-done | bytes 4120
  5.9 0.7 %copy-done.5 = f32[4,256]{1,0:T(4,128)S(1)} copy-done((f32[4,256]{1,0:T(4,128)S(1)}, f32[4,256]{1,0:T(4,128)}, u32[]{:S(2)}) %copy-start.5) | copy-done | bytes 4120
  7.2 0.2 select_add_fusion
  7.5 0.1 broadcast_multiply_fusion.30
  7.6 0.4 %pad_add_fusion = f32[5,16,48]{2,1,0:T(8,128)S(1)} fusion(f32[5,16,16]{2,1,0:T(8,128)S(1)} %get-tuple-element.64, f32[5,16,16]{2,1,0:T(8,128)S(1)} %get-tuple-element.65, f32[5,16,16]{2,1,0:T(8,128)S(1)} %get-tuple-element.66, f32[5,16,16]{2,1,0:T(8,128)S(1)} %get-tuple-element.67, f32[5,16,16]{2,1,0:T(8,128)S(1)} %get-tuple-element.68, ...), kind=kLoop, calls=%fused_computation.121 | loop fusion | flops 115200 | bytes 174080 | tf_op jit(solution)/shard_map/add | solution.py:450
  8.1 0.1 broadcast_in_dim.157
  8.3 0.1 broadcast_in_dim.160
  8.5 0.1 select_select_fusion.1
  8.6 0.6 %copy-done.3 = f32[5,4,128]{2,1,0:T(4,128)S(1)} copy-done((f32[5,4,128]{2,1,0:T(4,128)S(1)}, f32[5,4,128]{2,1,0:T(4,128)}, u32[]{:S(2)}) %copy-start.3) | copy-done | bytes 10264
  9.2 0.8 %select_select_fusion = f32[16,5,4,128]{3,2,1,0:T(4,128)} fusion(f32[16,5,2,128]{3,2,1,0:T(2,128)S(1)} %select_select_fusion.1, f32[5,4,128]{2,1,0:T(4,128)S(1)} %copy-done.4, f32[5,4,128]{2,1,0:T(4,128)S(1)} %copy-done.3, pred[16]{0:T(512)(128)(4,1)S(1)} %get-tuple-element.96, pred[16]{0:T(512)(128)(4,1)S(1)} %get-tuple-element.94, ...), kind=kLoop, calls=%fused_computation.1 | loop fusion | flops 122880 | bytes 266288 | tf_op jit(solution)/shard_map/jit(_where)/select_n | solution.py:467
  10.0 7.5 %all-to-all-start = ((f32[16,5,4,128]{3,2,1,0:T(4,128)}), f32[16,5,4,128]{3,2,1,0:T(4,128)S(1)}, u32[]{:S(2)}, u32[]{:S(2)}) async-start(f32[16,5,4,128]{3,2,1,0:T(4,128)} %select_select_fusion), calls=%async_computation | async-start | bytes 327680 | tf_op jit(solution)/shard_map/all_to_all | solution.py:470
  17.5 1.6 %collective-permute-start = (f32[5,4,4,128]{3,2,1,0:T(4,128)S(1)}, f32[5,4,4,128]{3,2,1,0:T(4,128)S(1)}, u32[]{:S(2)}, u32[]{:S(2)}) collective-permute-start(f32[5,4,4,128]{3,2,1,0:T(4,128)S(1)} %bitcast.82), channel_id=1, source_target_pairs={{0,8},{8,0},{1,9},{9,1},{2,10},{10,2},{3,11},{11,3},{4,12},{12,4},... | collective-permute-start | bytes 122888 | tf_op jit(solution)/shard_map/ppermute | solution.py:432
  19.1 2.5 %collective-permute-done.first_ref = f32[5,4,4,128]{3,2,1,0:T(4,128)S(1)} collective-permute-done((f32[5,4,4,128]{3,2,1,0:T(4,128)S(1)}, f32[5,4,4,128]{3,2,1,0:T(4,128)S(1)}, u32[]{:S(2)}, u32[]{:S(2)}) %collective-permute-start) | collective-permute-done | bytes 40992 | tf_op jit(solution)/shard_map/ppermute | solution.py:432
  21.6 0.6 %copy-done = f32[5,4,4,128]{3,2,1,0:T(4,128)} copy-done((f32[5,4,4,128]{3,2,1,0:T(4,128)}, f32[5,4,4,128]{3,2,1,0:T(4,128)S(1)}, u32[]{:S(2)}) %copy-start) | copy-done | bytes 40984
  22.2 2.4 %shard_map.78.grad_ref = f32[1,5,4,4,4,128]{5,4,3,2,1,0:T(4,128)} custom-call(f32[1,5,4,4,4,128]{5,4,3,2,1,0:T(4,128)} %adj_ref.5, bf16[1,5,4,4,4,128]{5,4,3,2,1,0:T(4,128)(2,1)} %flow_ref.3, f32[5,4,4,128]{3,2,1,0:T(4,128)} %copy-done), custom_call_target="tpu_custom_call" | custom-call | tf_op jit(solution)/shard_map/pallas_call | solution.py:487
  24.6 1.0 %all-to-all-done = f32[16,5,4,128]{3,2,1,0:T(4,128)S(1)} async-done(((f32[16,5,4,128]{3,2,1,0:T(4,128)}), f32[16,5,4,128]{3,2,1,0:T(4,128)S(1)}, u32[]{:S(2)}, u32[]{:S(2)}) %all-to-all-start) | async-done | bytes 163872 | tf_op jit(solution)/shard_map/all_to_all | solution.py:470
  25.6 0.6 %dynamic-slice_bitcast_fusion.2 = (f32[5,4,128]{2,1,0:T(4,128)S(1)}, f32[5,4,128]{2,1,0:T(4,128)S(1)}, f32[5,4,128]{2,1,0:T(4,128)S(1)}, f32[5,4,128]{2,1,0:T(4,128)}, f32[5,4,128]{2,1,0:T(4,128)}) fusion(f32[16,5,4,128]{3,2,1,0:T(4,128)S(1)} %all-to-all-done, s32[]{:T(128)S(6)} %select_n.200, s32[]{:T(128)S(6)} %select_n.204, s32[]{:T(128)S(6)} %select_n.202, ...), kind=kLoop, calls=%fused_computation.156 | loop fusion | bytes 102420 | tf_op jit(solution)/shard_map/jit(dynamic_index_in_dim)/squeeze | solution.py:476
  26.5 1.4 %fusion.2 = f32[5,16,16]{2,1,0:T(8,128)} fusion(f32[5,16,16]{2,1,0:T(8,128)S(1)} %reshape.126, f32[5,16,16]{2,1,0:T(8,128)S(1)} %reshape.125, f32[5,16,16]{2,1,0:T(8,128)S(1)} %reshape.124, f32[16,16]{1,0:T(8,128)S(1)} %get-tuple-element.25, f32[16,16]{1,0:T(8,128)S(1)} %get-tuple-element.26, f32[16,16]{1,0:T(8,128)S(1)} %get-tuple-element.27, ...), kind=kLoop, calls=%fused_computation.6 | loop fusion | flops 119040 | bytes 52225 | tf_op jit(solution)/shard_map/jit(_where)/select_n | solution.py:484
  27.9 2.6 %shard_map.79 = (f32[1,5,4,4,4,128]{5,4,3,2,1,0:T(4,128)}, f32[1,5,4,4,4,128]{5,4,3,2,1,0:T(4,128)}) custom-call(f32[1,5,4,4,4,128]{5,4,3,2,1,0:T(4,128)} %adj_ref.5, bf16[1,5,4,4,4,128]{5,4,3,2,1,0:T(4,128)(2,1)} %flow_ref.3, f32[1,5,4,4,4,128]{5,4,3,2,1,0:T(4,128)} %shard_map.78.grad_ref, f32[5,4,128]{2,1,0:T(4,128)} %get-tuple-element.59.up_az_ref, ...), custom_call_target="tpu_custom_call" | custom-call | tf_op jit(solution)/shard_map/pallas_call | solution.py:488
  (36 shorter events, 1.2 us)
Async XLA Ops:
  5.2 0.7 %copy-start.6 = (s32[4,256]{1,0:T(4,128)S(1)}, s32[4,256]{1,0:T(4,128)}, u32[]{:S(2)}) copy-start(s32[4,256]{1,0:T(4,128)} %get-tuple-element.14) | copy-start | bytes 12292
  5.9 0.7 %copy-start.5 = (f32[4,256]{1,0:T(4,128)S(1)}, f32[4,256]{1,0:T(4,128)}, u32[]{:S(2)}) copy-start(f32[4,256]{1,0:T(4,128)} %get-tuple-element.15) | copy-start | bytes 12292
  8.5 0.7 %copy-start.3 = (f32[5,4,128]{2,1,0:T(4,128)S(1)}, f32[5,4,128]{2,1,0:T(4,128)}, u32[]{:S(2)}) copy-start(f32[5,4,128]{2,1,0:T(4,128)} %get-tuple-element.11) | copy-start | bytes 30724
  8.5 0.7 %copy-start.4 = (f32[5,4,128]{2,1,0:T(4,128)S(1)}, f32[5,4,128]{2,1,0:T(4,128)}, u32[]{:S(2)}) copy-start(f32[5,4,128]{2,1,0:T(4,128)} %get-tuple-element.12) | copy-start | bytes 30724
  10.0 7.5 %copy-start.1 = (f32[5,4,4,128]{3,2,1,0:T(4,128)S(1)}, f32[5,4,4,128]{3,2,1,0:T(4,128)}, u32[]{:S(2)}) copy-start(f32[5,4,4,128]{3,2,1,0:T(4,128)} %get-tuple-element.10) | copy-start | bytes 122884
  10.0 7.5 %copy-start.2 = (f32[5,4,4,128]{3,2,1,0:T(4,128)S(1)}, f32[5,4,4,128]{3,2,1,0:T(4,128)}, u32[]{:S(2)}) copy-start(f32[5,4,4,128]{3,2,1,0:T(4,128)} %get-tuple-element.9) | copy-start | bytes 122884
  10.0 15.6 %all-to-all-start = ((f32[16,5,4,128]{3,2,1,0:T(4,128)}), f32[16,5,4,128]{3,2,1,0:T(4,128)S(1)}, u32[]{:S(2)}, u32[]{:S(2)}) async-start(f32[16,5,4,128]{3,2,1,0:T(4,128)} %select_select_fusion), calls=%async_computation | async-start | bytes 327680 | tf_op jit(solution)/shard_map/all_to_all | solution.py:470
  17.5 4.1 %collective-permute-start = (f32[5,4,4,128]{3,2,1,0:T(4,128)S(1)}, f32[5,4,4,128]{3,2,1,0:T(4,128)S(1)}, u32[]{:S(2)}, u32[]{:S(2)}) collective-permute-start(f32[5,4,4,128]{3,2,1,0:T(4,128)S(1)} %bitcast.82), channel_id=1, source_target_pairs={{0,8},{8,0},{1,9},{9,1},{2,10},{10,2},{3,11},{11,3},{4,12},{12,4},... | collective-permute-start | bytes 122888 | tf_op jit(solution)/shard_map/ppermute | solution.py:432
  21.6 0.6 %copy-start = (f32[5,4,4,128]{3,2,1,0:T(4,128)}, f32[5,4,4,128]{3,2,1,0:T(4,128)S(1)}, u32[]{:S(2)}) copy-start(f32[5,4,4,128]{3,2,1,0:T(4,128)S(1)} %collective-permute-done.first_ref) | copy-start | bytes 122884
